TPU v7x, 512 devices: a whole 4x4x16 slice. The times are simulated.
512 devices in a mesh: seq: 32 (over y, x, core), tp: 16 (over z).
Axes of the slice: x: 4, y: 4, z: 16, core: 2. Of those that a mesh axis runs over, the one named last changes fastest.
Arguments:
- query_vectors: bfloat16 [24576, 4096], P('seq', 'tp'), may hold values from -6 to 6
- key_vectors: bfloat16 [24576, 4096], P('seq', 'tp'), may hold values from -6 to 6
- value_vectors: bfloat16 [24576, 4096], P('seq', 'tp'), may hold values from -6 to 6
- decay_exp: int32 [32, 24576], P('tp', 'seq'), may hold values from 0 to 16
- norm_gain: float32 [4096], P('tp'), may hold values from 0.25 to 1.75
- out_weight: bfloat16 [4096, 5120], P(None, 'tp'), may hold values from -0.09375 to 0.09375
- residual: bfloat16 [24576, 5120], P('seq', 'tp'), may hold values from -6 to 6
Outputs:
- layer_out: bfloat16 [24576, 5120], P('seq', 'tp')
All inputs are finite; a program needn't handle non-finite values.
Results may differ from a plain program's by a relative error of at most 0.0051.
Values may be sent and summed in bfloat16 or wider, within the bound.
No kernel may reach another device: no remote copies, remote signals or barrier semaphores. Data moves between devices by JAX's collectives and lax.ppermute only.
A program may use at most 64 MiB of HBM per device.

v0:
```python
import jax
import jax.numpy as jnp
from jax import lax
from jax.sharding import PartitionSpec as P

HD = 128


def factor(exponents):
    return jnp.exp2(-exponents.astype(jnp.float32) / 16.0)


def local(query_vectors, key_vectors, value_vectors, decay_exp, norm_gain, out_weight, residual):
    tok_rows = query_vectors.shape[0]
    head_count = decay_exp.shape[0]
    query_heads = query_vectors.reshape(tok_rows, head_count, HD)
    key_heads = key_vectors.reshape(tok_rows, head_count, HD)
    value_heads = value_vectors.reshape(tok_rows, head_count, HD)
    local_exp = jnp.cumsum(decay_exp, axis=1)
    block_exp = local_exp[:, -1]
    local_rows = local_exp.T
    scores = jnp.einsum("thd,shd->hts", query_heads, key_heads, preferred_element_type=jnp.float32)
    exp_gap = jnp.abs(local_exp[:, :, None] - local_exp[:, None, :])
    local_weights = (scores * factor(exp_gap)).astype(jnp.bfloat16)
    local_part = jnp.einsum(
        "hts,shd->thd", local_weights, value_heads, preferred_element_type=jnp.float32
    )
    tail_factor = factor(block_exp[None, :] - local_rows)
    head_factor = factor(local_rows)
    keys_fwd = (key_heads * tail_factor[:, :, None]).astype(jnp.bfloat16)
    keys_bwd = (key_heads * head_factor[:, :, None]).astype(jnp.bfloat16)
    summary_fwd = jnp.einsum(
        "shd,she->hde", keys_fwd, value_heads, preferred_element_type=jnp.float32
    )
    summary_bwd = jnp.einsum(
        "shd,she->hde", keys_bwd, value_heads, preferred_element_type=jnp.float32
    )
    block_decay = factor(block_exp)
    zero_state = jnp.zeros((head_count, HD, HD), jnp.float32)
    all_decay, all_fwd, all_bwd = (
        lax.all_gather(block_decay[None], "seq", axis=0, tiled=True),
        lax.all_gather(summary_fwd[None], "seq", axis=0, tiled=True),
        lax.all_gather(summary_bwd[None], "seq", axis=0, tiled=True),
    )
    seq_count = lax.axis_size("seq")
    my_index = lax.axis_index("seq")

    def forward_turn(source, state_pair):
        running, chosen = state_pair
        chosen = jnp.where(source == my_index, running, chosen)
        running = all_decay[source][:, None, None] * running + all_fwd[source]
        return (running, chosen)

    def backward_turn(step_index, state_pair):
        running, chosen = state_pair
        source = seq_count - 1 - step_index
        chosen = jnp.where(source == my_index, running, chosen)
        running = all_decay[source][:, None, None] * running + all_bwd[source]
        return (running, chosen)

    _, state_fwd = lax.fori_loop(0, seq_count, forward_turn, (zero_state, zero_state))
    _, state_bwd = lax.fori_loop(0, seq_count, backward_turn, (zero_state, zero_state))
    state_fwd = state_fwd.astype(jnp.bfloat16)
    state_bwd = state_bwd.astype(jnp.bfloat16)
    remote_fwd = (
        jnp.einsum("thd,hde->the", query_heads, state_fwd, preferred_element_type=jnp.float32)
        * head_factor[:, :, None]
    )
    remote_bwd = (
        jnp.einsum("thd,hde->the", query_heads, state_bwd, preferred_element_type=jnp.float32)
        * tail_factor[:, :, None]
    )
    attention = local_part + remote_fwd + remote_bwd
    scale = lax.rsqrt(jnp.mean(attention * attention, axis=-1, keepdims=True) + 1e-06)
    normed = (attention * scale * norm_gain.reshape(head_count, HD)[None, :, :]).astype(
        jnp.bfloat16
    )
    normed = normed.reshape(tok_rows, head_count * HD)
    mixed = jnp.dot(
        lax.all_gather(normed, "tp", axis=1, tiled=True),
        out_weight,
        preferred_element_type=jnp.float32,
    )
    return (residual.astype(jnp.float32) + mixed).astype(jnp.bfloat16)


def solution(mesh):
    in_specs = (
        P("seq", "tp"),
        P("seq", "tp"),
        P("seq", "tp"),
        P("tp", "seq"),
        P("tp"),
        P(None, "tp"),
        P("seq", "tp"),
    )
    out_specs = P("seq", "tp")
    return jax.shard_map(local, mesh=mesh, in_specs=in_specs, out_specs=out_specs, check_vma=False)
```

profile of v0, /device:TPU:6, one launch (start us, length us, event | category | flops | bytes accessed | tf_op | source)
XLA Modules:
  0.0 277.3 jit_solution(4047780758424585383)
XLA Ops:
  8.5 1.2 copy.35
  9.6 1.9 fusion.11
  11.9 1.9 fusion.13
  14.1 1.2 dynamic-slice
  16.2 53.2 %all-reduce = f32[64]{0:T(128)S(1)} all-reduce(f32[64]{0:T(128)S(1)} %dynamic-update-slice), channel_id=2, replica_groups=mesh['seq'=32,'tp'=16] {'seq'}, use_global_device_ids=true, to_apply=%add | all-reduce | flops 64 | bytes 512
  69.5 4.2 %fusion.3 = f32[768,2,128]{0,2,1:T(8,128)} fusion(s32[2,768]{1,0:T(2,128)S(1)} %get-tuple-element.337, bf16[768,2,128]{0,2,1:T(8,128)(2,1)S(1)} %bitcast.92, bf16[768,256]{1,0:T(8,128)(2,1)} %param.13, bf16[768,256]{1,0:T(8,128)(2,1)} %param.11), kind=kOutput, calls=%fused_computation.9 | convolution fusion | flops 612237312 | bytes 1972224 | tf_op jit(solution)/shard_map/hts,shd->thd/dot_general | solution.py:25
  73.7 3.5 %all-gather.11.cloned.1.call-done = f32[64,128,128]{2,1,0:T(8,128)} async-done(((f32[2,128,128]{2,1,0:T(8,128)}), f32[64,128,128]{2,1,0:T(8,128)}) %all-gather.11.cloned.1.call-update) | async-done | bytes 4194320 | tf_op jit(solution)/shard_map/all_gather | solution.py:43
  77.2 35.0 %while.35 = (s32[]{:T(128)}, f32[2,128,128]{2,1,0:T(8,128)S(1)}, bf16[2,128,128]{2,1,0:T(8,128)(2,1)S(1)}, f32[32,2]{1,0:T(8,128)S(1)}, f32[32,2,128,128]{3,2,1,...) while((s32[]{:T(128)}, f32[2,128,128]{2,1,0:T(8,128)S(1)}, ...), condition=%wide.region_5.6_spmd.clone, body=%wide.region_4.5_spmd.clone.sunk | while | flops 196616 | bytes 655568 | solution.py:62
  78.4 1.0 bitcast_add_fusion.5
  79.5 1.0 bitcast_add_fusion.5
  80.6 1.0 bitcast_add_fusion.5
  81.7 1.0 bitcast_add_fusion.5
  82.8 1.0 bitcast_add_fusion.5
  83.9 1.0 bitcast_add_fusion.5
  85.0 1.0 bitcast_add_fusion.5
  86.1 1.0 bitcast_add_fusion.5
  87.2 1.0 bitcast_add_fusion.5
  89.3 1.0 bitcast_add_fusion.5
  90.4 1.0 bitcast_add_fusion.5
  91.5 1.0 bitcast_add_fusion.5
  92.6 1.0 bitcast_add_fusion.5
  93.7 1.0 bitcast_add_fusion.5
  95.9 1.0 bitcast_add_fusion.5
  97.0 1.0 bitcast_add_fusion.5
  98.1 1.0 bitcast_add_fusion.5
  100.3 1.0 bitcast_add_fusion.5
  101.4 1.0 bitcast_add_fusion.5
  102.5 1.0 bitcast_add_fusion.5
  103.6 1.0 bitcast_add_fusion.5
  104.7 1.0 bitcast_add_fusion.5
  105.8 1.0 bitcast_add_fusion.5
  106.9 1.0 bitcast_add_fusion.5
  108.0 1.0 bitcast_add_fusion.5
  109.1 1.0 bitcast_add_fusion.5
  111.3 1.0 bitcast_add_fusion.5
  112.3 29.0 %all-gather.9.cloned.1.call-done = f32[64,128,128]{2,1,0:T(8,128)} async-done(((f32[2,128,128]{2,1,0:T(8,128)}), f32[64,128,128]{2,1,0:T(8,128)}) %all-gather.9.cloned.1.call-update) | async-done | bytes 4194320 | tf_op jit(solution)/shard_map/all_gather | solution.py:42
  141.2 34.8 %while.34 = (s32[]{:T(128)}, f32[2,128,128]{2,1,0:T(8,128)S(1)}, bf16[2,128,128]{2,1,0:T(8,128)(2,1)S(1)}, f32[32,2]{1,0:T(8,128)S(1)}, f32[32,2,128,128]{3,2,1,0:T(8,128)}, /*index=5*/s32[]{:T(128)}, s32[]{:T(128)}, s32[]{:T(128)}) while((s32[]{:T(128)}, f32[2,128,128]{2,1,0:T(8,128)S(1)}, bf16[2,128,128]{2,1,0:T(8,128)(2,1)S(1)}, ...), condition=%wide.region_3.4_spmd.clone, body=%wide.region_2.3_spmd.clone.sunk | while | flops 196612 | bytes 655506 | solution.py:61
  142.4 1.0 bitcast_add_fusion.4
  143.5 1.0 bitcast_add_fusion.4
  144.6 1.0 bitcast_add_fusion.4
  145.7 1.0 bitcast_add_fusion.4
  146.7 1.0 bitcast_add_fusion.4
  148.9 1.0 bitcast_add_fusion.4
  150.0 1.0 bitcast_add_fusion.4
  152.2 1.0 bitcast_add_fusion.4
  153.3 1.0 bitcast_add_fusion.4
  155.5 1.0 bitcast_add_fusion.4
  156.6 1.0 bitcast_add_fusion.4
  158.7 1.0 bitcast_add_fusion.4
  159.8 1.0 bitcast_add_fusion.4
  160.9 1.0 bitcast_add_fusion.4
  162.0 1.0 bitcast_add_fusion.4
  163.1 1.0 bitcast_add_fusion.4
  164.2 1.0 bitcast_add_fusion.4
  165.3 1.0 bitcast_add_fusion.4
  166.4 1.0 bitcast_add_fusion.4
  167.4 1.0 bitcast_add_fusion.4
  169.6 1.0 bitcast_add_fusion.4
  170.7 1.0 bitcast_add_fusion.4
  172.9 1.0 bitcast_add_fusion.4
  174.0 1.0 bitcast_add_fusion.4
  176.1 1.4 fusion.7
  178.8 86.1 %all-gather.7.cloned.1.call-done = bf16[768,4096]{0,1:T(8,128)(2,1)} async-done(((bf16[768,256]{0,1:T(8,128)(2,1)}), bf16[768,4096]{0,1:T(8,128)(2,1)}) %all-gather.7.cloned.1.call-update) | async-done | bytes 6291472 | tf_op jit(solution)/shard_map/all_gather | solution.py:80
  264.9 5.8 %fusion.8 = bf16[768,320]{0,1:T(8,128)(2,1)} fusion(bf16[4096,320]{0,1:T(8,128)(2,1)S(1)} %copy-done, bf16[768,4096]{0,1:T(8,128)(2,1)} %all-gather.7.cloned.1.call-done, bf16[768,320]{0,1:T(8,128)(2,1)} %param.17), kind=kOutput, calls=%fused_computation.17 | convolution fusion | flops 2014003200 | bytes 9895936 | tf_op jit(solution)/shard_map/dot_general | solution.py:79
  (172 shorter events, 21.4 us)
Async XLA Ops:
  6.5 258.4 %copy-start = (bf16[4096,320]{0,1:T(8,128)(2,1)S(1)}, bf16[4096,320]{0,1:T(8,128)(2,1)}, u32[]{:S(2)}) copy-start(bf16[4096,320]{0,1:T(8,128)(2,1)} %param.16) | copy-start | bytes 7864324
  6.5 70.7 %all-gather.11.cloned.1.call-start = ((), (), s32[]{:S(2)}) async-start(), calls=%async_computation.2 | async-start | bytes 4325376 | tf_op jit(solution)/shard_map/all_gather | solution.py:43
  11.6 129.7 %all-gather.9.cloned.1.call-start = ((), (), s32[]{:S(2)}) async-start(), calls=%async_computation.1 | async-start | bytes 4325376 | tf_op jit(solution)/shard_map/all_gather | solution.py:42
  13.8 251.1 %all-gather.7.cloned.1.call-start = ((), (), s32[]{:S(2)}) async-start(), calls=%async_computation | async-start | bytes 6684672 | tf_op jit(solution)/shard_map/all_gather | solution.py:80
  73.7 102.4 %copy-start.1 = (bf16[768,256]{1,0:T(8,128)(2,1)S(1)}, bf16[768,256]{1,0:T(8,128)(2,1)}, u32[]{:S(2)}) copy-start(bf16[768,256]{1,0:T(8,128)(2,1)} %param.11) | copy-start | bytes 1179652
  77.2 100.7 %copy-start.2 = (f32[256]{0:T(256)S(1)}, f32[256]{0:T(256)}, u32[]{:S(2)}) copy-start(f32[256]{0:T(256)} %param.15) | copy-start | bytes 3076
Sparse Core Ops, SparseCore 0:
  11.7 65.4 all-gather.10
  80.4 60.8 all-gather.8
  178.9 85.9 all-gather.6
where the time goes:
time: 279 us; the launch traced here: 277 us
  waiting for transfers between devices  119 us (43%)
  other arithmetic  69 us (25%)
  blocking collectives  53.2 us (19%)
  matrix products  15.7 us (6%)
  between operations  13.8 us (5%)
  local copies, waits for them, and re-layouts  4.62 us (2%)
    all_gather x1, waiting for transfers between devices, local(): lax.all_gather(normed, 'tp', axis=1, tiled=True)  86.1 us
    unnamed x1, blocking collectives  53.2 us
    add x32, other arithmetic, backward_turn(): running = all_decay[source][:, None, None] * running + all_bwd[source]  31.6 us
    add x32, other arithmetic, forward_turn(): running = all_decay[source][:, None, None] * running + all_fwd[source]  31.6 us
    all_gather x1, waiting for transfers between devices, local(): lax.all_gather(summary_fwd[None], 'seq', axis=0, tiled=True)  29 us
    dot_general x1, matrix products, local(): jnp.dot(lax.all_gather(normed, 'tp', axis=1, tiled=True), out_weight, pre...  5.81 us
  transfers between devices with their start and end apart: 3, of which 3 were waited for; matrix products, arithmetic and copies ran while one was open for 15% of the time, Pallas kernels for 0%

commit v1 on v0

--- a/solution.py
+++ b/solution.py
@@ -8,6 +8,31 @@
 
 def factor(exponents):
     return jnp.exp2(-exponents.astype(jnp.float32) / 16.0)
+
+
+def prefix_scan(decay, summary, direction):
+    seq_count = lax.axis_size("seq")
+    inc_p, inc_s = decay, summary
+    exc_p = jnp.ones_like(decay)
+    exc_s = jnp.zeros_like(summary)
+    shift = 1
+    while shift < seq_count:
+        if direction > 0:
+            pairs = [(i, i + shift) for i in range(seq_count - shift)]
+        else:
+            pairs = [(i + shift, i) for i in range(seq_count - shift)]
+        packed = jnp.concatenate(
+            [inc_s, jnp.broadcast_to(inc_p[:, None, None], (inc_p.shape[0], 8, HD))], axis=1
+        )
+        packed = lax.ppermute(packed, "seq", pairs)
+        got_s, got_p = packed[:, :HD], packed[:, HD, 0]
+        exc_s = exc_p[:, None, None] * got_s + exc_s
+        exc_p = got_p * exc_p
+        if 2 * shift < seq_count:
+            inc_s = inc_p[:, None, None] * got_s + inc_s
+            inc_p = got_p * inc_p
+        shift *= 2
+    return exc_s
 
 
 def local(query_vectors, key_vectors, value_vectors, decay_exp, norm_gain, out_weight, residual):
@@ -36,30 +61,8 @@
         "shd,she->hde", keys_bwd, value_heads, preferred_element_type=jnp.float32
     )
     block_decay = factor(block_exp)
-    zero_state = jnp.zeros((head_count, HD, HD), jnp.float32)
-    all_decay, all_fwd, all_bwd = (
-        lax.all_gather(block_decay[None], "seq", axis=0, tiled=True),
-        lax.all_gather(summary_fwd[None], "seq", axis=0, tiled=True),
-        lax.all_gather(summary_bwd[None], "seq", axis=0, tiled=True),
-    )
-    seq_count = lax.axis_size("seq")
-    my_index = lax.axis_index("seq")
-
-    def forward_turn(source, state_pair):
-        running, chosen = state_pair
-        chosen = jnp.where(source == my_index, running, chosen)
-        running = all_decay[source][:, None, None] * running + all_fwd[source]
-        return (running, chosen)
-
-    def backward_turn(step_index, state_pair):
-        running, chosen = state_pair
-        source = seq_count - 1 - step_index
-        chosen = jnp.where(source == my_index, running, chosen)
-        running = all_decay[source][:, None, None] * running + all_bwd[source]
-        return (running, chosen)
-
-    _, state_fwd = lax.fori_loop(0, seq_count, forward_turn, (zero_state, zero_state))
-    _, state_bwd = lax.fori_loop(0, seq_count, backward_turn, (zero_state, zero_state))
+    state_fwd = prefix_scan(block_decay, summary_fwd, 1)
+    state_bwd = prefix_scan(block_decay, summary_bwd, -1)
     state_fwd = state_fwd.astype(jnp.bfloat16)
     state_bwd = state_bwd.astype(jnp.bfloat16)
     remote_fwd = (

time: 279 us -> 184 us (0.66)
  other arithmetic: 69 us -> 9.45 us
  blocking collectives: 53.2 us -> 0 us
  starting transfers between devices: 0.09 us -> 35.3 us
  waiting for transfers between devices: 119 us -> 105 us
    add x64 -> x6, other arithmetic: 63.1 us -> 1.5 us  [prefix_scan(): inc_s = inc_p[:, None, None] * got_s + inc_s]
    unnamed x1 -> x0, blocking collectives: 53.2 us -> none
    ppermute x0 -> x10, starting transfers between devices: none -> 35.3 us  [prefix_scan(): packed = lax.ppermute(packed, 'seq', pairs)]
    all_gather x2 -> x0, waiting for transfers between devices: 32.5 us -> none  [the longest x1 29 us: local(): lax.all_gather(summary_fwd[None], 'seq', axis=0, tiled=True)]
    ppermute x0 -> x10, waiting for transfers between devices: none -> 17 us  [prefix_scan(): packed = lax.ppermute(packed, 'seq', pairs)]
    mul x0 -> x5, other arithmetic: none -> 3.91 us  [the longest x3 2.3 us: prefix_scan(): inc_p = got_p * inc_p]
    select_n x64 -> x0, other arithmetic: 3.87 us -> none  [the longest x32 1.93 us: forward_turn(): chosen = jnp.where(source == my_index, running, chosen)]
  transfers between devices with their start and end apart: 3 -> 11, of which waited for: 3 -> 8; matrix products, arithmetic and copies ran while one was open for 15% -> 6% of each run, Pallas kernels for 0% -> 0%
where the time goes in v1:
time: 184 us; the launch traced here: 183 us
  waiting for transfers between devices  105 us (57%)
  starting transfers between devices  35.3 us (19%)
  matrix products  15.7 us (9%)
  between operations  13.7 us (7%)
  other arithmetic  9.45 us (5%)
  local copies, waits for them, and re-layouts  3.85 us (2%)
    all_gather x1, waiting for transfers between devices, local(): lax.all_gather(normed, 'tp', axis=1, tiled=True)  87.8 us
    ppermute x10, starting transfers between devices, prefix_scan(): packed = lax.ppermute(packed, 'seq', pairs)  35.3 us
    ppermute x10, waiting for transfers between devices, prefix_scan(): packed = lax.ppermute(packed, 'seq', pairs)  17 us
    dot_general x1, matrix products, local(): jnp.dot(lax.all_gather(normed, 'tp', axis=1, tiled=True), out_weight, pre...  5.81 us
    dot_general x1, matrix products, local(): jnp.einsum('hts,shd->thd', local_weights, value_heads, preferred_element_...  4.16 us
  transfers between devices with their start and end apart: 11, of which 8 were waited for; matrix products, arithmetic and copies ran while one was open for 6% of the time, Pallas kernels for 0%

profile of v1, /device:TPU:6, one launch (start us, length us, event | category | flops | bytes accessed | tf_op | source)
XLA Modules:
  0.0 182.9 jit_solution(5005880839742577590)
XLA Ops:
  6.5 0.0 all-gather.2.cloned.1.call-start
  6.5 0.9 reshape.93
  7.4 0.6 reduce-window.6
  8.0 0.2 slice_reduce_fusion
  8.2 0.2 reduce-window.9
  8.4 0.1 add_bitcast_fusion
  8.5 0.2 slice_reduce_fusion.1
  8.7 0.1 exponential_bitcast_fusion
  8.8 1.9 %copy.29 = bf16[768,256]{0,1:T(8,128)(2,1)} copy(bf16[768,256]{1,0:T(8,128)(2,1)} %param.8) | data formatting | bytes 786432 | tf_op args[1]
  10.7 1.4 fusion.11
  12.1 1.4 fusion.13
  13.5 0.1 broadcast_in_dim.30
  13.6 0.0 copy-done.7
  13.6 2.2 %collective-permute-start.5 = (f32[2,136,128]{2,1,0:T(8,128)S(1)}, f32[2,136,128]{2,1,0:T(8,128)S(1)}, u32[]{:S(2)}, u32[]{:S(2)}) collective-permute-start(f32[2,136,128]{2,1,0:T(8,128)S(1)} %get-tuple-element.25), channel_id=1, source_target_pairs={{16,0},{32,16},{48,32},{64,48},{80,64},{96,80},{112,96},{128,112},... | collective-permute-start | bytes 417800 | tf_op jit(solution)/shard_map/ppermute | solution.py:27
  15.8 2.2 %collective-permute-start = (f32[2,136,128]{2,1,0:T(8,128)S(1)}, f32[2,136,128]{2,1,0:T(8,128)S(1)}, u32[]{:S(2)}, u32[]{:S(2)}) collective-permute-start(f32[2,136,128]{2,1,0:T(8,128)S(1)} %get-tuple-element.26), channel_id=1, source_target_pairs={{0,16},{16,32},{32,48},{48,64},{64,80},{80,96},{96,112},{112,128},... | collective-permute-start | bytes 417800 | tf_op jit(solution)/shard_map/ppermute | solution.py:27
  17.9 0.1 multiply_exponential_fusion
  18.0 0.3 collective-permute-done.5
  18.3 3.8 %collective-permute-done = f32[2,136,128]{2,1,0:T(8,128)S(1)} collective-permute-done((f32[2,136,128]{2,1,0:T(8,128)S(1)}, f32[2,136,128]{2,1,0:T(8,128)S(1)}, u32[]{:S(2)}, u32[]{:S(2)}) %collective-permute-start) | collective-permute-done | bytes 139296 | tf_op jit(solution)/shard_map/ppermute | solution.py:27
  22.1 0.1 multiply_add_fusion.3
  22.2 0.7 slice_reduce_fusion.2
  22.9 0.1 broadcast_in_dim.32
  23.0 7.3 %collective-permute-start.1 = (f32[2,136,128]{2,1,0:T(8,128)S(1)}, f32[2,136,128]{2,1,0:T(8,128)S(1)}, u32[]{:S(2)}, u32[]{:S(2)}) collective-permute-start(f32[2,136,128]{2,1,0:T(8,128)S(1)} %pad_maximum_fusion.2), channel_id=1, source_target_pairs={{0,32},{16,48},{32,64},{48,80},{64,96},{80,112},{96,128},{112,144}... | collective-permute-start | bytes 417800 | tf_op jit(solution)/shard_map/ppermute | solution.py:27
  30.4 0.1 broadcast_in_dim.39
  30.5 1.9 %collective-permute-start.6 = (f32[2,136,128]{2,1,0:T(8,128)S(1)}, f32[2,136,128]{2,1,0:T(8,128)S(1)}, u32[]{:S(2)}, u32[]{:S(2)}) collective-permute-start(f32[2,136,128]{2,1,0:T(8,128)S(1)} %pad_maximum_fusion.6), channel_id=1, source_target_pairs={{32,0},{48,16},{64,32},{80,48},{96,64},{112,80},{128,96},{144,112}... | collective-permute-start | bytes 417800 | tf_op jit(solution)/shard_map/ppermute | solution.py:27
  32.4 0.0 copy-done.5
  32.4 0.5 collective-permute-done.1
  33.0 0.1 multiply_add_fusion.6
  33.0 6.5 %collective-permute-done.6 = f32[2,136,128]{2,1,0:T(8,128)S(1)} collective-permute-done((f32[2,136,128]{2,1,0:T(8,128)S(1)}, f32[2,136,128]{2,1,0:T(8,128)S(1)}, u32[]{:S(2)}, u32[]{:S(2)}) %collective-permute-start.6) | collective-permute-done | bytes 139296 | tf_op jit(solution)/shard_map/ppermute | solution.py:27
  39.5 0.6 fusion.53
  40.2 0.1 broadcast_in_dim.33
  40.2 0.7 pad_maximum_fusion.3
  40.9 1.9 %collective-permute-start.2 = (f32[2,136,128]{2,1,0:T(8,128)}, f32[2,136,128]{2,1,0:T(8,128)}, u32[]{:S(2)}, u32[]{:S(2)}) collective-permute-start(f32[2,136,128]{2,1,0:T(8,128)} %pad_maximum_fusion.3), channel_id=1, source_target_pairs={{0,64},{16,80},{32,96},{48,112},{64,128},{80,144},{96,160},{112,17... | collective-permute-start | bytes 417800 | tf_op jit(solution)/shard_map/ppermute | solution.py:27
  42.8 0.1 multiply_add_fusion.2
  42.9 0.1 broadcast_in_dim.40
  43.0 0.7 pad_maximum_fusion.7
  43.7 6.1 %collective-permute-start.7 = (f32[2,136,128]{2,1,0:T(8,128)}, f32[2,136,128]{2,1,0:T(8,128)}, u32[]{:S(2)}, u32[]{:S(2)}) collective-permute-start(f32[2,136,128]{2,1,0:T(8,128)} %pad_maximum_fusion.7), channel_id=1, source_target_pairs={{64,0},{80,16},{96,32},{112,48},{128,64},{144,80},{160,96},{176,11... | collective-permute-start | bytes 417800 | tf_op jit(solution)/shard_map/ppermute | solution.py:27
  49.8 4.2 %fusion.3 = f32[768,2,128]{0,2,1:T(8,128)} fusion(s32[2,768]{1,0:T(2,128)} %copy-done.5, bf16[768,2,128]{0,2,1:T(8,128)(2,1)} %bitcast.73, bf16[768,256]{1,0:T(8,128)(2,1)} %param.9, bf16[768,256]{1,0:T(8,128)(2,1)S(1)} %copy-done.1), kind=kOutput, calls=%fused_computation.3 | convolution fusion | flops 612237312 | bytes 1972224 | tf_op jit(solution)/shard_map/hts,shd->thd/dot_general | solution.py:50
  53.9 0.0 collective-permute-done.2
  53.9 0.9 fusion.48
  54.8 0.0 collective-permute-done.7
  54.8 1.1 multiply_add_fusion.1
  55.9 0.1 broadcast_in_dim.35
  56.0 3.0 %collective-permute-start.3 = (f32[2,136,128]{2,1,0:T(8,128)S(1)}, f32[2,136,128]{2,1,0:T(8,128)S(1)}, u32[]{:S(2)}, u32[]{:S(2)}) collective-permute-start(f32[2,136,128]{2,1,0:T(8,128)S(1)} %pad_maximum_fusion.4), channel_id=1, source_target_pairs={{0,128},{16,144},{32,160},{48,176},{64,192},{80,208},{96,224},{112... | collective-permute-start | bytes 417800 | tf_op jit(solution)/shard_map/ppermute | solution.py:27
  59.0 0.8 fusion.50
  59.8 0.1 broadcast_in_dim.42
  59.9 1.3 collective-permute-start.8
  61.2 0.4 collective-permute-done.3
  61.5 0.1 multiply_add_fusion.4
  61.6 0.8 multiply_reduce_fusion.4
  62.4 0.1 broadcast_in_dim.37
  62.5 8.2 %collective-permute-start.4 = (f32[2,136,128]{2,1,0:T(8,128)S(1)}, f32[2,136,128]{2,1,0:T(8,128)S(1)}, u32[]{:S(2)}, u32[]{:S(2)}) collective-permute-start(f32[2,136,128]{2,1,0:T(8,128)S(1)} %pad_maximum_fusion.5), channel_id=1, source_target_pairs={{0,256},{16,272},{32,288},{48,304},{64,320},{80,336},{96,352},{112... | collective-permute-start | bytes 417800 | tf_op jit(solution)/shard_map/ppermute | solution.py:27
  70.7 0.0 collective-permute-done.8
  70.7 0.1 multiply_add_fusion
  70.8 0.8 multiply_reduce_fusion.2
  71.6 0.1 broadcast_in_dim.44
  71.7 1.3 collective-permute-start.9
  73.0 0.3 collective-permute-done.4
  73.3 1.7 fusion.7
  75.0 5.2 %collective-permute-done.9 = f32[2,136,128]{2,1,0:T(8,128)S(1)} collective-permute-done((f32[2,136,128]{2,1,0:T(8,128)S(1)}, f32[2,136,128]{2,1,0:T(8,128)S(1)}, u32[]{:S(2)}, u32[]{:S(2)}) %collective-permute-start.9) | collective-permute-done | bytes 139296 | tf_op jit(solution)/shard_map/ppermute | solution.py:27
  80.2 1.3 multiply_reduce_fusion
  81.6 0.9 multiply_convert_fusion.4
  82.4 0.0 all-gather.2.cloned.1.call-update
  82.4 87.8 %all-gather.2.cloned.1.call-done = bf16[768,4096]{0,1:T(8,128)(2,1)} async-done(((bf16[768,256]{0,1:T(8,128)(2,1)}), bf16[768,4096]{0,1:T(8,128)(2,1)}) %all-gather.2.cloned.1.call-update) | async-done | bytes 6291472 | tf_op jit(solution)/shard_map/all_gather | solution.py:83
  170.3 5.8 %fusion.8 = bf16[768,320]{0,1:T(8,128)(2,1)} fusion(bf16[4096,320]{0,1:T(8,128)(2,1)S(1)} %copy-done, bf16[768,4096]{0,1:T(8,128)(2,1)} %all-gather.2.cloned.1.call-done, bf16[768,320]{0,1:T(8,128)(2,1)} %param.13), kind=kOutput, calls=%fused_computation.11 | convolution fusion | flops 2014003200 | bytes 9895936 | tf_op jit(solution)/shard_map/dot_general | solution.py:82
  (34 shorter events, 0.2 us)
Async XLA Ops:
  6.5 163.7 %copy-start = (bf16[4096,320]{0,1:T(8,128)(2,1)S(1)}, bf16[4096,320]{0,1:T(8,128)(2,1)}, u32[]{:S(2)}) copy-start(bf16[4096,320]{0,1:T(8,128)(2,1)} %param.12) | copy-start | bytes 7864324
  6.5 43.2 %copy-start.1 = (bf16[768,256]{1,0:T(8,128)(2,1)S(1)}, bf16[768,256]{1,0:T(8,128)(2,1)}, u32[]{:S(2)}) copy-start(bf16[768,256]{1,0:T(8,128)(2,1)} %param.7) | copy-start | bytes 1179652
  6.5 163.7 %all-gather.2.cloned.1.call-start = ((), (), s32[]{:S(2)}) async-start(), calls=%async_computation | async-start | bytes 6684672 | tf_op jit(solution)/shard_map/all_gather | solution.py:83
  8.5 3.6 %copy-start.6 = (f32[768,2]{0,1:T(2,128)}, f32[768,2]{0,1:T(2,128)S(1)}, u32[]{:S(2)}) copy-start(f32[768,2]{0,1:T(2,128)S(1)} %get-tuple-element.21) | copy-start | bytes 18436
  8.5 23.9 %copy-start.5 = (s32[2,768]{1,0:T(2,128)}, s32[2,768]{1,0:T(2,128)S(1)}, u32[]{:S(2)}) copy-start(s32[2,768]{1,0:T(2,128)S(1)} %get-tuple-element.22) | copy-start | bytes 18436
  8.8 4.8 %copy-start.7 = (f32[768,2]{0,1:T(2,128)}, f32[768,2]{0,1:T(2,128)S(1)}, u32[]{:S(2)}) copy-start(f32[768,2]{0,1:T(2,128)S(1)} %exponential_bitcast_fusion) | copy-start | bytes 18436
  13.6 4.8 %collective-permute-start.5 = (f32[2,136,128]{2,1,0:T(8,128)S(1)}, f32[2,136,128]{2,1,0:T(8,128)S(1)}, u32[]{:S(2)}, u32[]{:S(2)}) collective-permute-start(f32[2,136,128]{2,1,0:T(8,128)S(1)} %get-tuple-element.25), channel_id=1, source_target_pairs={{16,0},{32,16},{48,32},{64,48},{80,64},{96,80},{112,96},{128,112},... | collective-permute-start | bytes 417800 | tf_op jit(solution)/shard_map/ppermute | solution.py:27
  15.8 6.4 %collective-permute-start = (f32[2,136,128]{2,1,0:T(8,128)S(1)}, f32[2,136,128]{2,1,0:T(8,128)S(1)}, u32[]{:S(2)}, u32[]{:S(2)}) collective-permute-start(f32[2,136,128]{2,1,0:T(8,128)S(1)} %get-tuple-element.26), channel_id=1, source_target_pairs={{0,16},{16,32},{32,48},{48,64},{64,80},{80,96},{96,112},{112,128},... | collective-permute-start | bytes 417800 | tf_op jit(solution)/shard_map/ppermute | solution.py:27
  23.0 9.9 %collective-permute-start.1 = (f32[2,136,128]{2,1,0:T(8,128)S(1)}, f32[2,136,128]{2,1,0:T(8,128)S(1)}, u32[]{:S(2)}, u32[]{:S(2)}) collective-permute-start(f32[2,136,128]{2,1,0:T(8,128)S(1)} %pad_maximum_fusion.2), channel_id=1, source_target_pairs={{0,32},{16,48},{32,64},{48,80},{64,96},{80,112},{96,128},{112,144}... | collective-permute-start | bytes 417800 | tf_op jit(solution)/shard_map/ppermute | solution.py:27
  30.5 9.1 %collective-permute-start.6 = (f32[2,136,128]{2,1,0:T(8,128)S(1)}, f32[2,136,128]{2,1,0:T(8,128)S(1)}, u32[]{:S(2)}, u32[]{:S(2)}) collective-permute-start(f32[2,136,128]{2,1,0:T(8,128)S(1)} %pad_maximum_fusion.6), channel_id=1, source_target_pairs={{32,0},{48,16},{64,32},{80,48},{96,64},{112,80},{128,96},{144,112}... | collective-permute-start | bytes 417800 | tf_op jit(solution)/shard_map/ppermute | solution.py:27
  33.0 10.0 %copy-start.4 = (f32[2,136,128]{2,1,0:T(8,128)}, f32[2,136,128]{2,1,0:T(8,128)S(1)}, u32[]{:S(2)}) copy-start(f32[2,136,128]{2,1,0:T(8,128)S(1)} %collective-permute-done.1) | copy-start | bytes 417796
  39.5 3.4 %copy-start.2 = (f32[2,136,128]{2,1,0:T(8,128)}, f32[2,136,128]{2,1,0:T(8,128)S(1)}, u32[]{:S(2)}) copy-start(f32[2,136,128]{2,1,0:T(8,128)S(1)} %collective-permute-done.6) | copy-start | bytes 417796
  40.2 3.5 %copy-start.9 = (f32[2]{0:T(128)}, f32[2]{0:T(128)S(1)}, u32[]{:S(2)}) copy-start(f32[2]{0:T(128)S(1)} %get-tuple-element.19) | copy-start | bytes 28
  40.2 3.5 %copy-start.10 = (f32[2]{0:T(128)}, f32[2]{0:T(128)S(1)}, u32[]{:S(2)}) copy-start(f32[2]{0:T(128)S(1)} %get-tuple-element.28) | copy-start | bytes 28
  40.9 13.0 %collective-permute-start.2 = (f32[2,136,128]{2,1,0:T(8,128)}, f32[2,136,128]{2,1,0:T(8,128)}, u32[]{:S(2)}, u32[]{:S(2)}) collective-permute-start(f32[2,136,128]{2,1,0:T(8,128)} %pad_maximum_fusion.3), channel_id=1, source_target_pairs={{0,64},{16,80},{32,96},{48,112},{64,128},{80,144},{96,160},{112,17... | collective-permute-start | bytes 417800 | tf_op jit(solution)/shard_map/ppermute | solution.py:27
  43.7 11.1 %collective-permute-start.7 = (f32[2,136,128]{2,1,0:T(8,128)}, f32[2,136,128]{2,1,0:T(8,128)}, u32[]{:S(2)}, u32[]{:S(2)}) collective-permute-start(f32[2,136,128]{2,1,0:T(8,128)} %pad_maximum_fusion.7), channel_id=1, source_target_pairs={{64,0},{80,16},{96,32},{112,48},{128,64},{144,80},{160,96},{176,11... | collective-permute-start | bytes 417800 | tf_op jit(solution)/shard_map/ppermute | solution.py:27
  53.9 26.3 %copy-start.3 = (f32[2,136,128]{2,1,0:T(8,128)S(1)}, f32[2,136,128]{2,1,0:T(8,128)}, u32[]{:S(2)}) copy-start(f32[2,136,128]{2,1,0:T(8,128)} %copy-done.2) | copy-start | bytes 417796
  53.9 26.3 %copy-start.8 = (f32[768,2]{0,1:T(2,128)S(1)}, f32[768,2]{0,1:T(2,128)}, u32[]{:S(2)}) copy-start(f32[768,2]{0,1:T(2,128)} %copy-done.7) | copy-start | bytes 18436
  53.9 26.3 %copy-start.11 = (f32[2]{0:T(128)S(1)}, f32[2]{0:T(128)}, u32[]{:S(2)}) copy-start(f32[2]{0:T(128)} %get-tuple-element.11) | copy-start | bytes 28
  53.9 27.6 %copy-start.12 = (f32[256]{0:T(256)S(1)}, f32[256]{0:T(256)}, u32[]{:S(2)}) copy-start(f32[256]{0:T(256)} %param.11) | copy-start | bytes 3076
  56.0 5.5 %collective-permute-start.3 = (f32[2,136,128]{2,1,0:T(8,128)S(1)}, f32[2,136,128]{2,1,0:T(8,128)S(1)}, u32[]{:S(2)}, u32[]{:S(2)}) collective-permute-start(f32[2,136,128]{2,1,0:T(8,128)S(1)} %pad_maximum_fusion.4), channel_id=1, source_target_pairs={{0,128},{16,144},{32,160},{48,176},{64,192},{80,208},{96,224},{112... | collective-permute-start | bytes 417800 | tf_op jit(solution)/shard_map/ppermute | solution.py:27
  59.9 10.9 %collective-permute-start.8 = (f32[2,136,128]{2,1,0:T(8,128)S(1)}, f32[2,136,128]{2,1,0:T(8,128)S(1)}, u32[]{:S(2)}, u32[]{:S(2)}) collective-permute-start(f32[2,136,128]{2,1,0:T(8,128)S(1)} %pad_maximum_fusion.8), channel_id=1, source_target_pairs={{128,0},{144,16},{160,32},{176,48},{192,64},{208,80},{224,96},{240... | collective-permute-start | bytes 417800 | tf_op jit(solution)/shard_map/ppermute | solution.py:27
  62.5 10.8 %collective-permute-start.4 = (f32[2,136,128]{2,1,0:T(8,128)S(1)}, f32[2,136,128]{2,1,0:T(8,128)S(1)}, u32[]{:S(2)}, u32[]{:S(2)}) collective-permute-start(f32[2,136,128]{2,1,0:T(8,128)S(1)} %pad_maximum_fusion.5), channel_id=1, source_target_pairs={{0,256},{16,272},{32,288},{48,304},{64,320},{80,336},{96,352},{112... | collective-permute-start | bytes 417800 | tf_op jit(solution)/shard_map/ppermute | solution.py:27
  71.7 8.5 %collective-permute-start.9 = (f32[2,136,128]{2,1,0:T(8,128)S(1)}, f32[2,136,128]{2,1,0:T(8,128)S(1)}, u32[]{:S(2)}, u32[]{:S(2)}) collective-permute-start(f32[2,136,128]{2,1,0:T(8,128)S(1)} %pad_maximum_fusion.9), channel_id=1, source_target_pairs={{256,0},{272,16},{288,32},{304,48},{320,64},{336,80},{352,96},{368... | collective-permute-start | bytes 417800 | tf_op jit(solution)/shard_map/ppermute | solution.py:27
Sparse Core Ops, SparseCore 0:
  82.6 87.6 all-gather.1

commit v2 on v1

--- a/solution.py
+++ b/solution.py
@@ -10,29 +10,38 @@
     return jnp.exp2(-exponents.astype(jnp.float32) / 16.0)
 
 
-def prefix_scan(decay, summary, direction):
+def block_scan(decay, summary_fwd, summary_bwd):
     seq_count = lax.axis_size("seq")
-    inc_p, inc_s = decay, summary
-    exc_p = jnp.ones_like(decay)
-    exc_s = jnp.zeros_like(summary)
+    me = lax.axis_index("seq")
+    heads = decay.shape[0]
+    total_p, total_f, total_b = decay, summary_fwd, summary_bwd
+    prefix_pf = jnp.ones_like(decay)
+    prefix_pb = jnp.ones_like(decay)
+    prefix_f = jnp.zeros_like(summary_fwd)
+    prefix_b = jnp.zeros_like(summary_bwd)
     shift = 1
     while shift < seq_count:
-        if direction > 0:
-            pairs = [(i, i + shift) for i in range(seq_count - shift)]
-        else:
-            pairs = [(i + shift, i) for i in range(seq_count - shift)]
+        pairs = [(i, i ^ shift) for i in range(seq_count)]
         packed = jnp.concatenate(
-            [inc_s, jnp.broadcast_to(inc_p[:, None, None], (inc_p.shape[0], 8, HD))], axis=1
+            [total_f, total_b, jnp.broadcast_to(total_p[:, None, None], (heads, 8, HD))], axis=1
         )
         packed = lax.ppermute(packed, "seq", pairs)
-        got_s, got_p = packed[:, :HD], packed[:, HD, 0]
-        exc_s = exc_p[:, None, None] * got_s + exc_s
-        exc_p = got_p * exc_p
+        got_f, got_b, got_p = packed[:, :HD], packed[:, HD : 2 * HD], packed[:, 2 * HD, 0]
+        lower = (me & shift) != 0
+        prefix_f = prefix_f + jnp.where(lower, prefix_pf, 0.0)[:, None, None] * got_f
+        prefix_b = prefix_b + jnp.where(lower, 0.0, prefix_pb)[:, None, None] * got_b
+        prefix_pf = jnp.where(lower, got_p * prefix_pf, prefix_pf)
+        prefix_pb = jnp.where(lower, prefix_pb, got_p * prefix_pb)
         if 2 * shift < seq_count:
-            inc_s = inc_p[:, None, None] * got_s + inc_s
-            inc_p = got_p * inc_p
+            own_f = jnp.where(lower, 1.0, got_p)[:, None, None]
+            new_f = jnp.where(lower, total_p, 1.0)[:, None, None]
+            own_b = jnp.where(lower, got_p, 1.0)[:, None, None]
+            new_b = jnp.where(lower, 1.0, total_p)[:, None, None]
+            total_f = own_f * total_f + new_f * got_f
+            total_b = own_b * total_b + new_b * got_b
+            total_p = total_p * got_p
         shift *= 2
-    return exc_s
+    return prefix_f, prefix_b
 
 
 def local(query_vectors, key_vectors, value_vectors, decay_exp, norm_gain, out_weight, residual):
@@ -61,8 +70,7 @@
         "shd,she->hde", keys_bwd, value_heads, preferred_element_type=jnp.float32
     )
     block_decay = factor(block_exp)
-    state_fwd = prefix_scan(block_decay, summary_fwd, 1)
-    state_bwd = prefix_scan(block_decay, summary_bwd, -1)
+    state_fwd, state_bwd = block_scan(block_decay, summary_fwd, summary_bwd)
     state_fwd = state_fwd.astype(jnp.bfloat16)
     state_bwd = state_bwd.astype(jnp.bfloat16)
     remote_fwd = (

time: 184 us -> 178 us (0.967)
  starting transfers between devices: 35.3 us -> 16.1 us
  waiting for transfers between devices: 105 us -> 115 us
  other arithmetic: 9.45 us -> 13.4 us
    ppermute x10 -> x5, starting transfers between devices: 35.3 us -> 16.1 us  [block_scan(): packed = lax.ppermute(packed, 'seq', pairs)]
    ppermute x10 -> x5, waiting for transfers between devices: 17 us -> 27.7 us  [block_scan(): packed = lax.ppermute(packed, 'seq', pairs)]
    select_n x0 -> x5, other arithmetic: none -> 5.31 us  [the longest x3 3.47 us: block_scan(): jnp.where(lower, 0.0, prefix_pb)[:, None, None] * got_b]
    mul x5 -> x0, other arithmetic: 3.91 us -> none  [the longest x3 2.3 us: prefix_scan(): inc_p = got_p * inc_p]
  transfers between devices with their start and end apart: 11 -> 6, of which waited for: 8 -> 6; matrix products, arithmetic and copies ran while one was open for 6% -> 2% of each run, Pallas kernels for 0% -> 0%
where the time goes in v2:
time: 178 us; the launch traced here: 177 us
  waiting for transfers between devices  115 us (65%)
  starting transfers between devices  16.1 us (9%)
  matrix products  15.9 us (9%)
  between operations  13.6 us (8%)
  other arithmetic  13.4 us (8%)
  local copies, waits for them, and re-layouts  2.81 us (2%)
    all_gather x1, waiting for transfers between devices, local(): lax.all_gather(normed, 'tp', axis=1, tiled=True)  87.3 us
    ppermute x5, waiting for transfers between devices, block_scan(): packed = lax.ppermute(packed, 'seq', pairs)  27.7 us
    ppermute x5, starting transfers between devices, block_scan(): packed = lax.ppermute(packed, 'seq', pairs)  16.1 us
    dot_general x1, matrix products, local(): jnp.dot(lax.all_gather(normed, 'tp', axis=1, tiled=True), out_weight, pre...  5.81 us
    dot_general x1, matrix products, local(): jnp.einsum('hts,shd->thd', local_weights, value_heads, preferred_element_...  4.16 us
  transfers between devices with their start and end apart: 6, of which 6 were waited for; matrix products, arithmetic and copies ran while one was open for 2% of the time, Pallas kernels for 0%

profile of v2, /device:TPU:6, one launch (start us, length us, event | category | flops | bytes accessed | tf_op | source)
XLA Modules:
  0.0 176.9 jit_solution(3562451099176625884)
XLA Ops:
  6.5 0.0 copy-start
  6.5 0.0 all-gather.2.cloned.1.call-start
  6.5 0.9 reshape.103
  7.4 0.6 reduce-window.6
  8.0 0.2 slice_reduce_fusion
  8.2 0.2 reduce-window.9
  8.4 0.1 add_bitcast_fusion
  8.5 0.0 copy-start.7
  8.5 0.0 copy-start.9
  8.5 0.2 slice_reduce_fusion.1
  8.7 0.1 exponential_bitcast_fusion
  8.8 0.0 copy-start.8
  8.8 0.6 broadcast_select_fusion.29
  9.3 1.2 copy.27
  10.5 0.0 copy-start.6
  10.5 1.4 fusion.11
  11.9 0.0 copy-start.4
  11.9 1.3 fusion.13
  13.2 0.0 copy-start.5
  13.2 0.1 broadcast_in_dim.48
  13.3 0.0 copy-done.6
  13.3 0.0 copy-done.4
  13.3 0.7 pad_maximum_fusion
  14.0 0.0 copy-done.5
  14.0 1.9 %collective-permute-start = (f32[2,264,128]{2,1,0:T(8,128)}, f32[2,264,128]{2,1,0:T(8,128)S(1)}, u32[]{:S(2)}, u32[]{:S(2)}) collective-permute-start(f32[2,264,128]{2,1,0:T(8,128)} %pad_maximum_fusion), channel_id=1, source_target_pairs={{0,16},{16,0},{32,48},{48,32},{64,80},{80,64},{96,112},{112,96},{1... | collective-permute-start | bytes 811016 | tf_op jit(solution)/shard_map/ppermute | solution.py:28
  16.0 0.1 multiply_exponential_fusion
  16.0 1.6 collective-permute-done
  17.7 0.7 fusion.52
  18.4 0.0 copy-done.7
  18.4 0.0 copy-done.9
  18.4 0.0 copy-done.8
  18.4 1.1 multiply_add_fusion.7
  19.5 0.1 broadcast_in_dim.51
  19.5 0.7 pad_maximum_fusion.1
  20.3 2.7 %collective-permute-start.1 = (f32[2,264,128]{2,1,0:T(8,128)}, f32[2,264,128]{2,1,0:T(8,128)}, u32[]{:S(2)}, u32[]{:S(2)}) collective-permute-start(f32[2,264,128]{2,1,0:T(8,128)} %pad_maximum_fusion.1), channel_id=1, source_target_pairs={{0,32},{16,48},{32,0},{48,16},{64,96},{80,112},{96,64},{112,80},{1... | collective-permute-start | bytes 811016 | tf_op jit(solution)/shard_map/ppermute | solution.py:28
  23.0 8.0 %collective-permute-done.1 = f32[2,264,128]{2,1,0:T(8,128)} collective-permute-done((f32[2,264,128]{2,1,0:T(8,128)}, f32[2,264,128]{2,1,0:T(8,128)}, u32[]{:S(2)}, u32[]{:S(2)}) %collective-permute-start.1) | collective-permute-done | bytes 270368 | tf_op jit(solution)/shard_map/ppermute | solution.py:28
  31.0 1.4 fusion.58
  32.4 1.1 multiply_add_fusion.5
  33.4 0.1 broadcast_in_dim.53
  33.5 7.5 %collective-permute-start.2 = (f32[2,264,128]{2,1,0:T(8,128)S(1)}, f32[2,264,128]{2,1,0:T(8,128)S(1)}, u32[]{:S(2)}, u32[]{:S(2)}) collective-permute-start(f32[2,264,128]{2,1,0:T(8,128)S(1)} %pad_maximum_fusion.2), channel_id=1, source_target_pairs={{0,64},{16,80},{32,96},{48,112},{64,0},{80,16},{96,32},{112,48},{1... | collective-permute-start | bytes 811016 | tf_op jit(solution)/shard_map/ppermute | solution.py:28
  41.0 6.3 %collective-permute-done.2 = f32[2,264,128]{2,1,0:T(8,128)S(1)} collective-permute-done((f32[2,264,128]{2,1,0:T(8,128)S(1)}, f32[2,264,128]{2,1,0:T(8,128)S(1)}, u32[]{:S(2)}, u32[]{:S(2)}) %collective-permute-start.2) | collective-permute-done | bytes 270368 | tf_op jit(solution)/shard_map/ppermute | solution.py:28
  47.3 1.3 broadcast_select_fusion.16
  48.6 0.1 multiply_add_fusion.3
  48.7 0.0 copy-done.2
  48.7 0.1 broadcast_in_dim.55
  48.8 0.7 pad_maximum_fusion.3
  49.5 1.9 %collective-permute-start.3 = (f32[2,264,128]{2,1,0:T(8,128)}, f32[2,264,128]{2,1,0:T(8,128)}, u32[]{:S(2)}, u32[]{:S(2)}) collective-permute-start(f32[2,264,128]{2,1,0:T(8,128)} %pad_maximum_fusion.3), channel_id=1, source_target_pairs={{0,128},{16,144},{32,160},{48,176},{64,192},{80,208},{96,224},{112... | collective-permute-start | bytes 811016 | tf_op jit(solution)/shard_map/ppermute | solution.py:28
  51.5 7.7 %collective-permute-done.3 = f32[2,264,128]{2,1,0:T(8,128)} collective-permute-done((f32[2,264,128]{2,1,0:T(8,128)}, f32[2,264,128]{2,1,0:T(8,128)}, u32[]{:S(2)}, u32[]{:S(2)}) %collective-permute-start.3) | collective-permute-done | bytes 270368 | tf_op jit(solution)/shard_map/ppermute | solution.py:28
  59.2 1.4 fusion.66
  60.5 1.1 multiply_add_fusion.1
  61.6 0.1 broadcast_in_dim.110
  61.7 0.7 pad_maximum_fusion.4
  62.4 2.0 %collective-permute-start.4 = (f32[2,264,128]{2,1,0:T(8,128)}, f32[2,264,128]{2,1,0:T(8,128)}, u32[]{:S(2)}, u32[]{:S(2)}) collective-permute-start(f32[2,264,128]{2,1,0:T(8,128)} %pad_maximum_fusion.4), channel_id=1, source_target_pairs={{0,256},{16,272},{32,288},{48,304},{64,320},{80,336},{96,352},{112... | collective-permute-start | bytes 811016 | tf_op jit(solution)/shard_map/ppermute | solution.py:28
  64.5 0.0 copy-done.1
  64.5 4.2 %fusion.3 = f32[768,2,128]{0,2,1:T(8,128)} fusion(s32[2,768]{1,0:T(2,128)} %copy-done.7, bf16[768,2,128]{0,2,1:T(8,128)(2,1)} %bitcast.72, bf16[768,256]{1,0:T(8,128)(2,1)} %param.9, bf16[768,256]{1,0:T(8,128)(2,1)S(1)} %copy-done.1), kind=kOutput, calls=%fused_computation.3 | convolution fusion | flops 612237312 | bytes 1972224 | tf_op jit(solution)/shard_map/hts,shd->thd/dot_general | solution.py:59
  68.6 4.1 %collective-permute-done.4 = f32[2,264,128]{2,1,0:T(8,128)} collective-permute-done((f32[2,264,128]{2,1,0:T(8,128)}, f32[2,264,128]{2,1,0:T(8,128)}, u32[]{:S(2)}, u32[]{:S(2)}) %collective-permute-start.4) | collective-permute-done | bytes 270368 | tf_op jit(solution)/shard_map/ppermute | solution.py:28
  72.8 0.0 copy-done.3
  72.8 1.7 fusion.7
  74.5 1.5 multiply_reduce_fusion
  76.0 0.0 copy-done.10
  76.0 0.9 multiply_convert_fusion.4
  76.9 0.0 all-gather.2.cloned.1.call-update
  76.9 87.3 %all-gather.2.cloned.1.call-done = bf16[768,4096]{0,1:T(8,128)(2,1)} async-done(((bf16[768,256]{0,1:T(8,128)(2,1)}), bf16[768,4096]{0,1:T(8,128)(2,1)}) %all-gather.2.cloned.1.call-update) | async-done | bytes 6291472 | tf_op jit(solution)/shard_map/all_gather | solution.py:91
  164.2 5.8 %fusion.8 = bf16[768,320]{0,1:T(8,128)(2,1)} fusion(bf16[4096,320]{0,1:T(8,128)(2,1)S(1)} %copy-done, bf16[768,4096]{0,1:T(8,128)(2,1)} %all-gather.2.cloned.1.call-done, bf16[768,320]{0,1:T(8,128)(2,1)} %param.13), kind=kOutput, calls=%fused_computation.11 | convolution fusion | flops 2014003200 | bytes 9895936 | tf_op jit(solution)/shard_map/dot_general | solution.py:90
  (8 shorter events, 0.1 us)
Async XLA Ops:
  6.5 157.7 %copy-start = (bf16[4096,320]{0,1:T(8,128)(2,1)S(1)}, bf16[4096,320]{0,1:T(8,128)(2,1)}, u32[]{:S(2)}) copy-start(bf16[4096,320]{0,1:T(8,128)(2,1)} %param.12) | copy-start | bytes 7864324
  6.5 57.9 %copy-start.1 = (bf16[768,256]{1,0:T(8,128)(2,1)S(1)}, bf16[768,256]{1,0:T(8,128)(2,1)}, u32[]{:S(2)}) copy-start(bf16[768,256]{1,0:T(8,128)(2,1)} %param.7) | copy-start | bytes 1179652
  6.5 157.7 %all-gather.2.cloned.1.call-start = ((), (), s32[]{:S(2)}) async-start(), calls=%async_computation | async-start | bytes 6684672 | tf_op jit(solution)/shard_map/all_gather | solution.py:91
  8.5 9.9 %copy-start.7 = (s32[2,768]{1,0:T(2,128)}, s32[2,768]{1,0:T(2,128)S(1)}, u32[]{:S(2)}) copy-start(s32[2,768]{1,0:T(2,128)S(1)} %get-tuple-element.35) | copy-start | bytes 18436
  8.5 9.9 %copy-start.9 = (f32[768,2]{0,1:T(2,128)}, f32[768,2]{0,1:T(2,128)S(1)}, u32[]{:S(2)}) copy-start(f32[768,2]{0,1:T(2,128)S(1)} %get-tuple-element.34) | copy-start | bytes 18436
  8.8 9.6 %copy-start.8 = (f32[768,2]{0,1:T(2,128)}, f32[768,2]{0,1:T(2,128)S(1)}, u32[]{:S(2)}) copy-start(f32[768,2]{0,1:T(2,128)S(1)} %exponential_bitcast_fusion) | copy-start | bytes 18436
  10.5 2.8 %copy-start.6 = (bf16[768,256]{0,1:T(8,128)(2,1)}, bf16[768,256]{0,1:T(8,128)(2,1)S(1)}, u32[]{:S(2)}) copy-start(bf16[768,256]{0,1:T(8,128)(2,1)S(1)} %copy.27) | copy-start | bytes 1179652
  11.9 1.4 copy-start.4
  13.2 0.8 copy-start.5
  14.0 3.6 %collective-permute-start = (f32[2,264,128]{2,1,0:T(8,128)}, f32[2,264,128]{2,1,0:T(8,128)S(1)}, u32[]{:S(2)}, u32[]{:S(2)}) collective-permute-start(f32[2,264,128]{2,1,0:T(8,128)} %pad_maximum_fusion), channel_id=1, source_target_pairs={{0,16},{16,0},{32,48},{48,32},{64,80},{80,64},{96,112},{112,96},{1... | collective-permute-start | bytes 811016 | tf_op jit(solution)/shard_map/ppermute | solution.py:28
  20.3 10.7 %collective-permute-start.1 = (f32[2,264,128]{2,1,0:T(8,128)}, f32[2,264,128]{2,1,0:T(8,128)}, u32[]{:S(2)}, u32[]{:S(2)}) collective-permute-start(f32[2,264,128]{2,1,0:T(8,128)} %pad_maximum_fusion.1), channel_id=1, source_target_pairs={{0,32},{16,48},{32,0},{48,16},{64,96},{80,112},{96,64},{112,80},{1... | collective-permute-start | bytes 811016 | tf_op jit(solution)/shard_map/ppermute | solution.py:28
  33.5 13.8 %collective-permute-start.2 = (f32[2,264,128]{2,1,0:T(8,128)S(1)}, f32[2,264,128]{2,1,0:T(8,128)S(1)}, u32[]{:S(2)}, u32[]{:S(2)}) collective-permute-start(f32[2,264,128]{2,1,0:T(8,128)S(1)} %pad_maximum_fusion.2), channel_id=1, source_target_pairs={{0,64},{16,80},{32,96},{48,112},{64,0},{80,16},{96,32},{112,48},{1... | collective-permute-start | bytes 811016 | tf_op jit(solution)/shard_map/ppermute | solution.py:28
  47.3 1.4 copy-start.2
  49.5 9.6 %collective-permute-start.3 = (f32[2,264,128]{2,1,0:T(8,128)}, f32[2,264,128]{2,1,0:T(8,128)}, u32[]{:S(2)}, u32[]{:S(2)}) collective-permute-start(f32[2,264,128]{2,1,0:T(8,128)} %pad_maximum_fusion.3), channel_id=1, source_target_pairs={{0,128},{16,144},{32,160},{48,176},{64,192},{80,208},{96,224},{112... | collective-permute-start | bytes 811016 | tf_op jit(solution)/shard_map/ppermute | solution.py:28
  62.4 10.3 %copy-start.3 = (f32[2,264,128]{2,1,0:T(8,128)S(1)}, f32[2,264,128]{2,1,0:T(8,128)}, u32[]{:S(2)}) copy-start(f32[2,264,128]{2,1,0:T(8,128)} %copy-done.2) | copy-start | bytes 811012
  62.4 10.3 %collective-permute-start.4 = (f32[2,264,128]{2,1,0:T(8,128)}, f32[2,264,128]{2,1,0:T(8,128)}, u32[]{:S(2)}, u32[]{:S(2)}) collective-permute-start(f32[2,264,128]{2,1,0:T(8,128)} %pad_maximum_fusion.4), channel_id=1, source_target_pairs={{0,256},{16,272},{32,288},{48,304},{64,320},{80,336},{96,352},{112... | collective-permute-start | bytes 811016 | tf_op jit(solution)/shard_map/ppermute | solution.py:28
  68.6 7.4 %copy-start.10 = (f32[256]{0:T(256)S(1)}, f32[256]{0:T(256)}, u32[]{:S(2)}) copy-start(f32[256]{0:T(256)} %param.11) | copy-start | bytes 3076
Sparse Core Ops, SparseCore 0:
  77.0 87.1 all-gather.1

commit v3 on v2

--- a/solution.py
+++ b/solution.py
@@ -10,38 +10,46 @@
     return jnp.exp2(-exponents.astype(jnp.float32) / 16.0)
 
 
+def pack(summary, decay):
+    heads = decay.shape[0]
+    return jnp.concatenate(
+        [summary, jnp.broadcast_to(decay[:, None, None], (heads, 8, HD))], axis=1
+    )
+
+
 def block_scan(decay, summary_fwd, summary_bwd):
     seq_count = lax.axis_size("seq")
     me = lax.axis_index("seq")
-    heads = decay.shape[0]
-    total_p, total_f, total_b = decay, summary_fwd, summary_bwd
-    prefix_pf = jnp.ones_like(decay)
-    prefix_pb = jnp.ones_like(decay)
-    prefix_f = jnp.zeros_like(summary_fwd)
-    prefix_b = jnp.zeros_like(summary_bwd)
+    second = (me % 2) == 1
+    chip = me // 2
+    mine = jnp.where(second, summary_bwd, summary_fwd)
+    other = jnp.where(second, summary_fwd, summary_bwd)
+    got = lax.ppermute(pack(other, decay), "seq", [(i, i ^ 1) for i in range(seq_count)])
+    got_s, got_p = got[:, :HD], got[:, HD, 0]
+    total_s = got_p[:, None, None] * mine + got_s
+    total_p = decay * got_p
+    prefix_s = jnp.zeros_like(mine)
+    prefix_p = jnp.ones_like(decay)
     shift = 1
-    while shift < seq_count:
-        pairs = [(i, i ^ shift) for i in range(seq_count)]
-        packed = jnp.concatenate(
-            [total_f, total_b, jnp.broadcast_to(total_p[:, None, None], (heads, 8, HD))], axis=1
-        )
-        packed = lax.ppermute(packed, "seq", pairs)
-        got_f, got_b, got_p = packed[:, :HD], packed[:, HD : 2 * HD], packed[:, 2 * HD, 0]
-        lower = (me & shift) != 0
-        prefix_f = prefix_f + jnp.where(lower, prefix_pf, 0.0)[:, None, None] * got_f
-        prefix_b = prefix_b + jnp.where(lower, 0.0, prefix_pb)[:, None, None] * got_b
-        prefix_pf = jnp.where(lower, got_p * prefix_pf, prefix_pf)
-        prefix_pb = jnp.where(lower, prefix_pb, got_p * prefix_pb)
-        if 2 * shift < seq_count:
-            own_f = jnp.where(lower, 1.0, got_p)[:, None, None]
-            new_f = jnp.where(lower, total_p, 1.0)[:, None, None]
-            own_b = jnp.where(lower, got_p, 1.0)[:, None, None]
-            new_b = jnp.where(lower, 1.0, total_p)[:, None, None]
-            total_f = own_f * total_f + new_f * got_f
-            total_b = own_b * total_b + new_b * got_b
+    while 2 * shift < seq_count:
+        pairs = [(i, i ^ (2 * shift)) for i in range(seq_count)]
+        got = lax.ppermute(pack(total_s, total_p), "seq", pairs)
+        got_s, got_p = got[:, :HD], got[:, HD, 0]
+        earlier = ((chip & shift) != 0) != second
+        prefix_s = prefix_s + jnp.where(earlier, prefix_p, 0.0)[:, None, None] * got_s
+        prefix_p = jnp.where(earlier, got_p * prefix_p, prefix_p)
+        if 4 * shift < seq_count:
+            own = jnp.where(earlier, 1.0, got_p)[:, None, None]
+            new = jnp.where(earlier, total_p, 1.0)[:, None, None]
+            total_s = own * total_s + new * got_s
             total_p = total_p * got_p
         shift *= 2
-    return prefix_f, prefix_b
+    handed = lax.ppermute(
+        decay[:, None, None] * prefix_s + mine, "seq", [(i, i ^ 1) for i in range(seq_count)]
+    )
+    state_fwd = jnp.where(second, handed, prefix_s)
+    state_bwd = jnp.where(second, prefix_s, handed)
+    return state_fwd, state_bwd
 
 
 def local(query_vectors, key_vectors, value_vectors, decay_exp, norm_gain, out_weight, residual):

time: 178 us -> 172 us (0.966)
  waiting for transfers between devices: 115 us -> 110 us
  starting transfers between devices: 16.1 us -> 18.7 us
    ppermute x5 -> x6, waiting for transfers between devices: 27.7 us -> 21.1 us  [the longest x4 19.9 us: block_scan(): got = lax.ppermute(pack(total_s, total_p), 'seq', pairs)]
    ppermute x5 -> x6, starting transfers between devices: 16.1 us -> 18.7 us  [the longest x4 14.7 us: block_scan(): got = lax.ppermute(pack(total_s, total_p), 'seq', pairs)]
    select_n x5 -> x2, other arithmetic: 5.31 us -> 2.76 us  [block_scan(): jnp.where(earlier, prefix_p, 0.0)[:, None, None] * got_s]
    mul x0 -> x2, other arithmetic: none -> 1.9 us  [the longest x1 1.32 us: block_scan(): total_p = total_p * got_p]
    add x4 -> x5, other arithmetic: 3.31 us -> 4.08 us  [the longest x3 2.06 us: block_scan(): total_s = own * total_s + new * got_s]
  transfers between devices with their start and end apart: 6 -> 7, of which waited for: 6 -> 6; matrix products, arithmetic and copies ran while one was open for 2% -> 2% of each run, Pallas kernels for 0% -> 0%
where the time goes in v3:
time: 172 us
  waiting for transfers between devices  110 us (64%)
  starting transfers between devices  18.7 us (11%)
  matrix products  14.2 us (8%)
  between operations  13.7 us (8%)
  other arithmetic  12.7 us (7%)
  local copies, waits for them, and re-layouts  2.8 us (2%)
    all_gather x1, waiting for transfers between devices, local(): lax.all_gather(normed, 'tp', axis=1, tiled=True)  88.4 us
    ppermute x4, waiting for transfers between devices, block_scan(): got = lax.ppermute(pack(total_s, total_p), 'seq', pairs)  19.9 us
    ppermute x4, starting transfers between devices, block_scan(): got = lax.ppermute(pack(total_s, total_p), 'seq', pairs)  14.7 us
    dot_general x1, matrix products, local(): jnp.dot(lax.all_gather(normed, 'tp', axis=1, tiled=True), out_weight, pre...  5.81 us
    dot_general x1, matrix products, local(): jnp.einsum('hts,shd->thd', local_weights, value_heads, preferred_element_...  4.04 us
  transfers between devices with their start and end apart: 7, of which 6 were waited for; matrix products, arithmetic and copies ran while one was open for 2% of the time, Pallas kernels for 0%

profile of v3, /device:TPU:6, one launch (start us, length us, event | category | flops | bytes accessed | tf_op | source)
XLA Modules:
  0.0 171.6 jit_solution(12659889532665378565)
XLA Ops:
  6.5 0.0 copy-start
  6.5 0.0 copy-start.1
  6.5 0.0 all-gather.2.cloned.1.call-start
  6.5 0.9 reshape.92
  7.4 0.6 reduce-window.6
  8.0 0.2 slice_reduce_fusion
  8.2 0.2 reduce-window.9
  8.4 0.1 add_bitcast_fusion
  8.5 0.0 copy-start.5
  8.5 0.0 copy-start.6
  8.5 0.2 slice_reduce_fusion.1
  8.7 0.0 copy-start.8
  8.7 0.1 exponential_bitcast_fusion
  8.8 1.2 copy.27
  10.0 1.3 fusion.11
  11.2 0.0 copy-start.2
  11.2 1.3 broadcast_select_fusion.1
  12.5 0.0 copy-start.3
  12.6 0.1 broadcast_in_dim.32
  12.6 0.0 copy-done.8
  12.7 1.9 %collective-permute-start = (f32[2,136,128]{2,1,0:T(8,128)S(1)}, f32[2,136,128]{2,1,0:T(8,128)S(1)}, u32[]{:S(2)}, u32[]{:S(2)}) collective-permute-start(f32[2,136,128]{2,1,0:T(8,128)S(1)} %pad_maximum_fusion), channel_id=1, source_target_pairs={{0,16},{16,0},{32,48},{48,32},{64,80},{80,64},{96,112},{112,96},{1... | collective-permute-start | bytes 417800 | tf_op jit(solution)/shard_map/ppermute | solution.py:27
  14.6 0.1 multiply_exponential_fusion
  14.7 1.2 collective-permute-done
  15.9 0.6 fusion.47
  16.5 0.0 copy-done.5
  16.5 0.0 copy-done.6
  16.5 0.0 copy-done.2
  16.5 0.1 slice_add_fusion
  16.6 0.0 copy-done.3
  16.6 0.1 broadcast_in_dim.34
  16.7 0.7 pad_maximum_fusion.1
  17.3 2.7 %collective-permute-start.1 = (f32[2,136,128]{2,1,0:T(8,128)}, f32[2,136,128]{2,1,0:T(8,128)}, u32[]{:S(2)}, u32[]{:S(2)}) collective-permute-start(f32[2,136,128]{2,1,0:T(8,128)} %pad_maximum_fusion.1), channel_id=1, source_target_pairs={{0,32},{16,48},{32,0},{48,16},{64,96},{80,112},{96,64},{112,80},{1... | collective-permute-start | bytes 417800 | tf_op jit(solution)/shard_map/ppermute | solution.py:36
  20.1 5.2 %collective-permute-done.1 = f32[2,136,128]{2,1,0:T(8,128)} collective-permute-done((f32[2,136,128]{2,1,0:T(8,128)}, f32[2,136,128]{2,1,0:T(8,128)}, u32[]{:S(2)}, u32[]{:S(2)}) %collective-permute-start.1) | collective-permute-done | bytes 139296 | tf_op jit(solution)/shard_map/ppermute | solution.py:36
  25.3 1.4 fusion.34
  26.6 1.0 multiply_add_fusion.3
  27.6 0.1 broadcast_in_dim.37
  27.7 7.5 %collective-permute-start.2 = (f32[2,136,128]{2,1,0:T(8,128)S(1)}, f32[2,136,128]{2,1,0:T(8,128)S(1)}, u32[]{:S(2)}, u32[]{:S(2)}) collective-permute-start(f32[2,136,128]{2,1,0:T(8,128)S(1)} %pad_maximum_fusion.2), channel_id=1, source_target_pairs={{0,64},{16,80},{32,96},{48,112},{64,0},{80,16},{96,32},{112,48},{1... | collective-permute-start | bytes 417800 | tf_op jit(solution)/shard_map/ppermute | solution.py:36
  35.2 3.5 %collective-permute-done.2 = f32[2,136,128]{2,1,0:T(8,128)S(1)} collective-permute-done((f32[2,136,128]{2,1,0:T(8,128)S(1)}, f32[2,136,128]{2,1,0:T(8,128)S(1)}, u32[]{:S(2)}, u32[]{:S(2)}) %collective-permute-start.2) | collective-permute-done | bytes 139296 | tf_op jit(solution)/shard_map/ppermute | solution.py:36
  38.7 0.0 copy-start.4
  38.7 1.3 fusion.46
  40.0 0.1 multiply_add_fusion.2
  40.1 0.0 copy-done.4
  40.1 0.1 broadcast_in_dim.39
  40.2 0.7 pad_maximum_fusion.3
  40.8 1.9 %collective-permute-start.3 = (f32[2,136,128]{2,1,0:T(8,128)}, f32[2,136,128]{2,1,0:T(8,128)}, u32[]{:S(2)}, u32[]{:S(2)}) collective-permute-start(f32[2,136,128]{2,1,0:T(8,128)} %pad_maximum_fusion.3), channel_id=1, source_target_pairs={{0,128},{16,144},{32,160},{48,176},{64,192},{80,208},{96,224},{112... | collective-permute-start | bytes 417800 | tf_op jit(solution)/shard_map/ppermute | solution.py:36
  42.8 5.3 %collective-permute-done.3 = f32[2,136,128]{2,1,0:T(8,128)} collective-permute-done((f32[2,136,128]{2,1,0:T(8,128)}, f32[2,136,128]{2,1,0:T(8,128)}, u32[]{:S(2)}, u32[]{:S(2)}) %collective-permute-start.3) | collective-permute-done | bytes 139296 | tf_op jit(solution)/shard_map/ppermute | solution.py:36
  48.1 1.4 fusion.42
  49.5 1.0 multiply_add_fusion.1
  50.5 0.1 broadcast_in_dim.41
  50.6 2.6 %collective-permute-start.4 = (f32[2,136,128]{2,1,0:T(8,128)S(1)}, f32[2,136,128]{2,1,0:T(8,128)}, u32[]{:S(2)}, u32[]{:S(2)}) collective-permute-start(f32[2,136,128]{2,1,0:T(8,128)S(1)} %pad_maximum_fusion.4), channel_id=1, source_target_pairs={{0,256},{16,272},{32,288},{48,304},{64,320},{80,336},{96,352},{112... | collective-permute-start | bytes 417800 | tf_op jit(solution)/shard_map/ppermute | solution.py:36
  53.2 5.9 %collective-permute-done.4 = f32[2,136,128]{2,1,0:T(8,128)} collective-permute-done((f32[2,136,128]{2,1,0:T(8,128)S(1)}, f32[2,136,128]{2,1,0:T(8,128)}, u32[]{:S(2)}, u32[]{:S(2)}) %collective-permute-start.4) | collective-permute-done | bytes 139296 | tf_op jit(solution)/shard_map/ppermute | solution.py:36
  59.1 1.9 %multiply_add_fusion = (bf16[2,128,128]{2,1,0:T(8,128)(2,1)}, bf16[2,128,128]{2,1,0:T(8,128)(2,1)S(1)}) fusion(f32[2]{0:T(128)} %copy-done.8, f32[2,128,128]{2,1,0:T(8,128)} %copy-done.2, f32[2,128,128]{2,1,0:T(8,128)} %copy-done.3, pred[]{:T(512)S(6)} %eq.5, f32[2,136,128]{2,1,0:T(8,128)} %collective-permute-done.4, f32[2]{0:T(128)} %get-tuple-element.11, ...), kind=kLoop, calls=%fused_computation.44 | loop fusion | flops 393216 | bytes 917541 | tf_op jit(solution)/shard_map/add | solution.py:48
  61.1 2.0 %collective-permute-start.5 = (bf16[2,128,128]{2,1,0:T(8,128)(2,1)}, bf16[2,128,128]{2,1,0:T(8,128)(2,1)S(1)}, u32[]{:S(2)}, u32[]{:S(2)}) collective-permute-start(bf16[2,128,128]{2,1,0:T(8,128)(2,1)} %get-tuple-element.17), channel_id=1, source_target_pairs={{0,16},{16,0},{32,48},{48,32},{64,80},{80,64},{96,112},{112,96},{1... | collective-permute-start | bytes 196616 | tf_op jit(solution)/shard_map/ppermute | solution.py:47
  63.1 0.0 copy-done.1
  63.1 4.0 %fusion.3 = f32[768,2,128]{0,2,1:T(8,128)} fusion(s32[2,768]{1,0:T(2,128)} %copy-done.5, bf16[768,2,128]{0,2,1:T(8,128)(2,1)S(1)} %bitcast.73, bf16[768,256]{1,0:T(8,128)(2,1)} %param.9, bf16[768,256]{1,0:T(8,128)(2,1)S(1)} %copy-done.1), kind=kOutput, calls=%fused_computation.3 | convolution fusion | flops 612237312 | bytes 1972224 | tf_op jit(solution)/shard_map/hts,shd->thd/dot_general | solution.py:67
  67.2 0.0 collective-permute-done.5
  67.2 0.0 copy-done.7
  67.2 1.4 fusion.7
  68.6 0.3 multiply_reduce_fusion
  69.0 1.5 multiply_convert_fusion.4
  70.5 0.0 all-gather.2.cloned.1.call-update
  70.6 88.4 %all-gather.2.cloned.1.call-done = bf16[768,4096]{0,1:T(8,128)(2,1)} async-done(((bf16[768,256]{0,1:T(8,128)(2,1)}), bf16[768,4096]{0,1:T(8,128)(2,1)}) %all-gather.2.cloned.1.call-update) | async-done | bytes 6291472 | tf_op jit(solution)/shard_map/all_gather | solution.py:99
  158.9 0.0 copy-done
  158.9 5.8 %fusion.8 = bf16[768,320]{0,1:T(8,128)(2,1)} fusion(bf16[4096,320]{0,1:T(8,128)(2,1)S(1)} %copy-done, bf16[768,4096]{0,1:T(8,128)(2,1)} %all-gather.2.cloned.1.call-done, bf16[768,320]{0,1:T(8,128)(2,1)} %param.13), kind=kOutput, calls=%fused_computation.11 | convolution fusion | flops 2014003200 | bytes 9895936 | tf_op jit(solution)/shard_map/dot_general | solution.py:98
  (7 shorter events, 0.1 us)
Async XLA Ops:
  6.5 152.4 %copy-start = (bf16[4096,320]{0,1:T(8,128)(2,1)S(1)}, bf16[4096,320]{0,1:T(8,128)(2,1)}, u32[]{:S(2)}) copy-start(bf16[4096,320]{0,1:T(8,128)(2,1)} %param.12) | copy-start | bytes 7864324
  6.5 56.6 %copy-start.1 = (bf16[768,256]{1,0:T(8,128)(2,1)S(1)}, bf16[768,256]{1,0:T(8,128)(2,1)}, u32[]{:S(2)}) copy-start(bf16[768,256]{1,0:T(8,128)(2,1)} %param.7) | copy-start | bytes 1179652
  6.5 152.4 %all-gather.2.cloned.1.call-start = ((), (), s32[]{:S(2)}) async-start(), calls=%async_computation | async-start | bytes 6684672 | tf_op jit(solution)/shard_map/all_gather | solution.py:99
  8.5 8.0 %copy-start.5 = (s32[2,768]{1,0:T(2,128)}, s32[2,768]{1,0:T(2,128)S(1)}, u32[]{:S(2)}) copy-start(s32[2,768]{1,0:T(2,128)S(1)} %get-tuple-element.24) | copy-start | bytes 18436
  8.5 8.0 %copy-start.6 = (f32[768,2]{0,1:T(2,128)}, f32[768,2]{0,1:T(2,128)S(1)}, u32[]{:S(2)}) copy-start(f32[768,2]{0,1:T(2,128)S(1)} %get-tuple-element.23) | copy-start | bytes 18436
  8.7 4.0 %copy-start.8 = (f32[2]{0:T(128)}, f32[2]{0:T(128)S(1)}, u32[]{:S(2)}) copy-start(f32[2]{0:T(128)S(1)} %multiply_exponential_fusion.1) | copy-start | bytes 28
  11.2 5.3 %copy-start.2 = (f32[2,128,128]{2,1,0:T(8,128)}, f32[2,128,128]{2,1,0:T(8,128)S(1)}, u32[]{:S(2)}) copy-start(f32[2,128,128]{2,1,0:T(8,128)S(1)} %fusion.11) | copy-start | bytes 393220
  12.5 4.0 %copy-start.3 = (f32[2,128,128]{2,1,0:T(8,128)}, f32[2,128,128]{2,1,0:T(8,128)S(1)}, u32[]{:S(2)}) copy-start(f32[2,128,128]{2,1,0:T(8,128)S(1)} %get-tuple-element.29) | copy-start | bytes 393220
  12.7 3.3 %collective-permute-start = (f32[2,136,128]{2,1,0:T(8,128)S(1)}, f32[2,136,128]{2,1,0:T(8,128)S(1)}, u32[]{:S(2)}, u32[]{:S(2)}) collective-permute-start(f32[2,136,128]{2,1,0:T(8,128)S(1)} %pad_maximum_fusion), channel_id=1, source_target_pairs={{0,16},{16,0},{32,48},{48,32},{64,80},{80,64},{96,112},{112,96},{1... | collective-permute-start | bytes 417800 | tf_op jit(solution)/shard_map/ppermute | solution.py:27
  17.3 7.9 %collective-permute-start.1 = (f32[2,136,128]{2,1,0:T(8,128)}, f32[2,136,128]{2,1,0:T(8,128)}, u32[]{:S(2)}, u32[]{:S(2)}) collective-permute-start(f32[2,136,128]{2,1,0:T(8,128)} %pad_maximum_fusion.1), channel_id=1, source_target_pairs={{0,32},{16,48},{32,0},{48,16},{64,96},{80,112},{96,64},{112,80},{1... | collective-permute-start | bytes 417800 | tf_op jit(solution)/shard_map/ppermute | solution.py:36
  27.7 11.0 %collective-permute-start.2 = (f32[2,136,128]{2,1,0:T(8,128)S(1)}, f32[2,136,128]{2,1,0:T(8,128)S(1)}, u32[]{:S(2)}, u32[]{:S(2)}) collective-permute-start(f32[2,136,128]{2,1,0:T(8,128)S(1)} %pad_maximum_fusion.2), channel_id=1, source_target_pairs={{0,64},{16,80},{32,96},{48,112},{64,0},{80,16},{96,32},{112,48},{1... | collective-permute-start | bytes 417800 | tf_op jit(solution)/shard_map/ppermute | solution.py:36
  38.7 1.4 copy-start.4
  40.8 7.3 %collective-permute-start.3 = (f32[2,136,128]{2,1,0:T(8,128)}, f32[2,136,128]{2,1,0:T(8,128)}, u32[]{:S(2)}, u32[]{:S(2)}) collective-permute-start(f32[2,136,128]{2,1,0:T(8,128)} %pad_maximum_fusion.3), channel_id=1, source_target_pairs={{0,128},{16,144},{32,160},{48,176},{64,192},{80,208},{96,224},{112... | collective-permute-start | bytes 417800 | tf_op jit(solution)/shard_map/ppermute | solution.py:36
  50.6 8.6 %collective-permute-start.4 = (f32[2,136,128]{2,1,0:T(8,128)S(1)}, f32[2,136,128]{2,1,0:T(8,128)}, u32[]{:S(2)}, u32[]{:S(2)}) collective-permute-start(f32[2,136,128]{2,1,0:T(8,128)S(1)} %pad_maximum_fusion.4), channel_id=1, source_target_pairs={{0,256},{16,272},{32,288},{48,304},{64,320},{80,336},{96,352},{112... | collective-permute-start | bytes 417800 | tf_op jit(solution)/shard_map/ppermute | solution.py:36
  61.1 6.1 %copy-start.7 = (f32[768,2]{0,1:T(2,128)S(1)}, f32[768,2]{0,1:T(2,128)}, u32[]{:S(2)}) copy-start(f32[768,2]{0,1:T(2,128)} %copy-done.6) | copy-start | bytes 18436
  61.1 6.1 %collective-permute-start.5 = (bf16[2,128,128]{2,1,0:T(8,128)(2,1)}, bf16[2,128,128]{2,1,0:T(8,128)(2,1)S(1)}, u32[]{:S(2)}, u32[]{:S(2)}) collective-permute-start(bf16[2,128,128]{2,1,0:T(8,128)(2,1)} %get-tuple-element.17), channel_id=1, source_target_pairs={{0,16},{16,0},{32,48},{48,32},{64,80},{80,64},{96,112},{112,96},{1... | collective-permute-start | bytes 196616 | tf_op jit(solution)/shard_map/ppermute | solution.py:47
Sparse Core Ops, SparseCore 0:
  70.7 88.1 all-gather.1

commit v4 on v3

--- a/solution.py
+++ b/solution.py
@@ -17,38 +17,65 @@
     )
 
 
+def unpack(packed):
+    return packed[:, :HD], packed[:, HD, 0]
+
+
+def gather_line(total_s, total_p, line, stride, seq_count):
+    got = []
+    for shift in range(1, line):
+        pairs = []
+        for i in range(seq_count):
+            at = (i // stride) % line
+            step = -shift if i % 2 else shift
+            pairs.append((i, i + (((at + step) % line) - at) * stride))
+        got.append(unpack(lax.ppermute(pack(total_s, total_p), "seq", pairs)))
+    return got
+
+
 def block_scan(decay, summary_fwd, summary_bwd):
     seq_count = lax.axis_size("seq")
+    line = 4
     me = lax.axis_index("seq")
     second = (me % 2) == 1
-    chip = me // 2
+    x = (me // 2) % line
+    y = me // (2 * line)
+    pos_x = jnp.where(second, line - 1 - x, x)
+    pos_y = jnp.where(second, line - 1 - y, y)
     mine = jnp.where(second, summary_bwd, summary_fwd)
     other = jnp.where(second, summary_fwd, summary_bwd)
-    got = lax.ppermute(pack(other, decay), "seq", [(i, i ^ 1) for i in range(seq_count)])
-    got_s, got_p = got[:, :HD], got[:, HD, 0]
-    total_s = got_p[:, None, None] * mine + got_s
-    total_p = decay * got_p
-    prefix_s = jnp.zeros_like(mine)
-    prefix_p = jnp.ones_like(decay)
-    shift = 1
-    while 2 * shift < seq_count:
-        pairs = [(i, i ^ (2 * shift)) for i in range(seq_count)]
-        got = lax.ppermute(pack(total_s, total_p), "seq", pairs)
-        got_s, got_p = got[:, :HD], got[:, HD, 0]
-        earlier = ((chip & shift) != 0) != second
-        prefix_s = prefix_s + jnp.where(earlier, prefix_p, 0.0)[:, None, None] * got_s
-        prefix_p = jnp.where(earlier, got_p * prefix_p, prefix_p)
-        if 4 * shift < seq_count:
-            own = jnp.where(earlier, 1.0, got_p)[:, None, None]
-            new = jnp.where(earlier, total_p, 1.0)[:, None, None]
-            total_s = own * total_s + new * got_s
-            total_p = total_p * got_p
-        shift *= 2
+    got_s, got_p = unpack(
+        lax.ppermute(pack(other, decay), "seq", [(i, i ^ 1) for i in range(seq_count)])
+    )
+    chip_s = got_p[:, None, None] * mine + got_s
+    chip_p = decay * got_p
+
+    def prefix(got, pos):
+        acc_s = jnp.zeros_like(chip_s)
+        acc_p = jnp.ones_like(chip_p)
+        for m, (s, p) in enumerate(got, start=1):
+            valid = pos >= m
+            acc_s = acc_s + jnp.where(valid, acc_p, 0.0)[:, None, None] * s
+            acc_p = jnp.where(valid, acc_p * p, acc_p)
+        return acc_s, acc_p
+
+    row = gather_line(chip_s, chip_p, line, 2, seq_count)
+    row_prefix_s, row_prefix_p = prefix(row, pos_x)
+    row_s = chip_p[:, None, None] * row_prefix_s + chip_s
+    row_p = chip_p
+    for m in range(1, line):
+        s, p = row[line - 1 - m]
+        valid = pos_x <= line - 1 - m
+        row_s = jnp.where(valid, p, 1.0)[:, None, None] * row_s + jnp.where(valid, 1.0, 0.0) * s
+        row_p = row_p * p
+    col = gather_line(row_s, row_p, line, 2 * line, seq_count)
+    col_prefix_s, _ = prefix(col, pos_y)
+    state = row_prefix_p[:, None, None] * col_prefix_s + row_prefix_s
     handed = lax.ppermute(
-        decay[:, None, None] * prefix_s + mine, "seq", [(i, i ^ 1) for i in range(seq_count)]
+        decay[:, None, None] * state + mine, "seq", [(i, i ^ 1) for i in range(seq_count)]
     )
-    state_fwd = jnp.where(second, handed, prefix_s)
-    state_bwd = jnp.where(second, prefix_s, handed)
+    state_fwd = jnp.where(second, handed, state)
+    state_bwd = jnp.where(second, state, handed)
     return state_fwd, state_bwd
 
 

time: 172 us -> 168 us (0.977)
  waiting for transfers between devices: 110 us -> 99 us
  starting transfers between devices: 18.7 us -> 26 us
  other arithmetic: 12.7 us -> 10.7 us
    ppermute x5 -> x7, waiting for transfers between devices: 19.9 us -> 7.98 us  [the longest x6 7.98 us: gather_line(): got.append(unpack(lax.ppermute(pack(total_s, total_p), 'seq', pairs)))]
    ppermute x5 -> x7, starting transfers between devices: 16.8 us -> 24 us  [the longest x6 22 us: gather_line(): got.append(unpack(lax.ppermute(pack(total_s, total_p), 'seq', pairs)))]
    mul x2 -> x0, other arithmetic: 1.9 us -> none  [the longest x1 1.32 us: block_scan(): total_p = total_p * got_p]
    add x5 -> x3, other arithmetic: 4.08 us -> 3.35 us  [the longest x1 2.04 us: block_scan(): decay[:, None, None] * state + mine]
  transfers between devices with their start and end apart: 7 -> 9, of which waited for: 6 -> 6; matrix products, arithmetic and copies ran while one was open for 2% -> 3% of each run, Pallas kernels for 0% -> 0%
where the time goes in v4:
time: 168 us; the launch traced here: 167 us
  waiting for transfers between devices  99 us (59%)
  starting transfers between devices  26 us (15%)
  matrix products  14.2 us (8%)
  between operations  13.7 us (8%)
  other arithmetic  10.7 us (6%)
  local copies, waits for them, and re-layouts  3.89 us (2%)
    all_gather x1, waiting for transfers between devices, local(): lax.all_gather(normed, 'tp', axis=1, tiled=True)  89.8 us
    ppermute x6, starting transfers between devices, gather_line(): got.append(unpack(lax.ppermute(pack(total_s, total_p), 'seq', pairs)))  22 us
    ppermute x6, waiting for transfers between devices, gather_line(): got.append(unpack(lax.ppermute(pack(total_s, total_p), 'seq', pairs)))  7.98 us
    dot_general x1, matrix products, local(): jnp.dot(lax.all_gather(normed, 'tp', axis=1, tiled=True), out_weight, pre...  5.81 us
    dot_general x1, matrix products, local(): jnp.einsum('hts,shd->thd', local_weights, value_heads, preferred_element_...  4.02 us
  transfers between devices with their start and end apart: 9, of which 6 were waited for; matrix products, arithmetic and copies ran while one was open for 3% of the time, Pallas kernels for 0%

profile of v4, /device:TPU:6, one launch (start us, length us, event | category | flops | bytes accessed | tf_op | source)
XLA Modules:
  0.0 167.5 jit_solution(11104040567315425378)
XLA Ops:
  6.5 0.0 copy-start
  6.5 0.0 copy-start.1
  6.5 0.0 all-gather.2.cloned.1.call-start
  6.5 0.9 reshape.87
  7.4 0.6 reduce-window.6
  8.0 0.2 slice_reduce_fusion
  8.2 0.2 reduce-window.9
  8.4 0.1 add_bitcast_fusion
  8.4 0.6 exponential_bitcast_fusion.1
  9.1 0.2 slice_reduce_fusion.1
  9.2 0.6 multiply_exponential_fusion.1
  9.8 0.1 exponential_bitcast_fusion
  9.9 1.2 copy.27
  11.1 1.3 fusion.11
  12.4 1.3 broadcast_select_fusion.1
  13.6 0.0 copy-start.2
  13.7 0.7 broadcast_in_dim.22
  14.4 1.9 %collective-permute-start = (f32[2,136,128]{2,1,0:T(8,128)S(1)}, f32[2,136,128]{2,1,0:T(8,128)S(1)}, u32[]{:S(2)}, u32[]{:S(2)}) collective-permute-start(f32[2,136,128]{2,1,0:T(8,128)S(1)} %pad_maximum_fusion), channel_id=1, source_target_pairs={{0,16},{16,0},{32,48},{48,32},{64,80},{80,64},{96,112},{112,96},{1... | collective-permute-start | bytes 417800 | tf_op jit(solution)/shard_map/ppermute | solution.py:48
  16.3 0.1 multiply_exponential_fusion
  16.4 0.0 copy-start.6
  16.4 1.2 collective-permute-done
  17.7 0.0 copy-start.5
  17.7 0.1 slice_reduce_fusion.2
  17.8 0.0 copy-done.2
  17.8 0.1 slice_add_fusion
  17.9 0.0 copy-start.3
  17.9 0.1 broadcast_in_dim.24
  17.9 0.6 copy-done.3
  18.5 0.7 pad_maximum_fusion.1
  19.2 0.0 copy-done.5
  19.2 2.7 %collective-permute-start.3 = (f32[2,136,128]{2,1,0:T(8,128)}, f32[2,136,128]{2,1,0:T(8,128)}, u32[]{:S(2)}, u32[]{:S(2)}) collective-permute-start(f32[2,136,128]{2,1,0:T(8,128)} %pad_maximum_fusion.1), channel_id=1, source_target_pairs={{0,96},{16,48},{32,0},{48,80},{64,32},{80,112},{96,64},{112,16},{1... | collective-permute-start | bytes 417800 | tf_op jit(solution)/shard_map/ppermute | solution.py:32
  21.9 0.0 copy-done.6
  21.9 8.4 %collective-permute-start.2 = (f32[2,136,128]{2,1,0:T(8,128)}, f32[2,136,128]{2,1,0:T(8,128)}, u32[]{:S(2)}, u32[]{:S(2)}) collective-permute-start(f32[2,136,128]{2,1,0:T(8,128)} %pad_maximum_fusion.1), channel_id=1, source_target_pairs={{0,64},{16,80},{32,96},{48,112},{64,0},{80,16},{96,32},{112,48},{1... | collective-permute-start | bytes 417800 | tf_op jit(solution)/shard_map/ppermute | solution.py:32
  30.3 0.0 copy-done.9
  30.3 1.9 %collective-permute-start.1 = (f32[2,136,128]{2,1,0:T(8,128)}, f32[2,136,128]{2,1,0:T(8,128)}, u32[]{:S(2)}, u32[]{:S(2)}) collective-permute-start(f32[2,136,128]{2,1,0:T(8,128)} %pad_maximum_fusion.1), channel_id=1, source_target_pairs={{0,32},{16,112},{32,64},{48,16},{64,96},{80,48},{96,0},{112,80},{1... | collective-permute-start | bytes 417800 | tf_op jit(solution)/shard_map/ppermute | solution.py:32
  32.3 0.0 collective-permute-done.3
  32.3 2.1 %collective-permute-done.2 = f32[2,136,128]{2,1,0:T(8,128)} collective-permute-done((f32[2,136,128]{2,1,0:T(8,128)}, f32[2,136,128]{2,1,0:T(8,128)}, u32[]{:S(2)}, u32[]{:S(2)}) %collective-permute-start.2) | collective-permute-done | bytes 139296 | tf_op jit(solution)/shard_map/ppermute | solution.py:32
  34.5 3.2 %collective-permute-done.1 = f32[2,136,128]{2,1,0:T(8,128)} collective-permute-done((f32[2,136,128]{2,1,0:T(8,128)}, f32[2,136,128]{2,1,0:T(8,128)}, u32[]{:S(2)}, u32[]{:S(2)}) %collective-permute-start.1) | collective-permute-done | bytes 139296 | tf_op jit(solution)/shard_map/ppermute | solution.py:32
  37.6 1.3 fusion.43
  39.0 1.2 multiply_add_fusion.1
  40.2 0.0 copy-done.7
  40.2 0.0 copy-done.8
  40.2 0.1 broadcast_in_dim.27
  40.3 0.7 pad_maximum_fusion.2
  40.9 1.9 %collective-permute-start.5 = (f32[2,136,128]{2,1,0:T(8,128)}, f32[2,136,128]{2,1,0:T(8,128)}, u32[]{:S(2)}, u32[]{:S(2)}) collective-permute-start(f32[2,136,128]{2,1,0:T(8,128)} %pad_maximum_fusion.2), channel_id=1, source_target_pairs={{0,256},{16,272},{32,288},{48,304},{64,320},{80,336},{96,352},{112... | collective-permute-start | bytes 417800 | tf_op jit(solution)/shard_map/ppermute | solution.py:32
  42.9 1.9 %collective-permute-start.4 = (f32[2,136,128]{2,1,0:T(8,128)}, f32[2,136,128]{2,1,0:T(8,128)}, u32[]{:S(2)}, u32[]{:S(2)}) collective-permute-start(f32[2,136,128]{2,1,0:T(8,128)} %pad_maximum_fusion.2), channel_id=1, source_target_pairs={{0,128},{16,400},{32,160},{48,432},{64,192},{80,464},{96,224},{112... | collective-permute-start | bytes 417800 | tf_op jit(solution)/shard_map/ppermute | solution.py:32
  44.8 5.1 %collective-permute-start.6 = (f32[2,136,128]{2,1,0:T(8,128)}, f32[2,136,128]{2,1,0:T(8,128)}, u32[]{:S(2)}, u32[]{:S(2)}) collective-permute-start(f32[2,136,128]{2,1,0:T(8,128)} %pad_maximum_fusion.2), channel_id=1, source_target_pairs={{0,384},{16,144},{32,416},{48,176},{64,448},{80,208},{96,480},{112... | collective-permute-start | bytes 417800 | tf_op jit(solution)/shard_map/ppermute | solution.py:32
  50.0 0.0 collective-permute-done.5
  50.0 2.6 %collective-permute-done.4 = f32[2,136,128]{2,1,0:T(8,128)} collective-permute-done((f32[2,136,128]{2,1,0:T(8,128)}, f32[2,136,128]{2,1,0:T(8,128)}, u32[]{:S(2)}, u32[]{:S(2)}) %collective-permute-start.4) | collective-permute-done | bytes 139296 | tf_op jit(solution)/shard_map/ppermute | solution.py:32
  52.5 0.8 fusion.42
  53.4 0.1 collective-permute-done.6
  53.5 2.0 %multiply_add_fusion = (bf16[2,128,128]{2,1,0:T(8,128)(2,1)}, bf16[2,128,128]{2,1,0:T(8,128)(2,1)}) fusion(f32[2]{0:T(128)} %multiply_exponential_fusion.1, f32[2,128,128]{2,1,0:T(8,128)S(1)} %fusion.11, f32[2,128,128]{2,1,0:T(8,128)} %copy-done.2, pred[]{:T(512)S(6)} %eq.6, f32[2,136,128]{2,1,0:T(8,128)} %collective-permute-done.3, f32[2]{0:T(128)} %copy-done.8, ...), kind=kLoop, calls=%fused_computation.47 | loop fusion | flops 557056 | bytes 1179705 | tf_op jit(solution)/shard_map/add | solution.py:75
  55.6 2.0 %collective-permute-start.7 = (bf16[2,128,128]{2,1,0:T(8,128)(2,1)}, bf16[2,128,128]{2,1,0:T(8,128)(2,1)S(1)}, u32[]{:S(2)}, u32[]{:S(2)}) collective-permute-start(bf16[2,128,128]{2,1,0:T(8,128)(2,1)} %get-tuple-element.16), channel_id=1, source_target_pairs={{0,16},{16,0},{32,48},{48,32},{64,80},{80,64},{96,112},{112,96},{1... | collective-permute-start | bytes 196616 | tf_op jit(solution)/shard_map/ppermute | solution.py:74
  57.6 0.0 copy-done.1
  57.6 4.0 %fusion.3 = f32[768,2,128]{0,2,1:T(8,128)} fusion(s32[2,768]{1,0:T(2,128)S(1)} %get-tuple-element.19, bf16[768,2,128]{0,2,1:T(8,128)(2,1)S(1)} %bitcast.73, bf16[768,256]{1,0:T(8,128)(2,1)} %param.9, bf16[768,256]{1,0:T(8,128)(2,1)S(1)} %copy-done.1), kind=kOutput, calls=%fused_computation.3 | convolution fusion | flops 612237312 | bytes 1972224 | tf_op jit(solution)/shard_map/hts,shd->thd/dot_general | solution.py:94
  61.6 0.0 collective-permute-done.7
  61.6 0.0 copy-done.4
  61.6 1.4 fusion.7
  63.1 0.4 multiply_reduce_fusion
  63.5 1.5 multiply_convert_fusion.4
  65.0 0.0 all-gather.2.cloned.1.call-update
  65.0 89.8 %all-gather.2.cloned.1.call-done = bf16[768,4096]{0,1:T(8,128)(2,1)} async-done(((bf16[768,256]{0,1:T(8,128)(2,1)}), bf16[768,4096]{0,1:T(8,128)(2,1)}) %all-gather.2.cloned.1.call-update) | async-done | bytes 6291472 | tf_op jit(solution)/shard_map/all_gather | solution.py:126
  154.8 0.0 copy-done
  154.8 5.8 %fusion.8 = bf16[768,320]{0,1:T(8,128)(2,1)} fusion(bf16[4096,320]{0,1:T(8,128)(2,1)S(1)} %copy-done, bf16[768,4096]{0,1:T(8,128)(2,1)} %all-gather.2.cloned.1.call-done, bf16[768,320]{0,1:T(8,128)(2,1)} %param.13), kind=kOutput, calls=%fused_computation.11 | convolution fusion | flops 2014003200 | bytes 9895936 | tf_op jit(solution)/shard_map/dot_general | solution.py:125
  (6 shorter events, 0.0 us)
Async XLA Ops:
  6.5 148.3 %copy-start = (bf16[4096,320]{0,1:T(8,128)(2,1)S(1)}, bf16[4096,320]{0,1:T(8,128)(2,1)}, u32[]{:S(2)}) copy-start(bf16[4096,320]{0,1:T(8,128)(2,1)} %param.12) | copy-start | bytes 7864324
  6.5 51.1 %copy-start.1 = (bf16[768,256]{1,0:T(8,128)(2,1)S(1)}, bf16[768,256]{1,0:T(8,128)(2,1)}, u32[]{:S(2)}) copy-start(bf16[768,256]{1,0:T(8,128)(2,1)} %param.7) | copy-start | bytes 1179652
  6.5 148.3 %all-gather.2.cloned.1.call-start = ((), (), s32[]{:S(2)}) async-start(), calls=%async_computation | async-start | bytes 6684672 | tf_op jit(solution)/shard_map/all_gather | solution.py:126
  13.6 4.1 %copy-start.2 = (f32[2,128,128]{2,1,0:T(8,128)}, f32[2,128,128]{2,1,0:T(8,128)S(1)}, u32[]{:S(2)}) copy-start(f32[2,128,128]{2,1,0:T(8,128)S(1)} %get-tuple-element.21) | copy-start | bytes 393220
  14.4 3.3 %collective-permute-start = (f32[2,136,128]{2,1,0:T(8,128)S(1)}, f32[2,136,128]{2,1,0:T(8,128)S(1)}, u32[]{:S(2)}, u32[]{:S(2)}) collective-permute-start(f32[2,136,128]{2,1,0:T(8,128)S(1)} %pad_maximum_fusion), channel_id=1, source_target_pairs={{0,16},{16,0},{32,48},{48,32},{64,80},{80,64},{96,112},{112,96},{1... | collective-permute-start | bytes 417800 | tf_op jit(solution)/shard_map/ppermute | solution.py:48
  16.4 5.5 %copy-start.6 = (f32[2,1]{1,0:T(2,128)}, f32[2,1]{1,0:T(2,128)S(1)}, u32[]{:S(2)}) copy-start(f32[2,1]{1,0:T(2,128)S(1)} %multiply_exponential_fusion) | copy-start | bytes 28
  17.7 1.5 copy-start.5
  17.8 12.6 %copy-start.9 = (f32[2]{0:T(128)}, f32[2]{0:T(128)S(1)}, u32[]{:S(2)}) copy-start(f32[2]{0:T(128)S(1)} %get-tuple-element.14) | copy-start | bytes 28
  17.9 0.6 copy-start.3
  19.2 13.1 %collective-permute-start.3 = (f32[2,136,128]{2,1,0:T(8,128)}, f32[2,136,128]{2,1,0:T(8,128)}, u32[]{:S(2)}, u32[]{:S(2)}) collective-permute-start(f32[2,136,128]{2,1,0:T(8,128)} %pad_maximum_fusion.1), channel_id=1, source_target_pairs={{0,96},{16,48},{32,0},{48,80},{64,32},{80,112},{96,64},{112,16},{1... | collective-permute-start | bytes 417800 | tf_op jit(solution)/shard_map/ppermute | solution.py:32
  21.9 12.5 %collective-permute-start.2 = (f32[2,136,128]{2,1,0:T(8,128)}, f32[2,136,128]{2,1,0:T(8,128)}, u32[]{:S(2)}, u32[]{:S(2)}) collective-permute-start(f32[2,136,128]{2,1,0:T(8,128)} %pad_maximum_fusion.1), channel_id=1, source_target_pairs={{0,64},{16,80},{32,96},{48,112},{64,0},{80,16},{96,32},{112,48},{1... | collective-permute-start | bytes 417800 | tf_op jit(solution)/shard_map/ppermute | solution.py:32
  30.3 7.3 %collective-permute-start.1 = (f32[2,136,128]{2,1,0:T(8,128)}, f32[2,136,128]{2,1,0:T(8,128)}, u32[]{:S(2)}, u32[]{:S(2)}) collective-permute-start(f32[2,136,128]{2,1,0:T(8,128)} %pad_maximum_fusion.1), channel_id=1, source_target_pairs={{0,32},{16,112},{32,64},{48,16},{64,96},{80,48},{96,0},{112,80},{1... | collective-permute-start | bytes 417800 | tf_op jit(solution)/shard_map/ppermute | solution.py:32
  38.9 1.2 copy-start.7
  38.9 1.2 copy-start.8
  40.9 9.0 %collective-permute-start.5 = (f32[2,136,128]{2,1,0:T(8,128)}, f32[2,136,128]{2,1,0:T(8,128)}, u32[]{:S(2)}, u32[]{:S(2)}) collective-permute-start(f32[2,136,128]{2,1,0:T(8,128)} %pad_maximum_fusion.2), channel_id=1, source_target_pairs={{0,256},{16,272},{32,288},{48,304},{64,320},{80,336},{96,352},{112... | collective-permute-start | bytes 417800 | tf_op jit(solution)/shard_map/ppermute | solution.py:32
  42.9 9.7 %collective-permute-start.4 = (f32[2,136,128]{2,1,0:T(8,128)}, f32[2,136,128]{2,1,0:T(8,128)}, u32[]{:S(2)}, u32[]{:S(2)}) collective-permute-start(f32[2,136,128]{2,1,0:T(8,128)} %pad_maximum_fusion.2), channel_id=1, source_target_pairs={{0,128},{16,400},{32,160},{48,432},{64,192},{80,464},{96,224},{112... | collective-permute-start | bytes 417800 | tf_op jit(solution)/shard_map/ppermute | solution.py:32
  44.8 8.7 %collective-permute-start.6 = (f32[2,136,128]{2,1,0:T(8,128)}, f32[2,136,128]{2,1,0:T(8,128)}, u32[]{:S(2)}, u32[]{:S(2)}) collective-permute-start(f32[2,136,128]{2,1,0:T(8,128)} %pad_maximum_fusion.2), channel_id=1, source_target_pairs={{0,384},{16,144},{32,416},{48,176},{64,448},{80,208},{96,480},{112... | collective-permute-start | bytes 417800 | tf_op jit(solution)/shard_map/ppermute | solution.py:32
  55.5 6.1 %copy-start.4 = (bf16[2,128,128]{2,1,0:T(8,128)(2,1)S(1)}, bf16[2,128,128]{2,1,0:T(8,128)(2,1)}, u32[]{:S(2)}) copy-start(bf16[2,128,128]{2,1,0:T(8,128)(2,1)} %get-tuple-element.17) | copy-start | bytes 196612
  55.6 6.1 %collective-permute-start.7 = (bf16[2,128,128]{2,1,0:T(8,128)(2,1)}, bf16[2,128,128]{2,1,0:T(8,128)(2,1)S(1)}, u32[]{:S(2)}, u32[]{:S(2)}) collective-permute-start(bf16[2,128,128]{2,1,0:T(8,128)(2,1)} %get-tuple-element.16), channel_id=1, source_target_pairs={{0,16},{16,0},{32,48},{48,32},{64,80},{80,64},{96,112},{112,96},{1... | collective-permute-start | bytes 196616 | tf_op jit(solution)/shard_map/ppermute | solution.py:74
Sparse Core Ops, SparseCore 0:
  65.1 89.6 all-gather.1

commit v5 on v4

--- a/solution.py
+++ b/solution.py
@@ -79,6 +79,29 @@
     return state_fwd, state_bwd
 
 
+def ring_project(normed, out_weight):
+    tp_count = lax.axis_size("tp")
+    me = lax.axis_index("tp")
+    width = normed.shape[1]
+
+    def part(shard, source):
+        rows = lax.dynamic_slice_in_dim(out_weight, source * width, width, axis=0)
+        return jnp.dot(shard, rows, preferred_element_type=jnp.float32)
+
+    up = [(j, (j + 1) % tp_count) for j in range(tp_count)]
+    down = [(j, (j - 1) % tp_count) for j in range(tp_count)]
+    mixed = part(normed, me)
+    rising, falling = normed, normed
+    for step in range(1, tp_count // 2 + 1):
+        rising = lax.ppermute(rising, "tp", up)
+        if step < tp_count - step:
+            falling = lax.ppermute(falling, "tp", down)
+        mixed = mixed + part(rising, (me - step) % tp_count)
+        if step < tp_count - step:
+            mixed = mixed + part(falling, (me + step) % tp_count)
+    return mixed
+
+
 def local(query_vectors, key_vectors, value_vectors, decay_exp, norm_gain, out_weight, residual):
     tok_rows = query_vectors.shape[0]
     head_count = decay_exp.shape[0]
@@ -122,11 +145,7 @@
         jnp.bfloat16
     )
     normed = normed.reshape(tok_rows, head_count * HD)
-    mixed = jnp.dot(
-        lax.all_gather(normed, "tp", axis=1, tiled=True),
-        out_weight,
-        preferred_element_type=jnp.float32,
-    )
+    mixed = ring_project(normed, out_weight)
     return (residual.astype(jnp.float32) + mixed).astype(jnp.bfloat16)
 
 

time: 168 us -> 169 us (level)
  starting transfers between devices: 26 us -> 85.1 us
  waiting for transfers between devices: 99 us -> 53.6 us
  between operations: 13.7 us -> 0.85 us
    all_gather x1 -> x0, waiting for transfers between devices: 89.8 us -> none  [local(): lax.all_gather(normed, 'tp', axis=1, tiled=True)]
    ppermute x0 -> x15, starting transfers between devices: none -> 59.7 us  [the longest x7 44.4 us: ring_project(): falling = lax.ppermute(falling, 'tp', down)]
    ppermute x0 -> x15, waiting for transfers between devices: none -> 43.4 us  [the longest x7 25.9 us: ring_project(): falling = lax.ppermute(falling, 'tp', down)]
    dot_general x1 -> x16, matrix products: 5.81 us -> 6.49 us  [part(): return jnp.dot(shard, rows, preferred_element_type=jnp.float32)]
  transfers between devices with their start and end apart: 9 -> 23, of which waited for: 6 -> 13; matrix products, arithmetic and copies ran while one was open for 3% -> 6% of each run, Pallas kernels for 0% -> 0%
where the time goes in v5:
time: 169 us; the launch traced here: 168 us
  starting transfers between devices  85.1 us (50%)
  waiting for transfers between devices  53.6 us (32%)
  matrix products  14.9 us (9%)
  other arithmetic  9.29 us (5%)
  local copies, waits for them, and re-layouts  3.89 us (2%)
    ppermute x7, starting transfers between devices, ring_project(): falling = lax.ppermute(falling, 'tp', down)  44.4 us
    ppermute x7, waiting for transfers between devices, ring_project(): falling = lax.ppermute(falling, 'tp', down)  25.9 us
    ppermute x6, starting transfers between devices, gather_line(): got.append(unpack(lax.ppermute(pack(total_s, total_p), 'seq', pairs)))  21.4 us
    ppermute x8, waiting for transfers between devices, ring_project(): rising = lax.ppermute(rising, 'tp', up)  17.5 us
    ppermute x8, starting transfers between devices, ring_project(): rising = lax.ppermute(rising, 'tp', up)  15.3 us
    ppermute x6, waiting for transfers between devices, gather_line(): got.append(unpack(lax.ppermute(pack(total_s, total_p), 'seq', pairs)))  8.95 us
    dot_general x16, matrix products, part(): return jnp.dot(shard, rows, preferred_element_type=jnp.float32)  6.49 us
    dot_general x1, matrix products, local(): jnp.einsum('hts,shd->thd', local_weights, value_heads, preferred_element_...  4.01 us
  transfers between devices with their start and end apart: 23, of which 13 were waited for; matrix products, arithmetic and copies ran while one was open for 6% of the time, Pallas kernels for 0%

profile of v5, /device:TPU:6, one launch (start us, length us, event | category | flops | bytes accessed | tf_op | source)
XLA Modules:
  0.0 167.6 jit_solution(5845551787305752316)
XLA Ops:
  0.0 0.8 reshape.87
  0.9 0.6 reduce-window.6
  1.9 0.6 exponential_bitcast_fusion.1
  2.8 0.6 multiply_exponential_fusion.1
  3.4 1.2 copy.27
  4.5 1.3 fusion.18
  5.9 1.3 broadcast_select_fusion.1
  7.2 0.7 broadcast_in_dim.22
  7.9 1.9 %collective-permute-start = (f32[2,136,128]{2,1,0:T(8,128)S(1)}, f32[2,136,128]{2,1,0:T(8,128)S(1)}, u32[]{:S(2)}, u32[]{:S(2)}) collective-permute-start(f32[2,136,128]{2,1,0:T(8,128)S(1)} %pad_maximum_fusion), channel_id=1, source_target_pairs={{0,16},{16,0},{32,48},{48,32},{64,80},{80,64},{96,112},{112,96},{1... | collective-permute-start | bytes 417800 | tf_op jit(solution)/shard_map/ppermute | solution.py:48
  9.9 1.2 collective-permute-done
  11.5 0.6 copy-done.3
  12.0 0.7 pad_maximum_fusion.1
  12.7 7.8 %collective-permute-start.1 = (f32[2,136,128]{2,1,0:T(8,128)}, f32[2,136,128]{2,1,0:T(8,128)}, u32[]{:S(2)}, u32[]{:S(2)}) collective-permute-start(f32[2,136,128]{2,1,0:T(8,128)} %pad_maximum_fusion.1), channel_id=1, source_target_pairs={{0,32},{16,112},{32,64},{48,16},{64,96},{80,48},{96,0},{112,80},{1... | collective-permute-start | bytes 417800 | tf_op jit(solution)/shard_map/ppermute | solution.py:32
  20.5 1.9 %collective-permute-start.2 = (f32[2,136,128]{2,1,0:T(8,128)}, f32[2,136,128]{2,1,0:T(8,128)}, u32[]{:S(2)}, u32[]{:S(2)}) collective-permute-start(f32[2,136,128]{2,1,0:T(8,128)} %pad_maximum_fusion.1), channel_id=1, source_target_pairs={{0,64},{16,80},{32,96},{48,112},{64,0},{80,16},{96,32},{112,48},{1... | collective-permute-start | bytes 417800 | tf_op jit(solution)/shard_map/ppermute | solution.py:32
  22.4 2.8 %collective-permute-start.3 = (f32[2,136,128]{2,1,0:T(8,128)}, f32[2,136,128]{2,1,0:T(8,128)}, u32[]{:S(2)}, u32[]{:S(2)}) collective-permute-start(f32[2,136,128]{2,1,0:T(8,128)} %pad_maximum_fusion.1), channel_id=1, source_target_pairs={{0,96},{16,48},{32,0},{48,80},{64,32},{80,112},{96,64},{112,16},{1... | collective-permute-start | bytes 417800 | tf_op jit(solution)/shard_map/ppermute | solution.py:32
  25.2 4.0 %collective-permute-done.2 = f32[2,136,128]{2,1,0:T(8,128)} collective-permute-done((f32[2,136,128]{2,1,0:T(8,128)}, f32[2,136,128]{2,1,0:T(8,128)}, u32[]{:S(2)}, u32[]{:S(2)}) %collective-permute-start.2) | collective-permute-done | bytes 139296 | tf_op jit(solution)/shard_map/ppermute | solution.py:32
  29.2 1.6 collective-permute-done.3
  30.9 1.3 fusion.89
  32.2 1.2 multiply_add_fusion.1
  33.5 0.7 pad_maximum_fusion.2
  34.2 1.9 %collective-permute-start.4 = (f32[2,136,128]{2,1,0:T(8,128)}, f32[2,136,128]{2,1,0:T(8,128)}, u32[]{:S(2)}, u32[]{:S(2)}) collective-permute-start(f32[2,136,128]{2,1,0:T(8,128)} %pad_maximum_fusion.2), channel_id=1, source_target_pairs={{0,128},{16,400},{32,160},{48,432},{64,192},{80,464},{96,224},{112... | collective-permute-start | bytes 417800 | tf_op jit(solution)/shard_map/ppermute | solution.py:32
  36.1 3.4 %collective-permute-start.5 = (f32[2,136,128]{2,1,0:T(8,128)}, f32[2,136,128]{2,1,0:T(8,128)}, u32[]{:S(2)}, u32[]{:S(2)}) collective-permute-start(f32[2,136,128]{2,1,0:T(8,128)} %pad_maximum_fusion.2), channel_id=1, source_target_pairs={{0,256},{16,272},{32,288},{48,304},{64,320},{80,336},{96,352},{112... | collective-permute-start | bytes 417800 | tf_op jit(solution)/shard_map/ppermute | solution.py:32
  39.5 3.6 %collective-permute-start.6 = (f32[2,136,128]{2,1,0:T(8,128)}, f32[2,136,128]{2,1,0:T(8,128)}, u32[]{:S(2)}, u32[]{:S(2)}) collective-permute-start(f32[2,136,128]{2,1,0:T(8,128)} %pad_maximum_fusion.2), channel_id=1, source_target_pairs={{0,384},{16,144},{32,416},{48,176},{64,448},{80,208},{96,480},{112... | collective-permute-start | bytes 417800 | tf_op jit(solution)/shard_map/ppermute | solution.py:32
  43.2 3.1 %collective-permute-done.4 = f32[2,136,128]{2,1,0:T(8,128)} collective-permute-done((f32[2,136,128]{2,1,0:T(8,128)}, f32[2,136,128]{2,1,0:T(8,128)}, u32[]{:S(2)}, u32[]{:S(2)}) %collective-permute-start.4) | collective-permute-done | bytes 139296 | tf_op jit(solution)/shard_map/ppermute | solution.py:32
  46.3 0.8 fusion.88
  47.4 2.0 %multiply_add_fusion = (bf16[2,128,128]{2,1,0:T(8,128)(2,1)}, bf16[2,128,128]{2,1,0:T(8,128)(2,1)}) fusion(f32[2]{0:T(128)} %multiply_exponential_fusion.1, f32[2,128,128]{2,1,0:T(8,128)S(1)} %fusion.18, f32[2,128,128]{2,1,0:T(8,128)} %copy-done.2, pred[]{:T(512)S(6)} %eq.21, f32[2,136,128]{2,1,0:T(8,128)} %collective-permute-done.3, f32[2]{0:T(128)} %copy-done.9, ...), kind=kLoop, calls=%fused_computation.85 | loop fusion | flops 557056 | bytes 1179705 | tf_op jit(solution)/shard_map/add | solution.py:75
  49.4 2.0 %collective-permute-start.7 = (bf16[2,128,128]{2,1,0:T(8,128)(2,1)}, bf16[2,128,128]{2,1,0:T(8,128)(2,1)S(1)}, u32[]{:S(2)}, u32[]{:S(2)}) collective-permute-start(bf16[2,128,128]{2,1,0:T(8,128)(2,1)} %get-tuple-element.16), channel_id=1, source_target_pairs={{0,16},{16,0},{32,48},{48,32},{64,80},{80,64},{96,112},{112,96},{1... | collective-permute-start | bytes 196616 | tf_op jit(solution)/shard_map/ppermute | solution.py:74
  51.5 4.0 %fusion.10 = f32[768,2,128]{0,2,1:T(8,128)} fusion(s32[2,768]{1,0:T(2,128)S(1)} %get-tuple-element.19, bf16[768,2,128]{0,2,1:T(8,128)(2,1)S(1)} %bitcast.87, bf16[768,256]{1,0:T(8,128)(2,1)} %param.9, bf16[768,256]{1,0:T(8,128)(2,1)S(1)} %copy-done.1), kind=kOutput, calls=%fused_computation.19 | convolution fusion | flops 612237312 | bytes 1972224 | tf_op jit(solution)/shard_map/hts,shd->thd/dot_general | solution.py:117
  55.5 1.5 fusion.14
  57.0 0.3 multiply_reduce_fusion
  57.5 10.8 %collective-permute-start.9 = (bf16[768,256]{0,1:T(8,128)(2,1)S(1)}, bf16[768,256]{0,1:T(8,128)(2,1)}, u32[]{:S(2)}, u32[]{:S(2)}) collective-permute-start(bf16[768,256]{0,1:T(8,128)(2,1)S(1)} %bitcast.88), channel_id=1, source_target_pairs={{0,15},{1,0},{2,1},{3,2},{4,3},{5,4},{6,5},{7,6},{8,7},{9,8},{10,9... | collective-permute-start | bytes 1179656 | tf_op jit(solution)/shard_map/ppermute | solution.py:98
  68.3 1.9 %collective-permute-start.8 = (bf16[768,256]{0,1:T(8,128)(2,1)S(1)}, bf16[768,256]{0,1:T(8,128)(2,1)S(1)}, u32[]{:S(2)}, u32[]{:S(2)}) collective-permute-start(bf16[768,256]{0,1:T(8,128)(2,1)S(1)} %bitcast.89), channel_id=1, source_target_pairs={{0,1},{1,2},{2,3},{3,4},{4,5},{5,6},{6,7},{7,8},{8,9},{9,10},{10,1... | collective-permute-start | bytes 1179656 | tf_op jit(solution)/shard_map/ppermute | solution.py:96
  70.5 0.3 fusion.59
  70.8 6.5 %collective-permute-done.9 = bf16[768,256]{0,1:T(8,128)(2,1)} collective-permute-done((bf16[768,256]{0,1:T(8,128)(2,1)S(1)}, bf16[768,256]{0,1:T(8,128)(2,1)}, u32[]{:S(2)}, u32[]{:S(2)}) %collective-permute-start.9) | collective-permute-done | bytes 393248 | tf_op jit(solution)/shard_map/ppermute | solution.py:98
  77.3 5.7 %collective-permute-start.11 = (bf16[768,256]{0,1:T(8,128)(2,1)}, bf16[768,256]{0,1:T(8,128)(2,1)S(1)}, u32[]{:S(2)}, u32[]{:S(2)}) collective-permute-start(bf16[768,256]{0,1:T(8,128)(2,1)} %collective-permute-done.9), channel_id=1, source_target_pairs={{0,15},{1,0},{2,1},{3,2},{4,3},{5,4},{6,5},{7,6},{8,7},{9,8},{10,9... | collective-permute-start | bytes 1179656 | tf_op jit(solution)/shard_map/ppermute | solution.py:98
  83.0 1.9 %collective-permute-start.10 = (bf16[768,256]{0,1:T(8,128)(2,1)S(1)}, bf16[768,256]{0,1:T(8,128)(2,1)S(1)}, u32[]{:S(2)}, u32[]{:S(2)}) collective-permute-start(bf16[768,256]{0,1:T(8,128)(2,1)S(1)} %collective-permute-done.8), channel_id=1, source_target_pairs={{0,1},{1,2},{2,3},{3,4},{4,5},{5,6},{6,7},{7,8},{8,9},{9,10},{10,1... | collective-permute-start | bytes 1179656 | tf_op jit(solution)/shard_map/ppermute | solution.py:96
  85.0 0.3 convolution_add_fusion.8
  85.3 1.3 convolution_add_fusion.7
  86.6 5.0 %collective-permute-done.11 = bf16[768,256]{0,1:T(8,128)(2,1)S(1)} collective-permute-done((bf16[768,256]{0,1:T(8,128)(2,1)}, bf16[768,256]{0,1:T(8,128)(2,1)S(1)}, u32[]{:S(2)}, u32[]{:S(2)}) %collective-permute-start.11) | collective-permute-done | bytes 393248 | tf_op jit(solution)/shard_map/ppermute | solution.py:98
  91.6 5.5 %collective-permute-start.13 = (bf16[768,256]{0,1:T(8,128)(2,1)S(1)}, bf16[768,256]{0,1:T(8,128)(2,1)S(1)}, u32[]{:S(2)}, u32[]{:S(2)}) collective-permute-start(bf16[768,256]{0,1:T(8,128)(2,1)S(1)} %collective-permute-done.11), channel_id=1, source_target_pairs={{0,15},{1,0},{2,1},{3,2},{4,3},{5,4},{6,5},{7,6},{8,7},{9,8},{10,9... | collective-permute-start | bytes 1179656 | tf_op jit(solution)/shard_map/ppermute | solution.py:98
  97.1 1.9 %collective-permute-start.12 = (bf16[768,256]{0,1:T(8,128)(2,1)S(1)}, bf16[768,256]{0,1:T(8,128)(2,1)S(1)}, u32[]{:S(2)}, u32[]{:S(2)}) collective-permute-start(bf16[768,256]{0,1:T(8,128)(2,1)S(1)} %collective-permute-done.10), channel_id=1, source_target_pairs={{0,1},{1,2},{2,3},{3,4},{4,5},{5,6},{6,7},{7,8},{8,9},{9,10},{10,1... | collective-permute-start | bytes 1179656 | tf_op jit(solution)/shard_map/ppermute | solution.py:96
  99.0 0.3 fusion.54
  99.6 4.8 %collective-permute-done.13 = bf16[768,256]{0,1:T(8,128)(2,1)S(1)} collective-permute-done((bf16[768,256]{0,1:T(8,128)(2,1)S(1)}, bf16[768,256]{0,1:T(8,128)(2,1)S(1)}, u32[]{:S(2)}, u32[]{:S(2)}) %collective-permute-start.13) | collective-permute-done | bytes 393248 | tf_op jit(solution)/shard_map/ppermute | solution.py:98
  104.4 5.6 %collective-permute-start.15 = (bf16[768,256]{0,1:T(8,128)(2,1)S(1)}, bf16[768,256]{0,1:T(8,128)(2,1)S(1)}, u32[]{:S(2)}, u32[]{:S(2)}) collective-permute-start(bf16[768,256]{0,1:T(8,128)(2,1)S(1)} %collective-permute-done.13), channel_id=1, source_target_pairs={{0,15},{1,0},{2,1},{3,2},{4,3},{5,4},{6,5},{7,6},{8,7},{9,8},{10,9... | collective-permute-start | bytes 1179656 | tf_op jit(solution)/shard_map/ppermute | solution.py:98
  110.0 1.9 %collective-permute-start.14 = (bf16[768,256]{0,1:T(8,128)(2,1)S(1)}, bf16[768,256]{0,1:T(8,128)(2,1)S(1)}, u32[]{:S(2)}, u32[]{:S(2)}) collective-permute-start(bf16[768,256]{0,1:T(8,128)(2,1)S(1)} %collective-permute-done.12), channel_id=1, source_target_pairs={{0,1},{1,2},{2,3},{3,4},{4,5},{5,6},{6,7},{7,8},{8,9},{9,10},{10,1... | collective-permute-start | bytes 1179656 | tf_op jit(solution)/shard_map/ppermute | solution.py:96
  112.2 0.3 fusion.8
  112.5 3.9 %collective-permute-done.15 = bf16[768,256]{0,1:T(8,128)(2,1)S(1)} collective-permute-done((bf16[768,256]{0,1:T(8,128)(2,1)S(1)}, bf16[768,256]{0,1:T(8,128)(2,1)S(1)}, u32[]{:S(2)}, u32[]{:S(2)}) %collective-permute-start.15) | collective-permute-done | bytes 393248 | tf_op jit(solution)/shard_map/ppermute | solution.py:98
  116.4 5.6 %collective-permute-start.17 = (bf16[768,256]{0,1:T(8,128)(2,1)S(1)}, bf16[768,256]{0,1:T(8,128)(2,1)S(1)}, u32[]{:S(2)}, u32[]{:S(2)}) collective-permute-start(bf16[768,256]{0,1:T(8,128)(2,1)S(1)} %collective-permute-done.15), channel_id=1, source_target_pairs={{0,15},{1,0},{2,1},{3,2},{4,3},{5,4},{6,5},{7,6},{8,7},{9,8},{10,9... | collective-permute-start | bytes 1179656 | tf_op jit(solution)/shard_map/ppermute | solution.py:98
  122.0 1.9 %collective-permute-start.16 = (bf16[768,256]{0,1:T(8,128)(2,1)S(1)}, bf16[768,256]{0,1:T(8,128)(2,1)S(1)}, u32[]{:S(2)}, u32[]{:S(2)}) collective-permute-start(bf16[768,256]{0,1:T(8,128)(2,1)S(1)} %collective-permute-done.14), channel_id=1, source_target_pairs={{0,1},{1,2},{2,3},{3,4},{4,5},{5,6},{6,7},{7,8},{8,9},{9,10},{10,1... | collective-permute-start | bytes 1179656 | tf_op jit(solution)/shard_map/ppermute | solution.py:96
  124.2 0.3 fusion.7
  124.5 3.0 %collective-permute-done.17 = bf16[768,256]{0,1:T(8,128)(2,1)S(1)} collective-permute-done((bf16[768,256]{0,1:T(8,128)(2,1)S(1)}, bf16[768,256]{0,1:T(8,128)(2,1)S(1)}, u32[]{:S(2)}, u32[]{:S(2)}) %collective-permute-start.17) | collective-permute-done | bytes 393248 | tf_op jit(solution)/shard_map/ppermute | solution.py:98
  127.5 5.6 %collective-permute-start.19 = (bf16[768,256]{0,1:T(8,128)(2,1)S(1)}, bf16[768,256]{0,1:T(8,128)(2,1)S(1)}, u32[]{:S(2)}, u32[]{:S(2)}) collective-permute-start(bf16[768,256]{0,1:T(8,128)(2,1)S(1)} %collective-permute-done.17), channel_id=1, source_target_pairs={{0,15},{1,0},{2,1},{3,2},{4,3},{5,4},{6,5},{7,6},{8,7},{9,8},{10,9... | collective-permute-start | bytes 1179656 | tf_op jit(solution)/shard_map/ppermute | solution.py:98
  133.1 1.9 %collective-permute-start.18 = (bf16[768,256]{0,1:T(8,128)(2,1)S(1)}, bf16[768,256]{0,1:T(8,128)(2,1)S(1)}, u32[]{:S(2)}, u32[]{:S(2)}) collective-permute-start(bf16[768,256]{0,1:T(8,128)(2,1)S(1)} %collective-permute-done.16), channel_id=1, source_target_pairs={{0,1},{1,2},{2,3},{3,4},{4,5},{5,6},{6,7},{7,8},{8,9},{9,10},{10,1... | collective-permute-start | bytes 1179656 | tf_op jit(solution)/shard_map/ppermute | solution.py:96
  135.0 0.3 fusion.45
  135.3 0.3 fusion.6
  135.6 2.7 %collective-permute-done.19 = bf16[768,256]{0,1:T(8,128)(2,1)S(1)} collective-permute-done((bf16[768,256]{0,1:T(8,128)(2,1)S(1)}, bf16[768,256]{0,1:T(8,128)(2,1)S(1)}, u32[]{:S(2)}, u32[]{:S(2)}) %collective-permute-start.19) | collective-permute-done | bytes 393248 | tf_op jit(solution)/shard_map/ppermute | solution.py:98
  138.4 5.6 %collective-permute-start.21 = (bf16[768,256]{0,1:T(8,128)(2,1)S(1)}, bf16[768,256]{0,1:T(8,128)(2,1)S(1)}, u32[]{:S(2)}, u32[]{:S(2)}) collective-permute-start(bf16[768,256]{0,1:T(8,128)(2,1)S(1)} %collective-permute-done.19), channel_id=1, source_target_pairs={{0,15},{1,0},{2,1},{3,2},{4,3},{5,4},{6,5},{7,6},{8,7},{9,8},{10,9... | collective-permute-start | bytes 1179656 | tf_op jit(solution)/shard_map/ppermute | solution.py:98
  144.0 1.9 %collective-permute-start.20 = (bf16[768,256]{0,1:T(8,128)(2,1)S(1)}, bf16[768,256]{0,1:T(8,128)(2,1)S(1)}, u32[]{:S(2)}, u32[]{:S(2)}) collective-permute-start(bf16[768,256]{0,1:T(8,128)(2,1)S(1)} %collective-permute-done.18), channel_id=1, source_target_pairs={{0,1},{1,2},{2,3},{3,4},{4,5},{5,6},{6,7},{7,8},{8,9},{9,10},{10,1... | collective-permute-start | bytes 1179656 | tf_op jit(solution)/shard_map/ppermute | solution.py:96
  145.9 0.3 fusion.42
  146.5 9.1 %collective-permute-done.20 = bf16[768,256]{0,1:T(8,128)(2,1)S(1)} collective-permute-done((bf16[768,256]{0,1:T(8,128)(2,1)S(1)}, bf16[768,256]{0,1:T(8,128)(2,1)S(1)}, u32[]{:S(2)}, u32[]{:S(2)}) %collective-permute-start.20) | collective-permute-done | bytes 393248 | tf_op jit(solution)/shard_map/ppermute | solution.py:96
  155.6 1.9 %collective-permute-start.22 = (bf16[768,256]{0,1:T(8,128)(2,1)S(1)}, bf16[768,256]{0,1:T(8,128)(2,1)S(1)}, u32[]{:S(2)}, u32[]{:S(2)}) collective-permute-start(bf16[768,256]{0,1:T(8,128)(2,1)S(1)} %collective-permute-done.20), channel_id=1, source_target_pairs={{0,1},{1,2},{2,3},{3,4},{4,5},{5,6},{6,7},{7,8},{8,9},{9,10},{10,1... | collective-permute-start | bytes 1179656 | tf_op jit(solution)/shard_map/ppermute | solution.py:96
  157.6 0.3 fusion.39
  158.2 8.3 %collective-permute-done.22 = bf16[768,256]{0,1:T(8,128)(2,1)S(1)} collective-permute-done((bf16[768,256]{0,1:T(8,128)(2,1)S(1)}, bf16[768,256]{0,1:T(8,128)(2,1)S(1)}, u32[]{:S(2)}, u32[]{:S(2)}) %collective-permute-start.22) | collective-permute-done | bytes 393248 | tf_op jit(solution)/shard_map/ppermute | solution.py:96
  166.5 1.1 fusion.15
  (52 shorter events, 3.1 us)
Async XLA Ops:
  0.0 70.5 %copy-start = (bf16[4096,320]{0,1:T(8,128)(2,1)S(1)}, bf16[4096,320]{0,1:T(8,128)(2,1)}, u32[]{:S(2)}) copy-start(bf16[4096,320]{0,1:T(8,128)(2,1)} %param.12) | copy-start | bytes 7864324
  4.5 46.9 %copy-start.1 = (bf16[768,256]{1,0:T(8,128)(2,1)S(1)}, bf16[768,256]{1,0:T(8,128)(2,1)}, u32[]{:S(2)}) copy-start(bf16[768,256]{1,0:T(8,128)(2,1)} %param.7) | copy-start | bytes 1179652
  7.1 4.1 %copy-start.2 = (f32[2,128,128]{2,1,0:T(8,128)}, f32[2,128,128]{2,1,0:T(8,128)S(1)}, u32[]{:S(2)}) copy-start(f32[2,128,128]{2,1,0:T(8,128)S(1)} %get-tuple-element.21) | copy-start | bytes 393220
  7.9 3.3 %collective-permute-start = (f32[2,136,128]{2,1,0:T(8,128)S(1)}, f32[2,136,128]{2,1,0:T(8,128)S(1)}, u32[]{:S(2)}, u32[]{:S(2)}) collective-permute-start(f32[2,136,128]{2,1,0:T(8,128)S(1)} %pad_maximum_fusion), channel_id=1, source_target_pairs={{0,16},{16,0},{32,48},{48,32},{64,80},{80,64},{96,112},{112,96},{1... | collective-permute-start | bytes 417800 | tf_op jit(solution)/shard_map/ppermute | solution.py:48
  9.9 10.5 %copy-start.7 = (f32[2,1]{1,0:T(2,128)}, f32[2,1]{1,0:T(2,128)S(1)}, u32[]{:S(2)}) copy-start(f32[2,1]{1,0:T(2,128)S(1)} %multiply_exponential_fusion) | copy-start | bytes 28
  11.2 1.5 copy-start.6
  11.3 11.1 %copy-start.10 = (f32[2]{0:T(128)}, f32[2]{0:T(128)S(1)}, u32[]{:S(2)}) copy-start(f32[2]{0:T(128)S(1)} %get-tuple-element.14) | copy-start | bytes 28
  11.4 0.6 copy-start.3
  12.7 12.5 %collective-permute-start.1 = (f32[2,136,128]{2,1,0:T(8,128)}, f32[2,136,128]{2,1,0:T(8,128)}, u32[]{:S(2)}, u32[]{:S(2)}) collective-permute-start(f32[2,136,128]{2,1,0:T(8,128)} %pad_maximum_fusion.1), channel_id=1, source_target_pairs={{0,32},{16,112},{32,64},{48,16},{64,96},{80,48},{96,0},{112,80},{1... | collective-permute-start | bytes 417800 | tf_op jit(solution)/shard_map/ppermute | solution.py:32
  20.5 8.8 %collective-permute-start.2 = (f32[2,136,128]{2,1,0:T(8,128)}, f32[2,136,128]{2,1,0:T(8,128)}, u32[]{:S(2)}, u32[]{:S(2)}) collective-permute-start(f32[2,136,128]{2,1,0:T(8,128)} %pad_maximum_fusion.1), channel_id=1, source_target_pairs={{0,64},{16,80},{32,96},{48,112},{64,0},{80,16},{96,32},{112,48},{1... | collective-permute-start | bytes 417800 | tf_op jit(solution)/shard_map/ppermute | solution.py:32
  22.4 8.5 %collective-permute-start.3 = (f32[2,136,128]{2,1,0:T(8,128)}, f32[2,136,128]{2,1,0:T(8,128)}, u32[]{:S(2)}, u32[]{:S(2)}) collective-permute-start(f32[2,136,128]{2,1,0:T(8,128)} %pad_maximum_fusion.1), channel_id=1, source_target_pairs={{0,96},{16,48},{32,0},{48,80},{64,32},{80,112},{96,64},{112,16},{1... | collective-permute-start | bytes 417800 | tf_op jit(solution)/shard_map/ppermute | solution.py:32
  32.2 1.2 copy-start.8
  32.2 1.2 copy-start.9
  34.2 12.1 %collective-permute-start.4 = (f32[2,136,128]{2,1,0:T(8,128)}, f32[2,136,128]{2,1,0:T(8,128)}, u32[]{:S(2)}, u32[]{:S(2)}) collective-permute-start(f32[2,136,128]{2,1,0:T(8,128)} %pad_maximum_fusion.2), channel_id=1, source_target_pairs={{0,128},{16,400},{32,160},{48,432},{64,192},{80,464},{96,224},{112... | collective-permute-start | bytes 417800 | tf_op jit(solution)/shard_map/ppermute | solution.py:32
  36.1 10.2 %collective-permute-start.5 = (f32[2,136,128]{2,1,0:T(8,128)}, f32[2,136,128]{2,1,0:T(8,128)}, u32[]{:S(2)}, u32[]{:S(2)}) collective-permute-start(f32[2,136,128]{2,1,0:T(8,128)} %pad_maximum_fusion.2), channel_id=1, source_target_pairs={{0,256},{16,272},{32,288},{48,304},{64,320},{80,336},{96,352},{112... | collective-permute-start | bytes 417800 | tf_op jit(solution)/shard_map/ppermute | solution.py:32
  39.5 7.8 %collective-permute-start.6 = (f32[2,136,128]{2,1,0:T(8,128)}, f32[2,136,128]{2,1,0:T(8,128)}, u32[]{:S(2)}, u32[]{:S(2)}) collective-permute-start(f32[2,136,128]{2,1,0:T(8,128)} %pad_maximum_fusion.2), channel_id=1, source_target_pairs={{0,384},{16,144},{32,416},{48,176},{64,448},{80,208},{96,480},{112... | collective-permute-start | bytes 417800 | tf_op jit(solution)/shard_map/ppermute | solution.py:32
  49.4 6.1 %copy-start.4 = (bf16[2,128,128]{2,1,0:T(8,128)(2,1)S(1)}, bf16[2,128,128]{2,1,0:T(8,128)(2,1)}, u32[]{:S(2)}) copy-start(bf16[2,128,128]{2,1,0:T(8,128)(2,1)} %get-tuple-element.17) | copy-start | bytes 196612
  49.4 6.1 %collective-permute-start.7 = (bf16[2,128,128]{2,1,0:T(8,128)(2,1)}, bf16[2,128,128]{2,1,0:T(8,128)(2,1)S(1)}, u32[]{:S(2)}, u32[]{:S(2)}) collective-permute-start(bf16[2,128,128]{2,1,0:T(8,128)(2,1)} %get-tuple-element.16), channel_id=1, source_target_pairs={{0,16},{16,0},{32,48},{48,32},{64,80},{80,64},{96,112},{112,96},{1... | collective-permute-start | bytes 196616 | tf_op jit(solution)/shard_map/ppermute | solution.py:74
  55.5 1.8 %copy-start.11 = (f32[256]{0:T(256)S(1)}, f32[256]{0:T(256)}, u32[]{:S(2)}) copy-start(f32[256]{0:T(256)} %param.11) | copy-start | bytes 3076
  57.5 19.9 %collective-permute-start.9 = (bf16[768,256]{0,1:T(8,128)(2,1)S(1)}, bf16[768,256]{0,1:T(8,128)(2,1)}, u32[]{:S(2)}, u32[]{:S(2)}) collective-permute-start(bf16[768,256]{0,1:T(8,128)(2,1)S(1)} %bitcast.88), channel_id=1, source_target_pairs={{0,15},{1,0},{2,1},{3,2},{4,3},{5,4},{6,5},{7,6},{8,7},{9,8},{10,9... | collective-permute-start | bytes 1179656 | tf_op jit(solution)/shard_map/ppermute | solution.py:98
  68.3 14.7 %collective-permute-start.8 = (bf16[768,256]{0,1:T(8,128)(2,1)S(1)}, bf16[768,256]{0,1:T(8,128)(2,1)S(1)}, u32[]{:S(2)}, u32[]{:S(2)}) collective-permute-start(bf16[768,256]{0,1:T(8,128)(2,1)S(1)} %bitcast.89), channel_id=1, source_target_pairs={{0,1},{1,2},{2,3},{3,4},{4,5},{5,6},{6,7},{7,8},{8,9},{9,10},{10,1... | collective-permute-start | bytes 1179656 | tf_op jit(solution)/shard_map/ppermute | solution.py:96
  77.3 14.2 %collective-permute-start.11 = (bf16[768,256]{0,1:T(8,128)(2,1)}, bf16[768,256]{0,1:T(8,128)(2,1)S(1)}, u32[]{:S(2)}, u32[]{:S(2)}) collective-permute-start(bf16[768,256]{0,1:T(8,128)(2,1)} %collective-permute-done.9), channel_id=1, source_target_pairs={{0,15},{1,0},{2,1},{3,2},{4,3},{5,4},{6,5},{7,6},{8,7},{9,8},{10,9... | collective-permute-start | bytes 1179656 | tf_op jit(solution)/shard_map/ppermute | solution.py:98
  83.0 14.0 %collective-permute-start.10 = (bf16[768,256]{0,1:T(8,128)(2,1)S(1)}, bf16[768,256]{0,1:T(8,128)(2,1)S(1)}, u32[]{:S(2)}, u32[]{:S(2)}) collective-permute-start(bf16[768,256]{0,1:T(8,128)(2,1)S(1)} %collective-permute-done.8), channel_id=1, source_target_pairs={{0,1},{1,2},{2,3},{3,4},{4,5},{5,6},{6,7},{7,8},{8,9},{9,10},{10,1... | collective-permute-start | bytes 1179656 | tf_op jit(solution)/shard_map/ppermute | solution.py:96
  91.6 12.8 %collective-permute-start.13 = (bf16[768,256]{0,1:T(8,128)(2,1)S(1)}, bf16[768,256]{0,1:T(8,128)(2,1)S(1)}, u32[]{:S(2)}, u32[]{:S(2)}) collective-permute-start(bf16[768,256]{0,1:T(8,128)(2,1)S(1)} %collective-permute-done.11), channel_id=1, source_target_pairs={{0,15},{1,0},{2,1},{3,2},{4,3},{5,4},{6,5},{7,6},{8,7},{9,8},{10,9... | collective-permute-start | bytes 1179656 | tf_op jit(solution)/shard_map/ppermute | solution.py:98
  97.1 12.9 %collective-permute-start.12 = (bf16[768,256]{0,1:T(8,128)(2,1)S(1)}, bf16[768,256]{0,1:T(8,128)(2,1)S(1)}, u32[]{:S(2)}, u32[]{:S(2)}) collective-permute-start(bf16[768,256]{0,1:T(8,128)(2,1)S(1)} %collective-permute-done.10), channel_id=1, source_target_pairs={{0,1},{1,2},{2,3},{3,4},{4,5},{5,6},{6,7},{7,8},{8,9},{9,10},{10,1... | collective-permute-start | bytes 1179656 | tf_op jit(solution)/shard_map/ppermute | solution.py:96
  104.4 12.0 %collective-permute-start.15 = (bf16[768,256]{0,1:T(8,128)(2,1)S(1)}, bf16[768,256]{0,1:T(8,128)(2,1)S(1)}, u32[]{:S(2)}, u32[]{:S(2)}) collective-permute-start(bf16[768,256]{0,1:T(8,128)(2,1)S(1)} %collective-permute-done.13), channel_id=1, source_target_pairs={{0,15},{1,0},{2,1},{3,2},{4,3},{5,4},{6,5},{7,6},{8,7},{9,8},{10,9... | collective-permute-start | bytes 1179656 | tf_op jit(solution)/shard_map/ppermute | solution.py:98
  110.0 12.0 %collective-permute-start.14 = (bf16[768,256]{0,1:T(8,128)(2,1)S(1)}, bf16[768,256]{0,1:T(8,128)(2,1)S(1)}, u32[]{:S(2)}, u32[]{:S(2)}) collective-permute-start(bf16[768,256]{0,1:T(8,128)(2,1)S(1)} %collective-permute-done.12), channel_id=1, source_target_pairs={{0,1},{1,2},{2,3},{3,4},{4,5},{5,6},{6,7},{7,8},{8,9},{9,10},{10,1... | collective-permute-start | bytes 1179656 | tf_op jit(solution)/shard_map/ppermute | solution.py:96
  116.4 11.1 %collective-permute-start.17 = (bf16[768,256]{0,1:T(8,128)(2,1)S(1)}, bf16[768,256]{0,1:T(8,128)(2,1)S(1)}, u32[]{:S(2)}, u32[]{:S(2)}) collective-permute-start(bf16[768,256]{0,1:T(8,128)(2,1)S(1)} %collective-permute-done.15), channel_id=1, source_target_pairs={{0,15},{1,0},{2,1},{3,2},{4,3},{5,4},{6,5},{7,6},{8,7},{9,8},{10,9... | collective-permute-start | bytes 1179656 | tf_op jit(solution)/shard_map/ppermute | solution.py:98
  122.0 11.1 %collective-permute-start.16 = (bf16[768,256]{0,1:T(8,128)(2,1)S(1)}, bf16[768,256]{0,1:T(8,128)(2,1)S(1)}, u32[]{:S(2)}, u32[]{:S(2)}) collective-permute-start(bf16[768,256]{0,1:T(8,128)(2,1)S(1)} %collective-permute-done.14), channel_id=1, source_target_pairs={{0,1},{1,2},{2,3},{3,4},{4,5},{5,6},{6,7},{7,8},{8,9},{9,10},{10,1... | collective-permute-start | bytes 1179656 | tf_op jit(solution)/shard_map/ppermute | solution.py:96
  127.5 10.9 %collective-permute-start.19 = (bf16[768,256]{0,1:T(8,128)(2,1)S(1)}, bf16[768,256]{0,1:T(8,128)(2,1)S(1)}, u32[]{:S(2)}, u32[]{:S(2)}) collective-permute-start(bf16[768,256]{0,1:T(8,128)(2,1)S(1)} %collective-permute-done.17), channel_id=1, source_target_pairs={{0,15},{1,0},{2,1},{3,2},{4,3},{5,4},{6,5},{7,6},{8,7},{9,8},{10,9... | collective-permute-start | bytes 1179656 | tf_op jit(solution)/shard_map/ppermute | solution.py:98
  133.1 10.9 %collective-permute-start.18 = (bf16[768,256]{0,1:T(8,128)(2,1)S(1)}, bf16[768,256]{0,1:T(8,128)(2,1)S(1)}, u32[]{:S(2)}, u32[]{:S(2)}) collective-permute-start(bf16[768,256]{0,1:T(8,128)(2,1)S(1)} %collective-permute-done.16), channel_id=1, source_target_pairs={{0,1},{1,2},{2,3},{3,4},{4,5},{5,6},{6,7},{7,8},{8,9},{9,10},{10,1... | collective-permute-start | bytes 1179656 | tf_op jit(solution)/shard_map/ppermute | solution.py:96
  138.4 19.2 %collective-permute-start.21 = (bf16[768,256]{0,1:T(8,128)(2,1)S(1)}, bf16[768,256]{0,1:T(8,128)(2,1)S(1)}, u32[]{:S(2)}, u32[]{:S(2)}) collective-permute-start(bf16[768,256]{0,1:T(8,128)(2,1)S(1)} %collective-permute-done.19), channel_id=1, source_target_pairs={{0,15},{1,0},{2,1},{3,2},{4,3},{5,4},{6,5},{7,6},{8,7},{9,8},{10,9... | collective-permute-start | bytes 1179656 | tf_op jit(solution)/shard_map/ppermute | solution.py:98
  144.0 11.6 %collective-permute-start.20 = (bf16[768,256]{0,1:T(8,128)(2,1)S(1)}, bf16[768,256]{0,1:T(8,128)(2,1)S(1)}, u32[]{:S(2)}, u32[]{:S(2)}) collective-permute-start(bf16[768,256]{0,1:T(8,128)(2,1)S(1)} %collective-permute-done.18), channel_id=1, source_target_pairs={{0,1},{1,2},{2,3},{3,4},{4,5},{5,6},{6,7},{7,8},{8,9},{9,10},{10,1... | collective-permute-start | bytes 1179656 | tf_op jit(solution)/shard_map/ppermute | solution.py:96
  146.5 20.0 %copy-start.5 = (bf16[768,320]{0,1:T(8,128)(2,1)S(1)}, bf16[768,320]{0,1:T(8,128)(2,1)}, u32[]{:S(2)}) copy-start(bf16[768,320]{0,1:T(8,128)(2,1)} %param.13) | copy-start | bytes 1474564
  155.6 10.9 %collective-permute-start.22 = (bf16[768,256]{0,1:T(8,128)(2,1)S(1)}, bf16[768,256]{0,1:T(8,128)(2,1)S(1)}, u32[]{:S(2)}, u32[]{:S(2)}) collective-permute-start(bf16[768,256]{0,1:T(8,128)(2,1)S(1)} %collective-permute-done.20), channel_id=1, source_target_pairs={{0,1},{1,2},{2,3},{3,4},{4,5},{5,6},{6,7},{7,8},{8,9},{9,10},{10,1... | collective-permute-start | bytes 1179656 | tf_op jit(solution)/shard_map/ppermute | solution.py:96

commit v6 on v5

--- a/solution.py
+++ b/solution.py
@@ -83,15 +83,19 @@
     tp_count = lax.axis_size("tp")
     me = lax.axis_index("tp")
     width = normed.shape[1]
+    half = width // 2
+    gathered = lax.all_gather(normed[:, :half], "tp", axis=1, tiled=True)
+    first_rows = out_weight.reshape(tp_count, width, -1)[:, :half].reshape(tp_count * half, -1)
 
     def part(shard, source):
-        rows = lax.dynamic_slice_in_dim(out_weight, source * width, width, axis=0)
+        rows = lax.dynamic_slice_in_dim(out_weight, source * width + half, half, axis=0)
         return jnp.dot(shard, rows, preferred_element_type=jnp.float32)
 
     up = [(j, (j + 1) % tp_count) for j in range(tp_count)]
     down = [(j, (j - 1) % tp_count) for j in range(tp_count)]
-    mixed = part(normed, me)
-    rising, falling = normed, normed
+    own = normed[:, half:]
+    mixed = part(own, me)
+    rising, falling = own, own
     for step in range(1, tp_count // 2 + 1):
         rising = lax.ppermute(rising, "tp", up)
         if step < tp_count - step:
@@ -99,7 +103,7 @@
         mixed = mixed + part(rising, (me - step) % tp_count)
         if step < tp_count - step:
             mixed = mixed + part(falling, (me + step) % tp_count)
-    return mixed
+    return mixed + jnp.dot(gathered, first_rows, preferred_element_type=jnp.float32)
 
 
 def local(query_vectors, key_vectors, value_vectors, decay_exp, norm_gain, out_weight, residual):

time: 169 us -> 170 us (level)
  between operations: 0.85 us -> 14.3 us
  waiting for transfers between devices: 53.6 us -> 44.9 us
  other arithmetic: 9.29 us -> 1.86 us
  matrix products: 14.9 us -> 17 us
  local copies, waits for them, and re-layouts: 3.89 us -> 5.75 us
    ppermute x8, waiting for transfers between devices: 17.5 us -> 7.94 us  [ring_project(): rising = lax.ppermute(rising, 'tp', up)]
    dot_general x0 -> x1, matrix products: none -> 3.57 us  [ring_project(): jnp.dot(gathered, first_rows, preferred_element_type=jnp.float32)]
    slice x1 -> x3, local copies, waits for them, and re-layouts: 0.21 us -> 2.3 us  [the longest x1 1.31 us: ring_project(): out_weight.reshape(tp_count, width, -1)[:, :half]]
    add x1, other arithmetic: 2.04 us -> 0.14 us  [block_scan(): decay[:, None, None] * state + mine]
    dot_general x1, matrix products: 4.01 us -> 2.15 us  [local(): jnp.einsum('hts,shd->thd', local_weights, value_heads, preferred_element_...]
  transfers between devices with their start and end apart: 23 -> 24, of which waited for: 13 -> 13; matrix products, arithmetic and copies ran while one was open for 6% -> 8% of each run, Pallas kernels for 0% -> 0%
where the time goes in v6:
time: 170 us; the launch traced here: 169 us
  starting transfers between devices  84.8 us (50%)
  waiting for transfers between devices  44.9 us (26%)
  matrix products  17 us (10%)
  between operations  14.3 us (8%)
  local copies, waits for them, and re-layouts  5.75 us (3%)
  other arithmetic  1.86 us (1%)
    ppermute x7, starting transfers between devices, ring_project(): falling = lax.ppermute(falling, 'tp', down)  42.9 us
    ppermute x7, waiting for transfers between devices, ring_project(): falling = lax.ppermute(falling, 'tp', down)  26.7 us
    ppermute x6, starting transfers between devices, gather_line(): got.append(unpack(lax.ppermute(pack(total_s, total_p), 'seq', pairs)))  21.4 us
    ppermute x8, starting transfers between devices, ring_project(): rising = lax.ppermute(rising, 'tp', up)  16.7 us
    ppermute x6, waiting for transfers between devices, gather_line(): got.append(unpack(lax.ppermute(pack(total_s, total_p), 'seq', pairs)))  9.05 us
    dot_general x16, matrix products, part(): return jnp.dot(shard, rows, preferred_element_type=jnp.float32)  8.05 us
    ppermute x8, waiting for transfers between devices, ring_project(): rising = lax.ppermute(rising, 'tp', up)  7.94 us
    dot_general x1, matrix products, ring_project(): jnp.dot(gathered, first_rows, preferred_element_type=jnp.float32)  3.57 us
  transfers between devices with their start and end apart: 24, of which 13 were waited for; matrix products, arithmetic and copies ran while one was open for 8% of the time, Pallas kernels for 0%

profile of v6, /device:TPU:6, one launch (start us, length us, event | category | flops | bytes accessed | tf_op | source)
XLA Modules:
  0.0 168.7 jit_solution(14773617828485512259)
XLA Ops:
  6.5 0.8 reshape.93
  7.3 0.6 reduce-window.6
  8.7 1.2 copy.27
  9.8 1.3 fusion.22
  11.2 1.3 broadcast_select_fusion.1
  12.5 1.9 %collective-permute-start = (f32[2,136,128]{2,1,0:T(8,128)S(1)}, f32[2,136,128]{2,1,0:T(8,128)S(1)}, u32[]{:S(2)}, u32[]{:S(2)}) collective-permute-start(f32[2,136,128]{2,1,0:T(8,128)S(1)} %pad_maximum_fusion), channel_id=1, source_target_pairs={{0,16},{16,0},{32,48},{48,32},{64,80},{80,64},{96,112},{112,96},{1... | collective-permute-start | bytes 417800 | tf_op jit(solution)/shard_map/ppermute | solution.py:48
  14.5 1.2 collective-permute-done
  16.1 7.8 %collective-permute-start.1 = (f32[2,136,128]{2,1,0:T(8,128)S(1)}, f32[2,136,128]{2,1,0:T(8,128)S(1)}, u32[]{:S(2)}, u32[]{:S(2)}) collective-permute-start(f32[2,136,128]{2,1,0:T(8,128)S(1)} %pad_maximum_fusion.1), channel_id=1, source_target_pairs={{0,32},{16,112},{32,64},{48,16},{64,96},{80,48},{96,0},{112,80},{1... | collective-permute-start | bytes 417800 | tf_op jit(solution)/shard_map/ppermute | solution.py:32
  23.8 1.9 %collective-permute-start.2 = (f32[2,136,128]{2,1,0:T(8,128)S(1)}, f32[2,136,128]{2,1,0:T(8,128)S(1)}, u32[]{:S(2)}, u32[]{:S(2)}) collective-permute-start(f32[2,136,128]{2,1,0:T(8,128)S(1)} %pad_maximum_fusion.1), channel_id=1, source_target_pairs={{0,64},{16,80},{32,96},{48,112},{64,0},{80,16},{96,32},{112,48},{1... | collective-permute-start | bytes 417800 | tf_op jit(solution)/shard_map/ppermute | solution.py:32
  25.8 2.8 %collective-permute-start.3 = (f32[2,136,128]{2,1,0:T(8,128)S(1)}, f32[2,136,128]{2,1,0:T(8,128)S(1)}, u32[]{:S(2)}, u32[]{:S(2)}) collective-permute-start(f32[2,136,128]{2,1,0:T(8,128)S(1)} %pad_maximum_fusion.1), channel_id=1, source_target_pairs={{0,96},{16,48},{32,0},{48,80},{64,32},{80,112},{96,64},{112,16},{1... | collective-permute-start | bytes 417800 | tf_op jit(solution)/shard_map/ppermute | solution.py:32
  28.6 3.7 %collective-permute-done.2 = f32[2,136,128]{2,1,0:T(8,128)S(1)} collective-permute-done((f32[2,136,128]{2,1,0:T(8,128)S(1)}, f32[2,136,128]{2,1,0:T(8,128)S(1)}, u32[]{:S(2)}, u32[]{:S(2)}) %collective-permute-start.2) | collective-permute-done | bytes 139296 | tf_op jit(solution)/shard_map/ppermute | solution.py:32
  32.3 1.6 collective-permute-done.3
  34.3 1.9 %collective-permute-start.4 = (f32[2,136,128]{2,1,0:T(8,128)S(1)}, f32[2,136,128]{2,1,0:T(8,128)S(1)}, u32[]{:S(2)}, u32[]{:S(2)}) collective-permute-start(f32[2,136,128]{2,1,0:T(8,128)S(1)} %pad_maximum_fusion.2), channel_id=1, source_target_pairs={{0,128},{16,400},{32,160},{48,432},{64,192},{80,464},{96,224},{112... | collective-permute-start | bytes 417800 | tf_op jit(solution)/shard_map/ppermute | solution.py:32
  36.2 3.4 %collective-permute-start.5 = (f32[2,136,128]{2,1,0:T(8,128)S(1)}, f32[2,136,128]{2,1,0:T(8,128)S(1)}, u32[]{:S(2)}, u32[]{:S(2)}) collective-permute-start(f32[2,136,128]{2,1,0:T(8,128)S(1)} %pad_maximum_fusion.2), channel_id=1, source_target_pairs={{0,256},{16,272},{32,288},{48,304},{64,320},{80,336},{96,352},{112... | collective-permute-start | bytes 417800 | tf_op jit(solution)/shard_map/ppermute | solution.py:32
  39.6 3.6 %collective-permute-start.6 = (f32[2,136,128]{2,1,0:T(8,128)S(1)}, f32[2,136,128]{2,1,0:T(8,128)S(1)}, u32[]{:S(2)}, u32[]{:S(2)}) collective-permute-start(f32[2,136,128]{2,1,0:T(8,128)S(1)} %pad_maximum_fusion.2), channel_id=1, source_target_pairs={{0,384},{16,144},{32,416},{48,176},{64,448},{80,208},{96,480},{112... | collective-permute-start | bytes 417800 | tf_op jit(solution)/shard_map/ppermute | solution.py:32
  43.3 2.8 %collective-permute-done.4 = f32[2,136,128]{2,1,0:T(8,128)S(1)} collective-permute-done((f32[2,136,128]{2,1,0:T(8,128)S(1)}, f32[2,136,128]{2,1,0:T(8,128)S(1)}, u32[]{:S(2)}, u32[]{:S(2)}) %collective-permute-start.4) | collective-permute-done | bytes 139296 | tf_op jit(solution)/shard_map/ppermute | solution.py:32
  46.2 1.0 collective-permute-done.6
  47.3 1.9 %collective-permute-start.7 = (bf16[2,128,128]{2,1,0:T(8,128)(2,1)S(1)}, bf16[2,128,128]{2,1,0:T(8,128)(2,1)S(1)}, u32[]{:S(2)}, u32[]{:S(2)}) collective-permute-start(bf16[2,128,128]{2,1,0:T(8,128)(2,1)S(1)} %get-tuple-element.16), channel_id=1, source_target_pairs={{0,16},{16,0},{32,48},{48,32},{64,80},{80,64},{96,112},{112,96},{1... | collective-permute-start | bytes 196616 | tf_op jit(solution)/shard_map/ppermute | solution.py:74
  49.2 2.1 %fusion.14 = f32[768,2,128]{0,2,1:T(8,128)S(1)} fusion(s32[2,768]{1,0:T(2,128)S(1)} %get-tuple-element.19, bf16[768,2,128]{0,2,1:T(8,128)(2,1)S(1)} %bitcast.101, bf16[768,256]{1,0:T(8,128)(2,1)S(1)} %copy-done.4, bf16[768,256]{1,0:T(8,128)(2,1)S(1)} %copy-done), kind=kOutput, calls=%fused_computation.23 | convolution fusion | flops 612237312 | bytes 1972224 | tf_op jit(solution)/shard_map/hts,shd->thd/dot_general | solution.py:121
  51.4 0.3 fusion.18
  51.7 0.4 multiply_reduce_fusion
  52.2 0.8 fusion.99
  53.6 0.8 copy.44
  54.4 1.3 slice.92
  55.8 3.2 %collective-permute-start.8 = (bf16[768,128]{0,1:T(8,128)(2,1)}, bf16[768,128]{0,1:T(8,128)(2,1)S(1)}, u32[]{:S(2)}, u32[]{:S(2)}) collective-permute-start(bf16[768,128]{0,1:T(8,128)(2,1)} %get-tuple-element.20), channel_id=1, source_target_pairs={{0,1},{1,2},{2,3},{3,4},{4,5},{5,6},{6,7},{7,8},{8,9},{9,10},{10,1... | collective-permute-start | bytes 589832 | tf_op jit(solution)/shard_map/ppermute | solution.py:100
  59.0 9.5 %collective-permute-start.9 = (bf16[768,128]{0,1:T(8,128)(2,1)}, bf16[768,128]{0,1:T(8,128)(2,1)S(1)}, u32[]{:S(2)}, u32[]{:S(2)}) collective-permute-start(bf16[768,128]{0,1:T(8,128)(2,1)} %get-tuple-element.20), channel_id=1, source_target_pairs={{0,15},{1,0},{2,1},{3,2},{4,3},{5,4},{6,5},{7,6},{8,7},{9,8},{10,9... | collective-permute-start | bytes 589832 | tf_op jit(solution)/shard_map/ppermute | solution.py:102
  68.5 0.3 fusion.67
  68.8 6.1 %collective-permute-done.9 = bf16[768,128]{0,1:T(8,128)(2,1)S(1)} collective-permute-done((bf16[768,128]{0,1:T(8,128)(2,1)}, bf16[768,128]{0,1:T(8,128)(2,1)S(1)}, u32[]{:S(2)}, u32[]{:S(2)}) %collective-permute-start.9) | collective-permute-done | bytes 196640 | tf_op jit(solution)/shard_map/ppermute | solution.py:102
  74.9 5.5 %collective-permute-start.11 = (bf16[768,128]{0,1:T(8,128)(2,1)S(1)}, bf16[768,128]{0,1:T(8,128)(2,1)S(1)}, u32[]{:S(2)}, u32[]{:S(2)}) collective-permute-start(bf16[768,128]{0,1:T(8,128)(2,1)S(1)} %collective-permute-done.9), channel_id=1, source_target_pairs={{0,15},{1,0},{2,1},{3,2},{4,3},{5,4},{6,5},{7,6},{8,7},{9,8},{10,9... | collective-permute-start | bytes 589832 | tf_op jit(solution)/shard_map/ppermute | solution.py:102
  80.4 1.9 %collective-permute-start.10 = (bf16[768,128]{0,1:T(8,128)(2,1)S(1)}, bf16[768,128]{0,1:T(8,128)(2,1)S(1)}, u32[]{:S(2)}, u32[]{:S(2)}) collective-permute-start(bf16[768,128]{0,1:T(8,128)(2,1)S(1)} %collective-permute-done.8), channel_id=1, source_target_pairs={{0,1},{1,2},{2,3},{3,4},{4,5},{5,6},{6,7},{7,8},{8,9},{9,10},{10,1... | collective-permute-start | bytes 589832 | tf_op jit(solution)/shard_map/ppermute | solution.py:100
  82.3 0.3 convolution_add_fusion.8
  82.6 0.3 convolution_add_fusion.7
  82.9 5.8 %collective-permute-done.11 = bf16[768,128]{0,1:T(8,128)(2,1)S(1)} collective-permute-done((bf16[768,128]{0,1:T(8,128)(2,1)S(1)}, bf16[768,128]{0,1:T(8,128)(2,1)S(1)}, u32[]{:S(2)}, u32[]{:S(2)}) %collective-permute-start.11) | collective-permute-done | bytes 196640 | tf_op jit(solution)/shard_map/ppermute | solution.py:102
  88.7 5.6 %collective-permute-start.13 = (bf16[768,128]{0,1:T(8,128)(2,1)S(1)}, bf16[768,128]{0,1:T(8,128)(2,1)S(1)}, u32[]{:S(2)}, u32[]{:S(2)}) collective-permute-start(bf16[768,128]{0,1:T(8,128)(2,1)S(1)} %collective-permute-done.11), channel_id=1, source_target_pairs={{0,15},{1,0},{2,1},{3,2},{4,3},{5,4},{6,5},{7,6},{8,7},{9,8},{10,9... | collective-permute-start | bytes 589832 | tf_op jit(solution)/shard_map/ppermute | solution.py:102
  94.3 1.9 %collective-permute-start.12 = (bf16[768,128]{0,1:T(8,128)(2,1)S(1)}, bf16[768,128]{0,1:T(8,128)(2,1)S(1)}, u32[]{:S(2)}, u32[]{:S(2)}) collective-permute-start(bf16[768,128]{0,1:T(8,128)(2,1)S(1)} %collective-permute-done.10), channel_id=1, source_target_pairs={{0,1},{1,2},{2,3},{3,4},{4,5},{5,6},{6,7},{7,8},{8,9},{9,10},{10,1... | collective-permute-start | bytes 589832 | tf_op jit(solution)/shard_map/ppermute | solution.py:100
  96.3 0.3 fusion.62
  96.5 0.3 fusion.10
  96.8 4.8 %collective-permute-done.13 = bf16[768,128]{0,1:T(8,128)(2,1)S(1)} collective-permute-done((bf16[768,128]{0,1:T(8,128)(2,1)S(1)}, bf16[768,128]{0,1:T(8,128)(2,1)S(1)}, u32[]{:S(2)}, u32[]{:S(2)}) %collective-permute-start.13) | collective-permute-done | bytes 196640 | tf_op jit(solution)/shard_map/ppermute | solution.py:102
  101.6 5.6 %collective-permute-start.15 = (bf16[768,128]{0,1:T(8,128)(2,1)S(1)}, bf16[768,128]{0,1:T(8,128)(2,1)S(1)}, u32[]{:S(2)}, u32[]{:S(2)}) collective-permute-start(bf16[768,128]{0,1:T(8,128)(2,1)S(1)} %collective-permute-done.13), channel_id=1, source_target_pairs={{0,15},{1,0},{2,1},{3,2},{4,3},{5,4},{6,5},{7,6},{8,7},{9,8},{10,9... | collective-permute-start | bytes 589832 | tf_op jit(solution)/shard_map/ppermute | solution.py:102
  107.2 1.9 %collective-permute-start.14 = (bf16[768,128]{0,1:T(8,128)(2,1)S(1)}, bf16[768,128]{0,1:T(8,128)(2,1)S(1)}, u32[]{:S(2)}, u32[]{:S(2)}) collective-permute-start(bf16[768,128]{0,1:T(8,128)(2,1)S(1)} %collective-permute-done.12), channel_id=1, source_target_pairs={{0,1},{1,2},{2,3},{3,4},{4,5},{5,6},{6,7},{7,8},{8,9},{9,10},{10,1... | collective-permute-start | bytes 589832 | tf_op jit(solution)/shard_map/ppermute | solution.py:100
  109.1 0.3 fusion.59
  109.4 0.3 fusion.9
  109.7 4.7 %collective-permute-done.15 = bf16[768,128]{0,1:T(8,128)(2,1)S(1)} collective-permute-done((bf16[768,128]{0,1:T(8,128)(2,1)S(1)}, bf16[768,128]{0,1:T(8,128)(2,1)S(1)}, u32[]{:S(2)}, u32[]{:S(2)}) %collective-permute-start.15) | collective-permute-done | bytes 196640 | tf_op jit(solution)/shard_map/ppermute | solution.py:102
  114.4 5.6 %collective-permute-start.17 = (bf16[768,128]{0,1:T(8,128)(2,1)S(1)}, bf16[768,128]{0,1:T(8,128)(2,1)S(1)}, u32[]{:S(2)}, u32[]{:S(2)}) collective-permute-start(bf16[768,128]{0,1:T(8,128)(2,1)S(1)} %collective-permute-done.15), channel_id=1, source_target_pairs={{0,15},{1,0},{2,1},{3,2},{4,3},{5,4},{6,5},{7,6},{8,7},{9,8},{10,9... | collective-permute-start | bytes 589832 | tf_op jit(solution)/shard_map/ppermute | solution.py:102
  120.0 1.9 %collective-permute-start.16 = (bf16[768,128]{0,1:T(8,128)(2,1)S(1)}, bf16[768,128]{0,1:T(8,128)(2,1)S(1)}, u32[]{:S(2)}, u32[]{:S(2)}) collective-permute-start(bf16[768,128]{0,1:T(8,128)(2,1)S(1)} %collective-permute-done.14), channel_id=1, source_target_pairs={{0,1},{1,2},{2,3},{3,4},{4,5},{5,6},{6,7},{7,8},{8,9},{9,10},{10,1... | collective-permute-start | bytes 589832 | tf_op jit(solution)/shard_map/ppermute | solution.py:100
  121.9 0.3 fusion.56
  122.2 0.3 fusion.8
  122.5 4.2 %collective-permute-done.17 = bf16[768,128]{0,1:T(8,128)(2,1)S(1)} collective-permute-done((bf16[768,128]{0,1:T(8,128)(2,1)S(1)}, bf16[768,128]{0,1:T(8,128)(2,1)S(1)}, u32[]{:S(2)}, u32[]{:S(2)}) %collective-permute-start.17) | collective-permute-done | bytes 196640 | tf_op jit(solution)/shard_map/ppermute | solution.py:102
  126.7 5.6 %collective-permute-start.19 = (bf16[768,128]{0,1:T(8,128)(2,1)S(1)}, bf16[768,128]{0,1:T(8,128)(2,1)S(1)}, u32[]{:S(2)}, u32[]{:S(2)}) collective-permute-start(bf16[768,128]{0,1:T(8,128)(2,1)S(1)} %collective-permute-done.17), channel_id=1, source_target_pairs={{0,15},{1,0},{2,1},{3,2},{4,3},{5,4},{6,5},{7,6},{8,7},{9,8},{10,9... | collective-permute-start | bytes 589832 | tf_op jit(solution)/shard_map/ppermute | solution.py:102
  132.3 1.9 %collective-permute-start.18 = (bf16[768,128]{0,1:T(8,128)(2,1)S(1)}, bf16[768,128]{0,1:T(8,128)(2,1)S(1)}, u32[]{:S(2)}, u32[]{:S(2)}) collective-permute-start(bf16[768,128]{0,1:T(8,128)(2,1)S(1)} %collective-permute-done.16), channel_id=1, source_target_pairs={{0,1},{1,2},{2,3},{3,4},{4,5},{5,6},{6,7},{7,8},{8,9},{9,10},{10,1... | collective-permute-start | bytes 589832 | tf_op jit(solution)/shard_map/ppermute | solution.py:100
  134.2 0.3 fusion.53
  134.5 0.3 fusion.7
  134.8 1.0 collective-permute-done.19
  135.8 5.6 %collective-permute-start.21 = (bf16[768,128]{0,1:T(8,128)(2,1)S(1)}, bf16[768,128]{0,1:T(8,128)(2,1)S(1)}, u32[]{:S(2)}, u32[]{:S(2)}) collective-permute-start(bf16[768,128]{0,1:T(8,128)(2,1)S(1)} %collective-permute-done.19), channel_id=1, source_target_pairs={{0,15},{1,0},{2,1},{3,2},{4,3},{5,4},{6,5},{7,6},{8,7},{9,8},{10,9... | collective-permute-start | bytes 589832 | tf_op jit(solution)/shard_map/ppermute | solution.py:102
  141.4 1.9 %collective-permute-start.20 = (bf16[768,128]{0,1:T(8,128)(2,1)S(1)}, bf16[768,128]{0,1:T(8,128)(2,1)}, u32[]{:S(2)}, u32[]{:S(2)}) collective-permute-start(bf16[768,128]{0,1:T(8,128)(2,1)S(1)} %collective-permute-done.18), channel_id=1, source_target_pairs={{0,1},{1,2},{2,3},{3,4},{4,5},{5,6},{6,7},{7,8},{8,9},{9,10},{10,1... | collective-permute-start | bytes 589832 | tf_op jit(solution)/shard_map/ppermute | solution.py:100
  143.3 0.3 fusion.50
  143.6 0.3 fusion.6
  143.9 6.8 %collective-permute-done.20 = bf16[768,128]{0,1:T(8,128)(2,1)} collective-permute-done((bf16[768,128]{0,1:T(8,128)(2,1)S(1)}, bf16[768,128]{0,1:T(8,128)(2,1)}, u32[]{:S(2)}, u32[]{:S(2)}) %collective-permute-start.20) | collective-permute-done | bytes 196640 | tf_op jit(solution)/shard_map/ppermute | solution.py:100
  150.7 1.9 %collective-permute-start.22 = (bf16[768,128]{0,1:T(8,128)(2,1)}, bf16[768,128]{0,1:T(8,128)(2,1)}, u32[]{:S(2)}, u32[]{:S(2)}) collective-permute-start(bf16[768,128]{0,1:T(8,128)(2,1)} %collective-permute-done.20), channel_id=1, source_target_pairs={{0,1},{1,2},{2,3},{3,4},{4,5},{5,6},{6,7},{7,8},{8,9},{9,10},{10,1... | collective-permute-start | bytes 589832 | tf_op jit(solution)/shard_map/ppermute | solution.py:100
  152.6 0.3 fusion.47
  152.9 2.2 %fusion.5 = f32[768,320]{0,1:T(8,128)} fusion(f32[768,320]{0,1:T(8,128)S(1)} %fusion.47, f32[768,320]{0,1:T(8,128)S(1)} %fusion.6, bf16[768,128]{0,1:T(8,128)(2,1)} %collective-permute-done.20, bf16[4096,320]{0,1:T(8,128)(2,1)S(1)} %copy-done.1, s32[]{:T(128)S(6)} %select_n.321), kind=kOutput, calls=%fused_computation.7 | convolution fusion | flops 63406080 | bytes 3227652 | tf_op jit(solution)/shard_map/dot_general | solution.py:92
  155.1 3.6 %fusion.11 = f32[768,320]{0,1:T(8,128)S(1)} fusion(bf16[768,2048]{0,1:T(8,128)(2,1)} %all-gather.2.cloned.1.call-done, bf16[40,8,16,128]{3,2,1,0:T(8,128)(2,1)} %bitcast.102), kind=kOutput, calls=%fused_computation.20 | convolution fusion | flops 1006632960 | bytes 5439488 | tf_op jit(solution)/shard_map/dot_general | solution.py:106
  158.7 1.1 collective-permute-done.22
  159.8 2.0 %fusion.19 = bf16[768,320]{0,1:T(8,128)(2,1)} fusion(f32[768,320]{0,1:T(8,128)S(1)} %fusion.11, f32[768,320]{0,1:T(8,128)S(1)} %copy-done.2, bf16[768,128]{0,1:T(8,128)(2,1)} %collective-permute-done.22, bf16[768,320]{0,1:T(8,128)(2,1)S(1)} %copy-done.3, bf16[4096,320]{0,1:T(8,128)(2,1)S(1)} %copy-done.1, s32[]{:T(128)S(6)} %select_n.325), kind=kOutput, calls=%fused_computation.30 | convolution fusion | flops 64143360 | bytes 3227652 | tf_op jit(solution)/shard_map/dot_general | solution.py:92
  (47 shorter events, 2.2 us)
Async XLA Ops:
  6.5 42.7 %copy-start = (bf16[768,256]{1,0:T(8,128)(2,1)S(1)}, bf16[768,256]{1,0:T(8,128)(2,1)}, u32[]{:S(2)}) copy-start(bf16[768,256]{1,0:T(8,128)(2,1)} %param.7) | copy-start | bytes 1179652
  6.5 148.6 %all-gather.2.cloned.1.call-start = ((), (), s32[]{:S(2)}) async-start(), calls=%async_computation | async-start | bytes 3342336 | tf_op jit(solution)/shard_map/all_gather | solution.py:87
  9.8 39.4 %copy-start.4 = (bf16[768,256]{1,0:T(8,128)(2,1)S(1)}, bf16[768,256]{1,0:T(8,128)(2,1)}, u32[]{:S(2)}) copy-start(bf16[768,256]{1,0:T(8,128)(2,1)} %param.9) | copy-start | bytes 1179652
  12.5 3.3 %collective-permute-start = (f32[2,136,128]{2,1,0:T(8,128)S(1)}, f32[2,136,128]{2,1,0:T(8,128)S(1)}, u32[]{:S(2)}, u32[]{:S(2)}) collective-permute-start(f32[2,136,128]{2,1,0:T(8,128)S(1)} %pad_maximum_fusion), channel_id=1, source_target_pairs={{0,16},{16,0},{32,48},{48,32},{64,80},{80,64},{96,112},{112,96},{1... | collective-permute-start | bytes 417800 | tf_op jit(solution)/shard_map/ppermute | solution.py:48
  16.1 12.5 %collective-permute-start.1 = (f32[2,136,128]{2,1,0:T(8,128)S(1)}, f32[2,136,128]{2,1,0:T(8,128)S(1)}, u32[]{:S(2)}, u32[]{:S(2)}) collective-permute-start(f32[2,136,128]{2,1,0:T(8,128)S(1)} %pad_maximum_fusion.1), channel_id=1, source_target_pairs={{0,32},{16,112},{32,64},{48,16},{64,96},{80,48},{96,0},{112,80},{1... | collective-permute-start | bytes 417800 | tf_op jit(solution)/shard_map/ppermute | solution.py:32
  23.8 8.5 %collective-permute-start.2 = (f32[2,136,128]{2,1,0:T(8,128)S(1)}, f32[2,136,128]{2,1,0:T(8,128)S(1)}, u32[]{:S(2)}, u32[]{:S(2)}) collective-permute-start(f32[2,136,128]{2,1,0:T(8,128)S(1)} %pad_maximum_fusion.1), channel_id=1, source_target_pairs={{0,64},{16,80},{32,96},{48,112},{64,0},{80,16},{96,32},{112,48},{1... | collective-permute-start | bytes 417800 | tf_op jit(solution)/shard_map/ppermute | solution.py:32
  25.8 8.2 %collective-permute-start.3 = (f32[2,136,128]{2,1,0:T(8,128)S(1)}, f32[2,136,128]{2,1,0:T(8,128)S(1)}, u32[]{:S(2)}, u32[]{:S(2)}) collective-permute-start(f32[2,136,128]{2,1,0:T(8,128)S(1)} %pad_maximum_fusion.1), channel_id=1, source_target_pairs={{0,96},{16,48},{32,0},{48,80},{64,32},{80,112},{96,64},{112,16},{1... | collective-permute-start | bytes 417800 | tf_op jit(solution)/shard_map/ppermute | solution.py:32
  34.3 11.8 %collective-permute-start.4 = (f32[2,136,128]{2,1,0:T(8,128)S(1)}, f32[2,136,128]{2,1,0:T(8,128)S(1)}, u32[]{:S(2)}, u32[]{:S(2)}) collective-permute-start(f32[2,136,128]{2,1,0:T(8,128)S(1)} %pad_maximum_fusion.2), channel_id=1, source_target_pairs={{0,128},{16,400},{32,160},{48,432},{64,192},{80,464},{96,224},{112... | collective-permute-start | bytes 417800 | tf_op jit(solution)/shard_map/ppermute | solution.py:32
  36.2 9.9 %collective-permute-start.5 = (f32[2,136,128]{2,1,0:T(8,128)S(1)}, f32[2,136,128]{2,1,0:T(8,128)S(1)}, u32[]{:S(2)}, u32[]{:S(2)}) collective-permute-start(f32[2,136,128]{2,1,0:T(8,128)S(1)} %pad_maximum_fusion.2), channel_id=1, source_target_pairs={{0,256},{16,272},{32,288},{48,304},{64,320},{80,336},{96,352},{112... | collective-permute-start | bytes 417800 | tf_op jit(solution)/shard_map/ppermute | solution.py:32
  39.6 7.5 %collective-permute-start.6 = (f32[2,136,128]{2,1,0:T(8,128)S(1)}, f32[2,136,128]{2,1,0:T(8,128)S(1)}, u32[]{:S(2)}, u32[]{:S(2)}) collective-permute-start(f32[2,136,128]{2,1,0:T(8,128)S(1)} %pad_maximum_fusion.2), channel_id=1, source_target_pairs={{0,384},{16,144},{32,416},{48,176},{64,448},{80,208},{96,480},{112... | collective-permute-start | bytes 417800 | tf_op jit(solution)/shard_map/ppermute | solution.py:32
  47.3 4.1 %collective-permute-start.7 = (bf16[2,128,128]{2,1,0:T(8,128)(2,1)S(1)}, bf16[2,128,128]{2,1,0:T(8,128)(2,1)S(1)}, u32[]{:S(2)}, u32[]{:S(2)}) collective-permute-start(bf16[2,128,128]{2,1,0:T(8,128)(2,1)S(1)} %get-tuple-element.16), channel_id=1, source_target_pairs={{0,16},{16,0},{32,48},{48,32},{64,80},{80,64},{96,112},{112,96},{1... | collective-permute-start | bytes 196616 | tf_op jit(solution)/shard_map/ppermute | solution.py:74
  51.4 0.7 copy-start.5
  51.7 1.9 %copy-start.1 = (bf16[4096,320]{0,1:T(8,128)(2,1)S(1)}, bf16[4096,320]{0,1:T(8,128)(2,1)}, u32[]{:S(2)}) copy-start(bf16[4096,320]{0,1:T(8,128)(2,1)} %param.12) | copy-start | bytes 7864324
  55.8 24.7 %collective-permute-start.8 = (bf16[768,128]{0,1:T(8,128)(2,1)}, bf16[768,128]{0,1:T(8,128)(2,1)S(1)}, u32[]{:S(2)}, u32[]{:S(2)}) collective-permute-start(bf16[768,128]{0,1:T(8,128)(2,1)} %get-tuple-element.20), channel_id=1, source_target_pairs={{0,1},{1,2},{2,3},{3,4},{4,5},{5,6},{6,7},{7,8},{8,9},{9,10},{10,1... | collective-permute-start | bytes 589832 | tf_op jit(solution)/shard_map/ppermute | solution.py:100
  59.0 15.9 %collective-permute-start.9 = (bf16[768,128]{0,1:T(8,128)(2,1)}, bf16[768,128]{0,1:T(8,128)(2,1)S(1)}, u32[]{:S(2)}, u32[]{:S(2)}) collective-permute-start(bf16[768,128]{0,1:T(8,128)(2,1)} %get-tuple-element.20), channel_id=1, source_target_pairs={{0,15},{1,0},{2,1},{3,2},{4,3},{5,4},{6,5},{7,6},{8,7},{9,8},{10,9... | collective-permute-start | bytes 589832 | tf_op jit(solution)/shard_map/ppermute | solution.py:102
  74.9 13.8 %collective-permute-start.11 = (bf16[768,128]{0,1:T(8,128)(2,1)S(1)}, bf16[768,128]{0,1:T(8,128)(2,1)S(1)}, u32[]{:S(2)}, u32[]{:S(2)}) collective-permute-start(bf16[768,128]{0,1:T(8,128)(2,1)S(1)} %collective-permute-done.9), channel_id=1, source_target_pairs={{0,15},{1,0},{2,1},{3,2},{4,3},{5,4},{6,5},{7,6},{8,7},{9,8},{10,9... | collective-permute-start | bytes 589832 | tf_op jit(solution)/shard_map/ppermute | solution.py:102
  80.4 13.9 %collective-permute-start.10 = (bf16[768,128]{0,1:T(8,128)(2,1)S(1)}, bf16[768,128]{0,1:T(8,128)(2,1)S(1)}, u32[]{:S(2)}, u32[]{:S(2)}) collective-permute-start(bf16[768,128]{0,1:T(8,128)(2,1)S(1)} %collective-permute-done.8), channel_id=1, source_target_pairs={{0,1},{1,2},{2,3},{3,4},{4,5},{5,6},{6,7},{7,8},{8,9},{9,10},{10,1... | collective-permute-start | bytes 589832 | tf_op jit(solution)/shard_map/ppermute | solution.py:100
  88.7 12.9 %collective-permute-start.13 = (bf16[768,128]{0,1:T(8,128)(2,1)S(1)}, bf16[768,128]{0,1:T(8,128)(2,1)S(1)}, u32[]{:S(2)}, u32[]{:S(2)}) collective-permute-start(bf16[768,128]{0,1:T(8,128)(2,1)S(1)} %collective-permute-done.11), channel_id=1, source_target_pairs={{0,15},{1,0},{2,1},{3,2},{4,3},{5,4},{6,5},{7,6},{8,7},{9,8},{10,9... | collective-permute-start | bytes 589832 | tf_op jit(solution)/shard_map/ppermute | solution.py:102
  94.3 12.9 %collective-permute-start.12 = (bf16[768,128]{0,1:T(8,128)(2,1)S(1)}, bf16[768,128]{0,1:T(8,128)(2,1)S(1)}, u32[]{:S(2)}, u32[]{:S(2)}) collective-permute-start(bf16[768,128]{0,1:T(8,128)(2,1)S(1)} %collective-permute-done.10), channel_id=1, source_target_pairs={{0,1},{1,2},{2,3},{3,4},{4,5},{5,6},{6,7},{7,8},{8,9},{9,10},{10,1... | collective-permute-start | bytes 589832 | tf_op jit(solution)/shard_map/ppermute | solution.py:100
  101.6 12.8 %collective-permute-start.15 = (bf16[768,128]{0,1:T(8,128)(2,1)S(1)}, bf16[768,128]{0,1:T(8,128)(2,1)S(1)}, u32[]{:S(2)}, u32[]{:S(2)}) collective-permute-start(bf16[768,128]{0,1:T(8,128)(2,1)S(1)} %collective-permute-done.13), channel_id=1, source_target_pairs={{0,15},{1,0},{2,1},{3,2},{4,3},{5,4},{6,5},{7,6},{8,7},{9,8},{10,9... | collective-permute-start | bytes 589832 | tf_op jit(solution)/shard_map/ppermute | solution.py:102
  107.2 12.8 %collective-permute-start.14 = (bf16[768,128]{0,1:T(8,128)(2,1)S(1)}, bf16[768,128]{0,1:T(8,128)(2,1)S(1)}, u32[]{:S(2)}, u32[]{:S(2)}) collective-permute-start(bf16[768,128]{0,1:T(8,128)(2,1)S(1)} %collective-permute-done.12), channel_id=1, source_target_pairs={{0,1},{1,2},{2,3},{3,4},{4,5},{5,6},{6,7},{7,8},{8,9},{9,10},{10,1... | collective-permute-start | bytes 589832 | tf_op jit(solution)/shard_map/ppermute | solution.py:100
  114.4 12.3 %collective-permute-start.17 = (bf16[768,128]{0,1:T(8,128)(2,1)S(1)}, bf16[768,128]{0,1:T(8,128)(2,1)S(1)}, u32[]{:S(2)}, u32[]{:S(2)}) collective-permute-start(bf16[768,128]{0,1:T(8,128)(2,1)S(1)} %collective-permute-done.15), channel_id=1, source_target_pairs={{0,15},{1,0},{2,1},{3,2},{4,3},{5,4},{6,5},{7,6},{8,7},{9,8},{10,9... | collective-permute-start | bytes 589832 | tf_op jit(solution)/shard_map/ppermute | solution.py:102
  120.0 12.3 %collective-permute-start.16 = (bf16[768,128]{0,1:T(8,128)(2,1)S(1)}, bf16[768,128]{0,1:T(8,128)(2,1)S(1)}, u32[]{:S(2)}, u32[]{:S(2)}) collective-permute-start(bf16[768,128]{0,1:T(8,128)(2,1)S(1)} %collective-permute-done.14), channel_id=1, source_target_pairs={{0,1},{1,2},{2,3},{3,4},{4,5},{5,6},{6,7},{7,8},{8,9},{9,10},{10,1... | collective-permute-start | bytes 589832 | tf_op jit(solution)/shard_map/ppermute | solution.py:100
  126.7 9.1 %collective-permute-start.19 = (bf16[768,128]{0,1:T(8,128)(2,1)S(1)}, bf16[768,128]{0,1:T(8,128)(2,1)S(1)}, u32[]{:S(2)}, u32[]{:S(2)}) collective-permute-start(bf16[768,128]{0,1:T(8,128)(2,1)S(1)} %collective-permute-done.17), channel_id=1, source_target_pairs={{0,15},{1,0},{2,1},{3,2},{4,3},{5,4},{6,5},{7,6},{8,7},{9,8},{10,9... | collective-permute-start | bytes 589832 | tf_op jit(solution)/shard_map/ppermute | solution.py:102
  132.3 9.1 %collective-permute-start.18 = (bf16[768,128]{0,1:T(8,128)(2,1)S(1)}, bf16[768,128]{0,1:T(8,128)(2,1)S(1)}, u32[]{:S(2)}, u32[]{:S(2)}) collective-permute-start(bf16[768,128]{0,1:T(8,128)(2,1)S(1)} %collective-permute-done.16), channel_id=1, source_target_pairs={{0,1},{1,2},{2,3},{3,4},{4,5},{5,6},{6,7},{7,8},{8,9},{9,10},{10,1... | collective-permute-start | bytes 589832 | tf_op jit(solution)/shard_map/ppermute | solution.py:100
  135.8 16.8 %collective-permute-start.21 = (bf16[768,128]{0,1:T(8,128)(2,1)S(1)}, bf16[768,128]{0,1:T(8,128)(2,1)S(1)}, u32[]{:S(2)}, u32[]{:S(2)}) collective-permute-start(bf16[768,128]{0,1:T(8,128)(2,1)S(1)} %collective-permute-done.19), channel_id=1, source_target_pairs={{0,15},{1,0},{2,1},{3,2},{4,3},{5,4},{6,5},{7,6},{8,7},{9,8},{10,9... | collective-permute-start | bytes 589832 | tf_op jit(solution)/shard_map/ppermute | solution.py:102
  141.4 9.3 %collective-permute-start.20 = (bf16[768,128]{0,1:T(8,128)(2,1)S(1)}, bf16[768,128]{0,1:T(8,128)(2,1)}, u32[]{:S(2)}, u32[]{:S(2)}) collective-permute-start(bf16[768,128]{0,1:T(8,128)(2,1)S(1)} %collective-permute-done.18), channel_id=1, source_target_pairs={{0,1},{1,2},{2,3},{3,4},{4,5},{5,6},{6,7},{7,8},{8,9},{9,10},{10,1... | collective-permute-start | bytes 589832 | tf_op jit(solution)/shard_map/ppermute | solution.py:100
  150.7 9.1 %collective-permute-start.22 = (bf16[768,128]{0,1:T(8,128)(2,1)}, bf16[768,128]{0,1:T(8,128)(2,1)}, u32[]{:S(2)}, u32[]{:S(2)}) collective-permute-start(bf16[768,128]{0,1:T(8,128)(2,1)} %collective-permute-done.20), channel_id=1, source_target_pairs={{0,1},{1,2},{2,3},{3,4},{4,5},{5,6},{6,7},{7,8},{8,9},{9,10},{10,1... | collective-permute-start | bytes 589832 | tf_op jit(solution)/shard_map/ppermute | solution.py:100
  155.1 4.7 %copy-start.2 = (f32[768,320]{0,1:T(8,128)S(1)}, f32[768,320]{0,1:T(8,128)}, u32[]{:S(2)}) copy-start(f32[768,320]{0,1:T(8,128)} %fusion.5) | copy-start | bytes 2949124
  155.1 4.7 %copy-start.3 = (bf16[768,320]{0,1:T(8,128)(2,1)S(1)}, bf16[768,320]{0,1:T(8,128)(2,1)}, u32[]{:S(2)}) copy-start(bf16[768,320]{0,1:T(8,128)(2,1)} %param.13) | copy-start | bytes 1474564
Sparse Core Ops, SparseCore 0:
  53.2 84.1 all-gather.1

commit v7 on v5

--- a/solution.py
+++ b/solution.py
@@ -83,22 +83,28 @@
     tp_count = lax.axis_size("tp")
     me = lax.axis_index("tp")
     width = normed.shape[1]
+    half = width // 2
 
-    def part(shard, source):
-        rows = lax.dynamic_slice_in_dim(out_weight, source * width, width, axis=0)
+    def part(shard, source, offset=0):
+        rows = lax.dynamic_slice_in_dim(
+            out_weight, source * width + offset, shard.shape[1], axis=0
+        )
         return jnp.dot(shard, rows, preferred_element_type=jnp.float32)
 
     up = [(j, (j + 1) % tp_count) for j in range(tp_count)]
     down = [(j, (j - 1) % tp_count) for j in range(tp_count)]
     mixed = part(normed, me)
     rising, falling = normed, normed
-    for step in range(1, tp_count // 2 + 1):
+    for step in range(1, tp_count // 2):
         rising = lax.ppermute(rising, "tp", up)
-        if step < tp_count - step:
-            falling = lax.ppermute(falling, "tp", down)
+        falling = lax.ppermute(falling, "tp", down)
         mixed = mixed + part(rising, (me - step) % tp_count)
-        if step < tp_count - step:
-            mixed = mixed + part(falling, (me + step) % tp_count)
+        mixed = mixed + part(falling, (me + step) % tp_count)
+    far = (me + tp_count // 2) % tp_count
+    rising = lax.ppermute(rising[:, :half], "tp", up)
+    falling = lax.ppermute(falling[:, half:], "tp", down)
+    mixed = mixed + part(rising, far)
+    mixed = mixed + part(falling, far, half)
     return mixed
 
 

time: 169 us -> 169 us (level)
  waiting for transfers between devices: 53.6 us -> 48.3 us
  starting transfers between devices: 85.1 us -> 90 us
    ppermute x0 -> x2, starting transfers between devices: none -> 7.29 us  [the longest x1 5.37 us: ring_project(): falling = lax.ppermute(falling[:, half:], 'tp', down)]
    ppermute x8 -> x7, waiting for transfers between devices: 17.5 us -> 12.3 us  [ring_project(): rising = lax.ppermute(rising, 'tp', up)]
    ppermute x7, waiting for transfers between devices: 25.9 us -> 23.2 us  [ring_project(): falling = lax.ppermute(falling, 'tp', down)]
    ppermute x0 -> x2, waiting for transfers between devices: none -> 2.6 us  [the longest x1 1.45 us: ring_project(): falling = lax.ppermute(falling[:, half:], 'tp', down)]
    ppermute x8 -> x7, starting transfers between devices: 15.3 us -> 13.4 us  [ring_project(): rising = lax.ppermute(rising, 'tp', up)]
    dot_general x16 -> x17, matrix products: 6.49 us -> 6.85 us  [part(): return jnp.dot(shard, rows, preferred_element_type=jnp.float32)]
  transfers between devices with their start and end apart: 23 -> 24, of which waited for: 13 -> 14; matrix products, arithmetic and copies ran while one was open for 6% -> 6% of each run, Pallas kernels for 0% -> 0%
where the time goes in v7:
time: 169 us; the launch traced here: 168 us
  starting transfers between devices  90 us (53%)
  waiting for transfers between devices  48.3 us (29%)
  matrix products  15.2 us (9%)
  other arithmetic  9.29 us (5%)
  local copies, waits for them, and re-layouts  3.92 us (2%)
    ppermute x7, starting transfers between devices, ring_project(): falling = lax.ppermute(falling, 'tp', down)  43.9 us
    ppermute x7, waiting for transfers between devices, ring_project(): falling = lax.ppermute(falling, 'tp', down)  23.2 us
    ppermute x6, starting transfers between devices, gather_line(): got.append(unpack(lax.ppermute(pack(total_s, total_p), 'seq', pairs)))  21.4 us
    ppermute x7, starting transfers between devices, ring_project(): rising = lax.ppermute(rising, 'tp', up)  13.4 us
    ppermute x7, waiting for transfers between devices, ring_project(): rising = lax.ppermute(rising, 'tp', up)  12.3 us
    ppermute x6, waiting for transfers between devices, gather_line(): got.append(unpack(lax.ppermute(pack(total_s, total_p), 'seq', pairs)))  8.95 us
    dot_general x17, matrix products, part(): return jnp.dot(shard, rows, preferred_element_type=jnp.float32)  6.85 us
    ppermute x1, starting transfers between devices, ring_project(): falling = lax.ppermute(falling[:, half:], 'tp', down)  5.37 us
  transfers between devices with their start and end apart: 24, of which 14 were waited for; matrix products, arithmetic and copies ran while one was open for 6% of the time, Pallas kernels for 0%

profile of v7, /device:TPU:6, one launch (start us, length us, event | category | flops | bytes accessed | tf_op | source)
XLA Modules:
  0.0 167.6 jit_solution(3258336172636318651)
XLA Ops:
  0.0 0.8 reshape.87
  0.9 0.6 reduce-window.6
  1.9 0.6 exponential_bitcast_fusion.1
  2.8 0.6 multiply_exponential_fusion.1
  3.4 1.2 copy.27
  4.5 1.3 fusion.20
  5.9 1.3 broadcast_select_fusion.1
  7.2 0.7 broadcast_in_dim.22
  7.9 1.9 %collective-permute-start = (f32[2,136,128]{2,1,0:T(8,128)S(1)}, f32[2,136,128]{2,1,0:T(8,128)S(1)}, u32[]{:S(2)}, u32[]{:S(2)}) collective-permute-start(f32[2,136,128]{2,1,0:T(8,128)S(1)} %pad_maximum_fusion), channel_id=1, source_target_pairs={{0,16},{16,0},{32,48},{48,32},{64,80},{80,64},{96,112},{112,96},{1... | collective-permute-start | bytes 417800 | tf_op jit(solution)/shard_map/ppermute | solution.py:48
  9.9 1.2 collective-permute-done
  11.5 0.6 copy-done.3
  12.0 0.7 pad_maximum_fusion.1
  12.7 7.8 %collective-permute-start.1 = (f32[2,136,128]{2,1,0:T(8,128)}, f32[2,136,128]{2,1,0:T(8,128)}, u32[]{:S(2)}, u32[]{:S(2)}) collective-permute-start(f32[2,136,128]{2,1,0:T(8,128)} %pad_maximum_fusion.1), channel_id=1, source_target_pairs={{0,32},{16,112},{32,64},{48,16},{64,96},{80,48},{96,0},{112,80},{1... | collective-permute-start | bytes 417800 | tf_op jit(solution)/shard_map/ppermute | solution.py:32
  20.5 1.9 %collective-permute-start.2 = (f32[2,136,128]{2,1,0:T(8,128)}, f32[2,136,128]{2,1,0:T(8,128)}, u32[]{:S(2)}, u32[]{:S(2)}) collective-permute-start(f32[2,136,128]{2,1,0:T(8,128)} %pad_maximum_fusion.1), channel_id=1, source_target_pairs={{0,64},{16,80},{32,96},{48,112},{64,0},{80,16},{96,32},{112,48},{1... | collective-permute-start | bytes 417800 | tf_op jit(solution)/shard_map/ppermute | solution.py:32
  22.4 2.8 %collective-permute-start.3 = (f32[2,136,128]{2,1,0:T(8,128)}, f32[2,136,128]{2,1,0:T(8,128)}, u32[]{:S(2)}, u32[]{:S(2)}) collective-permute-start(f32[2,136,128]{2,1,0:T(8,128)} %pad_maximum_fusion.1), channel_id=1, source_target_pairs={{0,96},{16,48},{32,0},{48,80},{64,32},{80,112},{96,64},{112,16},{1... | collective-permute-start | bytes 417800 | tf_op jit(solution)/shard_map/ppermute | solution.py:32
  25.2 4.0 %collective-permute-done.2 = f32[2,136,128]{2,1,0:T(8,128)} collective-permute-done((f32[2,136,128]{2,1,0:T(8,128)}, f32[2,136,128]{2,1,0:T(8,128)}, u32[]{:S(2)}, u32[]{:S(2)}) %collective-permute-start.2) | collective-permute-done | bytes 139296 | tf_op jit(solution)/shard_map/ppermute | solution.py:32
  29.2 1.6 collective-permute-done.3
  30.9 1.3 fusion.95
  32.2 1.2 multiply_add_fusion.1
  33.5 0.7 pad_maximum_fusion.2
  34.2 1.9 %collective-permute-start.4 = (f32[2,136,128]{2,1,0:T(8,128)}, f32[2,136,128]{2,1,0:T(8,128)}, u32[]{:S(2)}, u32[]{:S(2)}) collective-permute-start(f32[2,136,128]{2,1,0:T(8,128)} %pad_maximum_fusion.2), channel_id=1, source_target_pairs={{0,128},{16,400},{32,160},{48,432},{64,192},{80,464},{96,224},{112... | collective-permute-start | bytes 417800 | tf_op jit(solution)/shard_map/ppermute | solution.py:32
  36.1 3.4 %collective-permute-start.5 = (f32[2,136,128]{2,1,0:T(8,128)}, f32[2,136,128]{2,1,0:T(8,128)}, u32[]{:S(2)}, u32[]{:S(2)}) collective-permute-start(f32[2,136,128]{2,1,0:T(8,128)} %pad_maximum_fusion.2), channel_id=1, source_target_pairs={{0,256},{16,272},{32,288},{48,304},{64,320},{80,336},{96,352},{112... | collective-permute-start | bytes 417800 | tf_op jit(solution)/shard_map/ppermute | solution.py:32
  39.5 3.6 %collective-permute-start.6 = (f32[2,136,128]{2,1,0:T(8,128)}, f32[2,136,128]{2,1,0:T(8,128)}, u32[]{:S(2)}, u32[]{:S(2)}) collective-permute-start(f32[2,136,128]{2,1,0:T(8,128)} %pad_maximum_fusion.2), channel_id=1, source_target_pairs={{0,384},{16,144},{32,416},{48,176},{64,448},{80,208},{96,480},{112... | collective-permute-start | bytes 417800 | tf_op jit(solution)/shard_map/ppermute | solution.py:32
  43.2 3.1 %collective-permute-done.4 = f32[2,136,128]{2,1,0:T(8,128)} collective-permute-done((f32[2,136,128]{2,1,0:T(8,128)}, f32[2,136,128]{2,1,0:T(8,128)}, u32[]{:S(2)}, u32[]{:S(2)}) %collective-permute-start.4) | collective-permute-done | bytes 139296 | tf_op jit(solution)/shard_map/ppermute | solution.py:32
  46.3 0.8 fusion.94
  47.4 2.0 %multiply_add_fusion = (bf16[2,128,128]{2,1,0:T(8,128)(2,1)}, bf16[2,128,128]{2,1,0:T(8,128)(2,1)}) fusion(f32[2]{0:T(128)} %multiply_exponential_fusion.1, f32[2,128,128]{2,1,0:T(8,128)S(1)} %fusion.20, f32[2,128,128]{2,1,0:T(8,128)} %copy-done.2, pred[]{:T(512)S(6)} %eq.21, f32[2,136,128]{2,1,0:T(8,128)} %collective-permute-done.3, f32[2]{0:T(128)} %copy-done.9, ...), kind=kLoop, calls=%fused_computation.85 | loop fusion | flops 557056 | bytes 1179705 | tf_op jit(solution)/shard_map/add | solution.py:75
  49.4 2.0 %collective-permute-start.7 = (bf16[2,128,128]{2,1,0:T(8,128)(2,1)}, bf16[2,128,128]{2,1,0:T(8,128)(2,1)S(1)}, u32[]{:S(2)}, u32[]{:S(2)}) collective-permute-start(bf16[2,128,128]{2,1,0:T(8,128)(2,1)} %get-tuple-element.16), channel_id=1, source_target_pairs={{0,16},{16,0},{32,48},{48,32},{64,80},{80,64},{96,112},{112,96},{1... | collective-permute-start | bytes 196616 | tf_op jit(solution)/shard_map/ppermute | solution.py:74
  51.5 4.0 %fusion.12 = f32[768,2,128]{0,2,1:T(8,128)} fusion(s32[2,768]{1,0:T(2,128)S(1)} %get-tuple-element.19, bf16[768,2,128]{0,2,1:T(8,128)(2,1)S(1)} %bitcast.88, bf16[768,256]{1,0:T(8,128)(2,1)} %param.9, bf16[768,256]{1,0:T(8,128)(2,1)S(1)} %copy-done.1), kind=kOutput, calls=%fused_computation.20 | convolution fusion | flops 612237312 | bytes 1972224 | tf_op jit(solution)/shard_map/hts,shd->thd/dot_general | solution.py:123
  55.5 1.5 fusion.16
  57.0 0.3 multiply_reduce_fusion
  57.5 10.8 %collective-permute-start.9 = (bf16[768,256]{0,1:T(8,128)(2,1)S(1)}, bf16[768,256]{0,1:T(8,128)(2,1)}, u32[]{:S(2)}, u32[]{:S(2)}) collective-permute-start(bf16[768,256]{0,1:T(8,128)(2,1)S(1)} %bitcast.89), channel_id=1, source_target_pairs={{0,15},{1,0},{2,1},{3,2},{4,3},{5,4},{6,5},{7,6},{8,7},{9,8},{10,9... | collective-permute-start | bytes 1179656 | tf_op jit(solution)/shard_map/ppermute | solution.py:100
  68.3 1.9 %collective-permute-start.8 = (bf16[768,256]{0,1:T(8,128)(2,1)S(1)}, bf16[768,256]{0,1:T(8,128)(2,1)S(1)}, u32[]{:S(2)}, u32[]{:S(2)}) collective-permute-start(bf16[768,256]{0,1:T(8,128)(2,1)S(1)} %bitcast.90), channel_id=1, source_target_pairs={{0,1},{1,2},{2,3},{3,4},{4,5},{5,6},{6,7},{7,8},{8,9},{9,10},{10,1... | collective-permute-start | bytes 1179656 | tf_op jit(solution)/shard_map/ppermute | solution.py:99
  70.5 0.3 fusion.60
  70.8 6.5 %collective-permute-done.9 = bf16[768,256]{0,1:T(8,128)(2,1)} collective-permute-done((bf16[768,256]{0,1:T(8,128)(2,1)S(1)}, bf16[768,256]{0,1:T(8,128)(2,1)}, u32[]{:S(2)}, u32[]{:S(2)}) %collective-permute-start.9) | collective-permute-done | bytes 393248 | tf_op jit(solution)/shard_map/ppermute | solution.py:100
  77.3 5.7 %collective-permute-start.11 = (bf16[768,256]{0,1:T(8,128)(2,1)}, bf16[768,256]{0,1:T(8,128)(2,1)S(1)}, u32[]{:S(2)}, u32[]{:S(2)}) collective-permute-start(bf16[768,256]{0,1:T(8,128)(2,1)} %collective-permute-done.9), channel_id=1, source_target_pairs={{0,15},{1,0},{2,1},{3,2},{4,3},{5,4},{6,5},{7,6},{8,7},{9,8},{10,9... | collective-permute-start | bytes 1179656 | tf_op jit(solution)/shard_map/ppermute | solution.py:100
  83.0 1.9 %collective-permute-start.10 = (bf16[768,256]{0,1:T(8,128)(2,1)S(1)}, bf16[768,256]{0,1:T(8,128)(2,1)S(1)}, u32[]{:S(2)}, u32[]{:S(2)}) collective-permute-start(bf16[768,256]{0,1:T(8,128)(2,1)S(1)} %collective-permute-done.8), channel_id=1, source_target_pairs={{0,1},{1,2},{2,3},{3,4},{4,5},{5,6},{6,7},{7,8},{8,9},{9,10},{10,1... | collective-permute-start | bytes 1179656 | tf_op jit(solution)/shard_map/ppermute | solution.py:99
  85.0 0.3 convolution_add_fusion.7
  85.3 1.3 convolution_add_fusion.6
  86.6 5.0 %collective-permute-done.11 = bf16[768,256]{0,1:T(8,128)(2,1)S(1)} collective-permute-done((bf16[768,256]{0,1:T(8,128)(2,1)}, bf16[768,256]{0,1:T(8,128)(2,1)S(1)}, u32[]{:S(2)}, u32[]{:S(2)}) %collective-permute-start.11) | collective-permute-done | bytes 393248 | tf_op jit(solution)/shard_map/ppermute | solution.py:100
  91.6 5.5 %collective-permute-start.13 = (bf16[768,256]{0,1:T(8,128)(2,1)S(1)}, bf16[768,256]{0,1:T(8,128)(2,1)S(1)}, u32[]{:S(2)}, u32[]{:S(2)}) collective-permute-start(bf16[768,256]{0,1:T(8,128)(2,1)S(1)} %collective-permute-done.11), channel_id=1, source_target_pairs={{0,15},{1,0},{2,1},{3,2},{4,3},{5,4},{6,5},{7,6},{8,7},{9,8},{10,9... | collective-permute-start | bytes 1179656 | tf_op jit(solution)/shard_map/ppermute | solution.py:100
  97.1 1.9 %collective-permute-start.12 = (bf16[768,256]{0,1:T(8,128)(2,1)S(1)}, bf16[768,256]{0,1:T(8,128)(2,1)S(1)}, u32[]{:S(2)}, u32[]{:S(2)}) collective-permute-start(bf16[768,256]{0,1:T(8,128)(2,1)S(1)} %collective-permute-done.10), channel_id=1, source_target_pairs={{0,1},{1,2},{2,3},{3,4},{4,5},{5,6},{6,7},{7,8},{8,9},{9,10},{10,1... | collective-permute-start | bytes 1179656 | tf_op jit(solution)/shard_map/ppermute | solution.py:99
  99.0 0.3 fusion.55
  99.6 4.8 %collective-permute-done.13 = bf16[768,256]{0,1:T(8,128)(2,1)S(1)} collective-permute-done((bf16[768,256]{0,1:T(8,128)(2,1)S(1)}, bf16[768,256]{0,1:T(8,128)(2,1)S(1)}, u32[]{:S(2)}, u32[]{:S(2)}) %collective-permute-start.13) | collective-permute-done | bytes 393248 | tf_op jit(solution)/shard_map/ppermute | solution.py:100
  104.4 5.6 %collective-permute-start.15 = (bf16[768,256]{0,1:T(8,128)(2,1)S(1)}, bf16[768,256]{0,1:T(8,128)(2,1)S(1)}, u32[]{:S(2)}, u32[]{:S(2)}) collective-permute-start(bf16[768,256]{0,1:T(8,128)(2,1)S(1)} %collective-permute-done.13), channel_id=1, source_target_pairs={{0,15},{1,0},{2,1},{3,2},{4,3},{5,4},{6,5},{7,6},{8,7},{9,8},{10,9... | collective-permute-start | bytes 1179656 | tf_op jit(solution)/shard_map/ppermute | solution.py:100
  110.0 1.9 %collective-permute-start.14 = (bf16[768,256]{0,1:T(8,128)(2,1)S(1)}, bf16[768,256]{0,1:T(8,128)(2,1)S(1)}, u32[]{:S(2)}, u32[]{:S(2)}) collective-permute-start(bf16[768,256]{0,1:T(8,128)(2,1)S(1)} %collective-permute-done.12), channel_id=1, source_target_pairs={{0,1},{1,2},{2,3},{3,4},{4,5},{5,6},{6,7},{7,8},{8,9},{9,10},{10,1... | collective-permute-start | bytes 1179656 | tf_op jit(solution)/shard_map/ppermute | solution.py:99
  112.2 0.3 fusion.10
  112.5 3.9 %collective-permute-done.15 = bf16[768,256]{0,1:T(8,128)(2,1)S(1)} collective-permute-done((bf16[768,256]{0,1:T(8,128)(2,1)S(1)}, bf16[768,256]{0,1:T(8,128)(2,1)S(1)}, u32[]{:S(2)}, u32[]{:S(2)}) %collective-permute-start.15) | collective-permute-done | bytes 393248 | tf_op jit(solution)/shard_map/ppermute | solution.py:100
  116.4 5.6 %collective-permute-start.17 = (bf16[768,256]{0,1:T(8,128)(2,1)S(1)}, bf16[768,256]{0,1:T(8,128)(2,1)S(1)}, u32[]{:S(2)}, u32[]{:S(2)}) collective-permute-start(bf16[768,256]{0,1:T(8,128)(2,1)S(1)} %collective-permute-done.15), channel_id=1, source_target_pairs={{0,15},{1,0},{2,1},{3,2},{4,3},{5,4},{6,5},{7,6},{8,7},{9,8},{10,9... | collective-permute-start | bytes 1179656 | tf_op jit(solution)/shard_map/ppermute | solution.py:100
  122.0 1.9 %collective-permute-start.16 = (bf16[768,256]{0,1:T(8,128)(2,1)S(1)}, bf16[768,256]{0,1:T(8,128)(2,1)S(1)}, u32[]{:S(2)}, u32[]{:S(2)}) collective-permute-start(bf16[768,256]{0,1:T(8,128)(2,1)S(1)} %collective-permute-done.14), channel_id=1, source_target_pairs={{0,1},{1,2},{2,3},{3,4},{4,5},{5,6},{6,7},{7,8},{8,9},{9,10},{10,1... | collective-permute-start | bytes 1179656 | tf_op jit(solution)/shard_map/ppermute | solution.py:99
  124.2 0.3 fusion.9
  124.5 3.0 %collective-permute-done.17 = bf16[768,256]{0,1:T(8,128)(2,1)S(1)} collective-permute-done((bf16[768,256]{0,1:T(8,128)(2,1)S(1)}, bf16[768,256]{0,1:T(8,128)(2,1)S(1)}, u32[]{:S(2)}, u32[]{:S(2)}) %collective-permute-start.17) | collective-permute-done | bytes 393248 | tf_op jit(solution)/shard_map/ppermute | solution.py:100
  127.5 5.6 %collective-permute-start.19 = (bf16[768,256]{0,1:T(8,128)(2,1)S(1)}, bf16[768,256]{0,1:T(8,128)(2,1)S(1)}, u32[]{:S(2)}, u32[]{:S(2)}) collective-permute-start(bf16[768,256]{0,1:T(8,128)(2,1)S(1)} %collective-permute-done.17), channel_id=1, source_target_pairs={{0,15},{1,0},{2,1},{3,2},{4,3},{5,4},{6,5},{7,6},{8,7},{9,8},{10,9... | collective-permute-start | bytes 1179656 | tf_op jit(solution)/shard_map/ppermute | solution.py:100
  133.1 1.9 %collective-permute-start.18 = (bf16[768,256]{0,1:T(8,128)(2,1)S(1)}, bf16[768,256]{0,1:T(8,128)(2,1)S(1)}, u32[]{:S(2)}, u32[]{:S(2)}) collective-permute-start(bf16[768,256]{0,1:T(8,128)(2,1)S(1)} %collective-permute-done.16), channel_id=1, source_target_pairs={{0,1},{1,2},{2,3},{3,4},{4,5},{5,6},{6,7},{7,8},{8,9},{9,10},{10,1... | collective-permute-start | bytes 1179656 | tf_op jit(solution)/shard_map/ppermute | solution.py:99
  135.0 0.3 fusion.46
  135.3 0.3 fusion.8
  135.6 8.4 %collective-permute-done.18 = bf16[768,256]{0,1:T(8,128)(2,1)S(1)} collective-permute-done((bf16[768,256]{0,1:T(8,128)(2,1)S(1)}, bf16[768,256]{0,1:T(8,128)(2,1)S(1)}, u32[]{:S(2)}, u32[]{:S(2)}) %collective-permute-start.18) | collective-permute-done | bytes 393248 | tf_op jit(solution)/shard_map/ppermute | solution.py:99
  144.0 1.9 %collective-permute-start.20 = (bf16[768,256]{0,1:T(8,128)(2,1)S(1)}, bf16[768,256]{0,1:T(8,128)(2,1)S(1)}, u32[]{:S(2)}, u32[]{:S(2)}) collective-permute-start(bf16[768,256]{0,1:T(8,128)(2,1)S(1)} %collective-permute-done.18), channel_id=1, source_target_pairs={{0,1},{1,2},{2,3},{3,4},{4,5},{5,6},{6,7},{7,8},{8,9},{9,10},{10,1... | collective-permute-start | bytes 1179656 | tf_op jit(solution)/shard_map/ppermute | solution.py:99
  145.9 5.1 %collective-permute-start.21 = (bf16[768,256]{0,1:T(8,128)(2,1)S(1)}, bf16[768,256]{0,1:T(8,128)(2,1)S(1)}, u32[]{:S(2)}, u32[]{:S(2)}) collective-permute-start(bf16[768,256]{0,1:T(8,128)(2,1)S(1)} %collective-permute-done.19), channel_id=1, source_target_pairs={{0,15},{1,0},{2,1},{3,2},{4,3},{5,4},{6,5},{7,6},{8,7},{9,8},{10,9... | collective-permute-start | bytes 1179656 | tf_op jit(solution)/shard_map/ppermute | solution.py:100
  151.7 3.9 %collective-permute-done.20 = bf16[768,256]{0,1:T(8,128)(2,1)S(1)} collective-permute-done((bf16[768,256]{0,1:T(8,128)(2,1)S(1)}, bf16[768,256]{0,1:T(8,128)(2,1)S(1)}, u32[]{:S(2)}, u32[]{:S(2)}) %collective-permute-start.20) | collective-permute-done | bytes 393248 | tf_op jit(solution)/shard_map/ppermute | solution.py:99
  155.6 1.9 %collective-permute-start.22 = (bf16[768,128]{0,1:T(8,128)(2,1)S(1)}, bf16[768,128]{0,1:T(8,128)(2,1)S(1)}, u32[]{:S(2)}, u32[]{:S(2)}) collective-permute-start(bf16[768,128]{0,1:T(8,128)(2,1)S(1)} %slice.87), channel_id=1, source_target_pairs={{0,1},{1,2},{2,3},{3,4},{4,5},{5,6},{6,7},{7,8},{8,9},{9,10},{10,1... | collective-permute-start | bytes 589832 | tf_op jit(solution)/shard_map/ppermute | solution.py:104
  157.6 5.4 %collective-permute-start.23 = (bf16[768,128]{0,1:T(8,128)(2,1)S(1)}, bf16[768,128]{0,1:T(8,128)(2,1)S(1)}, u32[]{:S(2)}, u32[]{:S(2)}) collective-permute-start(bf16[768,128]{0,1:T(8,128)(2,1)S(1)} %slice.88), channel_id=1, source_target_pairs={{0,15},{1,0},{2,1},{3,2},{4,3},{5,4},{6,5},{7,6},{8,7},{9,8},{10,9... | collective-permute-start | bytes 589832 | tf_op jit(solution)/shard_map/ppermute | solution.py:105
  163.3 1.1 collective-permute-done.22
  164.7 1.5 collective-permute-done.23
  166.4 1.2 fusion.17
  (57 shorter events, 3.9 us)
Async XLA Ops:
  0.0 70.5 %copy-start = (bf16[4096,320]{0,1:T(8,128)(2,1)S(1)}, bf16[4096,320]{0,1:T(8,128)(2,1)}, u32[]{:S(2)}) copy-start(bf16[4096,320]{0,1:T(8,128)(2,1)} %param.12) | copy-start | bytes 7864324
  4.5 46.9 %copy-start.1 = (bf16[768,256]{1,0:T(8,128)(2,1)S(1)}, bf16[768,256]{1,0:T(8,128)(2,1)}, u32[]{:S(2)}) copy-start(bf16[768,256]{1,0:T(8,128)(2,1)} %param.7) | copy-start | bytes 1179652
  7.1 4.1 %copy-start.2 = (f32[2,128,128]{2,1,0:T(8,128)}, f32[2,128,128]{2,1,0:T(8,128)S(1)}, u32[]{:S(2)}) copy-start(f32[2,128,128]{2,1,0:T(8,128)S(1)} %get-tuple-element.21) | copy-start | bytes 393220
  7.9 3.3 %collective-permute-start = (f32[2,136,128]{2,1,0:T(8,128)S(1)}, f32[2,136,128]{2,1,0:T(8,128)S(1)}, u32[]{:S(2)}, u32[]{:S(2)}) collective-permute-start(f32[2,136,128]{2,1,0:T(8,128)S(1)} %pad_maximum_fusion), channel_id=1, source_target_pairs={{0,16},{16,0},{32,48},{48,32},{64,80},{80,64},{96,112},{112,96},{1... | collective-permute-start | bytes 417800 | tf_op jit(solution)/shard_map/ppermute | solution.py:48
  9.9 10.5 %copy-start.7 = (f32[2,1]{1,0:T(2,128)}, f32[2,1]{1,0:T(2,128)S(1)}, u32[]{:S(2)}) copy-start(f32[2,1]{1,0:T(2,128)S(1)} %multiply_exponential_fusion) | copy-start | bytes 28
  11.2 1.5 copy-start.6
  11.3 11.1 %copy-start.10 = (f32[2]{0:T(128)}, f32[2]{0:T(128)S(1)}, u32[]{:S(2)}) copy-start(f32[2]{0:T(128)S(1)} %get-tuple-element.14) | copy-start | bytes 28
  11.4 0.6 copy-start.3
  12.7 12.5 %collective-permute-start.1 = (f32[2,136,128]{2,1,0:T(8,128)}, f32[2,136,128]{2,1,0:T(8,128)}, u32[]{:S(2)}, u32[]{:S(2)}) collective-permute-start(f32[2,136,128]{2,1,0:T(8,128)} %pad_maximum_fusion.1), channel_id=1, source_target_pairs={{0,32},{16,112},{32,64},{48,16},{64,96},{80,48},{96,0},{112,80},{1... | collective-permute-start | bytes 417800 | tf_op jit(solution)/shard_map/ppermute | solution.py:32
  20.5 8.8 %collective-permute-start.2 = (f32[2,136,128]{2,1,0:T(8,128)}, f32[2,136,128]{2,1,0:T(8,128)}, u32[]{:S(2)}, u32[]{:S(2)}) collective-permute-start(f32[2,136,128]{2,1,0:T(8,128)} %pad_maximum_fusion.1), channel_id=1, source_target_pairs={{0,64},{16,80},{32,96},{48,112},{64,0},{80,16},{96,32},{112,48},{1... | collective-permute-start | bytes 417800 | tf_op jit(solution)/shard_map/ppermute | solution.py:32
  22.4 8.5 %collective-permute-start.3 = (f32[2,136,128]{2,1,0:T(8,128)}, f32[2,136,128]{2,1,0:T(8,128)}, u32[]{:S(2)}, u32[]{:S(2)}) collective-permute-start(f32[2,136,128]{2,1,0:T(8,128)} %pad_maximum_fusion.1), channel_id=1, source_target_pairs={{0,96},{16,48},{32,0},{48,80},{64,32},{80,112},{96,64},{112,16},{1... | collective-permute-start | bytes 417800 | tf_op jit(solution)/shard_map/ppermute | solution.py:32
  32.2 1.2 copy-start.8
  32.2 1.2 copy-start.9
  34.2 12.1 %collective-permute-start.4 = (f32[2,136,128]{2,1,0:T(8,128)}, f32[2,136,128]{2,1,0:T(8,128)}, u32[]{:S(2)}, u32[]{:S(2)}) collective-permute-start(f32[2,136,128]{2,1,0:T(8,128)} %pad_maximum_fusion.2), channel_id=1, source_target_pairs={{0,128},{16,400},{32,160},{48,432},{64,192},{80,464},{96,224},{112... | collective-permute-start | bytes 417800 | tf_op jit(solution)/shard_map/ppermute | solution.py:32
  36.1 10.2 %collective-permute-start.5 = (f32[2,136,128]{2,1,0:T(8,128)}, f32[2,136,128]{2,1,0:T(8,128)}, u32[]{:S(2)}, u32[]{:S(2)}) collective-permute-start(f32[2,136,128]{2,1,0:T(8,128)} %pad_maximum_fusion.2), channel_id=1, source_target_pairs={{0,256},{16,272},{32,288},{48,304},{64,320},{80,336},{96,352},{112... | collective-permute-start | bytes 417800 | tf_op jit(solution)/shard_map/ppermute | solution.py:32
  39.5 7.8 %collective-permute-start.6 = (f32[2,136,128]{2,1,0:T(8,128)}, f32[2,136,128]{2,1,0:T(8,128)}, u32[]{:S(2)}, u32[]{:S(2)}) collective-permute-start(f32[2,136,128]{2,1,0:T(8,128)} %pad_maximum_fusion.2), channel_id=1, source_target_pairs={{0,384},{16,144},{32,416},{48,176},{64,448},{80,208},{96,480},{112... | collective-permute-start | bytes 417800 | tf_op jit(solution)/shard_map/ppermute | solution.py:32
  49.4 6.1 %copy-start.4 = (bf16[2,128,128]{2,1,0:T(8,128)(2,1)S(1)}, bf16[2,128,128]{2,1,0:T(8,128)(2,1)}, u32[]{:S(2)}) copy-start(bf16[2,128,128]{2,1,0:T(8,128)(2,1)} %get-tuple-element.17) | copy-start | bytes 196612
  49.4 6.1 %collective-permute-start.7 = (bf16[2,128,128]{2,1,0:T(8,128)(2,1)}, bf16[2,128,128]{2,1,0:T(8,128)(2,1)S(1)}, u32[]{:S(2)}, u32[]{:S(2)}) collective-permute-start(bf16[2,128,128]{2,1,0:T(8,128)(2,1)} %get-tuple-element.16), channel_id=1, source_target_pairs={{0,16},{16,0},{32,48},{48,32},{64,80},{80,64},{96,112},{112,96},{1... | collective-permute-start | bytes 196616 | tf_op jit(solution)/shard_map/ppermute | solution.py:74
  55.5 1.8 %copy-start.11 = (f32[256]{0:T(256)S(1)}, f32[256]{0:T(256)}, u32[]{:S(2)}) copy-start(f32[256]{0:T(256)} %param.11) | copy-start | bytes 3076
  57.5 19.9 %collective-permute-start.9 = (bf16[768,256]{0,1:T(8,128)(2,1)S(1)}, bf16[768,256]{0,1:T(8,128)(2,1)}, u32[]{:S(2)}, u32[]{:S(2)}) collective-permute-start(bf16[768,256]{0,1:T(8,128)(2,1)S(1)} %bitcast.89), channel_id=1, source_target_pairs={{0,15},{1,0},{2,1},{3,2},{4,3},{5,4},{6,5},{7,6},{8,7},{9,8},{10,9... | collective-permute-start | bytes 1179656 | tf_op jit(solution)/shard_map/ppermute | solution.py:100
  68.3 14.7 %collective-permute-start.8 = (bf16[768,256]{0,1:T(8,128)(2,1)S(1)}, bf16[768,256]{0,1:T(8,128)(2,1)S(1)}, u32[]{:S(2)}, u32[]{:S(2)}) collective-permute-start(bf16[768,256]{0,1:T(8,128)(2,1)S(1)} %bitcast.90), channel_id=1, source_target_pairs={{0,1},{1,2},{2,3},{3,4},{4,5},{5,6},{6,7},{7,8},{8,9},{9,10},{10,1... | collective-permute-start | bytes 1179656 | tf_op jit(solution)/shard_map/ppermute | solution.py:99
  77.3 14.2 %collective-permute-start.11 = (bf16[768,256]{0,1:T(8,128)(2,1)}, bf16[768,256]{0,1:T(8,128)(2,1)S(1)}, u32[]{:S(2)}, u32[]{:S(2)}) collective-permute-start(bf16[768,256]{0,1:T(8,128)(2,1)} %collective-permute-done.9), channel_id=1, source_target_pairs={{0,15},{1,0},{2,1},{3,2},{4,3},{5,4},{6,5},{7,6},{8,7},{9,8},{10,9... | collective-permute-start | bytes 1179656 | tf_op jit(solution)/shard_map/ppermute | solution.py:100
  83.0 14.0 %collective-permute-start.10 = (bf16[768,256]{0,1:T(8,128)(2,1)S(1)}, bf16[768,256]{0,1:T(8,128)(2,1)S(1)}, u32[]{:S(2)}, u32[]{:S(2)}) collective-permute-start(bf16[768,256]{0,1:T(8,128)(2,1)S(1)} %collective-permute-done.8), channel_id=1, source_target_pairs={{0,1},{1,2},{2,3},{3,4},{4,5},{5,6},{6,7},{7,8},{8,9},{9,10},{10,1... | collective-permute-start | bytes 1179656 | tf_op jit(solution)/shard_map/ppermute | solution.py:99
  91.6 12.8 %collective-permute-start.13 = (bf16[768,256]{0,1:T(8,128)(2,1)S(1)}, bf16[768,256]{0,1:T(8,128)(2,1)S(1)}, u32[]{:S(2)}, u32[]{:S(2)}) collective-permute-start(bf16[768,256]{0,1:T(8,128)(2,1)S(1)} %collective-permute-done.11), channel_id=1, source_target_pairs={{0,15},{1,0},{2,1},{3,2},{4,3},{5,4},{6,5},{7,6},{8,7},{9,8},{10,9... | collective-permute-start | bytes 1179656 | tf_op jit(solution)/shard_map/ppermute | solution.py:100
  97.1 12.9 %collective-permute-start.12 = (bf16[768,256]{0,1:T(8,128)(2,1)S(1)}, bf16[768,256]{0,1:T(8,128)(2,1)S(1)}, u32[]{:S(2)}, u32[]{:S(2)}) collective-permute-start(bf16[768,256]{0,1:T(8,128)(2,1)S(1)} %collective-permute-done.10), channel_id=1, source_target_pairs={{0,1},{1,2},{2,3},{3,4},{4,5},{5,6},{6,7},{7,8},{8,9},{9,10},{10,1... | collective-permute-start | bytes 1179656 | tf_op jit(solution)/shard_map/ppermute | solution.py:99
  104.4 12.0 %collective-permute-start.15 = (bf16[768,256]{0,1:T(8,128)(2,1)S(1)}, bf16[768,256]{0,1:T(8,128)(2,1)S(1)}, u32[]{:S(2)}, u32[]{:S(2)}) collective-permute-start(bf16[768,256]{0,1:T(8,128)(2,1)S(1)} %collective-permute-done.13), channel_id=1, source_target_pairs={{0,15},{1,0},{2,1},{3,2},{4,3},{5,4},{6,5},{7,6},{8,7},{9,8},{10,9... | collective-permute-start | bytes 1179656 | tf_op jit(solution)/shard_map/ppermute | solution.py:100
  110.0 12.0 %collective-permute-start.14 = (bf16[768,256]{0,1:T(8,128)(2,1)S(1)}, bf16[768,256]{0,1:T(8,128)(2,1)S(1)}, u32[]{:S(2)}, u32[]{:S(2)}) collective-permute-start(bf16[768,256]{0,1:T(8,128)(2,1)S(1)} %collective-permute-done.12), channel_id=1, source_target_pairs={{0,1},{1,2},{2,3},{3,4},{4,5},{5,6},{6,7},{7,8},{8,9},{9,10},{10,1... | collective-permute-start | bytes 1179656 | tf_op jit(solution)/shard_map/ppermute | solution.py:99
  116.4 11.1 %collective-permute-start.17 = (bf16[768,256]{0,1:T(8,128)(2,1)S(1)}, bf16[768,256]{0,1:T(8,128)(2,1)S(1)}, u32[]{:S(2)}, u32[]{:S(2)}) collective-permute-start(bf16[768,256]{0,1:T(8,128)(2,1)S(1)} %collective-permute-done.15), channel_id=1, source_target_pairs={{0,15},{1,0},{2,1},{3,2},{4,3},{5,4},{6,5},{7,6},{8,7},{9,8},{10,9... | collective-permute-start | bytes 1179656 | tf_op jit(solution)/shard_map/ppermute | solution.py:100
  122.0 11.1 %collective-permute-start.16 = (bf16[768,256]{0,1:T(8,128)(2,1)S(1)}, bf16[768,256]{0,1:T(8,128)(2,1)S(1)}, u32[]{:S(2)}, u32[]{:S(2)}) collective-permute-start(bf16[768,256]{0,1:T(8,128)(2,1)S(1)} %collective-permute-done.14), channel_id=1, source_target_pairs={{0,1},{1,2},{2,3},{3,4},{4,5},{5,6},{6,7},{7,8},{8,9},{9,10},{10,1... | collective-permute-start | bytes 1179656 | tf_op jit(solution)/shard_map/ppermute | solution.py:99
  127.5 18.4 %collective-permute-start.19 = (bf16[768,256]{0,1:T(8,128)(2,1)S(1)}, bf16[768,256]{0,1:T(8,128)(2,1)S(1)}, u32[]{:S(2)}, u32[]{:S(2)}) collective-permute-start(bf16[768,256]{0,1:T(8,128)(2,1)S(1)} %collective-permute-done.17), channel_id=1, source_target_pairs={{0,15},{1,0},{2,1},{3,2},{4,3},{5,4},{6,5},{7,6},{8,7},{9,8},{10,9... | collective-permute-start | bytes 1179656 | tf_op jit(solution)/shard_map/ppermute | solution.py:100
  133.1 10.9 %collective-permute-start.18 = (bf16[768,256]{0,1:T(8,128)(2,1)S(1)}, bf16[768,256]{0,1:T(8,128)(2,1)S(1)}, u32[]{:S(2)}, u32[]{:S(2)}) collective-permute-start(bf16[768,256]{0,1:T(8,128)(2,1)S(1)} %collective-permute-done.16), channel_id=1, source_target_pairs={{0,1},{1,2},{2,3},{3,4},{4,5},{5,6},{6,7},{7,8},{8,9},{9,10},{10,1... | collective-permute-start | bytes 1179656 | tf_op jit(solution)/shard_map/ppermute | solution.py:99
  144.0 11.6 %collective-permute-start.20 = (bf16[768,256]{0,1:T(8,128)(2,1)S(1)}, bf16[768,256]{0,1:T(8,128)(2,1)S(1)}, u32[]{:S(2)}, u32[]{:S(2)}) collective-permute-start(bf16[768,256]{0,1:T(8,128)(2,1)S(1)} %collective-permute-done.18), channel_id=1, source_target_pairs={{0,1},{1,2},{2,3},{3,4},{4,5},{5,6},{6,7},{7,8},{8,9},{9,10},{10,1... | collective-permute-start | bytes 1179656 | tf_op jit(solution)/shard_map/ppermute | solution.py:99
  145.9 11.6 %collective-permute-start.21 = (bf16[768,256]{0,1:T(8,128)(2,1)S(1)}, bf16[768,256]{0,1:T(8,128)(2,1)S(1)}, u32[]{:S(2)}, u32[]{:S(2)}) collective-permute-start(bf16[768,256]{0,1:T(8,128)(2,1)S(1)} %collective-permute-done.19), channel_id=1, source_target_pairs={{0,15},{1,0},{2,1},{3,2},{4,3},{5,4},{6,5},{7,6},{8,7},{9,8},{10,9... | collective-permute-start | bytes 1179656 | tf_op jit(solution)/shard_map/ppermute | solution.py:100
  151.7 14.7 %copy-start.5 = (bf16[768,320]{0,1:T(8,128)(2,1)S(1)}, bf16[768,320]{0,1:T(8,128)(2,1)}, u32[]{:S(2)}) copy-start(bf16[768,320]{0,1:T(8,128)(2,1)} %param.13) | copy-start | bytes 1474564
  155.6 8.8 %collective-permute-start.22 = (bf16[768,128]{0,1:T(8,128)(2,1)S(1)}, bf16[768,128]{0,1:T(8,128)(2,1)S(1)}, u32[]{:S(2)}, u32[]{:S(2)}) collective-permute-start(bf16[768,128]{0,1:T(8,128)(2,1)S(1)} %slice.87), channel_id=1, source_target_pairs={{0,1},{1,2},{2,3},{3,4},{4,5},{5,6},{6,7},{7,8},{8,9},{9,10},{10,1... | collective-permute-start | bytes 589832 | tf_op jit(solution)/shard_map/ppermute | solution.py:104
  157.6 8.5 %collective-permute-start.23 = (bf16[768,128]{0,1:T(8,128)(2,1)S(1)}, bf16[768,128]{0,1:T(8,128)(2,1)S(1)}, u32[]{:S(2)}, u32[]{:S(2)}) collective-permute-start(bf16[768,128]{0,1:T(8,128)(2,1)S(1)} %slice.88), channel_id=1, source_target_pairs={{0,15},{1,0},{2,1},{3,2},{4,3},{5,4},{6,5},{7,6},{8,7},{9,8},{10,9... | collective-permute-start | bytes 589832 | tf_op jit(solution)/shard_map/ppermute | solution.py:105

commit v8 on v4

--- a/solution.py
+++ b/solution.py
@@ -122,11 +122,15 @@
         jnp.bfloat16
     )
     normed = normed.reshape(tok_rows, head_count * HD)
-    mixed = jnp.dot(
-        lax.all_gather(normed, "tp", axis=1, tiled=True),
-        out_weight,
-        preferred_element_type=jnp.float32,
-    )
+    tp_count = lax.axis_size("tp")
+    rows = out_weight.reshape(tp_count, head_count, HD, -1)
+    mixed = None
+    for head in range(head_count):
+        gathered = lax.all_gather(normed[:, head * HD : (head + 1) * HD], "tp", axis=1, tiled=True)
+        part = jnp.dot(
+            gathered, rows[:, head].reshape(tp_count * HD, -1), preferred_element_type=jnp.float32
+        )
+        mixed = part if mixed is None else mixed + part
     return (residual.astype(jnp.float32) + mixed).astype(jnp.bfloat16)
 
 

time: 168 us -> 219 us (1.30)
  waiting for transfers between devices: 99 us -> 141 us
  local copies, waits for them, and re-layouts: 3.89 us -> 23 us
  other arithmetic: 10.7 us -> 1.86 us
    all_gather x1 -> x2, waiting for transfers between devices: 89.8 us -> 130 us  [local(): lax.all_gather(normed[:, head * HD:(head + 1) * HD], 'tp', axis=1, tiled=...]
    slice x1 -> x3, local copies, waits for them, and re-layouts: 0.21 us -> 16.3 us  [the longest x1 15.4 us: local(): rows[:, head].reshape(tp_count * HD, -1)]
    reshape x1 -> x2, local copies, waits for them, and re-layouts: 0.85 us -> 4.99 us  [the longest x1 4.24 us: local(): rows = out_weight.reshape(tp_count, head_count, HD, -1)]
    dot_general x1 -> x2, matrix products: 5.81 us -> 8.73 us  [local(): jnp.dot(gathered, rows[:, head].reshape(tp_count * HD, -1), preferred_ele...]
  transfers between devices with their start and end apart: 9 -> 10, of which waited for: 6 -> 7; matrix products, arithmetic and copies ran while one was open for 3% -> 12% of each run, Pallas kernels for 0% -> 0%
where the time goes in v8:
time: 219 us
  waiting for transfers between devices  141 us (64%)
  starting transfers between devices  25.3 us (12%)
  local copies, waits for them, and re-layouts  23 us (11%)
  matrix products  14.1 us (6%)
  between operations  13.7 us (6%)
    all_gather x2, waiting for transfers between devices, local(): lax.all_gather(normed[:, head * HD:(head + 1) * HD], 'tp', axis=1, tiled=...  130 us
    ppermute x6, starting transfers between devices, gather_line(): got.append(unpack(lax.ppermute(pack(total_s, total_p), 'seq', pairs)))  21.4 us
    slice x1, local copies, waits for them, and re-layouts, local(): rows[:, head].reshape(tp_count * HD, -1)  15.4 us
    ppermute x6, waiting for transfers between devices, gather_line(): got.append(unpack(lax.ppermute(pack(total_s, total_p), 'seq', pairs)))  9.06 us
    dot_general x2, matrix products, local(): jnp.dot(gathered, rows[:, head].reshape(tp_count * HD, -1), preferred_ele...  8.73 us
  transfers between devices with their start and end apart: 10, of which 7 were waited for; matrix products, arithmetic and copies ran while one was open for 12% of the time, Pallas kernels for 0%

profile of v8, /device:TPU:6, one launch (start us, length us, event | category | flops | bytes accessed | tf_op | source)
XLA Modules:
  0.0 218.7 jit_solution(4952317832375610689)
XLA Ops:
  6.5 0.0 copy-start
  6.5 0.0 all-gather.5.cloned.1.call-start
  6.5 0.8 reshape.90
  7.3 0.6 reduce-window.6
  7.9 0.2 slice_reduce_fusion.2
  8.1 0.2 reduce-window.9
  8.3 0.1 add_bitcast_fusion
  8.4 0.2 slice_reduce_fusion.3
  8.5 0.1 exponential_bitcast_fusion
  8.7 0.0 copy-start.2
  8.7 1.2 copy.29
  9.9 1.3 fusion.25
  11.2 1.3 broadcast_select_fusion.1
  12.4 0.1 broadcast_in_dim.22
  12.5 1.9 collective-permute-start
  14.5 0.1 multiply_exponential_fusion
  14.5 1.2 collective-permute-done
  15.8 0.1 slice_reduce_fusion.4
  15.9 0.1 slice_add_fusion
  16.0 0.1 broadcast_in_dim.24
  16.1 7.8 %collective-permute-start.1 = (f32[2,136,128]{2,1,0:T(8,128)S(1)}, f32[2,136,128]{2,1,0:T(8,128)S(1)}, u32[]{:S(2)}, u32[]{:S(2)}) collective-permute-start(f32[2,136,128]{2,1,0:T(8,128)S(1)} %pad_maximum_fusion.1), channel_id=1, source_target_pairs={{0,32},{16,112},{32,64},{48,16},{64,96},{80,48},{96,0},{112,80},{1... | collective-permute-start | bytes 417800 | tf_op jit(solution)/shard_map/ppermute | solution.py:32
  23.8 1.9 collective-permute-start.2
  25.8 2.8 %collective-permute-start.3 = (f32[2,136,128]{2,1,0:T(8,128)S(1)}, f32[2,136,128]{2,1,0:T(8,128)S(1)}, u32[]{:S(2)}, u32[]{:S(2)}) collective-permute-start(f32[2,136,128]{2,1,0:T(8,128)S(1)} %pad_maximum_fusion.1), channel_id=1, source_target_pairs={{0,96},{16,48},{32,0},{48,80},{64,32},{80,112},{96,64},{112,16},{1... | collective-permute-start | bytes 417800 | tf_op jit(solution)/shard_map/ppermute | solution.py:32
  28.6 0.0 collective-permute-done.1
  28.6 3.7 %collective-permute-done.2 = f32[2,136,128]{2,1,0:T(8,128)S(1)} collective-permute-done((f32[2,136,128]{2,1,0:T(8,128)S(1)}, f32[2,136,128]{2,1,0:T(8,128)S(1)}, u32[]{:S(2)}, u32[]{:S(2)}) %collective-permute-start.2) | collective-permute-done | bytes 139296 | tf_op jit(solution)/shard_map/ppermute | solution.py:32
  32.3 1.6 collective-permute-done.3
  33.9 0.1 fusion.57
  34.0 0.1 multiply_add_fusion.1
  34.2 0.1 broadcast_in_dim.27
  34.3 1.9 collective-permute-start.4
  36.2 3.4 %collective-permute-start.5 = (f32[2,136,128]{2,1,0:T(8,128)S(1)}, f32[2,136,128]{2,1,0:T(8,128)S(1)}, u32[]{:S(2)}, u32[]{:S(2)}) collective-permute-start(f32[2,136,128]{2,1,0:T(8,128)S(1)} %pad_maximum_fusion.2), channel_id=1, source_target_pairs={{0,256},{16,272},{32,288},{48,304},{64,320},{80,336},{96,352},{112... | collective-permute-start | bytes 417800 | tf_op jit(solution)/shard_map/ppermute | solution.py:32
  39.6 3.6 %collective-permute-start.6 = (f32[2,136,128]{2,1,0:T(8,128)S(1)}, f32[2,136,128]{2,1,0:T(8,128)S(1)}, u32[]{:S(2)}, u32[]{:S(2)}) collective-permute-start(f32[2,136,128]{2,1,0:T(8,128)S(1)} %pad_maximum_fusion.2), channel_id=1, source_target_pairs={{0,384},{16,144},{32,416},{48,176},{64,448},{80,208},{96,480},{112... | collective-permute-start | bytes 417800 | tf_op jit(solution)/shard_map/ppermute | solution.py:32
  43.3 2.8 %collective-permute-done.4 = f32[2,136,128]{2,1,0:T(8,128)S(1)} collective-permute-done((f32[2,136,128]{2,1,0:T(8,128)S(1)}, f32[2,136,128]{2,1,0:T(8,128)S(1)}, u32[]{:S(2)}, u32[]{:S(2)}) %collective-permute-start.4) | collective-permute-done | bytes 139296 | tf_op jit(solution)/shard_map/ppermute | solution.py:32
  46.0 0.0 collective-permute-done.5
  46.1 0.1 fusion.56
  46.2 1.0 collective-permute-done.6
  47.1 0.1 multiply_add_fusion
  47.3 1.9 collective-permute-start.7
  49.2 0.0 copy-done
  49.2 0.0 copy-done.2
  49.2 2.1 fusion.9
  51.4 0.0 copy-start.3
  51.4 0.0 collective-permute-done.7
  51.4 0.3 fusion.13
  51.7 0.4 multiply_reduce_fusion
  52.1 0.0 copy-done.3
  52.1 0.1 multiply_convert_fusion.4
  52.2 0.8 fusion.62
  53.0 0.0 all-gather.5.cloned.1.call-update
  53.0 0.0 all-gather.3.cloned.1.call-start
  53.1 0.7 all-gather.3.cloned.1.call-update
  53.8 4.2 %reshape.94 = bf16[16,2,128,320]{2,1,0,3:T(2,128)(2,1)S(1)} reshape(bf16[4096,320]{0,1:T(8,128)(2,1)} %param.12) | data formatting | bytes 5242880 | tf_op jit(solution)/shard_map/reshape | solution.py:126
  58.0 15.4 %slice_reduce_fusion.1 = (bf16[16,128,320]{1,0,2:T(8,128)(2,1)}, bf16[16,128,320]{1,0,2:T(8,128)(2,1)}) fusion(bf16[16,2,128,320]{2,1,0,3:T(2,128)(2,1)S(1)} %reshape.94), kind=kLoop, calls=%fused_computation.2 | loop fusion | bytes 5242880 | tf_op jit(solution)/shard_map/slice | solution.py:131
  73.4 59.0 %all-gather.5.cloned.1.call-done = bf16[768,2048]{0,1:T(8,128)(2,1)} async-done(((bf16[768,128]{0,1:T(8,128)(2,1)}), bf16[768,2048]{0,1:T(8,128)(2,1)}) %all-gather.5.cloned.1.call-update) | async-done | bytes 3145744 | tf_op jit(solution)/shard_map/all_gather | solution.py:129
  132.4 0.0 copy-start.1
  132.4 0.0 copy-start.4
  132.4 4.6 %fusion.3 = f32[768,320]{0,1:T(8,128)} fusion(bf16[768,2048]{0,1:T(8,128)(2,1)} %all-gather.5.cloned.1.call-done, bf16[40,8,16,128]{3,2,1,0:T(8,128)(2,1)} %bitcast.96), kind=kOutput, calls=%fused_computation.5 | convolution fusion | flops 1006632960 | bytes 5439488 | tf_op jit(solution)/shard_map/dot_general | solution.py:130
  137.0 70.7 %all-gather.3.cloned.1.call-done = bf16[768,2048]{0,1:T(8,128)(2,1)} async-done(((bf16[768,128]{0,1:T(8,128)(2,1)}), bf16[768,2048]{0,1:T(8,128)(2,1)}) %all-gather.3.cloned.1.call-update) | async-done | bytes 3145744 | tf_op jit(solution)/shard_map/all_gather | solution.py:129
  207.7 0.0 copy-done.1
  207.7 0.0 copy-done.4
  207.8 4.1 %fusion.20 = bf16[768,320]{0,1:T(8,128)(2,1)} fusion(f32[768,320]{0,1:T(8,128)} %fusion.3, bf16[768,2048]{0,1:T(8,128)(2,1)} %all-gather.3.cloned.1.call-done, bf16[40,8,16,128]{3,2,1,0:T(8,128)(2,1)S(1)} %bitcast.95, bf16[768,320]{0,1:T(8,128)(2,1)S(1)} %copy-done.4), kind=kOutput, calls=%fused_computation.20 | convolution fusion | flops 1007616000 | bytes 6422528 | tf_op jit(solution)/shard_map/dot_general | solution.py:130
  (6 shorter events, 0.1 us)
Async XLA Ops:
  6.5 42.7 %copy-start = (bf16[768,256]{1,0:T(8,128)(2,1)S(1)}, bf16[768,256]{1,0:T(8,128)(2,1)}, u32[]{:S(2)}) copy-start(bf16[768,256]{1,0:T(8,128)(2,1)} %param.7) | copy-start | bytes 1179652
  6.5 125.8 %all-gather.5.cloned.1.call-start = ((), (), s32[]{:S(2)}) async-start(), calls=%async_computation.1 | async-start | bytes 3342336 | tf_op jit(solution)/shard_map/all_gather | solution.py:129
  8.7 40.5 %copy-start.2 = (bf16[768,256]{1,0:T(8,128)(2,1)S(1)}, bf16[768,256]{1,0:T(8,128)(2,1)}, u32[]{:S(2)}) copy-start(bf16[768,256]{1,0:T(8,128)(2,1)} %param.9) | copy-start | bytes 1179652
  12.5 3.3 %collective-permute-start = (f32[2,136,128]{2,1,0:T(8,128)S(1)}, f32[2,136,128]{2,1,0:T(8,128)S(1)}, u32[]{:S(2)}, u32[]{:S(2)}) collective-permute-start(f32[2,136,128]{2,1,0:T(8,128)S(1)} %pad_maximum_fusion), channel_id=1, source_target_pairs={{0,16},{16,0},{32,48},{48,32},{64,80},{80,64},{96,112},{112,96},{1... | collective-permute-start | bytes 417800 | tf_op jit(solution)/shard_map/ppermute | solution.py:48
  16.1 12.5 %collective-permute-start.1 = (f32[2,136,128]{2,1,0:T(8,128)S(1)}, f32[2,136,128]{2,1,0:T(8,128)S(1)}, u32[]{:S(2)}, u32[]{:S(2)}) collective-permute-start(f32[2,136,128]{2,1,0:T(8,128)S(1)} %pad_maximum_fusion.1), channel_id=1, source_target_pairs={{0,32},{16,112},{32,64},{48,16},{64,96},{80,48},{96,0},{112,80},{1... | collective-permute-start | bytes 417800 | tf_op jit(solution)/shard_map/ppermute | solution.py:32
  23.8 8.5 %collective-permute-start.2 = (f32[2,136,128]{2,1,0:T(8,128)S(1)}, f32[2,136,128]{2,1,0:T(8,128)S(1)}, u32[]{:S(2)}, u32[]{:S(2)}) collective-permute-start(f32[2,136,128]{2,1,0:T(8,128)S(1)} %pad_maximum_fusion.1), channel_id=1, source_target_pairs={{0,64},{16,80},{32,96},{48,112},{64,0},{80,16},{96,32},{112,48},{1... | collective-permute-start | bytes 417800 | tf_op jit(solution)/shard_map/ppermute | solution.py:32
  25.8 8.2 %collective-permute-start.3 = (f32[2,136,128]{2,1,0:T(8,128)S(1)}, f32[2,136,128]{2,1,0:T(8,128)S(1)}, u32[]{:S(2)}, u32[]{:S(2)}) collective-permute-start(f32[2,136,128]{2,1,0:T(8,128)S(1)} %pad_maximum_fusion.1), channel_id=1, source_target_pairs={{0,96},{16,48},{32,0},{48,80},{64,32},{80,112},{96,64},{112,16},{1... | collective-permute-start | bytes 417800 | tf_op jit(solution)/shard_map/ppermute | solution.py:32
  34.3 11.8 %collective-permute-start.4 = (f32[2,136,128]{2,1,0:T(8,128)S(1)}, f32[2,136,128]{2,1,0:T(8,128)S(1)}, u32[]{:S(2)}, u32[]{:S(2)}) collective-permute-start(f32[2,136,128]{2,1,0:T(8,128)S(1)} %pad_maximum_fusion.2), channel_id=1, source_target_pairs={{0,128},{16,400},{32,160},{48,432},{64,192},{80,464},{96,224},{112... | collective-permute-start | bytes 417800 | tf_op jit(solution)/shard_map/ppermute | solution.py:32
  36.2 9.9 %collective-permute-start.5 = (f32[2,136,128]{2,1,0:T(8,128)S(1)}, f32[2,136,128]{2,1,0:T(8,128)S(1)}, u32[]{:S(2)}, u32[]{:S(2)}) collective-permute-start(f32[2,136,128]{2,1,0:T(8,128)S(1)} %pad_maximum_fusion.2), channel_id=1, source_target_pairs={{0,256},{16,272},{32,288},{48,304},{64,320},{80,336},{96,352},{112... | collective-permute-start | bytes 417800 | tf_op jit(solution)/shard_map/ppermute | solution.py:32
  39.6 7.5 %collective-permute-start.6 = (f32[2,136,128]{2,1,0:T(8,128)S(1)}, f32[2,136,128]{2,1,0:T(8,128)S(1)}, u32[]{:S(2)}, u32[]{:S(2)}) collective-permute-start(f32[2,136,128]{2,1,0:T(8,128)S(1)} %pad_maximum_fusion.2), channel_id=1, source_target_pairs={{0,384},{16,144},{32,416},{48,176},{64,448},{80,208},{96,480},{112... | collective-permute-start | bytes 417800 | tf_op jit(solution)/shard_map/ppermute | solution.py:32
  47.3 4.1 %collective-permute-start.7 = (bf16[2,128,128]{2,1,0:T(8,128)(2,1)S(1)}, bf16[2,128,128]{2,1,0:T(8,128)(2,1)S(1)}, u32[]{:S(2)}, u32[]{:S(2)}) collective-permute-start(bf16[2,128,128]{2,1,0:T(8,128)(2,1)S(1)} %get-tuple-element.18), channel_id=1, source_target_pairs={{0,16},{16,0},{32,48},{48,32},{64,80},{80,64},{96,112},{112,96},{1... | collective-permute-start | bytes 196616 | tf_op jit(solution)/shard_map/ppermute | solution.py:74
  51.4 0.7 copy-start.3
  53.0 154.7 %all-gather.3.cloned.1.call-start = ((), (), s32[]{:S(2)}) async-start(), calls=%async_computation | async-start | bytes 3342336 | tf_op jit(solution)/shard_map/all_gather | solution.py:129
  132.4 75.4 %copy-start.1 = (bf16[16,128,320]{1,0,2:T(8,128)(2,1)S(1)}, bf16[16,128,320]{1,0,2:T(8,128)(2,1)}, u32[]{:S(2)}) copy-start(bf16[16,128,320]{1,0,2:T(8,128)(2,1)} %get-tuple-element.5) | copy-start | bytes 3932164
  132.4 75.4 %copy-start.4 = (bf16[768,320]{0,1:T(8,128)(2,1)S(1)}, bf16[768,320]{0,1:T(8,128)(2,1)}, u32[]{:S(2)}) copy-start(bf16[768,320]{0,1:T(8,128)(2,1)} %param.13) | copy-start | bytes 1474564
Sparse Core Ops, SparseCore 0:
  53.1 79.1 all-gather.4
  134.4 73.2 all-gather.2

commit v9 on v4

--- a/solution.py
+++ b/solution.py
@@ -33,7 +33,7 @@
     return got
 
 
-def block_scan(decay, summary_fwd, summary_bwd):
+def block_scan(decay, mine, other):
     seq_count = lax.axis_size("seq")
     line = 4
     me = lax.axis_index("seq")
@@ -42,8 +42,6 @@
     y = me // (2 * line)
     pos_x = jnp.where(second, line - 1 - x, x)
     pos_y = jnp.where(second, line - 1 - y, y)
-    mine = jnp.where(second, summary_bwd, summary_fwd)
-    other = jnp.where(second, summary_fwd, summary_bwd)
     got_s, got_p = unpack(
         lax.ppermute(pack(other, decay), "seq", [(i, i ^ 1) for i in range(seq_count)])
     )
@@ -96,16 +94,19 @@
     )
     tail_factor = factor(block_exp[None, :] - local_rows)
     head_factor = factor(local_rows)
-    keys_fwd = (key_heads * tail_factor[:, :, None]).astype(jnp.bfloat16)
-    keys_bwd = (key_heads * head_factor[:, :, None]).astype(jnp.bfloat16)
-    summary_fwd = jnp.einsum(
-        "shd,she->hde", keys_fwd, value_heads, preferred_element_type=jnp.float32
+    second = (lax.axis_index("seq") % 2) == 1
+    mine_factor = jnp.where(second, head_factor, tail_factor)
+    other_factor = jnp.where(second, tail_factor, head_factor)
+    keys_mine = (key_heads * mine_factor[:, :, None]).astype(jnp.bfloat16)
+    keys_other = (key_heads * other_factor[:, :, None]).astype(jnp.bfloat16)
+    summary_mine = jnp.einsum(
+        "shd,she->hde", keys_mine, value_heads, preferred_element_type=jnp.float32
     )
-    summary_bwd = jnp.einsum(
-        "shd,she->hde", keys_bwd, value_heads, preferred_element_type=jnp.float32
+    summary_other = jnp.einsum(
+        "shd,she->hde", keys_other, value_heads, preferred_element_type=jnp.float32
     )
     block_decay = factor(block_exp)
-    state_fwd, state_bwd = block_scan(block_decay, summary_fwd, summary_bwd)
+    state_fwd, state_bwd = block_scan(block_decay, summary_mine, summary_other)
     state_fwd = state_fwd.astype(jnp.bfloat16)
     state_bwd = state_bwd.astype(jnp.bfloat16)
     remote_fwd = (

time: 168 us -> 167 us (level)
  no operation moved by 1% of the time
where the time goes in v9:
time: 167 us; the launch traced here: 166 us
  waiting for transfers between devices  98.8 us (59%)
  starting transfers between devices  26 us (16%)
  matrix products  14.8 us (9%)
  between operations  13.7 us (8%)
  other arithmetic  9.37 us (6%)
  local copies, waits for them, and re-layouts  3.18 us (2%)
    all_gather x1, waiting for transfers between devices, local(): lax.all_gather(normed, 'tp', axis=1, tiled=True)  89.8 us
    ppermute x6, starting transfers between devices, gather_line(): got.append(unpack(lax.ppermute(pack(total_s, total_p), 'seq', pairs)))  22 us
    ppermute x6, waiting for transfers between devices, gather_line(): got.append(unpack(lax.ppermute(pack(total_s, total_p), 'seq', pairs)))  7.76 us
    dot_general x1, matrix products, local(): jnp.dot(lax.all_gather(normed, 'tp', axis=1, tiled=True), out_weight, pre...  5.81 us
    dot_general x1, matrix products, local(): jnp.einsum('hts,shd->thd', local_weights, value_heads, preferred_element_...  4.01 us
  transfers between devices with their start and end apart: 9, of which 6 were waited for; matrix products, arithmetic and copies ran while one was open for 3% of the time, Pallas kernels for 0%

profile of v9, /device:TPU:6, one launch (start us, length us, event | category | flops | bytes accessed | tf_op | source)
XLA Modules:
  0.0 165.8 jit_solution(13449986280690746022)
XLA Ops:
  6.5 0.0 copy-start
  6.5 0.0 copy-start.1
  6.5 0.0 all-gather.2.cloned.1.call-start
  6.5 0.9 reshape.89
  7.4 0.6 reduce-window.6
  8.0 0.2 slice_reduce_fusion
  8.2 0.2 reduce-window.9
  8.4 0.1 add_bitcast_fusion
  8.4 0.6 exponential_bitcast_fusion.1
  9.1 0.2 slice_reduce_fusion.1
  9.3 0.0 copy-start.9
  9.3 0.1 broadcast_select_fusion.1
  9.3 0.0 copy-start.3
  9.4 1.2 copy.40
  10.5 1.3 fusion.13
  11.8 0.1 broadcast_in_dim.22
  11.9 1.9 %collective-permute-start = (f32[2,136,128]{2,1,0:T(8,128)S(1)}, f32[2,136,128]{2,1,0:T(8,128)S(1)}, u32[]{:S(2)}, u32[]{:S(2)}) collective-permute-start(f32[2,136,128]{2,1,0:T(8,128)S(1)} %pad_maximum_fusion), channel_id=1, source_target_pairs={{0,16},{16,0},{32,48},{48,32},{64,80},{80,64},{96,112},{112,96},{1... | collective-permute-start | bytes 417800 | tf_op jit(solution)/shard_map/ppermute | solution.py:46
  13.8 0.1 multiply_exponential_fusion
  13.9 0.0 copy-start.5
  13.9 1.2 collective-permute-done
  15.1 0.0 copy-start.2
  15.1 0.1 slice_reduce_fusion.2
  15.2 0.0 copy-done.9
  15.2 0.0 copy-done.3
  15.2 0.0 copy-done.5
  15.3 0.0 copy-start.8
  15.3 0.5 copy-done.2
  15.8 1.9 %slice_add_fusion = (f32[2,128,128]{2,1,0:T(8,128)S(1)}, f32[2,128,128]{2,1,0:T(8,128)}) fusion(f32[2,136,128]{2,1,0:T(8,128)S(1)} %collective-permute-done, f32[2]{0:T(128)S(1)} %get-tuple-element.13, bf16[768,2,128]{0,2,1:T(8,128)(2,1)S(1)} %bitcast.77, f32[768,2]{0,1:T(2,128)S(1)} %broadcast_select_fusion, bf16[768,256]{1,0:T(8,128)(2,1)} %param.9), kind=kOutput, calls=%fused_computation.44 | convolution fusion | flops 50987008 | bytes 1185800 | tf_op jit(solution)/shard_map/shd,she->hde/dot_general | solution.py:102
  17.7 0.1 broadcast_in_dim.24
  17.8 0.7 pad_maximum_fusion.1
  18.4 0.0 copy-done.8
  18.5 2.7 %collective-permute-start.3 = (f32[2,136,128]{2,1,0:T(8,128)}, f32[2,136,128]{2,1,0:T(8,128)}, u32[]{:S(2)}, u32[]{:S(2)}) collective-permute-start(f32[2,136,128]{2,1,0:T(8,128)} %pad_maximum_fusion.1), channel_id=1, source_target_pairs={{0,96},{16,48},{32,0},{48,80},{64,32},{80,112},{96,64},{112,16},{1... | collective-permute-start | bytes 417800 | tf_op jit(solution)/shard_map/ppermute | solution.py:32
  21.2 8.4 %collective-permute-start.2 = (f32[2,136,128]{2,1,0:T(8,128)}, f32[2,136,128]{2,1,0:T(8,128)}, u32[]{:S(2)}, u32[]{:S(2)}) collective-permute-start(f32[2,136,128]{2,1,0:T(8,128)} %pad_maximum_fusion.1), channel_id=1, source_target_pairs={{0,64},{16,80},{32,96},{48,112},{64,0},{80,16},{96,32},{112,48},{1... | collective-permute-start | bytes 417800 | tf_op jit(solution)/shard_map/ppermute | solution.py:32
  29.6 1.9 %collective-permute-start.1 = (f32[2,136,128]{2,1,0:T(8,128)}, f32[2,136,128]{2,1,0:T(8,128)}, u32[]{:S(2)}, u32[]{:S(2)}) collective-permute-start(f32[2,136,128]{2,1,0:T(8,128)} %pad_maximum_fusion.1), channel_id=1, source_target_pairs={{0,32},{16,112},{32,64},{48,16},{64,96},{80,48},{96,0},{112,80},{1... | collective-permute-start | bytes 417800 | tf_op jit(solution)/shard_map/ppermute | solution.py:32
  31.6 0.0 collective-permute-done.3
  31.6 2.1 %collective-permute-done.2 = f32[2,136,128]{2,1,0:T(8,128)} collective-permute-done((f32[2,136,128]{2,1,0:T(8,128)}, f32[2,136,128]{2,1,0:T(8,128)}, u32[]{:S(2)}, u32[]{:S(2)}) %collective-permute-start.2) | collective-permute-done | bytes 139296 | tf_op jit(solution)/shard_map/ppermute | solution.py:32
  33.7 3.1 %collective-permute-done.1 = f32[2,136,128]{2,1,0:T(8,128)} collective-permute-done((f32[2,136,128]{2,1,0:T(8,128)}, f32[2,136,128]{2,1,0:T(8,128)}, u32[]{:S(2)}, u32[]{:S(2)}) %collective-permute-start.1) | collective-permute-done | bytes 139296 | tf_op jit(solution)/shard_map/ppermute | solution.py:32
  36.9 1.4 fusion.43
  38.2 0.0 copy-start.6
  38.2 0.0 copy-start.7
  38.2 1.2 multiply_add_fusion.1
  39.4 0.0 copy-done.6
  39.4 0.0 copy-done.7
  39.4 0.1 broadcast_in_dim.27
  39.5 1.9 %collective-permute-start.5 = (f32[2,136,128]{2,1,0:T(8,128)S(1)}, f32[2,136,128]{2,1,0:T(8,128)}, u32[]{:S(2)}, u32[]{:S(2)}) collective-permute-start(f32[2,136,128]{2,1,0:T(8,128)S(1)} %pad_maximum_fusion.2), channel_id=1, source_target_pairs={{0,256},{16,272},{32,288},{48,304},{64,320},{80,336},{96,352},{112... | collective-permute-start | bytes 417800 | tf_op jit(solution)/shard_map/ppermute | solution.py:32
  41.4 1.9 %collective-permute-start.4 = (f32[2,136,128]{2,1,0:T(8,128)S(1)}, f32[2,136,128]{2,1,0:T(8,128)}, u32[]{:S(2)}, u32[]{:S(2)}) collective-permute-start(f32[2,136,128]{2,1,0:T(8,128)S(1)} %pad_maximum_fusion.2), channel_id=1, source_target_pairs={{0,128},{16,400},{32,160},{48,432},{64,192},{80,464},{96,224},{112... | collective-permute-start | bytes 417800 | tf_op jit(solution)/shard_map/ppermute | solution.py:32
  43.4 5.1 %collective-permute-start.6 = (f32[2,136,128]{2,1,0:T(8,128)S(1)}, f32[2,136,128]{2,1,0:T(8,128)}, u32[]{:S(2)}, u32[]{:S(2)}) collective-permute-start(f32[2,136,128]{2,1,0:T(8,128)S(1)} %pad_maximum_fusion.2), channel_id=1, source_target_pairs={{0,384},{16,144},{32,416},{48,176},{64,448},{80,208},{96,480},{112... | collective-permute-start | bytes 417800 | tf_op jit(solution)/shard_map/ppermute | solution.py:32
  48.5 0.0 collective-permute-done.5
  48.5 2.3 %collective-permute-done.4 = f32[2,136,128]{2,1,0:T(8,128)} collective-permute-done((f32[2,136,128]{2,1,0:T(8,128)S(1)}, f32[2,136,128]{2,1,0:T(8,128)}, u32[]{:S(2)}, u32[]{:S(2)}) %collective-permute-start.4) | collective-permute-done | bytes 139296 | tf_op jit(solution)/shard_map/ppermute | solution.py:32
  50.9 0.8 fusion.42
  51.7 0.2 collective-permute-done.6
  51.9 2.0 %multiply_add_fusion = (bf16[2,128,128]{2,1,0:T(8,128)(2,1)}, bf16[2,128,128]{2,1,0:T(8,128)(2,1)S(1)}) fusion(f32[2,128,128]{2,1,0:T(8,128)} %get-tuple-element.23, f32[2]{0:T(128)} %copy-done.9, f32[2,136,128]{2,1,0:T(8,128)} %collective-permute-done.3, f32[2]{0:T(128)} %copy-done.7, f32[2,136,128]{2,1,0:T(8,128)} %collective-permute-done.2, ...), kind=kLoop, calls=%fused_computation.47 | loop fusion | flops 524288 | bytes 1048632 | tf_op jit(solution)/shard_map/add | solution.py:73
  53.9 2.0 %collective-permute-start.7 = (bf16[2,128,128]{2,1,0:T(8,128)(2,1)}, bf16[2,128,128]{2,1,0:T(8,128)(2,1)S(1)}, u32[]{:S(2)}, u32[]{:S(2)}) collective-permute-start(bf16[2,128,128]{2,1,0:T(8,128)(2,1)} %get-tuple-element.16), channel_id=1, source_target_pairs={{0,16},{16,0},{32,48},{48,32},{64,80},{80,64},{96,112},{112,96},{1... | collective-permute-start | bytes 196616 | tf_op jit(solution)/shard_map/ppermute | solution.py:72
  55.9 0.0 copy-done.1
  56.0 4.0 %fusion.3 = f32[768,2,128]{0,2,1:T(8,128)} fusion(s32[2,768]{1,0:T(2,128)S(1)} %get-tuple-element.21, bf16[768,2,128]{0,2,1:T(8,128)(2,1)S(1)} %bitcast.78, bf16[768,256]{1,0:T(8,128)(2,1)} %param.9, bf16[768,256]{1,0:T(8,128)(2,1)S(1)} %copy-done.1), kind=kOutput, calls=%fused_computation.3 | convolution fusion | flops 612237312 | bytes 1972224 | tf_op jit(solution)/shard_map/hts,shd->thd/dot_general | solution.py:92
  60.0 0.0 collective-permute-done.7
  60.0 1.4 fusion.7
  61.4 0.0 copy-done.4
  61.4 0.4 multiply_reduce_fusion
  61.8 1.5 multiply_convert_fusion.4
  63.3 0.0 all-gather.2.cloned.1.call-update
  63.4 89.8 %all-gather.2.cloned.1.call-done = bf16[768,4096]{0,1:T(8,128)(2,1)} async-done(((bf16[768,256]{0,1:T(8,128)(2,1)}), bf16[768,4096]{0,1:T(8,128)(2,1)}) %all-gather.2.cloned.1.call-update) | async-done | bytes 6291472 | tf_op jit(solution)/shard_map/all_gather | solution.py:127
  153.2 0.0 copy-done
  153.2 5.8 %fusion.8 = bf16[768,320]{0,1:T(8,128)(2,1)} fusion(bf16[4096,320]{0,1:T(8,128)(2,1)S(1)} %copy-done, bf16[768,4096]{0,1:T(8,128)(2,1)} %all-gather.2.cloned.1.call-done, bf16[768,320]{0,1:T(8,128)(2,1)} %param.13), kind=kOutput, calls=%fused_computation.11 | convolution fusion | flops 2014003200 | bytes 9895936 | tf_op jit(solution)/shard_map/dot_general | solution.py:126
  (6 shorter events, 0.1 us)
Async XLA Ops:
  6.5 146.6 %copy-start = (bf16[4096,320]{0,1:T(8,128)(2,1)S(1)}, bf16[4096,320]{0,1:T(8,128)(2,1)}, u32[]{:S(2)}) copy-start(bf16[4096,320]{0,1:T(8,128)(2,1)} %param.12) | copy-start | bytes 7864324
  6.5 49.4 %copy-start.1 = (bf16[768,256]{1,0:T(8,128)(2,1)S(1)}, bf16[768,256]{1,0:T(8,128)(2,1)}, u32[]{:S(2)}) copy-start(bf16[768,256]{1,0:T(8,128)(2,1)} %param.7) | copy-start | bytes 1179652
  6.5 146.6 %all-gather.2.cloned.1.call-start = ((), (), s32[]{:S(2)}) async-start(), calls=%async_computation | async-start | bytes 6684672 | tf_op jit(solution)/shard_map/all_gather | solution.py:127
  9.3 6.0 %copy-start.9 = (f32[2]{0:T(128)}, f32[2]{0:T(128)S(1)}, u32[]{:S(2)}) copy-start(f32[2]{0:T(128)S(1)} %multiply_exponential_fusion.1) | copy-start | bytes 28
  9.3 5.9 %copy-start.3 = (f32[768,2]{0,1:T(2,128)}, f32[768,2]{0,1:T(2,128)S(1)}, u32[]{:S(2)}) copy-start(f32[768,2]{0,1:T(2,128)S(1)} %get-tuple-element.19) | copy-start | bytes 18436
  11.9 3.3 %collective-permute-start = (f32[2,136,128]{2,1,0:T(8,128)S(1)}, f32[2,136,128]{2,1,0:T(8,128)S(1)}, u32[]{:S(2)}, u32[]{:S(2)}) collective-permute-start(f32[2,136,128]{2,1,0:T(8,128)S(1)} %pad_maximum_fusion), channel_id=1, source_target_pairs={{0,16},{16,0},{32,48},{48,32},{64,80},{80,64},{96,112},{112,96},{1... | collective-permute-start | bytes 417800 | tf_op jit(solution)/shard_map/ppermute | solution.py:46
  13.9 1.3 copy-start.5
  15.1 0.7 copy-start.2
  15.3 3.2 %copy-start.8 = (f32[2]{0:T(128)}, f32[2]{0:T(128)S(1)}, u32[]{:S(2)}) copy-start(f32[2]{0:T(128)S(1)} %get-tuple-element.14) | copy-start | bytes 28
  18.5 13.1 %collective-permute-start.3 = (f32[2,136,128]{2,1,0:T(8,128)}, f32[2,136,128]{2,1,0:T(8,128)}, u32[]{:S(2)}, u32[]{:S(2)}) collective-permute-start(f32[2,136,128]{2,1,0:T(8,128)} %pad_maximum_fusion.1), channel_id=1, source_target_pairs={{0,96},{16,48},{32,0},{48,80},{64,32},{80,112},{96,64},{112,16},{1... | collective-permute-start | bytes 417800 | tf_op jit(solution)/shard_map/ppermute | solution.py:32
  21.2 12.5 %collective-permute-start.2 = (f32[2,136,128]{2,1,0:T(8,128)}, f32[2,136,128]{2,1,0:T(8,128)}, u32[]{:S(2)}, u32[]{:S(2)}) collective-permute-start(f32[2,136,128]{2,1,0:T(8,128)} %pad_maximum_fusion.1), channel_id=1, source_target_pairs={{0,64},{16,80},{32,96},{48,112},{64,0},{80,16},{96,32},{112,48},{1... | collective-permute-start | bytes 417800 | tf_op jit(solution)/shard_map/ppermute | solution.py:32
  29.6 7.3 %collective-permute-start.1 = (f32[2,136,128]{2,1,0:T(8,128)}, f32[2,136,128]{2,1,0:T(8,128)}, u32[]{:S(2)}, u32[]{:S(2)}) collective-permute-start(f32[2,136,128]{2,1,0:T(8,128)} %pad_maximum_fusion.1), channel_id=1, source_target_pairs={{0,32},{16,112},{32,64},{48,16},{64,96},{80,48},{96,0},{112,80},{1... | collective-permute-start | bytes 417800 | tf_op jit(solution)/shard_map/ppermute | solution.py:32
  38.2 1.2 copy-start.6
  38.2 1.2 copy-start.7
  39.5 9.0 %collective-permute-start.5 = (f32[2,136,128]{2,1,0:T(8,128)S(1)}, f32[2,136,128]{2,1,0:T(8,128)}, u32[]{:S(2)}, u32[]{:S(2)}) collective-permute-start(f32[2,136,128]{2,1,0:T(8,128)S(1)} %pad_maximum_fusion.2), channel_id=1, source_target_pairs={{0,256},{16,272},{32,288},{48,304},{64,320},{80,336},{96,352},{112... | collective-permute-start | bytes 417800 | tf_op jit(solution)/shard_map/ppermute | solution.py:32
  41.4 9.4 %collective-permute-start.4 = (f32[2,136,128]{2,1,0:T(8,128)S(1)}, f32[2,136,128]{2,1,0:T(8,128)}, u32[]{:S(2)}, u32[]{:S(2)}) collective-permute-start(f32[2,136,128]{2,1,0:T(8,128)S(1)} %pad_maximum_fusion.2), channel_id=1, source_target_pairs={{0,128},{16,400},{32,160},{48,432},{64,192},{80,464},{96,224},{112... | collective-permute-start | bytes 417800 | tf_op jit(solution)/shard_map/ppermute | solution.py:32
  43.4 8.5 %collective-permute-start.6 = (f32[2,136,128]{2,1,0:T(8,128)S(1)}, f32[2,136,128]{2,1,0:T(8,128)}, u32[]{:S(2)}, u32[]{:S(2)}) collective-permute-start(f32[2,136,128]{2,1,0:T(8,128)S(1)} %pad_maximum_fusion.2), channel_id=1, source_target_pairs={{0,384},{16,144},{32,416},{48,176},{64,448},{80,208},{96,480},{112... | collective-permute-start | bytes 417800 | tf_op jit(solution)/shard_map/ppermute | solution.py:32
  53.9 7.5 %copy-start.4 = (f32[768,2]{0,1:T(2,128)S(1)}, f32[768,2]{0,1:T(2,128)}, u32[]{:S(2)}) copy-start(f32[768,2]{0,1:T(2,128)} %copy-done.3) | copy-start | bytes 18436
  53.9 6.1 %collective-permute-start.7 = (bf16[2,128,128]{2,1,0:T(8,128)(2,1)}, bf16[2,128,128]{2,1,0:T(8,128)(2,1)S(1)}, u32[]{:S(2)}, u32[]{:S(2)}) collective-permute-start(bf16[2,128,128]{2,1,0:T(8,128)(2,1)} %get-tuple-element.16), channel_id=1, source_target_pairs={{0,16},{16,0},{32,48},{48,32},{64,80},{80,64},{96,112},{112,96},{1... | collective-permute-start | bytes 196616 | tf_op jit(solution)/shard_map/ppermute | solution.py:72
Sparse Core Ops, SparseCore 0:
  63.5 89.6 all-gather.1

commit v10 on v9

--- a/solution.py
+++ b/solution.py
@@ -17,11 +17,7 @@
     )
 
 
-def unpack(packed):
-    return packed[:, :HD], packed[:, HD, 0]
-
-
-def gather_line(total_s, total_p, line, stride, seq_count):
+def gather_line(packed, line, stride, seq_count):
     got = []
     for shift in range(1, line):
         pairs = []
@@ -29,7 +25,7 @@
             at = (i // stride) % line
             step = -shift if i % 2 else shift
             pairs.append((i, i + (((at + step) % line) - at) * stride))
-        got.append(unpack(lax.ppermute(pack(total_s, total_p), "seq", pairs)))
+        got.append(lax.ppermute(packed, "seq", pairs))
     return got
 
 
@@ -42,33 +38,33 @@
     y = me // (2 * line)
     pos_x = jnp.where(second, line - 1 - x, x)
     pos_y = jnp.where(second, line - 1 - y, y)
-    got_s, got_p = unpack(
-        lax.ppermute(pack(other, decay), "seq", [(i, i ^ 1) for i in range(seq_count)])
-    )
-    chip_s = got_p[:, None, None] * mine + got_s
-    chip_p = decay * got_p
+    is_s = lax.broadcasted_iota(jnp.int32, (1, HD + 8, 1), 1) < HD
+
+    def decay_of(packed):
+        return packed[:, HD : HD + 1, 0:1]
+
+    own = pack(mine, decay)
+    got = lax.ppermute(pack(other, decay), "seq", [(i, i ^ 1) for i in range(seq_count)])
+    chip = decay_of(got) * own + jnp.where(is_s, got, 0.0)
 
     def prefix(got, pos):
-        acc_s = jnp.zeros_like(chip_s)
-        acc_p = jnp.ones_like(chip_p)
-        for m, (s, p) in enumerate(got, start=1):
-            valid = pos >= m
-            acc_s = acc_s + jnp.where(valid, acc_p, 0.0)[:, None, None] * s
-            acc_p = jnp.where(valid, acc_p * p, acc_p)
-        return acc_s, acc_p
+        acc = jnp.where(is_s, 0.0, 1.0) * jnp.ones_like(chip)
+        for m, part in enumerate(got, start=1):
+            acc = jnp.where(pos >= m, decay_of(acc) * part + jnp.where(is_s, acc, 0.0), acc)
+        return acc
 
-    row = gather_line(chip_s, chip_p, line, 2, seq_count)
-    row_prefix_s, row_prefix_p = prefix(row, pos_x)
-    row_s = chip_p[:, None, None] * row_prefix_s + chip_s
-    row_p = chip_p
+    row = gather_line(chip, line, 2, seq_count)
+    row_prefix = prefix(row, pos_x)
+    total = jnp.where(is_s, decay_of(chip) * row_prefix + chip, chip)
     for m in range(1, line):
-        s, p = row[line - 1 - m]
+        part = row[line - 1 - m]
         valid = pos_x <= line - 1 - m
-        row_s = jnp.where(valid, p, 1.0)[:, None, None] * row_s + jnp.where(valid, 1.0, 0.0) * s
-        row_p = row_p * p
-    col = gather_line(row_s, row_p, line, 2 * line, seq_count)
-    col_prefix_s, _ = prefix(col, pos_y)
-    state = row_prefix_p[:, None, None] * col_prefix_s + row_prefix_s
+        total = jnp.where(
+            is_s, jnp.where(valid, decay_of(part) * total + part, total), total * decay_of(part)
+        )
+    col = gather_line(total, line, 2 * line, seq_count)
+    col_prefix = prefix(col, pos_y)
+    state = (decay_of(row_prefix) * col_prefix + row_prefix)[:, :HD]
     handed = lax.ppermute(
         decay[:, None, None] * state + mine, "seq", [(i, i ^ 1) for i in range(seq_count)]
     )

time: 167 us -> 162 us (0.970)
  other arithmetic: 9.37 us -> 4.24 us
    ppermute x6, waiting for transfers between devices: 7.76 us -> 11.9 us  [gather_line(): got.append(lax.ppermute(packed, 'seq', pairs))]
    all_gather x1, waiting for transfers between devices: 89.8 us -> 87.2 us  [local(): lax.all_gather(normed, 'tp', axis=1, tiled=True)]
  transfers between devices with their start and end apart: 9 -> 9, of which waited for: 6 -> 4; matrix products, arithmetic and copies ran while one was open for 3% -> 4% of each run, Pallas kernels for 0% -> 0%
where the time goes in v10:
time: 162 us; the launch traced here: 161 us
  waiting for transfers between devices  99.2 us (61%)
  starting transfers between devices  25.9 us (16%)
  matrix products  14.4 us (9%)
  between operations  13.7 us (8%)
  other arithmetic  4.24 us (3%)
  local copies, waits for them, and re-layouts  4.02 us (2%)
    all_gather x1, waiting for transfers between devices, local(): lax.all_gather(normed, 'tp', axis=1, tiled=True)  87.2 us
    ppermute x6, starting transfers between devices, gather_line(): got.append(lax.ppermute(packed, 'seq', pairs))  22 us
    ppermute x6, waiting for transfers between devices, gather_line(): got.append(lax.ppermute(packed, 'seq', pairs))  11.9 us
    dot_general x1, matrix products, local(): jnp.dot(lax.all_gather(normed, 'tp', axis=1, tiled=True), out_weight, pre...  5.82 us
    dot_general x1, matrix products, local(): jnp.einsum('hts,shd->thd', local_weights, value_heads, preferred_element_...  4.12 us
  transfers between devices with their start and end apart: 9, of which 4 were waited for; matrix products, arithmetic and copies ran while one was open for 4% of the time, Pallas kernels for 0%

profile of v10, /device:TPU:6, one launch (start us, length us, event | category | flops | bytes accessed | tf_op | source)
XLA Modules:
  0.0 161.4 jit_solution(11644948795616650554)
XLA Ops:
  6.5 0.0 copy-start
  6.5 0.0 copy-start.1
  6.5 0.0 all-gather.2.cloned.1.call-start
  6.5 0.9 reshape.87
  7.4 0.6 reduce-window.6
  8.0 0.2 slice_reduce_fusion
  8.2 0.2 reduce-window.9
  8.4 0.1 add_bitcast_fusion
  8.5 0.2 slice_reduce_fusion.11
  8.7 0.1 broadcast_select_fusion.1
  8.7 1.2 copy.37
  9.9 0.0 copy-start.3
  9.9 1.4 fusion.13
  11.3 0.1 broadcast_in_dim.105
  11.4 1.9 %collective-permute-start = (f32[2,136,128]{2,1,0:T(8,128)S(1)}, f32[2,136,128]{2,1,0:T(8,128)S(1)}, u32[]{:S(2)}, u32[]{:S(2)}) collective-permute-start(f32[2,136,128]{2,1,0:T(8,128)S(1)} %pad_maximum_fusion.1), channel_id=1, source_target_pairs={{0,16},{16,0},{32,48},{48,32},{64,80},{80,64},{96,112},{112,96},{1... | collective-permute-start | bytes 417800 | tf_op jit(solution)/shard_map/ppermute | solution.py:47
  13.4 1.3 fusion.11
  14.6 0.0 copy-start.2
  14.7 0.0 collective-permute-done
  14.7 0.0 copy-done.3
  14.7 0.1 slice_reduce_fusion.10
  14.8 0.5 copy-done.2
  15.3 0.1 fusion.34
  15.4 7.8 %collective-permute-start.1 = (f32[2,136,128]{2,1,0:T(8,128)S(1)}, f32[2,136,128]{2,1,0:T(8,128)S(1)}, u32[]{:S(2)}, u32[]{:S(2)}) collective-permute-start(f32[2,136,128]{2,1,0:T(8,128)S(1)} %fusion.34), channel_id=1, source_target_pairs={{0,32},{16,112},{32,64},{48,16},{64,96},{80,48},{96,0},{112,80},{1... | collective-permute-start | bytes 417800 | tf_op jit(solution)/shard_map/ppermute | solution.py:28
  23.2 1.9 %collective-permute-start.3 = (f32[2,136,128]{2,1,0:T(8,128)S(1)}, f32[2,136,128]{2,1,0:T(8,128)S(1)}, u32[]{:S(2)}, u32[]{:S(2)}) collective-permute-start(f32[2,136,128]{2,1,0:T(8,128)S(1)} %fusion.34), channel_id=1, source_target_pairs={{0,96},{16,48},{32,0},{48,80},{64,32},{80,112},{96,64},{112,16},{1... | collective-permute-start | bytes 417800 | tf_op jit(solution)/shard_map/ppermute | solution.py:28
  25.2 3.4 %collective-permute-start.2 = (f32[2,136,128]{2,1,0:T(8,128)S(1)}, f32[2,136,128]{2,1,0:T(8,128)S(1)}, u32[]{:S(2)}, u32[]{:S(2)}) collective-permute-start(f32[2,136,128]{2,1,0:T(8,128)S(1)} %fusion.34), channel_id=1, source_target_pairs={{0,64},{16,80},{32,96},{48,112},{64,0},{80,16},{96,32},{112,48},{1... | collective-permute-start | bytes 417800 | tf_op jit(solution)/shard_map/ppermute | solution.py:28
  28.5 0.1 slice_reduce_fusion.3
  28.6 0.0 collective-permute-done.1
  28.6 0.1 fusion.31
  28.7 0.1 slice_reduce_fusion.9
  28.9 5.5 %collective-permute-done.2 = f32[2,136,128]{2,1,0:T(8,128)S(1)} collective-permute-done((f32[2,136,128]{2,1,0:T(8,128)S(1)}, f32[2,136,128]{2,1,0:T(8,128)S(1)}, u32[]{:S(2)}, u32[]{:S(2)}) %collective-permute-start.2) | collective-permute-done | bytes 139296 | tf_op jit(solution)/shard_map/ppermute | solution.py:28
  34.4 0.1 add_select_fusion.3
  34.5 0.1 slice_reduce_fusion.8
  34.6 0.1 slice_reduce_fusion.5
  34.7 0.1 slice_reduce_fusion.6
  34.8 0.0 collective-permute-done.3
  34.8 0.1 slice_reduce_fusion.4
  34.9 0.8 select_select_fusion
  35.7 1.9 %collective-permute-start.4 = (f32[2,136,128]{2,1,0:T(8,128)}, f32[2,136,128]{2,1,0:T(8,128)S(1)}, u32[]{:S(2)}, u32[]{:S(2)}) collective-permute-start(f32[2,136,128]{2,1,0:T(8,128)} %get-tuple-element.7), channel_id=1, source_target_pairs={{0,128},{16,400},{32,160},{48,432},{64,192},{80,464},{96,224},{112... | collective-permute-start | bytes 417800 | tf_op jit(solution)/shard_map/ppermute | solution.py:28
  37.7 5.1 %collective-permute-start.6 = (f32[2,136,128]{2,1,0:T(8,128)}, f32[2,136,128]{2,1,0:T(8,128)S(1)}, u32[]{:S(2)}, u32[]{:S(2)}) collective-permute-start(f32[2,136,128]{2,1,0:T(8,128)} %get-tuple-element.7), channel_id=1, source_target_pairs={{0,384},{16,144},{32,416},{48,176},{64,448},{80,208},{96,480},{112... | collective-permute-start | bytes 417800 | tf_op jit(solution)/shard_map/ppermute | solution.py:28
  42.8 1.9 %collective-permute-start.5 = (f32[2,136,128]{2,1,0:T(8,128)}, f32[2,136,128]{2,1,0:T(8,128)S(1)}, u32[]{:S(2)}, u32[]{:S(2)}) collective-permute-start(f32[2,136,128]{2,1,0:T(8,128)} %get-tuple-element.7), channel_id=1, source_target_pairs={{0,256},{16,272},{32,288},{48,304},{64,320},{80,336},{96,352},{112... | collective-permute-start | bytes 417800 | tf_op jit(solution)/shard_map/ppermute | solution.py:28
  44.7 0.1 slice_reduce_fusion.7
  44.8 0.3 collective-permute-done.4
  45.1 0.1 fusion.32
  45.2 0.1 slice_reduce_fusion.2
  45.3 6.1 %collective-permute-done.5 = f32[2,136,128]{2,1,0:T(8,128)S(1)} collective-permute-done((f32[2,136,128]{2,1,0:T(8,128)}, f32[2,136,128]{2,1,0:T(8,128)S(1)}, u32[]{:S(2)}, u32[]{:S(2)}) %collective-permute-start.5) | collective-permute-done | bytes 139296 | tf_op jit(solution)/shard_map/ppermute | solution.py:28
  51.5 0.1 add_select_fusion.1
  51.6 0.1 slice_reduce_fusion.1
  51.7 0.0 collective-permute-done.6
  51.7 1.0 multiply_add_fusion
  52.7 0.0 copy-start.4
  52.8 1.9 %collective-permute-start.7 = (bf16[2,128,128]{2,1,0:T(8,128)(2,1)S(1)}, bf16[2,128,128]{2,1,0:T(8,128)(2,1)S(1)}, u32[]{:S(2)}, u32[]{:S(2)}) collective-permute-start(bf16[2,128,128]{2,1,0:T(8,128)(2,1)S(1)} %get-tuple-element.5), channel_id=1, source_target_pairs={{0,16},{16,0},{32,48},{48,32},{64,80},{80,64},{96,112},{112,96},{1... | collective-permute-start | bytes 196616 | tf_op jit(solution)/shard_map/ppermute | solution.py:68
  54.7 0.0 copy-done.1
  54.7 4.1 %fusion.3 = f32[768,2,128]{0,2,1:T(8,128)} fusion(s32[2,768]{1,0:T(2,128)S(1)} %get-tuple-element.12, bf16[768,2,128]{0,2,1:T(8,128)(2,1)} %bitcast.81, bf16[768,256]{1,0:T(8,128)(2,1)S(1)} %copy-done.1, bf16[768,256]{1,0:T(8,128)(2,1)} %param.9), kind=kOutput, calls=%fused_computation.3 | convolution fusion | flops 612237312 | bytes 1972224 | tf_op jit(solution)/shard_map/hts,shd->thd/dot_general | solution.py:88
  58.8 0.0 collective-permute-done.7
  58.8 1.4 fusion.7
  60.3 0.3 multiply_reduce_fusion
  60.7 0.0 copy-done.4
  60.7 0.9 multiply_convert_fusion.4
  61.5 0.0 all-gather.2.cloned.1.call-update
  61.5 87.2 %all-gather.2.cloned.1.call-done = bf16[768,4096]{0,1:T(8,128)(2,1)} async-done(((bf16[768,256]{0,1:T(8,128)(2,1)}), bf16[768,4096]{0,1:T(8,128)(2,1)}) %all-gather.2.cloned.1.call-update) | async-done | bytes 6291472 | tf_op jit(solution)/shard_map/all_gather | solution.py:123
  148.7 0.0 copy-done
  148.7 5.8 %fusion.8 = bf16[768,320]{0,1:T(8,128)(2,1)} fusion(bf16[4096,320]{0,1:T(8,128)(2,1)S(1)} %copy-done, bf16[768,4096]{0,1:T(8,128)(2,1)} %all-gather.2.cloned.1.call-done, bf16[768,320]{0,1:T(8,128)(2,1)} %param.13), kind=kOutput, calls=%fused_computation.11 | convolution fusion | flops 2014003200 | bytes 9895936 | tf_op jit(solution)/shard_map/dot_general | solution.py:122
  (8 shorter events, 0.1 us)
Async XLA Ops:
  6.5 142.2 %copy-start = (bf16[4096,320]{0,1:T(8,128)(2,1)S(1)}, bf16[4096,320]{0,1:T(8,128)(2,1)}, u32[]{:S(2)}) copy-start(bf16[4096,320]{0,1:T(8,128)(2,1)} %param.12) | copy-start | bytes 7864324
  6.5 48.2 %copy-start.1 = (bf16[768,256]{1,0:T(8,128)(2,1)S(1)}, bf16[768,256]{1,0:T(8,128)(2,1)}, u32[]{:S(2)}) copy-start(bf16[768,256]{1,0:T(8,128)(2,1)} %param.7) | copy-start | bytes 1179652
  6.5 142.2 %all-gather.2.cloned.1.call-start = ((), (), s32[]{:S(2)}) async-start(), calls=%async_computation | async-start | bytes 6684672 | tf_op jit(solution)/shard_map/all_gather | solution.py:123
  9.9 4.8 %copy-start.3 = (bf16[768,256]{0,1:T(8,128)(2,1)}, bf16[768,256]{0,1:T(8,128)(2,1)S(1)}, u32[]{:S(2)}) copy-start(bf16[768,256]{0,1:T(8,128)(2,1)S(1)} %copy.37) | copy-start | bytes 1179652
  11.4 3.3 %collective-permute-start = (f32[2,136,128]{2,1,0:T(8,128)S(1)}, f32[2,136,128]{2,1,0:T(8,128)S(1)}, u32[]{:S(2)}, u32[]{:S(2)}) collective-permute-start(f32[2,136,128]{2,1,0:T(8,128)S(1)} %pad_maximum_fusion.1), channel_id=1, source_target_pairs={{0,16},{16,0},{32,48},{48,32},{64,80},{80,64},{96,112},{112,96},{1... | collective-permute-start | bytes 417800 | tf_op jit(solution)/shard_map/ppermute | solution.py:47
  14.6 0.7 copy-start.2
  15.4 13.2 %collective-permute-start.1 = (f32[2,136,128]{2,1,0:T(8,128)S(1)}, f32[2,136,128]{2,1,0:T(8,128)S(1)}, u32[]{:S(2)}, u32[]{:S(2)}) collective-permute-start(f32[2,136,128]{2,1,0:T(8,128)S(1)} %fusion.34), channel_id=1, source_target_pairs={{0,32},{16,112},{32,64},{48,16},{64,96},{80,48},{96,0},{112,80},{1... | collective-permute-start | bytes 417800 | tf_op jit(solution)/shard_map/ppermute | solution.py:28
  23.2 11.6 %collective-permute-start.3 = (f32[2,136,128]{2,1,0:T(8,128)S(1)}, f32[2,136,128]{2,1,0:T(8,128)S(1)}, u32[]{:S(2)}, u32[]{:S(2)}) collective-permute-start(f32[2,136,128]{2,1,0:T(8,128)S(1)} %fusion.34), channel_id=1, source_target_pairs={{0,96},{16,48},{32,0},{48,80},{64,32},{80,112},{96,64},{112,16},{1... | collective-permute-start | bytes 417800 | tf_op jit(solution)/shard_map/ppermute | solution.py:28
  25.2 9.2 %collective-permute-start.2 = (f32[2,136,128]{2,1,0:T(8,128)S(1)}, f32[2,136,128]{2,1,0:T(8,128)S(1)}, u32[]{:S(2)}, u32[]{:S(2)}) collective-permute-start(f32[2,136,128]{2,1,0:T(8,128)S(1)} %fusion.34), channel_id=1, source_target_pairs={{0,64},{16,80},{32,96},{48,112},{64,0},{80,16},{96,32},{112,48},{1... | collective-permute-start | bytes 417800 | tf_op jit(solution)/shard_map/ppermute | solution.py:28
  35.7 9.4 %collective-permute-start.4 = (f32[2,136,128]{2,1,0:T(8,128)}, f32[2,136,128]{2,1,0:T(8,128)S(1)}, u32[]{:S(2)}, u32[]{:S(2)}) collective-permute-start(f32[2,136,128]{2,1,0:T(8,128)} %get-tuple-element.7), channel_id=1, source_target_pairs={{0,128},{16,400},{32,160},{48,432},{64,192},{80,464},{96,224},{112... | collective-permute-start | bytes 417800 | tf_op jit(solution)/shard_map/ppermute | solution.py:28
  37.7 14.0 %collective-permute-start.6 = (f32[2,136,128]{2,1,0:T(8,128)}, f32[2,136,128]{2,1,0:T(8,128)S(1)}, u32[]{:S(2)}, u32[]{:S(2)}) collective-permute-start(f32[2,136,128]{2,1,0:T(8,128)} %get-tuple-element.7), channel_id=1, source_target_pairs={{0,384},{16,144},{32,416},{48,176},{64,448},{80,208},{96,480},{112... | collective-permute-start | bytes 417800 | tf_op jit(solution)/shard_map/ppermute | solution.py:28
  42.8 8.7 %collective-permute-start.5 = (f32[2,136,128]{2,1,0:T(8,128)}, f32[2,136,128]{2,1,0:T(8,128)S(1)}, u32[]{:S(2)}, u32[]{:S(2)}) collective-permute-start(f32[2,136,128]{2,1,0:T(8,128)} %get-tuple-element.7), channel_id=1, source_target_pairs={{0,256},{16,272},{32,288},{48,304},{64,320},{80,336},{96,352},{112... | collective-permute-start | bytes 417800 | tf_op jit(solution)/shard_map/ppermute | solution.py:28
  52.7 7.9 %copy-start.4 = (f32[256]{0:T(256)S(1)}, f32[256]{0:T(256)}, u32[]{:S(2)}) copy-start(f32[256]{0:T(256)} %param.11) | copy-start | bytes 3076
  52.8 6.1 %collective-permute-start.7 = (bf16[2,128,128]{2,1,0:T(8,128)(2,1)S(1)}, bf16[2,128,128]{2,1,0:T(8,128)(2,1)S(1)}, u32[]{:S(2)}, u32[]{:S(2)}) collective-permute-start(bf16[2,128,128]{2,1,0:T(8,128)(2,1)S(1)} %get-tuple-element.5), channel_id=1, source_target_pairs={{0,16},{16,0},{32,48},{48,32},{64,80},{80,64},{96,112},{112,96},{1... | collective-permute-start | bytes 196616 | tf_op jit(solution)/shard_map/ppermute | solution.py:68
Sparse Core Ops, SparseCore 0:
  61.7 87.0 all-gather.1

commit v11 on v10

--- a/solution.py
+++ b/solution.py
@@ -29,7 +29,7 @@
     return got
 
 
-def block_scan(decay, mine, other):
+def block_scan(decay, mine, other, extra_fn, extra_args):
     seq_count = lax.axis_size("seq")
     line = 4
     me = lax.axis_index("seq")
@@ -46,6 +46,8 @@
     own = pack(mine, decay)
     got = lax.ppermute(pack(other, decay), "seq", [(i, i ^ 1) for i in range(seq_count)])
     chip = decay_of(got) * own + jnp.where(is_s, got, 0.0)
+    chip, extra_args = lax.optimization_barrier((chip, extra_args))
+    extra = extra_fn(*extra_args)
 
     def prefix(got, pos):
         acc = jnp.where(is_s, 0.0, 1.0) * jnp.ones_like(chip)
@@ -54,6 +56,7 @@
         return acc
 
     row = gather_line(chip, line, 2, seq_count)
+    row, extra = lax.optimization_barrier((row, extra))
     row_prefix = prefix(row, pos_x)
     total = jnp.where(is_s, decay_of(chip) * row_prefix + chip, chip)
     for m in range(1, line):
@@ -68,9 +71,7 @@
     handed = lax.ppermute(
         decay[:, None, None] * state + mine, "seq", [(i, i ^ 1) for i in range(seq_count)]
     )
-    state_fwd = jnp.where(second, handed, state)
-    state_bwd = jnp.where(second, state, handed)
-    return state_fwd, state_bwd
+    return state, handed, extra
 
 
 def local(query_vectors, key_vectors, value_vectors, decay_exp, norm_gain, out_weight, residual):
@@ -82,12 +83,17 @@
     local_exp = jnp.cumsum(decay_exp, axis=1)
     block_exp = local_exp[:, -1]
     local_rows = local_exp.T
-    scores = jnp.einsum("thd,shd->hts", query_heads, key_heads, preferred_element_type=jnp.float32)
-    exp_gap = jnp.abs(local_exp[:, :, None] - local_exp[:, None, :])
-    local_weights = (scores * factor(exp_gap)).astype(jnp.bfloat16)
-    local_part = jnp.einsum(
-        "hts,shd->thd", local_weights, value_heads, preferred_element_type=jnp.float32
-    )
+
+    def local_attention(query_heads, key_heads, value_heads, local_exp):
+        scores = jnp.einsum(
+            "thd,shd->hts", query_heads, key_heads, preferred_element_type=jnp.float32
+        )
+        exp_gap = jnp.abs(local_exp[:, :, None] - local_exp[:, None, :])
+        local_weights = (scores * factor(exp_gap)).astype(jnp.bfloat16)
+        return jnp.einsum(
+            "hts,shd->thd", local_weights, value_heads, preferred_element_type=jnp.float32
+        )
+
     tail_factor = factor(block_exp[None, :] - local_rows)
     head_factor = factor(local_rows)
     second = (lax.axis_index("seq") % 2) == 1
@@ -102,17 +108,23 @@
         "shd,she->hde", keys_other, value_heads, preferred_element_type=jnp.float32
     )
     block_decay = factor(block_exp)
-    state_fwd, state_bwd = block_scan(block_decay, summary_mine, summary_other)
-    state_fwd = state_fwd.astype(jnp.bfloat16)
-    state_bwd = state_bwd.astype(jnp.bfloat16)
-    remote_fwd = (
-        jnp.einsum("thd,hde->the", query_heads, state_fwd, preferred_element_type=jnp.float32)
-        * head_factor[:, :, None]
+    state_own, state_handed, local_part = block_scan(
+        block_decay,
+        summary_mine,
+        summary_other,
+        local_attention,
+        (query_heads, key_heads, value_heads, local_exp),
     )
-    remote_bwd = (
-        jnp.einsum("thd,hde->the", query_heads, state_bwd, preferred_element_type=jnp.float32)
-        * tail_factor[:, :, None]
+    remote_own = jnp.einsum(
+        "thd,hde->the", query_heads, state_own.astype(jnp.bfloat16),
+        preferred_element_type=jnp.float32,
     )
+    remote_handed = jnp.einsum(
+        "thd,hde->the", query_heads, state_handed.astype(jnp.bfloat16),
+        preferred_element_type=jnp.float32,
+    )
+    remote_fwd = jnp.where(second, remote_handed, remote_own) * head_factor[:, :, None]
+    remote_bwd = jnp.where(second, remote_own, remote_handed) * tail_factor[:, :, None]
     attention = local_part + remote_fwd + remote_bwd
     scale = lax.rsqrt(jnp.mean(attention * attention, axis=-1, keepdims=True) + 1e-06)
     normed = (attention * scale * norm_gain.reshape(head_count, HD)[None, :, :]).astype(

time: 162 us -> 169 us (1.043)
  other arithmetic: 4.24 us -> 12 us
  waiting for transfers between devices: 99.2 us -> 93.1 us
  local copies, waits for them, and re-layouts: 4.02 us -> 9.09 us
    ppermute x6, waiting for transfers between devices: 11.9 us -> 5.82 us  [gather_line(): got.append(lax.ppermute(packed, 'seq', pairs))]
    select_n x4, other arithmetic: 0.45 us -> 3.28 us  [prefix(): jnp.where(pos >= m, decay_of(acc) * part + jnp.where(is_s, acc, 0.0), acc)]
    reshape x1 -> x3, local copies, waits for them, and re-layouts: 0.85 us -> 3.53 us  [the longest x1 1.84 us: local(): value_heads = value_vectors.reshape(tok_rows, head_count, HD)]
    slice x11 -> x9, local copies, waits for them, and re-layouts: 1.01 us -> 2.93 us  [decay_of(): return packed[:, HD:HD + 1, 0:1]]
  transfers between devices with their start and end apart: 9 -> 9, of which waited for: 4 -> 4; matrix products, arithmetic and copies ran while one was open for 4% -> 7% of each run, Pallas kernels for 0% -> 0%
where the time goes in v11:
time: 169 us
  waiting for transfers between devices  93.1 us (55%)
  starting transfers between devices  25.8 us (15%)
  matrix products  14.8 us (9%)
  between operations  13.6 us (8%)
  other arithmetic  12 us (7%)
  local copies, waits for them, and re-layouts  9.09 us (5%)
    all_gather x1, waiting for transfers between devices, local(): lax.all_gather(normed, 'tp', axis=1, tiled=True)  86 us
    ppermute x6, starting transfers between devices, gather_line(): got.append(lax.ppermute(packed, 'seq', pairs))  22 us
    ppermute x6, waiting for transfers between devices, gather_line(): got.append(lax.ppermute(packed, 'seq', pairs))  5.82 us
    dot_general x1, matrix products, local(): jnp.dot(lax.all_gather(normed, 'tp', axis=1, tiled=True), out_weight, pre...  5.81 us
    dot_general x1, matrix products, local_attention(): jnp.einsum('hts,shd->thd', local_weights, value_heads, preferred_element_...  4.39 us
  transfers between devices with their start and end apart: 9, of which 4 were waited for; matrix products, arithmetic and copies ran while one was open for 7% of the time, Pallas kernels for 0%

profile of v11, /device:TPU:6, one launch (start us, length us, event | category | flops | bytes accessed | tf_op | source)
XLA Modules:
  0.0 168.5 jit_solution(14294542355955168979)
XLA Ops:
  6.5 0.0 copy-start
  6.5 0.0 all-gather.2.cloned.1.call-start
  6.5 0.9 reshape.64
  7.4 0.6 reduce-window.6
  8.0 0.2 slice_reduce_fusion
  8.2 0.2 reduce-window.9
  8.4 0.1 add_bitcast_fusion
  8.4 0.6 exponential_bitcast_fusion.1
  9.1 0.2 slice_reduce_fusion.7
  9.3 0.1 broadcast_select_fusion.1
  9.3 0.0 copy-start.3
  9.3 1.1 reshape.63
  10.4 1.0 copy.25
  11.5 1.4 fusion.11
  12.9 0.1 broadcast_in_dim.103
  13.0 0.7 pad_maximum_fusion.1
  13.6 1.9 %collective-permute-start = (f32[2,136,128]{2,1,0:T(8,128)}, f32[2,136,128]{2,1,0:T(8,128)}, u32[]{:S(2)}, u32[]{:S(2)}) collective-permute-start(f32[2,136,128]{2,1,0:T(8,128)} %pad_maximum_fusion.1), channel_id=1, source_target_pairs={{0,16},{16,0},{32,48},{48,32},{64,80},{80,64},{96,112},{112,96},{1... | collective-permute-start | bytes 417800 | tf_op jit(solution)/shard_map/ppermute | solution.py:47
  15.5 0.0 copy-done.4
  15.5 0.0 copy-done.3
  15.6 1.4 fusion.9
  17.0 0.0 copy-start.2
  17.0 0.5 iota_compare_fusion
  17.5 1.8 %reshape.66 = bf16[768,2,128]{2,1,0:T(2,128)(2,1)} reshape(bf16[768,256]{1,0:T(8,128)(2,1)} %param.9) | data formatting | bytes 786432 | tf_op jit(solution)/shard_map/reshape | solution.py:82
  19.4 0.0 copy-done.1
  19.4 0.8 reshape.67
  20.2 0.5 broadcast_select_fusion.2
  20.7 0.0 collective-permute-done
  20.7 0.8 slice_reduce_fusion.6
  21.5 1.7 fusion.33
  23.2 2.7 %collective-permute-start.3 = (f32[2,136,128]{2,1,0:T(8,128)}, f32[2,136,128]{2,1,0:T(8,128)}, u32[]{:S(2)}, u32[]{:S(2)}) collective-permute-start(f32[2,136,128]{2,1,0:T(8,128)} %fusion.33), channel_id=1, source_target_pairs={{0,96},{16,48},{32,0},{48,80},{64,32},{80,112},{96,64},{112,16},{1... | collective-permute-start | bytes 417800 | tf_op jit(solution)/shard_map/ppermute | solution.py:28
  25.9 0.0 copy-done.2
  25.9 8.4 %collective-permute-start.2 = (f32[2,136,128]{2,1,0:T(8,128)}, f32[2,136,128]{2,1,0:T(8,128)}, u32[]{:S(2)}, u32[]{:S(2)}) collective-permute-start(f32[2,136,128]{2,1,0:T(8,128)} %fusion.33), channel_id=1, source_target_pairs={{0,64},{16,80},{32,96},{48,112},{64,0},{80,16},{96,32},{112,48},{1... | collective-permute-start | bytes 417800 | tf_op jit(solution)/shard_map/ppermute | solution.py:28
  34.4 1.9 %collective-permute-start.1 = (f32[2,136,128]{2,1,0:T(8,128)}, f32[2,136,128]{2,1,0:T(8,128)S(1)}, u32[]{:S(2)}, u32[]{:S(2)}) collective-permute-start(f32[2,136,128]{2,1,0:T(8,128)} %fusion.33), channel_id=1, source_target_pairs={{0,32},{16,112},{32,64},{48,16},{64,96},{80,48},{96,0},{112,80},{1... | collective-permute-start | bytes 417800 | tf_op jit(solution)/shard_map/ppermute | solution.py:28
  36.3 4.4 %fusion.3 = f32[768,2,128]{0,2,1:T(8,128)} fusion(s32[2,768]{1,0:T(2,128)S(1)} %get-tuple-element.18, bf16[768,2,128]{2,1,0:T(2,128)(2,1)} %reshape.66, bf16[768,2,128]{2,1,0:T(2,128)(2,1)S(1)} %reshape.63, bf16[768,2,128]{2,1,0:T(2,128)(2,1)} %reshape.67), kind=kOutput, calls=%fused_computation.3 | convolution fusion | flops 612237312 | bytes 1972224 | tf_op jit(solution)/shard_map/hts,shd->thd/dot_general | solution.py:93
  40.7 0.8 slice_reduce_fusion.8
  41.5 0.0 collective-permute-done.3
  41.5 0.0 collective-permute-done.2
  41.5 0.0 collective-permute-done.1
  41.5 0.7 fusion.30
  42.3 0.1 slice_reduce_fusion.5
  42.4 0.8 slice_reduce_fusion.9
  43.2 1.0 add_select_fusion.3
  44.2 0.1 slice_reduce_fusion.4
  44.3 1.9 %select_select_fusion = (f32[2,136,128]{2,1,0:T(8,128)}, f32[2,136,128]{2,1,0:T(8,128)S(1)}) fusion(f32[2,136,128]{2,1,0:T(8,128)S(1)} %collective-permute-done.1, f32[2,136,128]{2,1,0:T(8,128)} %collective-permute-done.2, f32[2,136,128]{2,1,0:T(8,128)} %collective-permute-done.3, f32[2,136,128]{2,1,0:T(8,128)} %fusion.33, f32[2]{0:T(128)S(1)} %slice_reduce_fusion.8, ...), kind=kLoop, calls=%fused_computation.43 | loop fusion | flops 661504 | bytes 975028 | tf_op jit(solution)/shard_map/jit(_where)/select_n | solution.py:65
  46.2 1.9 %collective-permute-start.4 = (f32[2,136,128]{2,1,0:T(8,128)}, f32[2,136,128]{2,1,0:T(8,128)S(1)}, u32[]{:S(2)}, u32[]{:S(2)}) collective-permute-start(f32[2,136,128]{2,1,0:T(8,128)} %get-tuple-element.29), channel_id=1, source_target_pairs={{0,128},{16,400},{32,160},{48,432},{64,192},{80,464},{96,224},{112... | collective-permute-start | bytes 417800 | tf_op jit(solution)/shard_map/ppermute | solution.py:28
  48.1 5.1 %collective-permute-start.6 = (f32[2,136,128]{2,1,0:T(8,128)}, f32[2,136,128]{2,1,0:T(8,128)S(1)}, u32[]{:S(2)}, u32[]{:S(2)}) collective-permute-start(f32[2,136,128]{2,1,0:T(8,128)} %get-tuple-element.29), channel_id=1, source_target_pairs={{0,384},{16,144},{32,416},{48,176},{64,448},{80,208},{96,480},{112... | collective-permute-start | bytes 417800 | tf_op jit(solution)/shard_map/ppermute | solution.py:28
  53.3 1.9 %collective-permute-start.5 = (f32[2,136,128]{2,1,0:T(8,128)}, f32[2,136,128]{2,1,0:T(8,128)S(1)}, u32[]{:S(2)}, u32[]{:S(2)}) collective-permute-start(f32[2,136,128]{2,1,0:T(8,128)} %get-tuple-element.29), channel_id=1, source_target_pairs={{0,256},{16,272},{32,288},{48,304},{64,320},{80,336},{96,352},{112... | collective-permute-start | bytes 417800 | tf_op jit(solution)/shard_map/ppermute | solution.py:28
  55.2 0.1 slice_reduce_fusion.3
  55.3 0.4 collective-permute-done.4
  55.7 0.7 fusion.31
  56.5 0.1 slice_reduce_fusion.2
  56.6 5.3 %collective-permute-done.5 = f32[2,136,128]{2,1,0:T(8,128)S(1)} collective-permute-done((f32[2,136,128]{2,1,0:T(8,128)}, f32[2,136,128]{2,1,0:T(8,128)S(1)}, u32[]{:S(2)}, u32[]{:S(2)}) %collective-permute-start.5) | collective-permute-done | bytes 139296 | tf_op jit(solution)/shard_map/ppermute | solution.py:28
  61.9 0.8 add_select_fusion.1
  62.7 0.1 slice_reduce_fusion.1
  62.8 0.0 collective-permute-done.6
  62.8 1.0 multiply_add_fusion
  63.9 1.9 %collective-permute-start.7 = (bf16[2,128,128]{2,1,0:T(8,128)(2,1)S(1)}, bf16[2,128,128]{2,1,0:T(8,128)(2,1)S(1)}, u32[]{:S(2)}, u32[]{:S(2)}) collective-permute-start(bf16[2,128,128]{2,1,0:T(8,128)(2,1)S(1)} %get-tuple-element.27), channel_id=1, source_target_pairs={{0,16},{16,0},{32,48},{48,32},{64,80},{80,64},{96,112},{112,96},{1... | collective-permute-start | bytes 196616 | tf_op jit(solution)/shard_map/ppermute | solution.py:71
  65.8 1.2 collective-permute-done.7
  67.0 0.3 fusion.15
  67.3 1.6 multiply_reduce_fusion
  68.9 0.9 multiply_convert_fusion.4
  69.8 0.0 all-gather.2.cloned.1.call-update
  69.8 86.0 %all-gather.2.cloned.1.call-done = bf16[768,4096]{0,1:T(8,128)(2,1)} async-done(((bf16[768,256]{0,1:T(8,128)(2,1)}), bf16[768,4096]{0,1:T(8,128)(2,1)}) %all-gather.2.cloned.1.call-update) | async-done | bytes 6291472 | tf_op jit(solution)/shard_map/all_gather | solution.py:135
  155.8 5.8 %fusion.4 = bf16[768,320]{0,1:T(8,128)(2,1)} fusion(bf16[4096,320]{0,1:T(8,128)(2,1)S(1)} %copy-done, bf16[768,4096]{0,1:T(8,128)(2,1)} %all-gather.2.cloned.1.call-done, bf16[768,320]{0,1:T(8,128)(2,1)} %param.13), kind=kOutput, calls=%fused_computation.5 | convolution fusion | flops 2014003200 | bytes 9895936 | tf_op jit(solution)/shard_map/dot_general | solution.py:134
  (9 shorter events, 0.0 us)
Async XLA Ops:
  6.5 149.3 %copy-start = (bf16[4096,320]{0,1:T(8,128)(2,1)S(1)}, bf16[4096,320]{0,1:T(8,128)(2,1)}, u32[]{:S(2)}) copy-start(bf16[4096,320]{0,1:T(8,128)(2,1)} %param.12) | copy-start | bytes 7864324
  6.5 12.8 %copy-start.1 = (bf16[768,256]{1,0:T(8,128)(2,1)S(1)}, bf16[768,256]{1,0:T(8,128)(2,1)}, u32[]{:S(2)}) copy-start(bf16[768,256]{1,0:T(8,128)(2,1)} %param.7) | copy-start | bytes 1179652
  6.5 149.3 %all-gather.2.cloned.1.call-start = ((), (), s32[]{:S(2)}) async-start(), calls=%async_computation | async-start | bytes 6684672 | tf_op jit(solution)/shard_map/all_gather | solution.py:135
  9.2 6.3 %copy-start.4 = (f32[2]{0:T(128)}, f32[2]{0:T(128)S(1)}, u32[]{:S(2)}) copy-start(f32[2]{0:T(128)S(1)} %multiply_exponential_fusion) | copy-start | bytes 28
  9.3 6.2 %copy-start.3 = (f32[768,2]{0,1:T(2,128)}, f32[768,2]{0,1:T(2,128)S(1)}, u32[]{:S(2)}) copy-start(f32[768,2]{0,1:T(2,128)S(1)} %get-tuple-element.32) | copy-start | bytes 18436
  13.6 7.1 %collective-permute-start = (f32[2,136,128]{2,1,0:T(8,128)}, f32[2,136,128]{2,1,0:T(8,128)}, u32[]{:S(2)}, u32[]{:S(2)}) collective-permute-start(f32[2,136,128]{2,1,0:T(8,128)} %pad_maximum_fusion.1), channel_id=1, source_target_pairs={{0,16},{16,0},{32,48},{48,32},{64,80},{80,64},{96,112},{112,96},{1... | collective-permute-start | bytes 417800 | tf_op jit(solution)/shard_map/ppermute | solution.py:47
  17.0 9.0 %copy-start.2 = (f32[2,128,128]{2,1,0:T(8,128)}, f32[2,128,128]{2,1,0:T(8,128)S(1)}, u32[]{:S(2)}) copy-start(f32[2,128,128]{2,1,0:T(8,128)S(1)} %fusion.9) | copy-start | bytes 393220
  23.2 18.3 %collective-permute-start.3 = (f32[2,136,128]{2,1,0:T(8,128)}, f32[2,136,128]{2,1,0:T(8,128)}, u32[]{:S(2)}, u32[]{:S(2)}) collective-permute-start(f32[2,136,128]{2,1,0:T(8,128)} %fusion.33), channel_id=1, source_target_pairs={{0,96},{16,48},{32,0},{48,80},{64,32},{80,112},{96,64},{112,16},{1... | collective-permute-start | bytes 417800 | tf_op jit(solution)/shard_map/ppermute | solution.py:28
  25.9 15.5 %collective-permute-start.2 = (f32[2,136,128]{2,1,0:T(8,128)}, f32[2,136,128]{2,1,0:T(8,128)}, u32[]{:S(2)}, u32[]{:S(2)}) collective-permute-start(f32[2,136,128]{2,1,0:T(8,128)} %fusion.33), channel_id=1, source_target_pairs={{0,64},{16,80},{32,96},{48,112},{64,0},{80,16},{96,32},{112,48},{1... | collective-permute-start | bytes 417800 | tf_op jit(solution)/shard_map/ppermute | solution.py:28
  34.4 7.2 %collective-permute-start.1 = (f32[2,136,128]{2,1,0:T(8,128)}, f32[2,136,128]{2,1,0:T(8,128)S(1)}, u32[]{:S(2)}, u32[]{:S(2)}) collective-permute-start(f32[2,136,128]{2,1,0:T(8,128)} %fusion.33), channel_id=1, source_target_pairs={{0,32},{16,112},{32,64},{48,16},{64,96},{80,48},{96,0},{112,80},{1... | collective-permute-start | bytes 417800 | tf_op jit(solution)/shard_map/ppermute | solution.py:28
  40.7 28.3 %copy-start.5 = (f32[256]{0:T(256)S(1)}, f32[256]{0:T(256)}, u32[]{:S(2)}) copy-start(f32[256]{0:T(256)} %param.11) | copy-start | bytes 3076
  46.2 9.5 %collective-permute-start.4 = (f32[2,136,128]{2,1,0:T(8,128)}, f32[2,136,128]{2,1,0:T(8,128)S(1)}, u32[]{:S(2)}, u32[]{:S(2)}) collective-permute-start(f32[2,136,128]{2,1,0:T(8,128)} %get-tuple-element.29), channel_id=1, source_target_pairs={{0,128},{16,400},{32,160},{48,432},{64,192},{80,464},{96,224},{112... | collective-permute-start | bytes 417800 | tf_op jit(solution)/shard_map/ppermute | solution.py:28
  48.1 14.7 %collective-permute-start.6 = (f32[2,136,128]{2,1,0:T(8,128)}, f32[2,136,128]{2,1,0:T(8,128)S(1)}, u32[]{:S(2)}, u32[]{:S(2)}) collective-permute-start(f32[2,136,128]{2,1,0:T(8,128)} %get-tuple-element.29), channel_id=1, source_target_pairs={{0,384},{16,144},{32,416},{48,176},{64,448},{80,208},{96,480},{112... | collective-permute-start | bytes 417800 | tf_op jit(solution)/shard_map/ppermute | solution.py:28
  53.3 8.7 %collective-permute-start.5 = (f32[2,136,128]{2,1,0:T(8,128)}, f32[2,136,128]{2,1,0:T(8,128)S(1)}, u32[]{:S(2)}, u32[]{:S(2)}) collective-permute-start(f32[2,136,128]{2,1,0:T(8,128)} %get-tuple-element.29), channel_id=1, source_target_pairs={{0,256},{16,272},{32,288},{48,304},{64,320},{80,336},{96,352},{112... | collective-permute-start | bytes 417800 | tf_op jit(solution)/shard_map/ppermute | solution.py:28
  63.9 3.1 %collective-permute-start.7 = (bf16[2,128,128]{2,1,0:T(8,128)(2,1)S(1)}, bf16[2,128,128]{2,1,0:T(8,128)(2,1)S(1)}, u32[]{:S(2)}, u32[]{:S(2)}) collective-permute-start(bf16[2,128,128]{2,1,0:T(8,128)(2,1)S(1)} %get-tuple-element.27), channel_id=1, source_target_pairs={{0,16},{16,0},{32,48},{48,32},{64,80},{80,64},{96,112},{112,96},{1... | collective-permute-start | bytes 196616 | tf_op jit(solution)/shard_map/ppermute | solution.py:71
Sparse Core Ops, SparseCore 0:
  69.9 85.8 all-gather.1

commit v12 on v10

--- a/solution.py
+++ b/solution.py
@@ -29,7 +29,7 @@
     return got
 
 
-def block_scan(decay, mine, other):
+def block_scan(decay, mine, other, extra):
     seq_count = lax.axis_size("seq")
     line = 4
     me = lax.axis_index("seq")
@@ -63,6 +63,7 @@
             is_s, jnp.where(valid, decay_of(part) * total + part, total), total * decay_of(part)
         )
     col = gather_line(total, line, 2 * line, seq_count)
+    col, extra = lax.optimization_barrier((col, extra))
     col_prefix = prefix(col, pos_y)
     state = (decay_of(row_prefix) * col_prefix + row_prefix)[:, :HD]
     handed = lax.ppermute(
@@ -70,7 +71,7 @@
     )
     state_fwd = jnp.where(second, handed, state)
     state_bwd = jnp.where(second, state, handed)
-    return state_fwd, state_bwd
+    return state_fwd, state_bwd, extra
 
 
 def local(query_vectors, key_vectors, value_vectors, decay_exp, norm_gain, out_weight, residual):
@@ -102,7 +103,9 @@
         "shd,she->hde", keys_other, value_heads, preferred_element_type=jnp.float32
     )
     block_decay = factor(block_exp)
-    state_fwd, state_bwd = block_scan(block_decay, summary_mine, summary_other)
+    state_fwd, state_bwd, local_part = block_scan(
+        block_decay, summary_mine, summary_other, local_part
+    )
     state_fwd = state_fwd.astype(jnp.bfloat16)
     state_bwd = state_bwd.astype(jnp.bfloat16)
     remote_fwd = (

time: 162 us -> 160 us (0.988)
  waiting for transfers between devices: 99.2 us -> 96.3 us
    ppermute x6, waiting for transfers between devices: 11.9 us -> 7.22 us  [gather_line(): got.append(lax.ppermute(packed, 'seq', pairs))]
where the time goes in v12:
time: 160 us; the launch traced here: 159 us
  waiting for transfers between devices  96.3 us (60%)
  starting transfers between devices  24.8 us (16%)
  matrix products  14.5 us (9%)
  between operations  13.7 us (9%)
  local copies, waits for them, and re-layouts  4.97 us (3%)
  other arithmetic  4.57 us (3%)
    all_gather x1, waiting for transfers between devices, local(): lax.all_gather(normed, 'tp', axis=1, tiled=True)  87.8 us
    ppermute x6, starting transfers between devices, gather_line(): got.append(lax.ppermute(packed, 'seq', pairs))  20.9 us
    ppermute x6, waiting for transfers between devices, gather_line(): got.append(lax.ppermute(packed, 'seq', pairs))  7.22 us
    dot_general x1, matrix products, local(): jnp.dot(lax.all_gather(normed, 'tp', axis=1, tiled=True), out_weight, pre...  5.81 us
    dot_general x1, matrix products, local(): jnp.einsum('hts,shd->thd', local_weights, value_heads, preferred_element_...  4.08 us
  transfers between devices with their start and end apart: 9, of which 4 were waited for; matrix products, arithmetic and copies ran while one was open for 4% of the time, Pallas kernels for 0%

profile of v12, /device:TPU:6, one launch (start us, length us, event | category | flops | bytes accessed | tf_op | source)
XLA Modules:
  0.0 158.8 jit_solution(17625381437838941937)
XLA Ops:
  6.5 0.0 copy-start
  6.5 0.0 copy-start.1
  6.5 0.0 all-gather.2.cloned.1.call-start
  6.5 0.9 reshape.86
  7.4 0.6 reduce-window.6
  8.0 0.2 slice_reduce_fusion
  8.2 0.2 reduce-window.9
  8.4 0.1 add_bitcast_fusion
  8.5 0.2 slice_reduce_fusion.11
  8.7 0.1 broadcast_select_fusion.1
  8.7 1.2 copy.47
  9.9 0.0 copy-start.4
  9.9 1.4 fusion.11
  11.3 0.1 broadcast_in_dim.104
  11.4 1.9 %collective-permute-start = (f32[2,136,128]{2,1,0:T(8,128)S(1)}, f32[2,136,128]{2,1,0:T(8,128)S(1)}, u32[]{:S(2)}, u32[]{:S(2)}) collective-permute-start(f32[2,136,128]{2,1,0:T(8,128)S(1)} %pad_maximum_fusion.1), channel_id=1, source_target_pairs={{0,16},{16,0},{32,48},{48,32},{64,80},{80,64},{96,112},{112,96},{1... | collective-permute-start | bytes 417800 | tf_op jit(solution)/shard_map/ppermute | solution.py:47
  13.4 1.3 fusion.9
  14.7 0.0 copy-start.2
  14.7 0.0 collective-permute-done
  14.7 0.0 copy-done.4
  14.7 0.1 slice_reduce_fusion.10
  14.8 0.5 copy-done.2
  15.3 0.1 fusion.34
  15.4 7.8 %collective-permute-start.1 = (f32[2,136,128]{2,1,0:T(8,128)S(1)}, f32[2,136,128]{2,1,0:T(8,128)S(1)}, u32[]{:S(2)}, u32[]{:S(2)}) collective-permute-start(f32[2,136,128]{2,1,0:T(8,128)S(1)} %fusion.34), channel_id=1, source_target_pairs={{0,32},{16,112},{32,64},{48,16},{64,96},{80,48},{96,0},{112,80},{1... | collective-permute-start | bytes 417800 | tf_op jit(solution)/shard_map/ppermute | solution.py:28
  23.2 1.9 %collective-permute-start.3 = (f32[2,136,128]{2,1,0:T(8,128)S(1)}, f32[2,136,128]{2,1,0:T(8,128)S(1)}, u32[]{:S(2)}, u32[]{:S(2)}) collective-permute-start(f32[2,136,128]{2,1,0:T(8,128)S(1)} %fusion.34), channel_id=1, source_target_pairs={{0,96},{16,48},{32,0},{48,80},{64,32},{80,112},{96,64},{112,16},{1... | collective-permute-start | bytes 417800 | tf_op jit(solution)/shard_map/ppermute | solution.py:28
  25.2 3.4 %collective-permute-start.2 = (f32[2,136,128]{2,1,0:T(8,128)S(1)}, f32[2,136,128]{2,1,0:T(8,128)S(1)}, u32[]{:S(2)}, u32[]{:S(2)}) collective-permute-start(f32[2,136,128]{2,1,0:T(8,128)S(1)} %fusion.34), channel_id=1, source_target_pairs={{0,64},{16,80},{32,96},{48,112},{64,0},{80,16},{96,32},{112,48},{1... | collective-permute-start | bytes 417800 | tf_op jit(solution)/shard_map/ppermute | solution.py:28
  28.5 0.1 slice_reduce_fusion.6
  28.6 0.0 collective-permute-done.1
  28.6 0.1 fusion.31
  28.8 0.1 slice_reduce_fusion.5
  28.9 5.5 %collective-permute-done.2 = f32[2,136,128]{2,1,0:T(8,128)S(1)} collective-permute-done((f32[2,136,128]{2,1,0:T(8,128)S(1)}, f32[2,136,128]{2,1,0:T(8,128)S(1)}, u32[]{:S(2)}, u32[]{:S(2)}) %collective-permute-start.2) | collective-permute-done | bytes 139296 | tf_op jit(solution)/shard_map/ppermute | solution.py:28
  34.4 0.1 add_select_fusion.3
  34.5 0.1 slice_reduce_fusion.4
  34.6 0.1 slice_reduce_fusion.8
  34.7 0.1 slice_reduce_fusion.9
  34.8 0.0 collective-permute-done.3
  34.8 0.1 slice_reduce_fusion.7
  34.9 0.8 select_select_fusion
  35.8 0.0 copy-start.3
  35.8 2.0 %collective-permute-start.6 = (f32[2,136,128]{2,1,0:T(8,128)}, f32[2,136,128]{2,1,0:T(8,128)}, u32[]{:S(2)}, u32[]{:S(2)}) collective-permute-start(f32[2,136,128]{2,1,0:T(8,128)} %get-tuple-element.17), channel_id=1, source_target_pairs={{0,384},{16,144},{32,416},{48,176},{64,448},{80,208},{96,480},{112... | collective-permute-start | bytes 417800 | tf_op jit(solution)/shard_map/ppermute | solution.py:28
  37.8 2.3 %collective-permute-start.5 = (f32[2,136,128]{2,1,0:T(8,128)}, f32[2,136,128]{2,1,0:T(8,128)}, u32[]{:S(2)}, u32[]{:S(2)}) collective-permute-start(f32[2,136,128]{2,1,0:T(8,128)} %get-tuple-element.17), channel_id=1, source_target_pairs={{0,256},{16,272},{32,288},{48,304},{64,320},{80,336},{96,352},{112... | collective-permute-start | bytes 417800 | tf_op jit(solution)/shard_map/ppermute | solution.py:28
  40.1 3.6 %collective-permute-start.4 = (f32[2,136,128]{2,1,0:T(8,128)}, f32[2,136,128]{2,1,0:T(8,128)S(1)}, u32[]{:S(2)}, u32[]{:S(2)}) collective-permute-start(f32[2,136,128]{2,1,0:T(8,128)} %get-tuple-element.17), channel_id=1, source_target_pairs={{0,128},{16,400},{32,160},{48,432},{64,192},{80,464},{96,224},{112... | collective-permute-start | bytes 417800 | tf_op jit(solution)/shard_map/ppermute | solution.py:28
  43.7 0.0 copy-done.1
  43.7 4.1 %fusion.3 = f32[768,2,128]{2,0,1:T(8,128)} fusion(s32[2,768]{1,0:T(2,128)S(1)} %get-tuple-element.16, bf16[768,2,128]{0,2,1:T(8,128)(2,1)} %bitcast.81, bf16[768,256]{1,0:T(8,128)(2,1)S(1)} %copy-done.1, bf16[768,256]{1,0:T(8,128)(2,1)} %param.9), kind=kOutput, calls=%fused_computation.3 | convolution fusion | flops 612237312 | bytes 1972224 | tf_op jit(solution)/shard_map/hts,shd->thd/dot_general | solution.py:89
  47.8 0.1 slice_reduce_fusion.3
  47.9 0.0 collective-permute-done.6
  47.9 0.0 collective-permute-done.5
  47.9 1.7 %collective-permute-done.4 = f32[2,136,128]{2,1,0:T(8,128)S(1)} collective-permute-done((f32[2,136,128]{2,1,0:T(8,128)}, f32[2,136,128]{2,1,0:T(8,128)S(1)}, u32[]{:S(2)}, u32[]{:S(2)}) %collective-permute-start.4) | collective-permute-done | bytes 139296 | tf_op jit(solution)/shard_map/ppermute | solution.py:28
  49.6 0.1 fusion.32
  49.7 0.1 slice_reduce_fusion.2
  49.8 1.0 add_select_fusion.1
  50.8 0.1 slice_reduce_fusion.1
  50.9 0.0 copy-done.3
  50.9 1.0 multiply_add_fusion
  52.0 1.9 %collective-permute-start.7 = (bf16[2,128,128]{2,1,0:T(8,128)(2,1)S(1)}, bf16[2,128,128]{2,1,0:T(8,128)(2,1)S(1)}, u32[]{:S(2)}, u32[]{:S(2)}) collective-permute-start(bf16[2,128,128]{2,1,0:T(8,128)(2,1)S(1)} %get-tuple-element.13), channel_id=1, source_target_pairs={{0,16},{16,0},{32,48},{48,32},{64,80},{80,64},{96,112},{112,96},{1... | collective-permute-start | bytes 196616 | tf_op jit(solution)/shard_map/ppermute | solution.py:69
  53.9 1.2 collective-permute-done.7
  55.1 0.3 fusion.5
  55.4 1.7 %multiply_reduce_fusion = (f32[768,2]{0,1:T(2,128)S(1)}, f32[768,2,128]{2,0,1:T(8,128)S(1)}) fusion(f32[768,2]{0,1:T(2,128)S(1)} %get-tuple-element.20, bf16[2,128,128]{2,1,0:T(8,128)(2,1)S(1)} %get-tuple-element.14, bf16[2,128,128]{2,1,0:T(8,128)(2,1)S(1)} %collective-permute-done.7, pred[]{:T(512)S(6)} %eq.8, f32[768,2,128]{2,0,1:T(8,128)} %fusion.3, ...), kind=kOutput, calls=%fused_computation.15 | convolution fusion | flops 51345920 | bytes 2895873 | tf_op jit(solution)/shard_map/thd,hde->the/dot_general | solution.py:116
  57.1 0.0 copy-done.5
  57.1 0.3 multiply_convert_fusion.4
  57.4 0.9 copy.42
  58.3 0.0 all-gather.2.cloned.1.call-update
  58.4 87.8 %all-gather.2.cloned.1.call-done = bf16[768,4096]{0,1:T(8,128)(2,1)} async-done(((bf16[768,256]{0,1:T(8,128)(2,1)}), bf16[768,4096]{0,1:T(8,128)(2,1)}) %all-gather.2.cloned.1.call-update) | async-done | bytes 6291472 | tf_op jit(solution)/shard_map/all_gather | solution.py:126
  146.2 0.0 copy-done
  146.2 5.8 %fusion.6 = bf16[768,320]{0,1:T(8,128)(2,1)} fusion(bf16[4096,320]{0,1:T(8,128)(2,1)S(1)} %copy-done, bf16[768,4096]{0,1:T(8,128)(2,1)} %all-gather.2.cloned.1.call-done, bf16[768,320]{0,1:T(8,128)(2,1)} %param.13), kind=kOutput, calls=%fused_computation.9 | convolution fusion | flops 2014003200 | bytes 9895936 | tf_op jit(solution)/shard_map/dot_general | solution.py:125
  (9 shorter events, 0.1 us)
Async XLA Ops:
  6.5 139.7 %copy-start = (bf16[4096,320]{0,1:T(8,128)(2,1)S(1)}, bf16[4096,320]{0,1:T(8,128)(2,1)}, u32[]{:S(2)}) copy-start(bf16[4096,320]{0,1:T(8,128)(2,1)} %param.12) | copy-start | bytes 7864324
  6.5 37.1 %copy-start.1 = (bf16[768,256]{1,0:T(8,128)(2,1)S(1)}, bf16[768,256]{1,0:T(8,128)(2,1)}, u32[]{:S(2)}) copy-start(bf16[768,256]{1,0:T(8,128)(2,1)} %param.7) | copy-start | bytes 1179652
  6.5 139.6 %all-gather.2.cloned.1.call-start = ((), (), s32[]{:S(2)}) async-start(), calls=%async_computation | async-start | bytes 6684672 | tf_op jit(solution)/shard_map/all_gather | solution.py:126
  9.9 4.8 %copy-start.4 = (bf16[768,256]{0,1:T(8,128)(2,1)}, bf16[768,256]{0,1:T(8,128)(2,1)S(1)}, u32[]{:S(2)}) copy-start(bf16[768,256]{0,1:T(8,128)(2,1)S(1)} %copy.47) | copy-start | bytes 1179652
  11.4 3.3 %collective-permute-start = (f32[2,136,128]{2,1,0:T(8,128)S(1)}, f32[2,136,128]{2,1,0:T(8,128)S(1)}, u32[]{:S(2)}, u32[]{:S(2)}) collective-permute-start(f32[2,136,128]{2,1,0:T(8,128)S(1)} %pad_maximum_fusion.1), channel_id=1, source_target_pairs={{0,16},{16,0},{32,48},{48,32},{64,80},{80,64},{96,112},{112,96},{1... | collective-permute-start | bytes 417800 | tf_op jit(solution)/shard_map/ppermute | solution.py:47
  14.7 0.7 copy-start.2
  15.4 13.2 %collective-permute-start.1 = (f32[2,136,128]{2,1,0:T(8,128)S(1)}, f32[2,136,128]{2,1,0:T(8,128)S(1)}, u32[]{:S(2)}, u32[]{:S(2)}) collective-permute-start(f32[2,136,128]{2,1,0:T(8,128)S(1)} %fusion.34), channel_id=1, source_target_pairs={{0,32},{16,112},{32,64},{48,16},{64,96},{80,48},{96,0},{112,80},{1... | collective-permute-start | bytes 417800 | tf_op jit(solution)/shard_map/ppermute | solution.py:28
  23.2 11.6 %collective-permute-start.3 = (f32[2,136,128]{2,1,0:T(8,128)S(1)}, f32[2,136,128]{2,1,0:T(8,128)S(1)}, u32[]{:S(2)}, u32[]{:S(2)}) collective-permute-start(f32[2,136,128]{2,1,0:T(8,128)S(1)} %fusion.34), channel_id=1, source_target_pairs={{0,96},{16,48},{32,0},{48,80},{64,32},{80,112},{96,64},{112,16},{1... | collective-permute-start | bytes 417800 | tf_op jit(solution)/shard_map/ppermute | solution.py:28
  25.2 9.2 %collective-permute-start.2 = (f32[2,136,128]{2,1,0:T(8,128)S(1)}, f32[2,136,128]{2,1,0:T(8,128)S(1)}, u32[]{:S(2)}, u32[]{:S(2)}) collective-permute-start(f32[2,136,128]{2,1,0:T(8,128)S(1)} %fusion.34), channel_id=1, source_target_pairs={{0,64},{16,80},{32,96},{48,112},{64,0},{80,16},{96,32},{112,48},{1... | collective-permute-start | bytes 417800 | tf_op jit(solution)/shard_map/ppermute | solution.py:28
  35.8 15.2 %copy-start.3 = (f32[2,128,128]{2,1,0:T(8,128)S(1)}, f32[2,128,128]{2,1,0:T(8,128)}, u32[]{:S(2)}) copy-start(f32[2,128,128]{2,1,0:T(8,128)} %copy-done.2) | copy-start | bytes 393220
  35.8 12.1 %collective-permute-start.6 = (f32[2,136,128]{2,1,0:T(8,128)}, f32[2,136,128]{2,1,0:T(8,128)}, u32[]{:S(2)}, u32[]{:S(2)}) collective-permute-start(f32[2,136,128]{2,1,0:T(8,128)} %get-tuple-element.17), channel_id=1, source_target_pairs={{0,384},{16,144},{32,416},{48,176},{64,448},{80,208},{96,480},{112... | collective-permute-start | bytes 417800 | tf_op jit(solution)/shard_map/ppermute | solution.py:28
  37.8 10.1 %collective-permute-start.5 = (f32[2,136,128]{2,1,0:T(8,128)}, f32[2,136,128]{2,1,0:T(8,128)}, u32[]{:S(2)}, u32[]{:S(2)}) collective-permute-start(f32[2,136,128]{2,1,0:T(8,128)} %get-tuple-element.17), channel_id=1, source_target_pairs={{0,256},{16,272},{32,288},{48,304},{64,320},{80,336},{96,352},{112... | collective-permute-start | bytes 417800 | tf_op jit(solution)/shard_map/ppermute | solution.py:28
  40.1 9.5 %collective-permute-start.4 = (f32[2,136,128]{2,1,0:T(8,128)}, f32[2,136,128]{2,1,0:T(8,128)S(1)}, u32[]{:S(2)}, u32[]{:S(2)}) collective-permute-start(f32[2,136,128]{2,1,0:T(8,128)} %get-tuple-element.17), channel_id=1, source_target_pairs={{0,128},{16,400},{32,160},{48,432},{64,192},{80,464},{96,224},{112... | collective-permute-start | bytes 417800 | tf_op jit(solution)/shard_map/ppermute | solution.py:28
  47.8 9.3 %copy-start.5 = (f32[256]{0:T(256)S(1)}, f32[256]{0:T(256)}, u32[]{:S(2)}) copy-start(f32[256]{0:T(256)} %param.11) | copy-start | bytes 3076
  52.0 3.1 %collective-permute-start.7 = (bf16[2,128,128]{2,1,0:T(8,128)(2,1)S(1)}, bf16[2,128,128]{2,1,0:T(8,128)(2,1)S(1)}, u32[]{:S(2)}, u32[]{:S(2)}) collective-permute-start(bf16[2,128,128]{2,1,0:T(8,128)(2,1)S(1)} %get-tuple-element.13), channel_id=1, source_target_pairs={{0,16},{16,0},{32,48},{48,32},{64,80},{80,64},{96,112},{112,96},{1... | collective-permute-start | bytes 196616 | tf_op jit(solution)/shard_map/ppermute | solution.py:69
Sparse Core Ops, SparseCore 0:
  58.5 87.6 all-gather.1

commit v13 on v10

--- a/solution.py
+++ b/solution.py
@@ -29,7 +29,7 @@
     return got
 
 
-def block_scan(decay, mine, other):
+def block_scan(decay, mine, other, extra, own_fn=None):
     seq_count = lax.axis_size("seq")
     line = 4
     me = lax.axis_index("seq")
@@ -63,14 +63,16 @@
             is_s, jnp.where(valid, decay_of(part) * total + part, total), total * decay_of(part)
         )
     col = gather_line(total, line, 2 * line, seq_count)
+    col, extra = lax.optimization_barrier((col, extra))
     col_prefix = prefix(col, pos_y)
     state = (decay_of(row_prefix) * col_prefix + row_prefix)[:, :HD]
     handed = lax.ppermute(
         decay[:, None, None] * state + mine, "seq", [(i, i ^ 1) for i in range(seq_count)]
     )
-    state_fwd = jnp.where(second, handed, state)
-    state_bwd = jnp.where(second, state, handed)
-    return state_fwd, state_bwd
+    if own_fn is None:
+        return state, handed, extra
+    handed, own = lax.optimization_barrier((handed, own_fn(state)))
+    return own, handed, extra
 
 
 def local(query_vectors, key_vectors, value_vectors, decay_exp, norm_gain, out_weight, residual):
@@ -102,17 +104,20 @@
         "shd,she->hde", keys_other, value_heads, preferred_element_type=jnp.float32
     )
     block_decay = factor(block_exp)
-    state_fwd, state_bwd = block_scan(block_decay, summary_mine, summary_other)
-    state_fwd = state_fwd.astype(jnp.bfloat16)
-    state_bwd = state_bwd.astype(jnp.bfloat16)
-    remote_fwd = (
-        jnp.einsum("thd,hde->the", query_heads, state_fwd, preferred_element_type=jnp.float32)
-        * head_factor[:, :, None]
+    def project(state):
+        return jnp.einsum(
+            "thd,hde->the",
+            query_heads,
+            state.astype(jnp.bfloat16),
+            preferred_element_type=jnp.float32,
+        )
+
+    remote_own, state_handed, local_part = block_scan(
+        block_decay, summary_mine, summary_other, local_part, project
     )
-    remote_bwd = (
-        jnp.einsum("thd,hde->the", query_heads, state_bwd, preferred_element_type=jnp.float32)
-        * tail_factor[:, :, None]
-    )
+    remote_handed = project(state_handed)
+    remote_fwd = jnp.where(second, remote_handed, remote_own) * head_factor[:, :, None]
+    remote_bwd = jnp.where(second, remote_own, remote_handed) * tail_factor[:, :, None]
     attention = local_part + remote_fwd + remote_bwd
     scale = lax.rsqrt(jnp.mean(attention * attention, axis=-1, keepdims=True) + 1e-06)
     normed = (attention * scale * norm_gain.reshape(head_count, HD)[None, :, :]).astype(

time: 162 us -> 160 us (0.988)
  waiting for transfers between devices: 99.2 us -> 96 us
  other arithmetic: 4.24 us -> 6.46 us
    ppermute x6, waiting for transfers between devices: 11.9 us -> 7.21 us  [gather_line(): got.append(lax.ppermute(packed, 'seq', pairs))]
    reduce_sum x0 -> x1, other arithmetic: none -> 1.9 us  [local(): jnp.mean(attention * attention, axis=-1, keepdims=True) + 1e-06]
where the time goes in v13:
time: 160 us; the launch traced here: 159 us
  waiting for transfers between devices  96 us (60%)
  starting transfers between devices  24.8 us (16%)
  between operations  13.7 us (9%)
  matrix products  13 us (8%)
  other arithmetic  6.46 us (4%)
  local copies, waits for them, and re-layouts  4.97 us (3%)
    all_gather x1, waiting for transfers between devices, local(): lax.all_gather(normed, 'tp', axis=1, tiled=True)  87.8 us
    ppermute x6, starting transfers between devices, gather_line(): got.append(lax.ppermute(packed, 'seq', pairs))  20.9 us
    ppermute x6, waiting for transfers between devices, gather_line(): got.append(lax.ppermute(packed, 'seq', pairs))  7.21 us
    dot_general x1, matrix products, local(): jnp.dot(lax.all_gather(normed, 'tp', axis=1, tiled=True), out_weight, pre...  5.75 us
    dot_general x1, matrix products, local(): jnp.einsum('hts,shd->thd', local_weights, value_heads, preferred_element_...  4.09 us
  transfers between devices with their start and end apart: 9, of which 4 were waited for; matrix products, arithmetic and copies ran while one was open for 4% of the time, Pallas kernels for 0%

profile of v13, /device:TPU:6, one launch (start us, length us, event | category | flops | bytes accessed | tf_op | source)
XLA Modules:
  0.0 158.9 jit_solution(9697684818676801159)
XLA Ops:
  6.5 0.0 copy-start
  6.5 0.0 all-gather.2.cloned.1.call-start
  6.5 0.9 reshape.86
  7.4 0.6 reduce-window.6
  8.0 0.2 slice_reduce_fusion
  8.2 0.2 reduce-window.9
  8.4 0.1 add_bitcast_fusion
  8.5 0.2 slice_reduce_fusion.11
  8.7 0.1 broadcast_select_fusion.1
  8.7 1.2 copy.47
  9.9 0.0 copy-start.4
  9.9 1.4 fusion.9
  11.3 0.1 broadcast_in_dim.104
  11.4 1.9 %collective-permute-start = (f32[2,136,128]{2,1,0:T(8,128)S(1)}, f32[2,136,128]{2,1,0:T(8,128)S(1)}, u32[]{:S(2)}, u32[]{:S(2)}) collective-permute-start(f32[2,136,128]{2,1,0:T(8,128)S(1)} %pad_maximum_fusion.1), channel_id=1, source_target_pairs={{0,16},{16,0},{32,48},{48,32},{64,80},{80,64},{96,112},{112,96},{1... | collective-permute-start | bytes 417800 | tf_op jit(solution)/shard_map/ppermute | solution.py:47
  13.4 1.3 fusion.7
  14.6 0.0 copy-start.2
  14.7 0.0 collective-permute-done
  14.7 0.0 copy-done.4
  14.7 0.1 slice_reduce_fusion.10
  14.8 0.5 copy-done.2
  15.3 0.1 fusion.30
  15.4 7.8 %collective-permute-start.1 = (f32[2,136,128]{2,1,0:T(8,128)S(1)}, f32[2,136,128]{2,1,0:T(8,128)S(1)}, u32[]{:S(2)}, u32[]{:S(2)}) collective-permute-start(f32[2,136,128]{2,1,0:T(8,128)S(1)} %fusion.30), channel_id=1, source_target_pairs={{0,32},{16,112},{32,64},{48,16},{64,96},{80,48},{96,0},{112,80},{1... | collective-permute-start | bytes 417800 | tf_op jit(solution)/shard_map/ppermute | solution.py:28
  23.2 1.9 %collective-permute-start.3 = (f32[2,136,128]{2,1,0:T(8,128)S(1)}, f32[2,136,128]{2,1,0:T(8,128)S(1)}, u32[]{:S(2)}, u32[]{:S(2)}) collective-permute-start(f32[2,136,128]{2,1,0:T(8,128)S(1)} %fusion.30), channel_id=1, source_target_pairs={{0,96},{16,48},{32,0},{48,80},{64,32},{80,112},{96,64},{112,16},{1... | collective-permute-start | bytes 417800 | tf_op jit(solution)/shard_map/ppermute | solution.py:28
  25.1 3.4 %collective-permute-start.2 = (f32[2,136,128]{2,1,0:T(8,128)S(1)}, f32[2,136,128]{2,1,0:T(8,128)S(1)}, u32[]{:S(2)}, u32[]{:S(2)}) collective-permute-start(f32[2,136,128]{2,1,0:T(8,128)S(1)} %fusion.30), channel_id=1, source_target_pairs={{0,64},{16,80},{32,96},{48,112},{64,0},{80,16},{96,32},{112,48},{1... | collective-permute-start | bytes 417800 | tf_op jit(solution)/shard_map/ppermute | solution.py:28
  28.5 0.1 slice_reduce_fusion.6
  28.6 0.0 collective-permute-done.1
  28.6 0.1 fusion.27
  28.7 0.1 slice_reduce_fusion.5
  28.8 5.5 %collective-permute-done.2 = f32[2,136,128]{2,1,0:T(8,128)S(1)} collective-permute-done((f32[2,136,128]{2,1,0:T(8,128)S(1)}, f32[2,136,128]{2,1,0:T(8,128)S(1)}, u32[]{:S(2)}, u32[]{:S(2)}) %collective-permute-start.2) | collective-permute-done | bytes 139296 | tf_op jit(solution)/shard_map/ppermute | solution.py:28
  34.4 0.1 add_select_fusion.3
  34.5 0.1 slice_reduce_fusion.4
  34.6 0.1 slice_reduce_fusion.8
  34.7 0.1 slice_reduce_fusion.9
  34.8 0.0 collective-permute-done.3
  34.8 0.1 slice_reduce_fusion.7
  34.9 0.8 select_select_fusion
  35.7 2.0 %collective-permute-start.6 = (f32[2,136,128]{2,1,0:T(8,128)}, f32[2,136,128]{2,1,0:T(8,128)}, u32[]{:S(2)}, u32[]{:S(2)}) collective-permute-start(f32[2,136,128]{2,1,0:T(8,128)} %get-tuple-element.23), channel_id=1, source_target_pairs={{0,384},{16,144},{32,416},{48,176},{64,448},{80,208},{96,480},{112... | collective-permute-start | bytes 417800 | tf_op jit(solution)/shard_map/ppermute | solution.py:28
  37.8 2.3 %collective-permute-start.5 = (f32[2,136,128]{2,1,0:T(8,128)}, f32[2,136,128]{2,1,0:T(8,128)}, u32[]{:S(2)}, u32[]{:S(2)}) collective-permute-start(f32[2,136,128]{2,1,0:T(8,128)} %get-tuple-element.23), channel_id=1, source_target_pairs={{0,256},{16,272},{32,288},{48,304},{64,320},{80,336},{96,352},{112... | collective-permute-start | bytes 417800 | tf_op jit(solution)/shard_map/ppermute | solution.py:28
  40.1 3.6 %collective-permute-start.4 = (f32[2,136,128]{2,1,0:T(8,128)}, f32[2,136,128]{2,1,0:T(8,128)S(1)}, u32[]{:S(2)}, u32[]{:S(2)}) collective-permute-start(f32[2,136,128]{2,1,0:T(8,128)} %get-tuple-element.23), channel_id=1, source_target_pairs={{0,128},{16,400},{32,160},{48,432},{64,192},{80,464},{96,224},{112... | collective-permute-start | bytes 417800 | tf_op jit(solution)/shard_map/ppermute | solution.py:28
  43.7 0.0 copy-done.1
  43.7 4.1 %fusion.3 = f32[768,2,128]{2,0,1:T(8,128)} fusion(s32[2,768]{1,0:T(2,128)S(1)} %get-tuple-element.20, bf16[768,2,128]{0,2,1:T(8,128)(2,1)} %bitcast.73, bf16[768,256]{1,0:T(8,128)(2,1)S(1)} %copy-done.1, bf16[768,256]{1,0:T(8,128)(2,1)} %param.9), kind=kOutput, calls=%fused_computation.3 | convolution fusion | flops 612237312 | bytes 1972224 | tf_op jit(solution)/shard_map/hts,shd->thd/dot_general | solution.py:90
  47.8 0.1 slice_reduce_fusion.3
  47.9 0.0 collective-permute-done.6
  47.9 0.0 collective-permute-done.5
  47.9 1.7 %collective-permute-done.4 = f32[2,136,128]{2,1,0:T(8,128)S(1)} collective-permute-done((f32[2,136,128]{2,1,0:T(8,128)}, f32[2,136,128]{2,1,0:T(8,128)S(1)}, u32[]{:S(2)}, u32[]{:S(2)}) %collective-permute-start.4) | collective-permute-done | bytes 139296 | tf_op jit(solution)/shard_map/ppermute | solution.py:28
  49.5 0.1 fusion.28
  49.7 0.1 slice_reduce_fusion.2
  49.8 1.0 add_select_fusion.1
  50.8 0.1 slice_reduce_fusion.1
  50.9 0.0 copy-done.3
  50.9 1.0 multiply_add_fusion.1
  51.9 1.9 %collective-permute-start.7 = (bf16[2,128,128]{2,1,0:T(8,128)(2,1)S(1)}, bf16[2,128,128]{2,1,0:T(8,128)(2,1)S(1)}, u32[]{:S(2)}, u32[]{:S(2)}) collective-permute-start(bf16[2,128,128]{2,1,0:T(8,128)(2,1)S(1)} %get-tuple-element.21), channel_id=1, source_target_pairs={{0,16},{16,0},{32,48},{48,32},{64,80},{80,64},{96,112},{112,96},{1... | collective-permute-start | bytes 196616 | tf_op jit(solution)/shard_map/ppermute | solution.py:69
  53.9 0.2 convolution_bitcast_fusion.1
  54.1 1.0 collective-permute-done.7
  55.1 0.2 convolution_bitcast_fusion
  55.3 0.0 copy-start.6
  55.3 1.9 %multiply_reduce_fusion = (f32[768,2]{0,1:T(2,128)S(1)}, f32[768,2,128]{2,0,1:T(8,128)S(1)}) fusion(f32[768,2]{0,1:T(2,128)S(1)} %get-tuple-element.26, f32[768,2,128]{2,0,1:T(8,128)S(1)} %convolution_bitcast_fusion.1, f32[768,2,128]{2,0,1:T(8,128)S(1)} %convolution_bitcast_fusion, f32[768,2,128]{2,0,1:T(8,128)} %fusion.3, ...), kind=kLoop, calls=%fused_computation.13 | loop fusion | flops 1571328 | bytes 3164161 | tf_op jit(solution)/shard_map/reduce_sum | solution.py:122
  57.3 0.0 copy-done.5
  57.3 0.3 multiply_convert_fusion.4
  57.5 0.9 copy.42
  58.5 0.0 all-gather.2.cloned.1.call-update
  58.5 87.8 %all-gather.2.cloned.1.call-done = bf16[768,4096]{0,1:T(8,128)(2,1)} async-done(((bf16[768,256]{0,1:T(8,128)(2,1)}), bf16[768,4096]{0,1:T(8,128)(2,1)}) %all-gather.2.cloned.1.call-update) | async-done | bytes 6291472 | tf_op jit(solution)/shard_map/all_gather | solution.py:128
  146.3 0.0 copy-done
  146.3 5.8 %fusion.4 = bf16[768,320]{0,1:T(8,128)(2,1)} fusion(bf16[4096,320]{0,1:T(8,128)(2,1)S(1)} %copy-done, bf16[768,4096]{0,1:T(8,128)(2,1)} %all-gather.2.cloned.1.call-done, bf16[768,320]{0,1:T(8,128)(2,1)S(1)} %copy-done.6), kind=kOutput, calls=%fused_computation.7 | convolution fusion | flops 2014003200 | bytes 9895936 | tf_op jit(solution)/shard_map/dot_general | solution.py:127
  (12 shorter events, 0.1 us)
Async XLA Ops:
  6.5 139.8 %copy-start = (bf16[4096,320]{0,1:T(8,128)(2,1)S(1)}, bf16[4096,320]{0,1:T(8,128)(2,1)}, u32[]{:S(2)}) copy-start(bf16[4096,320]{0,1:T(8,128)(2,1)} %param.12) | copy-start | bytes 7864324
  6.5 37.1 %copy-start.1 = (bf16[768,256]{1,0:T(8,128)(2,1)S(1)}, bf16[768,256]{1,0:T(8,128)(2,1)}, u32[]{:S(2)}) copy-start(bf16[768,256]{1,0:T(8,128)(2,1)} %param.7) | copy-start | bytes 1179652
  6.5 139.8 %all-gather.2.cloned.1.call-start = ((), (), s32[]{:S(2)}) async-start(), calls=%async_computation | async-start | bytes 6684672 | tf_op jit(solution)/shard_map/all_gather | solution.py:128
  9.9 4.8 %copy-start.4 = (bf16[768,256]{0,1:T(8,128)(2,1)}, bf16[768,256]{0,1:T(8,128)(2,1)S(1)}, u32[]{:S(2)}) copy-start(bf16[768,256]{0,1:T(8,128)(2,1)S(1)} %copy.47) | copy-start | bytes 1179652
  11.4 3.3 %collective-permute-start = (f32[2,136,128]{2,1,0:T(8,128)S(1)}, f32[2,136,128]{2,1,0:T(8,128)S(1)}, u32[]{:S(2)}, u32[]{:S(2)}) collective-permute-start(f32[2,136,128]{2,1,0:T(8,128)S(1)} %pad_maximum_fusion.1), channel_id=1, source_target_pairs={{0,16},{16,0},{32,48},{48,32},{64,80},{80,64},{96,112},{112,96},{1... | collective-permute-start | bytes 417800 | tf_op jit(solution)/shard_map/ppermute | solution.py:47
  14.6 0.7 copy-start.2
  15.4 13.2 %collective-permute-start.1 = (f32[2,136,128]{2,1,0:T(8,128)S(1)}, f32[2,136,128]{2,1,0:T(8,128)S(1)}, u32[]{:S(2)}, u32[]{:S(2)}) collective-permute-start(f32[2,136,128]{2,1,0:T(8,128)S(1)} %fusion.30), channel_id=1, source_target_pairs={{0,32},{16,112},{32,64},{48,16},{64,96},{80,48},{96,0},{112,80},{1... | collective-permute-start | bytes 417800 | tf_op jit(solution)/shard_map/ppermute | solution.py:28
  23.2 11.6 %collective-permute-start.3 = (f32[2,136,128]{2,1,0:T(8,128)S(1)}, f32[2,136,128]{2,1,0:T(8,128)S(1)}, u32[]{:S(2)}, u32[]{:S(2)}) collective-permute-start(f32[2,136,128]{2,1,0:T(8,128)S(1)} %fusion.30), channel_id=1, source_target_pairs={{0,96},{16,48},{32,0},{48,80},{64,32},{80,112},{96,64},{112,16},{1... | collective-permute-start | bytes 417800 | tf_op jit(solution)/shard_map/ppermute | solution.py:28
  25.1 9.2 %collective-permute-start.2 = (f32[2,136,128]{2,1,0:T(8,128)S(1)}, f32[2,136,128]{2,1,0:T(8,128)S(1)}, u32[]{:S(2)}, u32[]{:S(2)}) collective-permute-start(f32[2,136,128]{2,1,0:T(8,128)S(1)} %fusion.30), channel_id=1, source_target_pairs={{0,64},{16,80},{32,96},{48,112},{64,0},{80,16},{96,32},{112,48},{1... | collective-permute-start | bytes 417800 | tf_op jit(solution)/shard_map/ppermute | solution.py:28
  35.7 15.2 %copy-start.3 = (f32[2,128,128]{2,1,0:T(8,128)S(1)}, f32[2,128,128]{2,1,0:T(8,128)}, u32[]{:S(2)}) copy-start(f32[2,128,128]{2,1,0:T(8,128)} %copy-done.2) | copy-start | bytes 393220
  35.7 12.1 %collective-permute-start.6 = (f32[2,136,128]{2,1,0:T(8,128)}, f32[2,136,128]{2,1,0:T(8,128)}, u32[]{:S(2)}, u32[]{:S(2)}) collective-permute-start(f32[2,136,128]{2,1,0:T(8,128)} %get-tuple-element.23), channel_id=1, source_target_pairs={{0,384},{16,144},{32,416},{48,176},{64,448},{80,208},{96,480},{112... | collective-permute-start | bytes 417800 | tf_op jit(solution)/shard_map/ppermute | solution.py:28
  37.8 10.1 %collective-permute-start.5 = (f32[2,136,128]{2,1,0:T(8,128)}, f32[2,136,128]{2,1,0:T(8,128)}, u32[]{:S(2)}, u32[]{:S(2)}) collective-permute-start(f32[2,136,128]{2,1,0:T(8,128)} %get-tuple-element.23), channel_id=1, source_target_pairs={{0,256},{16,272},{32,288},{48,304},{64,320},{80,336},{96,352},{112... | collective-permute-start | bytes 417800 | tf_op jit(solution)/shard_map/ppermute | solution.py:28
  40.1 9.5 %collective-permute-start.4 = (f32[2,136,128]{2,1,0:T(8,128)}, f32[2,136,128]{2,1,0:T(8,128)S(1)}, u32[]{:S(2)}, u32[]{:S(2)}) collective-permute-start(f32[2,136,128]{2,1,0:T(8,128)} %get-tuple-element.23), channel_id=1, source_target_pairs={{0,128},{16,400},{32,160},{48,432},{64,192},{80,464},{96,224},{112... | collective-permute-start | bytes 417800 | tf_op jit(solution)/shard_map/ppermute | solution.py:28
  47.8 9.5 %copy-start.5 = (f32[256]{0:T(256)S(1)}, f32[256]{0:T(256)}, u32[]{:S(2)}) copy-start(f32[256]{0:T(256)} %param.11) | copy-start | bytes 3076
  51.9 3.1 %collective-permute-start.7 = (bf16[2,128,128]{2,1,0:T(8,128)(2,1)S(1)}, bf16[2,128,128]{2,1,0:T(8,128)(2,1)S(1)}, u32[]{:S(2)}, u32[]{:S(2)}) collective-permute-start(bf16[2,128,128]{2,1,0:T(8,128)(2,1)S(1)} %get-tuple-element.21), channel_id=1, source_target_pairs={{0,16},{16,0},{32,48},{48,32},{64,80},{80,64},{96,112},{112,96},{1... | collective-permute-start | bytes 196616 | tf_op jit(solution)/shard_map/ppermute | solution.py:69
  55.3 91.0 %copy-start.6 = (bf16[768,320]{0,1:T(8,128)(2,1)S(1)}, bf16[768,320]{0,1:T(8,128)(2,1)}, u32[]{:S(2)}) copy-start(bf16[768,320]{0,1:T(8,128)(2,1)} %param.13) | copy-start | bytes 1474564
Sparse Core Ops, SparseCore 0:
  58.6 87.6 all-gather.1

commit v14 on v12

--- a/solution.py
+++ b/solution.py
@@ -121,10 +121,12 @@
     normed = (attention * scale * norm_gain.reshape(head_count, HD)[None, :, :]).astype(
         jnp.bfloat16
     )
-    normed = normed.reshape(tok_rows, head_count * HD)
-    mixed = jnp.dot(
-        lax.all_gather(normed, "tp", axis=1, tiled=True),
-        out_weight,
+    tp_count = lax.axis_size("tp")
+    gathered = lax.all_gather(normed.transpose(1, 0, 2)[None], "tp", axis=0, tiled=True)
+    mixed = lax.dot_general(
+        gathered,
+        out_weight.reshape(tp_count, head_count, HD, -1),
+        (((0, 1, 3), (0, 1, 2)), ((), ())),
         preferred_element_type=jnp.float32,
     )
     return (residual.astype(jnp.float32) + mixed).astype(jnp.bfloat16)

time: 160 us -> 159 us (level)
  waiting for transfers between devices: 96.3 us -> 93.8 us
  local copies, waits for them, and re-layouts: 4.97 us -> 6.98 us
    all_gather x1, waiting for transfers between devices: 87.8 us -> 84.3 us  [local(): lax.all_gather(normed.transpose(1, 0, 2)[None], 'tp', axis=0, tiled=True)]
    reshape x1 -> x2, local copies, waits for them, and re-layouts: 0.85 us -> 4.33 us  [the longest x1 3.55 us: local(): out_weight.reshape(tp_count, head_count, HD, -1)]
  transfers between devices with their start and end apart: 9 -> 9, of which waited for: 4 -> 4; matrix products, arithmetic and copies ran while one was open for 4% -> 5% of each run, Pallas kernels for 0% -> 0%
where the time goes in v14:
time: 159 us
  waiting for transfers between devices  93.8 us (59%)
  starting transfers between devices  24.6 us (15%)
  matrix products  14.3 us (9%)
  between operations  13.7 us (9%)
  local copies, waits for them, and re-layouts  6.98 us (4%)
  other arithmetic  5.32 us (3%)
    all_gather x1, waiting for transfers between devices, local(): lax.all_gather(normed.transpose(1, 0, 2)[None], 'tp', axis=0, tiled=True)  84.3 us
    ppermute x6, starting transfers between devices, gather_line(): got.append(lax.ppermute(packed, 'seq', pairs))  20.8 us
    ppermute x6, waiting for transfers between devices, gather_line(): got.append(lax.ppermute(packed, 'seq', pairs))  8.31 us
    dot_general x1, matrix products, local(): lax.dot_general(gathered, out_weight.reshape(tp_count, head_count, HD, -1...  6.8 us
    reshape x1, local copies, waits for them, and re-layouts, local(): out_weight.reshape(tp_count, head_count, HD, -1)  3.55 us
  transfers between devices with their start and end apart: 9, of which 4 were waited for; matrix products, arithmetic and copies ran while one was open for 5% of the time, Pallas kernels for 0%

profile of v14, /device:TPU:6, one launch (start us, length us, event | category | flops | bytes accessed | tf_op | source)
XLA Modules:
  0.0 158.8 jit_solution(4457875358700305816)
XLA Ops:
  6.5 0.0 copy-start
  6.5 0.0 copy-start.3
  6.5 0.0 all-gather.3.cloned.1.call-start
  6.5 0.8 reshape.86
  7.3 0.6 reduce-window.6
  7.9 0.2 slice_reduce_fusion
  8.1 0.2 reduce-window.9
  8.3 0.1 add_bitcast_fusion
  8.4 0.2 slice_reduce_fusion.11
  8.6 0.1 broadcast_select_fusion.1
  8.7 1.2 copy.62
  9.8 1.3 fusion.22
  11.1 0.1 broadcast_in_dim.107
  11.2 1.9 %collective-permute-start = (f32[2,136,128]{2,1,0:T(8,128)S(1)}, f32[2,136,128]{2,1,0:T(8,128)S(1)}, u32[]{:S(2)}, u32[]{:S(2)}) collective-permute-start(f32[2,136,128]{2,1,0:T(8,128)S(1)} %pad_maximum_fusion.1), channel_id=1, source_target_pairs={{0,16},{16,0},{32,48},{48,32},{64,80},{80,64},{96,112},{112,96},{1... | collective-permute-start | bytes 417800 | tf_op jit(solution)/shard_map/ppermute | solution.py:47
  13.1 1.3 fusion.20
  14.4 0.0 collective-permute-done
  14.5 0.1 slice_reduce_fusion.10
  14.6 0.1 fusion.45
  14.7 7.8 %collective-permute-start.1 = (f32[2,136,128]{2,1,0:T(8,128)S(1)}, f32[2,136,128]{2,1,0:T(8,128)S(1)}, u32[]{:S(2)}, u32[]{:S(2)}) collective-permute-start(f32[2,136,128]{2,1,0:T(8,128)S(1)} %fusion.45), channel_id=1, source_target_pairs={{0,32},{16,112},{32,64},{48,16},{64,96},{80,48},{96,0},{112,80},{1... | collective-permute-start | bytes 417800 | tf_op jit(solution)/shard_map/ppermute | solution.py:28
  22.5 1.9 %collective-permute-start.3 = (f32[2,136,128]{2,1,0:T(8,128)S(1)}, f32[2,136,128]{2,1,0:T(8,128)S(1)}, u32[]{:S(2)}, u32[]{:S(2)}) collective-permute-start(f32[2,136,128]{2,1,0:T(8,128)S(1)} %fusion.45), channel_id=1, source_target_pairs={{0,96},{16,48},{32,0},{48,80},{64,32},{80,112},{96,64},{112,16},{1... | collective-permute-start | bytes 417800 | tf_op jit(solution)/shard_map/ppermute | solution.py:28
  24.4 3.4 %collective-permute-start.2 = (f32[2,136,128]{2,1,0:T(8,128)S(1)}, f32[2,136,128]{2,1,0:T(8,128)S(1)}, u32[]{:S(2)}, u32[]{:S(2)}) collective-permute-start(f32[2,136,128]{2,1,0:T(8,128)S(1)} %fusion.45), channel_id=1, source_target_pairs={{0,64},{16,80},{32,96},{48,112},{64,0},{80,16},{96,32},{112,48},{1... | collective-permute-start | bytes 417800 | tf_op jit(solution)/shard_map/ppermute | solution.py:28
  27.8 0.1 slice_reduce_fusion.6
  27.9 0.0 collective-permute-done.1
  27.9 0.1 fusion.42
  28.0 0.1 slice_reduce_fusion.5
  28.1 5.5 %collective-permute-done.2 = f32[2,136,128]{2,1,0:T(8,128)S(1)} collective-permute-done((f32[2,136,128]{2,1,0:T(8,128)S(1)}, f32[2,136,128]{2,1,0:T(8,128)S(1)}, u32[]{:S(2)}, u32[]{:S(2)}) %collective-permute-start.2) | collective-permute-done | bytes 139296 | tf_op jit(solution)/shard_map/ppermute | solution.py:28
  33.6 0.1 add_select_fusion.3
  33.8 0.1 slice_reduce_fusion.4
  33.9 0.1 slice_reduce_fusion.8
  34.0 0.1 slice_reduce_fusion.9
  34.1 0.0 collective-permute-done.3
  34.1 0.1 slice_reduce_fusion.7
  34.2 0.8 select_select_fusion
  35.0 1.9 %collective-permute-start.6 = (f32[2,136,128]{2,1,0:T(8,128)}, f32[2,136,128]{2,1,0:T(8,128)}, u32[]{:S(2)}, u32[]{:S(2)}) collective-permute-start(f32[2,136,128]{2,1,0:T(8,128)} %get-tuple-element.17), channel_id=1, source_target_pairs={{0,384},{16,144},{32,416},{48,176},{64,448},{80,208},{96,480},{112... | collective-permute-start | bytes 417800 | tf_op jit(solution)/shard_map/ppermute | solution.py:28
  36.9 2.3 %collective-permute-start.5 = (f32[2,136,128]{2,1,0:T(8,128)}, f32[2,136,128]{2,1,0:T(8,128)}, u32[]{:S(2)}, u32[]{:S(2)}) collective-permute-start(f32[2,136,128]{2,1,0:T(8,128)} %get-tuple-element.17), channel_id=1, source_target_pairs={{0,256},{16,272},{32,288},{48,304},{64,320},{80,336},{96,352},{112... | collective-permute-start | bytes 417800 | tf_op jit(solution)/shard_map/ppermute | solution.py:28
  39.2 3.6 %collective-permute-start.4 = (f32[2,136,128]{2,1,0:T(8,128)}, f32[2,136,128]{2,1,0:T(8,128)S(1)}, u32[]{:S(2)}, u32[]{:S(2)}) collective-permute-start(f32[2,136,128]{2,1,0:T(8,128)} %get-tuple-element.17), channel_id=1, source_target_pairs={{0,128},{16,400},{32,160},{48,432},{64,192},{80,464},{96,224},{112... | collective-permute-start | bytes 417800 | tf_op jit(solution)/shard_map/ppermute | solution.py:28
  42.8 0.0 copy-done
  42.8 0.0 copy-done.3
  42.8 3.0 %fusion.8 = f32[768,2,128]{2,0,1:T(8,128)} fusion(s32[2,768]{1,0:T(2,128)S(1)} %get-tuple-element.16, bf16[768,2,128]{0,2,1:T(8,128)(2,1)S(1)} %bitcast.91, bf16[768,256]{1,0:T(8,128)(2,1)S(1)} %copy-done, bf16[768,256]{1,0:T(8,128)(2,1)S(1)} %copy-done.3), kind=kOutput, calls=%fused_computation.6 | convolution fusion | flops 612237312 | bytes 1972224 | tf_op jit(solution)/shard_map/hts,shd->thd/dot_general | solution.py:89
  45.8 0.0 copy-start.2
  45.8 0.0 copy-start.1
  45.8 0.1 slice_reduce_fusion.3
  45.9 0.0 collective-permute-done.6
  45.9 0.0 collective-permute-done.5
  45.9 2.8 %collective-permute-done.4 = f32[2,136,128]{2,1,0:T(8,128)S(1)} collective-permute-done((f32[2,136,128]{2,1,0:T(8,128)}, f32[2,136,128]{2,1,0:T(8,128)S(1)}, u32[]{:S(2)}, u32[]{:S(2)}) %collective-permute-start.4) | collective-permute-done | bytes 139296 | tf_op jit(solution)/shard_map/ppermute | solution.py:28
  48.7 0.1 fusion.43
  48.8 0.1 slice_reduce_fusion.2
  48.9 1.0 add_select_fusion.1
  49.9 0.1 slice_reduce_fusion.1
  50.0 1.0 multiply_add_fusion
  51.1 1.9 %collective-permute-start.7 = (bf16[2,128,128]{2,1,0:T(8,128)(2,1)S(1)}, bf16[2,128,128]{2,1,0:T(8,128)(2,1)S(1)}, u32[]{:S(2)}, u32[]{:S(2)}) collective-permute-start(bf16[2,128,128]{2,1,0:T(8,128)(2,1)S(1)} %get-tuple-element.13), channel_id=1, source_target_pairs={{0,16},{16,0},{32,48},{48,32},{64,80},{80,64},{96,112},{112,96},{1... | collective-permute-start | bytes 196616 | tf_op jit(solution)/shard_map/ppermute | solution.py:69
  53.0 1.2 collective-permute-done.7
  54.2 0.3 fusion.10
  54.5 1.7 %multiply_reduce_fusion = (f32[768,2]{0,1:T(2,128)S(1)}, f32[768,2,128]{2,0,1:T(8,128)S(1)}) fusion(f32[768,2]{0,1:T(2,128)S(1)} %get-tuple-element.20, bf16[2,128,128]{2,1,0:T(8,128)(2,1)S(1)} %get-tuple-element.14, bf16[2,128,128]{2,1,0:T(8,128)(2,1)S(1)} %collective-permute-done.7, pred[]{:T(512)S(6)} %eq.8, f32[768,2,128]{2,0,1:T(8,128)} %fusion.8, ...), kind=kOutput, calls=%fused_computation.18 | convolution fusion | flops 51345920 | bytes 2895873 | tf_op jit(solution)/shard_map/thd,hde->the/dot_general | solution.py:116
  56.2 0.0 copy-done.2
  56.2 1.0 fusion.19
  57.2 0.0 all-gather.3.cloned.1.call-update
  57.3 0.0 copy-done.1
  57.3 3.6 %reshape.90 = bf16[16,2,128,320]{2,1,0,3:T(2,128)(2,1)} reshape(bf16[4096,320]{0,1:T(8,128)(2,1)S(1)} %copy-done.1) | data formatting | bytes 5242880 | tf_op jit(solution)/shard_map/reshape | solution.py:128
  60.8 84.3 %all-gather.3.cloned.1.call-done = bf16[32,768,128]{2,1,0:T(8,128)(2,1)} async-done(((bf16[2,768,128]{2,1,0:T(8,128)(2,1)}), bf16[32,768,128]{2,1,0:T(8,128)(2,1)}) %all-gather.3.cloned.1.call-update) | async-done | bytes 6291472 | tf_op jit(solution)/shard_map/all_gather | solution.py:125
  145.1 6.8 %fusion.14 = bf16[768,320]{0,1:T(8,128)(2,1)} fusion(bf16[16,2,768,128]{3,2,1,0:T(8,128)(2,1)} %bitcast.95, bf16[16,2,128,320]{2,1,0,3:T(2,128)(2,1)} %reshape.90, bf16[768,320]{0,1:T(8,128)(2,1)} %param.13), kind=kOutput, calls=%fused_computation.12 | convolution fusion | flops 2014003200 | bytes 9895936 | tf_op jit(solution)/shard_map/dot_general | solution.py:126
  (8 shorter events, 0.1 us)
Async XLA Ops:
  6.5 36.3 %copy-start = (bf16[768,256]{1,0:T(8,128)(2,1)S(1)}, bf16[768,256]{1,0:T(8,128)(2,1)}, u32[]{:S(2)}) copy-start(bf16[768,256]{1,0:T(8,128)(2,1)} %param.7) | copy-start | bytes 1179652
  6.5 36.3 %copy-start.3 = (bf16[768,256]{1,0:T(8,128)(2,1)S(1)}, bf16[768,256]{1,0:T(8,128)(2,1)}, u32[]{:S(2)}) copy-start(bf16[768,256]{1,0:T(8,128)(2,1)} %param.9) | copy-start | bytes 1179652
  6.5 138.6 %all-gather.3.cloned.1.call-start = ((), (), s32[]{:S(2)}) async-start(), calls=%async_computation | async-start | bytes 6684672 | tf_op jit(solution)/shard_map/all_gather | solution.py:125
  11.2 3.3 %collective-permute-start = (f32[2,136,128]{2,1,0:T(8,128)S(1)}, f32[2,136,128]{2,1,0:T(8,128)S(1)}, u32[]{:S(2)}, u32[]{:S(2)}) collective-permute-start(f32[2,136,128]{2,1,0:T(8,128)S(1)} %pad_maximum_fusion.1), channel_id=1, source_target_pairs={{0,16},{16,0},{32,48},{48,32},{64,80},{80,64},{96,112},{112,96},{1... | collective-permute-start | bytes 417800 | tf_op jit(solution)/shard_map/ppermute | solution.py:47
  14.7 13.2 %collective-permute-start.1 = (f32[2,136,128]{2,1,0:T(8,128)S(1)}, f32[2,136,128]{2,1,0:T(8,128)S(1)}, u32[]{:S(2)}, u32[]{:S(2)}) collective-permute-start(f32[2,136,128]{2,1,0:T(8,128)S(1)} %fusion.45), channel_id=1, source_target_pairs={{0,32},{16,112},{32,64},{48,16},{64,96},{80,48},{96,0},{112,80},{1... | collective-permute-start | bytes 417800 | tf_op jit(solution)/shard_map/ppermute | solution.py:28
  22.5 11.6 %collective-permute-start.3 = (f32[2,136,128]{2,1,0:T(8,128)S(1)}, f32[2,136,128]{2,1,0:T(8,128)S(1)}, u32[]{:S(2)}, u32[]{:S(2)}) collective-permute-start(f32[2,136,128]{2,1,0:T(8,128)S(1)} %fusion.45), channel_id=1, source_target_pairs={{0,96},{16,48},{32,0},{48,80},{64,32},{80,112},{96,64},{112,16},{1... | collective-permute-start | bytes 417800 | tf_op jit(solution)/shard_map/ppermute | solution.py:28
  24.4 9.2 %collective-permute-start.2 = (f32[2,136,128]{2,1,0:T(8,128)S(1)}, f32[2,136,128]{2,1,0:T(8,128)S(1)}, u32[]{:S(2)}, u32[]{:S(2)}) collective-permute-start(f32[2,136,128]{2,1,0:T(8,128)S(1)} %fusion.45), channel_id=1, source_target_pairs={{0,64},{16,80},{32,96},{48,112},{64,0},{80,16},{96,32},{112,48},{1... | collective-permute-start | bytes 417800 | tf_op jit(solution)/shard_map/ppermute | solution.py:28
  35.0 10.9 %collective-permute-start.6 = (f32[2,136,128]{2,1,0:T(8,128)}, f32[2,136,128]{2,1,0:T(8,128)}, u32[]{:S(2)}, u32[]{:S(2)}) collective-permute-start(f32[2,136,128]{2,1,0:T(8,128)} %get-tuple-element.17), channel_id=1, source_target_pairs={{0,384},{16,144},{32,416},{48,176},{64,448},{80,208},{96,480},{112... | collective-permute-start | bytes 417800 | tf_op jit(solution)/shard_map/ppermute | solution.py:28
  36.9 9.0 %collective-permute-start.5 = (f32[2,136,128]{2,1,0:T(8,128)}, f32[2,136,128]{2,1,0:T(8,128)}, u32[]{:S(2)}, u32[]{:S(2)}) collective-permute-start(f32[2,136,128]{2,1,0:T(8,128)} %get-tuple-element.17), channel_id=1, source_target_pairs={{0,256},{16,272},{32,288},{48,304},{64,320},{80,336},{96,352},{112... | collective-permute-start | bytes 417800 | tf_op jit(solution)/shard_map/ppermute | solution.py:28
  39.2 9.5 %collective-permute-start.4 = (f32[2,136,128]{2,1,0:T(8,128)}, f32[2,136,128]{2,1,0:T(8,128)S(1)}, u32[]{:S(2)}, u32[]{:S(2)}) collective-permute-start(f32[2,136,128]{2,1,0:T(8,128)} %get-tuple-element.17), channel_id=1, source_target_pairs={{0,128},{16,400},{32,160},{48,432},{64,192},{80,464},{96,224},{112... | collective-permute-start | bytes 417800 | tf_op jit(solution)/shard_map/ppermute | solution.py:28
  45.8 10.4 %copy-start.2 = (f32[256]{0:T(256)S(1)}, f32[256]{0:T(256)}, u32[]{:S(2)}) copy-start(f32[256]{0:T(256)} %param.11) | copy-start | bytes 3076
  45.8 11.5 %copy-start.1 = (bf16[4096,320]{0,1:T(8,128)(2,1)S(1)}, bf16[4096,320]{0,1:T(8,128)(2,1)}, u32[]{:S(2)}) copy-start(bf16[4096,320]{0,1:T(8,128)(2,1)} %param.12) | copy-start | bytes 7864324
  51.1 3.1 %collective-permute-start.7 = (bf16[2,128,128]{2,1,0:T(8,128)(2,1)S(1)}, bf16[2,128,128]{2,1,0:T(8,128)(2,1)S(1)}, u32[]{:S(2)}, u32[]{:S(2)}) collective-permute-start(bf16[2,128,128]{2,1,0:T(8,128)(2,1)S(1)} %get-tuple-element.13), channel_id=1, source_target_pairs={{0,16},{16,0},{32,48},{48,32},{64,80},{80,64},{96,112},{112,96},{1... | collective-permute-start | bytes 196616 | tf_op jit(solution)/shard_map/ppermute | solution.py:69
Sparse Core Ops, SparseCore 0:
  57.4 87.6 all-gather.2

commit v15 on v14

--- a/solution.py
+++ b/solution.py
@@ -80,7 +80,15 @@
     query_heads = query_vectors.reshape(tok_rows, head_count, HD)
     key_heads = key_vectors.reshape(tok_rows, head_count, HD)
     value_heads = value_vectors.reshape(tok_rows, head_count, HD)
-    local_exp = jnp.cumsum(decay_exp, axis=1)
+    tok_dev = decay_exp.shape[1]
+    upper = (
+        lax.broadcasted_iota(jnp.int32, (tok_dev, tok_dev), 0)
+        <= lax.broadcasted_iota(jnp.int32, (tok_dev, tok_dev), 1)
+    ).astype(jnp.float32)
+    local_exp = jnp.dot(
+        decay_exp.astype(jnp.float32), upper, precision=lax.Precision.HIGHEST,
+        preferred_element_type=jnp.float32,
+    ).astype(jnp.int32)
     block_exp = local_exp[:, -1]
     local_rows = local_exp.T
     scores = jnp.einsum("thd,shd->hts", query_heads, key_heads, preferred_element_type=jnp.float32)

time: 159 us -> 159 us (level)
  no operation moved by 1% of the time
where the time goes in v15:
time: 159 us; the launch traced here: 158 us
  waiting for transfers between devices  93.8 us (59%)
  starting transfers between devices  24.6 us (15%)
  matrix products  15.5 us (10%)
  between operations  13.7 us (9%)
  local copies, waits for them, and re-layouts  6 us (4%)
  other arithmetic  4.48 us (3%)
    all_gather x1, waiting for transfers between devices, local(): lax.all_gather(normed.transpose(1, 0, 2)[None], 'tp', axis=0, tiled=True)  84.3 us
    ppermute x6, starting transfers between devices, gather_line(): got.append(lax.ppermute(packed, 'seq', pairs))  20.8 us
    ppermute x6, waiting for transfers between devices, gather_line(): got.append(lax.ppermute(packed, 'seq', pairs))  8.31 us
    dot_general x1, matrix products, local(): lax.dot_general(gathered, out_weight.reshape(tp_count, head_count, HD, -1...  6.8 us
    reshape x1, local copies, waits for them, and re-layouts, local(): out_weight.reshape(tp_count, head_count, HD, -1)  3.55 us
  transfers between devices with their start and end apart: 9, of which 4 were waited for; matrix products, arithmetic and copies ran while one was open for 5% of the time, Pallas kernels for 0%

profile of v15, /device:TPU:6, one launch (start us, length us, event | category | flops | bytes accessed | tf_op | source)
XLA Modules:
  0.0 158.1 jit_solution(12575842245312707439)
XLA Ops:
  6.5 0.0 copy-start
  6.5 0.0 copy-start.3
  6.5 0.0 all-gather.3.cloned.1.call-start
  6.5 1.2 fusion.18
  7.8 0.2 slice_reduce_fusion.10
  8.0 0.1 broadcast_select_fusion.1
  8.1 1.2 copy.48
  9.2 1.3 fusion.24
  10.5 0.1 broadcast_in_dim.107
  10.6 1.9 %collective-permute-start = (f32[2,136,128]{2,1,0:T(8,128)S(1)}, f32[2,136,128]{2,1,0:T(8,128)S(1)}, u32[]{:S(2)}, u32[]{:S(2)}) collective-permute-start(f32[2,136,128]{2,1,0:T(8,128)S(1)} %pad_maximum_fusion.1), channel_id=1, source_target_pairs={{0,16},{16,0},{32,48},{48,32},{64,80},{80,64},{96,112},{112,96},{1... | collective-permute-start | bytes 417800 | tf_op jit(solution)/shard_map/ppermute | solution.py:47
  12.5 1.3 fusion.22
  13.8 0.0 collective-permute-done
  13.8 0.1 slice_reduce_fusion.9
  13.9 0.1 fusion.47
  14.0 7.8 %collective-permute-start.1 = (f32[2,136,128]{2,1,0:T(8,128)S(1)}, f32[2,136,128]{2,1,0:T(8,128)S(1)}, u32[]{:S(2)}, u32[]{:S(2)}) collective-permute-start(f32[2,136,128]{2,1,0:T(8,128)S(1)} %fusion.47), channel_id=1, source_target_pairs={{0,32},{16,112},{32,64},{48,16},{64,96},{80,48},{96,0},{112,80},{1... | collective-permute-start | bytes 417800 | tf_op jit(solution)/shard_map/ppermute | solution.py:28
  21.9 1.9 %collective-permute-start.3 = (f32[2,136,128]{2,1,0:T(8,128)S(1)}, f32[2,136,128]{2,1,0:T(8,128)S(1)}, u32[]{:S(2)}, u32[]{:S(2)}) collective-permute-start(f32[2,136,128]{2,1,0:T(8,128)S(1)} %fusion.47), channel_id=1, source_target_pairs={{0,96},{16,48},{32,0},{48,80},{64,32},{80,112},{96,64},{112,16},{1... | collective-permute-start | bytes 417800 | tf_op jit(solution)/shard_map/ppermute | solution.py:28
  23.8 3.4 %collective-permute-start.2 = (f32[2,136,128]{2,1,0:T(8,128)S(1)}, f32[2,136,128]{2,1,0:T(8,128)S(1)}, u32[]{:S(2)}, u32[]{:S(2)}) collective-permute-start(f32[2,136,128]{2,1,0:T(8,128)S(1)} %fusion.47), channel_id=1, source_target_pairs={{0,64},{16,80},{32,96},{48,112},{64,0},{80,16},{96,32},{112,48},{1... | collective-permute-start | bytes 417800 | tf_op jit(solution)/shard_map/ppermute | solution.py:28
  27.2 0.1 slice_reduce_fusion.5
  27.3 0.0 collective-permute-done.1
  27.3 0.1 fusion.44
  27.4 0.1 slice_reduce_fusion.4
  27.5 5.5 %collective-permute-done.2 = f32[2,136,128]{2,1,0:T(8,128)S(1)} collective-permute-done((f32[2,136,128]{2,1,0:T(8,128)S(1)}, f32[2,136,128]{2,1,0:T(8,128)S(1)}, u32[]{:S(2)}, u32[]{:S(2)}) %collective-permute-start.2) | collective-permute-done | bytes 139296 | tf_op jit(solution)/shard_map/ppermute | solution.py:28
  33.0 0.1 add_select_fusion.3
  33.1 0.1 slice_reduce_fusion.3
  33.2 0.1 slice_reduce_fusion.7
  33.3 0.1 slice_reduce_fusion.8
  33.4 0.0 collective-permute-done.3
  33.5 0.1 slice_reduce_fusion.6
  33.6 0.8 select_select_fusion
  34.4 1.9 %collective-permute-start.6 = (f32[2,136,128]{2,1,0:T(8,128)}, f32[2,136,128]{2,1,0:T(8,128)}, u32[]{:S(2)}, u32[]{:S(2)}) collective-permute-start(f32[2,136,128]{2,1,0:T(8,128)} %get-tuple-element.15), channel_id=1, source_target_pairs={{0,384},{16,144},{32,416},{48,176},{64,448},{80,208},{96,480},{112... | collective-permute-start | bytes 417800 | tf_op jit(solution)/shard_map/ppermute | solution.py:28
  36.3 2.3 %collective-permute-start.5 = (f32[2,136,128]{2,1,0:T(8,128)}, f32[2,136,128]{2,1,0:T(8,128)}, u32[]{:S(2)}, u32[]{:S(2)}) collective-permute-start(f32[2,136,128]{2,1,0:T(8,128)} %get-tuple-element.15), channel_id=1, source_target_pairs={{0,256},{16,272},{32,288},{48,304},{64,320},{80,336},{96,352},{112... | collective-permute-start | bytes 417800 | tf_op jit(solution)/shard_map/ppermute | solution.py:28
  38.6 3.6 %collective-permute-start.4 = (f32[2,136,128]{2,1,0:T(8,128)}, f32[2,136,128]{2,1,0:T(8,128)S(1)}, u32[]{:S(2)}, u32[]{:S(2)}) collective-permute-start(f32[2,136,128]{2,1,0:T(8,128)} %get-tuple-element.15), channel_id=1, source_target_pairs={{0,128},{16,400},{32,160},{48,432},{64,192},{80,464},{96,224},{112... | collective-permute-start | bytes 417800 | tf_op jit(solution)/shard_map/ppermute | solution.py:28
  42.2 0.0 copy-done
  42.2 0.0 copy-done.3
  42.2 3.0 %fusion.9 = f32[768,2,128]{2,0,1:T(8,128)} fusion(s32[2,768]{1,0:T(2,128)S(1)} %bitcast.80, bf16[768,2,128]{0,2,1:T(8,128)(2,1)S(1)} %bitcast.77, bf16[768,256]{1,0:T(8,128)(2,1)S(1)} %copy-done, bf16[768,256]{1,0:T(8,128)(2,1)S(1)} %copy-done.3), kind=kOutput, calls=%fused_computation.8 | convolution fusion | flops 612237312 | bytes 1972224 | tf_op jit(solution)/shard_map/hts,shd->thd/dot_general | solution.py:97
  45.2 0.0 copy-start.2
  45.2 0.0 copy-start.1
  45.2 0.1 slice_reduce_fusion.2
  45.3 0.0 collective-permute-done.6
  45.3 0.0 collective-permute-done.5
  45.3 2.8 %collective-permute-done.4 = f32[2,136,128]{2,1,0:T(8,128)S(1)} collective-permute-done((f32[2,136,128]{2,1,0:T(8,128)}, f32[2,136,128]{2,1,0:T(8,128)S(1)}, u32[]{:S(2)}, u32[]{:S(2)}) %collective-permute-start.4) | collective-permute-done | bytes 139296 | tf_op jit(solution)/shard_map/ppermute | solution.py:28
  48.1 0.1 fusion.45
  48.2 0.1 slice_reduce_fusion.1
  48.3 1.0 add_select_fusion.1
  49.3 0.1 slice_reduce_fusion
  49.4 1.0 multiply_add_fusion
  50.4 1.9 %collective-permute-start.7 = (bf16[2,128,128]{2,1,0:T(8,128)(2,1)S(1)}, bf16[2,128,128]{2,1,0:T(8,128)(2,1)S(1)}, u32[]{:S(2)}, u32[]{:S(2)}) collective-permute-start(bf16[2,128,128]{2,1,0:T(8,128)(2,1)S(1)} %get-tuple-element.13), channel_id=1, source_target_pairs={{0,16},{16,0},{32,48},{48,32},{64,80},{80,64},{96,112},{112,96},{1... | collective-permute-start | bytes 196616 | tf_op jit(solution)/shard_map/ppermute | solution.py:69
  52.4 1.2 collective-permute-done.7
  53.6 0.3 fusion.11
  53.9 1.7 %multiply_reduce_fusion = (f32[768,2]{0,1:T(2,128)S(1)}, f32[768,2,128]{2,0,1:T(8,128)S(1)}) fusion(f32[768,2]{0,1:T(2,128)S(1)} %get-tuple-element.18, bf16[2,128,128]{2,1,0:T(8,128)(2,1)S(1)} %get-tuple-element.14, bf16[2,128,128]{2,1,0:T(8,128)(2,1)S(1)} %collective-permute-done.7, pred[]{:T(512)S(6)} %eq.8, f32[768,2,128]{2,0,1:T(8,128)} %fusion.9, ...), kind=kOutput, calls=%fused_computation.21 | convolution fusion | flops 51345920 | bytes 2895873 | tf_op jit(solution)/shard_map/thd,hde->the/dot_general | solution.py:124
  55.6 0.0 copy-done.2
  55.6 1.0 fusion.21
  56.6 0.0 all-gather.3.cloned.1.call-update
  56.7 0.0 copy-done.1
  56.7 3.6 %reshape.56 = bf16[16,2,128,320]{2,1,0,3:T(2,128)(2,1)} reshape(bf16[4096,320]{0,1:T(8,128)(2,1)S(1)} %copy-done.1) | data formatting | bytes 5242880 | tf_op jit(solution)/shard_map/reshape | solution.py:136
  60.2 84.3 %all-gather.3.cloned.1.call-done = bf16[32,768,128]{2,1,0:T(8,128)(2,1)} async-done(((bf16[2,768,128]{2,1,0:T(8,128)(2,1)}), bf16[32,768,128]{2,1,0:T(8,128)(2,1)}) %all-gather.3.cloned.1.call-update) | async-done | bytes 6291472 | tf_op jit(solution)/shard_map/all_gather | solution.py:133
  144.5 6.8 %fusion.15 = bf16[768,320]{0,1:T(8,128)(2,1)} fusion(bf16[16,2,768,128]{3,2,1,0:T(8,128)(2,1)} %bitcast.82, bf16[16,2,128,320]{2,1,0,3:T(2,128)(2,1)} %reshape.56, bf16[768,320]{0,1:T(8,128)(2,1)} %param.13), kind=kOutput, calls=%fused_computation.14 | convolution fusion | flops 2014003200 | bytes 9895936 | tf_op jit(solution)/shard_map/dot_general | solution.py:134
  (7 shorter events, 0.1 us)
Async XLA Ops:
  6.5 35.6 %copy-start = (bf16[768,256]{1,0:T(8,128)(2,1)S(1)}, bf16[768,256]{1,0:T(8,128)(2,1)}, u32[]{:S(2)}) copy-start(bf16[768,256]{1,0:T(8,128)(2,1)} %param.7) | copy-start | bytes 1179652
  6.5 35.6 %copy-start.3 = (bf16[768,256]{1,0:T(8,128)(2,1)S(1)}, bf16[768,256]{1,0:T(8,128)(2,1)}, u32[]{:S(2)}) copy-start(bf16[768,256]{1,0:T(8,128)(2,1)} %param.9) | copy-start | bytes 1179652
  6.5 137.9 %all-gather.3.cloned.1.call-start = ((), (), s32[]{:S(2)}) async-start(), calls=%async_computation | async-start | bytes 6684672 | tf_op jit(solution)/shard_map/all_gather | solution.py:133
  10.6 3.3 %collective-permute-start = (f32[2,136,128]{2,1,0:T(8,128)S(1)}, f32[2,136,128]{2,1,0:T(8,128)S(1)}, u32[]{:S(2)}, u32[]{:S(2)}) collective-permute-start(f32[2,136,128]{2,1,0:T(8,128)S(1)} %pad_maximum_fusion.1), channel_id=1, source_target_pairs={{0,16},{16,0},{32,48},{48,32},{64,80},{80,64},{96,112},{112,96},{1... | collective-permute-start | bytes 417800 | tf_op jit(solution)/shard_map/ppermute | solution.py:47
  14.0 13.2 %collective-permute-start.1 = (f32[2,136,128]{2,1,0:T(8,128)S(1)}, f32[2,136,128]{2,1,0:T(8,128)S(1)}, u32[]{:S(2)}, u32[]{:S(2)}) collective-permute-start(f32[2,136,128]{2,1,0:T(8,128)S(1)} %fusion.47), channel_id=1, source_target_pairs={{0,32},{16,112},{32,64},{48,16},{64,96},{80,48},{96,0},{112,80},{1... | collective-permute-start | bytes 417800 | tf_op jit(solution)/shard_map/ppermute | solution.py:28
  21.9 11.6 %collective-permute-start.3 = (f32[2,136,128]{2,1,0:T(8,128)S(1)}, f32[2,136,128]{2,1,0:T(8,128)S(1)}, u32[]{:S(2)}, u32[]{:S(2)}) collective-permute-start(f32[2,136,128]{2,1,0:T(8,128)S(1)} %fusion.47), channel_id=1, source_target_pairs={{0,96},{16,48},{32,0},{48,80},{64,32},{80,112},{96,64},{112,16},{1... | collective-permute-start | bytes 417800 | tf_op jit(solution)/shard_map/ppermute | solution.py:28
  23.8 9.2 %collective-permute-start.2 = (f32[2,136,128]{2,1,0:T(8,128)S(1)}, f32[2,136,128]{2,1,0:T(8,128)S(1)}, u32[]{:S(2)}, u32[]{:S(2)}) collective-permute-start(f32[2,136,128]{2,1,0:T(8,128)S(1)} %fusion.47), channel_id=1, source_target_pairs={{0,64},{16,80},{32,96},{48,112},{64,0},{80,16},{96,32},{112,48},{1... | collective-permute-start | bytes 417800 | tf_op jit(solution)/shard_map/ppermute | solution.py:28
  34.4 10.9 %collective-permute-start.6 = (f32[2,136,128]{2,1,0:T(8,128)}, f32[2,136,128]{2,1,0:T(8,128)}, u32[]{:S(2)}, u32[]{:S(2)}) collective-permute-start(f32[2,136,128]{2,1,0:T(8,128)} %get-tuple-element.15), channel_id=1, source_target_pairs={{0,384},{16,144},{32,416},{48,176},{64,448},{80,208},{96,480},{112... | collective-permute-start | bytes 417800 | tf_op jit(solution)/shard_map/ppermute | solution.py:28
  36.3 9.0 %collective-permute-start.5 = (f32[2,136,128]{2,1,0:T(8,128)}, f32[2,136,128]{2,1,0:T(8,128)}, u32[]{:S(2)}, u32[]{:S(2)}) collective-permute-start(f32[2,136,128]{2,1,0:T(8,128)} %get-tuple-element.15), channel_id=1, source_target_pairs={{0,256},{16,272},{32,288},{48,304},{64,320},{80,336},{96,352},{112... | collective-permute-start | bytes 417800 | tf_op jit(solution)/shard_map/ppermute | solution.py:28
  38.6 9.5 %collective-permute-start.4 = (f32[2,136,128]{2,1,0:T(8,128)}, f32[2,136,128]{2,1,0:T(8,128)S(1)}, u32[]{:S(2)}, u32[]{:S(2)}) collective-permute-start(f32[2,136,128]{2,1,0:T(8,128)} %get-tuple-element.15), channel_id=1, source_target_pairs={{0,128},{16,400},{32,160},{48,432},{64,192},{80,464},{96,224},{112... | collective-permute-start | bytes 417800 | tf_op jit(solution)/shard_map/ppermute | solution.py:28
  45.2 10.4 %copy-start.2 = (f32[256]{0:T(256)S(1)}, f32[256]{0:T(256)}, u32[]{:S(2)}) copy-start(f32[256]{0:T(256)} %param.11) | copy-start | bytes 3076
  45.2 11.5 %copy-start.1 = (bf16[4096,320]{0,1:T(8,128)(2,1)S(1)}, bf16[4096,320]{0,1:T(8,128)(2,1)}, u32[]{:S(2)}) copy-start(bf16[4096,320]{0,1:T(8,128)(2,1)} %param.12) | copy-start | bytes 7864324
  50.4 3.1 %collective-permute-start.7 = (bf16[2,128,128]{2,1,0:T(8,128)(2,1)S(1)}, bf16[2,128,128]{2,1,0:T(8,128)(2,1)S(1)}, u32[]{:S(2)}, u32[]{:S(2)}) collective-permute-start(bf16[2,128,128]{2,1,0:T(8,128)(2,1)S(1)} %get-tuple-element.13), channel_id=1, source_target_pairs={{0,16},{16,0},{32,48},{48,32},{64,80},{80,64},{96,112},{112,96},{1... | collective-permute-start | bytes 196616 | tf_op jit(solution)/shard_map/ppermute | solution.py:69
Sparse Core Ops, SparseCore 0:
  56.8 87.6 all-gather.2

commit v16 on v15

--- a/solution.py
+++ b/solution.py
@@ -25,7 +25,8 @@
             at = (i // stride) % line
             step = -shift if i % 2 else shift
             pairs.append((i, i + (((at + step) % line) - at) * stride))
-        got.append(lax.ppermute(packed, "seq", pairs))
+        sent = lax.ppermute(packed.astype(jnp.bfloat16), "seq", pairs)
+        got.append(sent.astype(jnp.float32))
     return got
 
 

time: 159 us -> 157 us (0.987)
  other arithmetic: 4.48 us -> 2.09 us
  transfers between devices with their start and end apart: 9 -> 9, of which waited for: 4 -> 5; matrix products, arithmetic and copies ran while one was open for 5% -> 6% of each run, Pallas kernels for 0% -> 0%
where the time goes in v16:
time: 157 us; the launch traced here: 156 us
  waiting for transfers between devices  94 us (60%)
  starting transfers between devices  24.8 us (16%)
  matrix products  15.3 us (10%)
  between operations  13.7 us (9%)
  local copies, waits for them, and re-layouts  6 us (4%)
  other arithmetic  2.09 us (1%)
    all_gather x1, waiting for transfers between devices, local(): lax.all_gather(normed.transpose(1, 0, 2)[None], 'tp', axis=0, tiled=True)  83.8 us
    ppermute x6, starting transfers between devices, gather_line(): sent = lax.ppermute(packed.astype(jnp.bfloat16), 'seq', pairs)  20.9 us
    ppermute x6, waiting for transfers between devices, gather_line(): sent = lax.ppermute(packed.astype(jnp.bfloat16), 'seq', pairs)  8.98 us
    dot_general x1, matrix products, local(): lax.dot_general(gathered, out_weight.reshape(tp_count, head_count, HD, -1...  6.8 us
    dot_general x1, matrix products, local(): jnp.einsum('hts,shd->thd', local_weights, value_heads, preferred_element_...  3.98 us
    reshape x1, local copies, waits for them, and re-layouts, local(): out_weight.reshape(tp_count, head_count, HD, -1)  3.55 us
  transfers between devices with their start and end apart: 9, of which 5 were waited for; matrix products, arithmetic and copies ran while one was open for 6% of the time, Pallas kernels for 0%

profile of v16, /device:TPU:6, one launch (start us, length us, event | category | flops | bytes accessed | tf_op | source)
XLA Modules:
  0.0 155.9 jit_solution(5013328746244364225)
XLA Ops:
  6.5 0.0 copy-start
  6.5 0.0 all-gather.3.cloned.1.call-start
  6.5 1.2 fusion.18
  7.7 0.2 slice_reduce_fusion.10
  7.9 0.1 broadcast_select_fusion.1
  8.0 1.2 copy.48
  9.2 1.3 fusion.24
  10.5 0.1 broadcast_in_dim.107
  10.6 1.9 %collective-permute-start = (f32[2,136,128]{2,1,0:T(8,128)S(1)}, f32[2,136,128]{2,1,0:T(8,128)S(1)}, u32[]{:S(2)}, u32[]{:S(2)}) collective-permute-start(f32[2,136,128]{2,1,0:T(8,128)S(1)} %pad_maximum_fusion.1), channel_id=1, source_target_pairs={{0,16},{16,0},{32,48},{48,32},{64,80},{80,64},{96,112},{112,96},{1... | collective-permute-start | bytes 417800 | tf_op jit(solution)/shard_map/ppermute | solution.py:48
  12.5 1.3 fusion.22
  13.8 0.0 copy-done
  13.8 4.0 %fusion.9 = f32[768,2,128]{2,0,1:T(8,128)} fusion(s32[2,768]{1,0:T(2,128)S(1)} %bitcast.80, bf16[768,2,128]{0,2,1:T(8,128)(2,1)S(1)} %bitcast.77, bf16[768,256]{1,0:T(8,128)(2,1)S(1)} %copy-done, bf16[768,256]{1,0:T(8,128)(2,1)} %param.9), kind=kOutput, calls=%fused_computation.8 | convolution fusion | flops 612237312 | bytes 1972224 | tf_op jit(solution)/shard_map/hts,shd->thd/dot_general | solution.py:98
  17.8 0.0 copy-start.3
  17.8 0.0 copy-start.2
  17.8 0.0 collective-permute-done
  17.8 0.1 slice_reduce_fusion.9
  17.9 0.1 fusion.55
  18.0 2.9 %collective-permute-start.3 = (bf16[2,136,128]{2,1,0:T(8,128)(2,1)S(1)}, bf16[2,136,128]{2,1,0:T(8,128)(2,1)S(1)}, u32[]{:S(2)}, u32[]{:S(2)}) collective-permute-start(bf16[2,136,128]{2,1,0:T(8,128)(2,1)S(1)} %get-tuple-element.17), channel_id=1, source_target_pairs={{0,96},{16,48},{32,0},{48,80},{64,32},{80,112},{96,64},{112,16},{1... | collective-permute-start | bytes 208904 | tf_op jit(solution)/shard_map/ppermute | solution.py:28
  20.9 8.4 %collective-permute-start.2 = (bf16[2,136,128]{2,1,0:T(8,128)(2,1)S(1)}, bf16[2,136,128]{2,1,0:T(8,128)(2,1)S(1)}, u32[]{:S(2)}, u32[]{:S(2)}) collective-permute-start(bf16[2,136,128]{2,1,0:T(8,128)(2,1)S(1)} %get-tuple-element.17), channel_id=1, source_target_pairs={{0,64},{16,80},{32,96},{48,112},{64,0},{80,16},{96,32},{112,48},{1... | collective-permute-start | bytes 208904 | tf_op jit(solution)/shard_map/ppermute | solution.py:28
  29.3 1.9 %collective-permute-start.1 = (bf16[2,136,128]{2,1,0:T(8,128)(2,1)S(1)}, bf16[2,136,128]{2,1,0:T(8,128)(2,1)S(1)}, u32[]{:S(2)}, u32[]{:S(2)}) collective-permute-start(bf16[2,136,128]{2,1,0:T(8,128)(2,1)S(1)} %get-tuple-element.17), channel_id=1, source_target_pairs={{0,32},{16,112},{32,64},{48,16},{64,96},{80,48},{96,0},{112,80},{1... | collective-permute-start | bytes 208904 | tf_op jit(solution)/shard_map/ppermute | solution.py:28
  31.2 0.1 slice_reduce_fusion.5
  31.3 4.2 %collective-permute-done.1 = bf16[2,136,128]{2,1,0:T(8,128)(2,1)S(1)} collective-permute-done((bf16[2,136,128]{2,1,0:T(8,128)(2,1)S(1)}, bf16[2,136,128]{2,1,0:T(8,128)(2,1)S(1)}, u32[]{:S(2)}, u32[]{:S(2)}) %collective-permute-start.1) | collective-permute-done | bytes 69664 | tf_op jit(solution)/shard_map/ppermute | solution.py:28
  35.5 0.1 fusion.44
  35.6 0.1 slice_reduce_fusion.4
  35.7 0.0 copy-start.1
  35.7 0.0 collective-permute-done.2
  35.7 0.1 add_select_fusion.3
  35.8 0.1 slice_reduce_fusion.3
  36.0 0.1 slice_reduce_fusion.8
  36.1 0.1 slice_reduce_fusion.7
  36.2 0.0 collective-permute-done.3
  36.2 0.1 slice_reduce_fusion.6
  36.3 0.2 select_convert_fusion
  36.5 1.9 %collective-permute-start.6 = (bf16[2,136,128]{2,1,0:T(8,128)(2,1)S(1)}, bf16[2,136,128]{2,1,0:T(8,128)(2,1)S(1)}, u32[]{:S(2)}, u32[]{:S(2)}) collective-permute-start(bf16[2,136,128]{2,1,0:T(8,128)(2,1)S(1)} %get-tuple-element.15), channel_id=1, source_target_pairs={{0,384},{16,144},{32,416},{48,176},{64,448},{80,208},{96,480},{112... | collective-permute-start | bytes 208904 | tf_op jit(solution)/shard_map/ppermute | solution.py:28
  38.4 1.9 %collective-permute-start.5 = (bf16[2,136,128]{2,1,0:T(8,128)(2,1)S(1)}, bf16[2,136,128]{2,1,0:T(8,128)(2,1)S(1)}, u32[]{:S(2)}, u32[]{:S(2)}) collective-permute-start(bf16[2,136,128]{2,1,0:T(8,128)(2,1)S(1)} %get-tuple-element.15), channel_id=1, source_target_pairs={{0,256},{16,272},{32,288},{48,304},{64,320},{80,336},{96,352},{112... | collective-permute-start | bytes 208904 | tf_op jit(solution)/shard_map/ppermute | solution.py:28
  40.3 3.9 %collective-permute-start.4 = (bf16[2,136,128]{2,1,0:T(8,128)(2,1)S(1)}, bf16[2,136,128]{2,1,0:T(8,128)(2,1)S(1)}, u32[]{:S(2)}, u32[]{:S(2)}) collective-permute-start(bf16[2,136,128]{2,1,0:T(8,128)(2,1)S(1)} %get-tuple-element.15), channel_id=1, source_target_pairs={{0,128},{16,400},{32,160},{48,432},{64,192},{80,464},{96,224},{112... | collective-permute-start | bytes 208904 | tf_op jit(solution)/shard_map/ppermute | solution.py:28
  44.3 0.1 slice_reduce_fusion.2
  44.4 0.0 collective-permute-done.6
  44.4 1.7 %collective-permute-done.5 = bf16[2,136,128]{2,1,0:T(8,128)(2,1)S(1)} collective-permute-done((bf16[2,136,128]{2,1,0:T(8,128)(2,1)S(1)}, bf16[2,136,128]{2,1,0:T(8,128)(2,1)S(1)}, u32[]{:S(2)}, u32[]{:S(2)}) %collective-permute-start.5) | collective-permute-done | bytes 69664 | tf_op jit(solution)/shard_map/ppermute | solution.py:28
  46.1 3.1 %collective-permute-done.4 = bf16[2,136,128]{2,1,0:T(8,128)(2,1)S(1)} collective-permute-done((bf16[2,136,128]{2,1,0:T(8,128)(2,1)S(1)}, bf16[2,136,128]{2,1,0:T(8,128)(2,1)S(1)}, u32[]{:S(2)}, u32[]{:S(2)}) %collective-permute-start.4) | collective-permute-done | bytes 69664 | tf_op jit(solution)/shard_map/ppermute | solution.py:28
  49.2 0.1 fusion.45
  49.3 0.1 slice_reduce_fusion.1
  49.4 0.1 add_select_fusion.1
  49.6 0.1 slice_reduce_fusion
  49.7 0.1 multiply_add_fusion
  49.8 1.9 %collective-permute-start.7 = (bf16[2,128,128]{2,1,0:T(8,128)(2,1)S(1)}, bf16[2,128,128]{2,1,0:T(8,128)(2,1)S(1)}, u32[]{:S(2)}, u32[]{:S(2)}) collective-permute-start(bf16[2,128,128]{2,1,0:T(8,128)(2,1)S(1)} %get-tuple-element.13), channel_id=1, source_target_pairs={{0,16},{16,0},{32,48},{48,32},{64,80},{80,64},{96,112},{112,96},{1... | collective-permute-start | bytes 196616 | tf_op jit(solution)/shard_map/ppermute | solution.py:70
  51.7 1.2 collective-permute-done.7
  52.9 0.3 fusion.11
  53.3 0.0 copy-done.2
  53.3 0.6 multiply_reduce_fusion
  53.8 0.0 copy-done.3
  53.8 1.0 fusion.21
  54.9 0.0 all-gather.3.cloned.1.call-update
  54.9 0.0 copy-done.1
  54.9 3.6 %reshape.56 = bf16[16,2,128,320]{2,1,0,3:T(2,128)(2,1)} reshape(bf16[4096,320]{0,1:T(8,128)(2,1)S(1)} %copy-done.1) | data formatting | bytes 5242880 | tf_op jit(solution)/shard_map/reshape | solution.py:137
  58.5 83.8 %all-gather.3.cloned.1.call-done = bf16[32,768,128]{2,1,0:T(8,128)(2,1)} async-done(((bf16[2,768,128]{2,1,0:T(8,128)(2,1)}), bf16[32,768,128]{2,1,0:T(8,128)(2,1)}) %all-gather.3.cloned.1.call-update) | async-done | bytes 6291472 | tf_op jit(solution)/shard_map/all_gather | solution.py:134
  142.2 6.8 %fusion.15 = bf16[768,320]{0,1:T(8,128)(2,1)} fusion(bf16[16,2,768,128]{3,2,1,0:T(8,128)(2,1)} %bitcast.82, bf16[16,2,128,320]{2,1,0,3:T(2,128)(2,1)} %reshape.56, bf16[768,320]{0,1:T(8,128)(2,1)} %param.13), kind=kOutput, calls=%fused_computation.14 | convolution fusion | flops 2014003200 | bytes 9895936 | tf_op jit(solution)/shard_map/dot_general | solution.py:135
  (13 shorter events, 0.1 us)
Async XLA Ops:
  6.5 7.2 %copy-start = (bf16[768,256]{1,0:T(8,128)(2,1)S(1)}, bf16[768,256]{1,0:T(8,128)(2,1)}, u32[]{:S(2)}) copy-start(bf16[768,256]{1,0:T(8,128)(2,1)} %param.7) | copy-start | bytes 1179652
  6.5 135.7 %all-gather.3.cloned.1.call-start = ((), (), s32[]{:S(2)}) async-start(), calls=%async_computation | async-start | bytes 6684672 | tf_op jit(solution)/shard_map/all_gather | solution.py:134
  10.6 7.2 %collective-permute-start = (f32[2,136,128]{2,1,0:T(8,128)S(1)}, f32[2,136,128]{2,1,0:T(8,128)S(1)}, u32[]{:S(2)}, u32[]{:S(2)}) collective-permute-start(f32[2,136,128]{2,1,0:T(8,128)S(1)} %pad_maximum_fusion.1), channel_id=1, source_target_pairs={{0,16},{16,0},{32,48},{48,32},{64,80},{80,64},{96,112},{112,96},{1... | collective-permute-start | bytes 417800 | tf_op jit(solution)/shard_map/ppermute | solution.py:48
  17.8 36.1 %copy-start.3 = (f32[256]{0:T(256)S(1)}, f32[256]{0:T(256)}, u32[]{:S(2)}) copy-start(f32[256]{0:T(256)} %param.11) | copy-start | bytes 3076
  17.8 35.5 %copy-start.2 = (f32[768,2,128]{2,0,1:T(8,128)S(1)}, f32[768,2,128]{2,0,1:T(8,128)}, u32[]{:S(2)}) copy-start(f32[768,2,128]{2,0,1:T(8,128)} %fusion.9) | copy-start | bytes 2359300
  18.0 18.2 %collective-permute-start.3 = (bf16[2,136,128]{2,1,0:T(8,128)(2,1)S(1)}, bf16[2,136,128]{2,1,0:T(8,128)(2,1)S(1)}, u32[]{:S(2)}, u32[]{:S(2)}) collective-permute-start(bf16[2,136,128]{2,1,0:T(8,128)(2,1)S(1)} %get-tuple-element.17), channel_id=1, source_target_pairs={{0,96},{16,48},{32,0},{48,80},{64,32},{80,112},{96,64},{112,16},{1... | collective-permute-start | bytes 208904 | tf_op jit(solution)/shard_map/ppermute | solution.py:28
  20.9 14.8 %collective-permute-start.2 = (bf16[2,136,128]{2,1,0:T(8,128)(2,1)S(1)}, bf16[2,136,128]{2,1,0:T(8,128)(2,1)S(1)}, u32[]{:S(2)}, u32[]{:S(2)}) collective-permute-start(bf16[2,136,128]{2,1,0:T(8,128)(2,1)S(1)} %get-tuple-element.17), channel_id=1, source_target_pairs={{0,64},{16,80},{32,96},{48,112},{64,0},{80,16},{96,32},{112,48},{1... | collective-permute-start | bytes 208904 | tf_op jit(solution)/shard_map/ppermute | solution.py:28
  29.3 6.2 %collective-permute-start.1 = (bf16[2,136,128]{2,1,0:T(8,128)(2,1)S(1)}, bf16[2,136,128]{2,1,0:T(8,128)(2,1)S(1)}, u32[]{:S(2)}, u32[]{:S(2)}) collective-permute-start(bf16[2,136,128]{2,1,0:T(8,128)(2,1)S(1)} %get-tuple-element.17), channel_id=1, source_target_pairs={{0,32},{16,112},{32,64},{48,16},{64,96},{80,48},{96,0},{112,80},{1... | collective-permute-start | bytes 208904 | tf_op jit(solution)/shard_map/ppermute | solution.py:28
  35.7 19.2 %copy-start.1 = (bf16[4096,320]{0,1:T(8,128)(2,1)S(1)}, bf16[4096,320]{0,1:T(8,128)(2,1)}, u32[]{:S(2)}) copy-start(bf16[4096,320]{0,1:T(8,128)(2,1)} %param.12) | copy-start | bytes 7864324
  36.5 7.9 %collective-permute-start.6 = (bf16[2,136,128]{2,1,0:T(8,128)(2,1)S(1)}, bf16[2,136,128]{2,1,0:T(8,128)(2,1)S(1)}, u32[]{:S(2)}, u32[]{:S(2)}) collective-permute-start(bf16[2,136,128]{2,1,0:T(8,128)(2,1)S(1)} %get-tuple-element.15), channel_id=1, source_target_pairs={{0,384},{16,144},{32,416},{48,176},{64,448},{80,208},{96,480},{112... | collective-permute-start | bytes 208904 | tf_op jit(solution)/shard_map/ppermute | solution.py:28
  38.4 7.7 %collective-permute-start.5 = (bf16[2,136,128]{2,1,0:T(8,128)(2,1)S(1)}, bf16[2,136,128]{2,1,0:T(8,128)(2,1)S(1)}, u32[]{:S(2)}, u32[]{:S(2)}) collective-permute-start(bf16[2,136,128]{2,1,0:T(8,128)(2,1)S(1)} %get-tuple-element.15), channel_id=1, source_target_pairs={{0,256},{16,272},{32,288},{48,304},{64,320},{80,336},{96,352},{112... | collective-permute-start | bytes 208904 | tf_op jit(solution)/shard_map/ppermute | solution.py:28
  40.3 8.9 %collective-permute-start.4 = (bf16[2,136,128]{2,1,0:T(8,128)(2,1)S(1)}, bf16[2,136,128]{2,1,0:T(8,128)(2,1)S(1)}, u32[]{:S(2)}, u32[]{:S(2)}) collective-permute-start(bf16[2,136,128]{2,1,0:T(8,128)(2,1)S(1)} %get-tuple-element.15), channel_id=1, source_target_pairs={{0,128},{16,400},{32,160},{48,432},{64,192},{80,464},{96,224},{112... | collective-permute-start | bytes 208904 | tf_op jit(solution)/shard_map/ppermute | solution.py:28
  49.8 3.1 %collective-permute-start.7 = (bf16[2,128,128]{2,1,0:T(8,128)(2,1)S(1)}, bf16[2,128,128]{2,1,0:T(8,128)(2,1)S(1)}, u32[]{:S(2)}, u32[]{:S(2)}) collective-permute-start(bf16[2,128,128]{2,1,0:T(8,128)(2,1)S(1)} %get-tuple-element.13), channel_id=1, source_target_pairs={{0,16},{16,0},{32,48},{48,32},{64,80},{80,64},{96,112},{112,96},{1... | collective-permute-start | bytes 196616 | tf_op jit(solution)/shard_map/ppermute | solution.py:70
Sparse Core Ops, SparseCore 0:
  55.0 87.1 all-gather.2

commit v17 on v15

--- a/solution.py
+++ b/solution.py
@@ -17,14 +17,15 @@
     )
 
 
-def gather_line(packed, line, stride, seq_count):
+def gather_line(packed, line, stride, seq_count, wrap=True):
     got = []
     for shift in range(1, line):
         pairs = []
         for i in range(seq_count):
             at = (i // stride) % line
             step = -shift if i % 2 else shift
-            pairs.append((i, i + (((at + step) % line) - at) * stride))
+            if wrap or 0 <= at + step < line:
+                pairs.append((i, i + (((at + step) % line) - at) * stride))
         got.append(lax.ppermute(packed, "seq", pairs))
     return got
 
@@ -62,7 +63,7 @@
         total = jnp.where(
             is_s, jnp.where(valid, decay_of(part) * total + part, total), total * decay_of(part)
         )
-    col = gather_line(total, line, 2 * line, seq_count)
+    col = gather_line(total, line, 2 * line, seq_count, wrap=False)
     col, extra = lax.optimization_barrier((col, extra))
     col_prefix = prefix(col, pos_y)
     state = (decay_of(row_prefix) * col_prefix + row_prefix)[:, :HD]

time: 159 us -> 156 us (0.981)
    ppermute x6, waiting for transfers between devices: 8.31 us -> 5.53 us  [gather_line(): got.append(lax.ppermute(packed, 'seq', pairs))]
  transfers between devices with their start and end apart: 9 -> 9, of which waited for: 4 -> 3; matrix products, arithmetic and copies ran while one was open for 5% -> 6% of each run, Pallas kernels for 0% -> 0%
where the time goes in v17:
time: 156 us
  waiting for transfers between devices  92.6 us (59%)
  starting transfers between devices  23.2 us (15%)
  matrix products  15.5 us (10%)
  between operations  13.7 us (9%)
  local copies, waits for them, and re-layouts  6 us (4%)
  other arithmetic  4.66 us (3%)
    all_gather x1, waiting for transfers between devices, local(): lax.all_gather(normed.transpose(1, 0, 2)[None], 'tp', axis=0, tiled=True)  85.9 us
    ppermute x6, starting transfers between devices, gather_line(): got.append(lax.ppermute(packed, 'seq', pairs))  19.4 us
    dot_general x1, matrix products, local(): lax.dot_general(gathered, out_weight.reshape(tp_count, head_count, HD, -1...  6.79 us
    ppermute x6, waiting for transfers between devices, gather_line(): got.append(lax.ppermute(packed, 'seq', pairs))  5.53 us
    reshape x1, local copies, waits for them, and re-layouts, local(): out_weight.reshape(tp_count, head_count, HD, -1)  3.55 us
  transfers between devices with their start and end apart: 9, of which 3 were waited for; matrix products, arithmetic and copies ran while one was open for 6% of the time, Pallas kernels for 0%

profile of v17, /device:TPU:6, one launch (start us, length us, event | category | flops | bytes accessed | tf_op | source)
XLA Modules:
  0.0 155.7 jit_solution(2825287222948664533)
XLA Ops:
  6.5 0.0 copy-start
  6.5 0.0 copy-start.3
  6.5 0.0 all-gather.3.cloned.1.call-start
  6.5 1.2 fusion.18
  7.8 0.2 slice_reduce_fusion.10
  8.0 0.1 broadcast_select_fusion.1
  8.1 1.2 copy.48
  9.2 1.3 fusion.24
  10.5 0.1 broadcast_in_dim.107
  10.6 1.9 %collective-permute-start = (f32[2,136,128]{2,1,0:T(8,128)S(1)}, f32[2,136,128]{2,1,0:T(8,128)S(1)}, u32[]{:S(2)}, u32[]{:S(2)}) collective-permute-start(f32[2,136,128]{2,1,0:T(8,128)S(1)} %pad_maximum_fusion.1), channel_id=1, source_target_pairs={{0,16},{16,0},{32,48},{48,32},{64,80},{80,64},{96,112},{112,96},{1... | collective-permute-start | bytes 417800 | tf_op jit(solution)/shard_map/ppermute | solution.py:48
  12.5 1.3 fusion.22
  13.8 0.0 collective-permute-done
  13.8 0.1 slice_reduce_fusion.9
  13.9 0.1 fusion.47
  14.0 7.8 %collective-permute-start.1 = (f32[2,136,128]{2,1,0:T(8,128)S(1)}, f32[2,136,128]{2,1,0:T(8,128)S(1)}, u32[]{:S(2)}, u32[]{:S(2)}) collective-permute-start(f32[2,136,128]{2,1,0:T(8,128)S(1)} %fusion.47), channel_id=1, source_target_pairs={{0,32},{16,112},{32,64},{48,16},{64,96},{80,48},{96,0},{112,80},{1... | collective-permute-start | bytes 417800 | tf_op jit(solution)/shard_map/ppermute | solution.py:29
  21.9 1.9 %collective-permute-start.3 = (f32[2,136,128]{2,1,0:T(8,128)S(1)}, f32[2,136,128]{2,1,0:T(8,128)S(1)}, u32[]{:S(2)}, u32[]{:S(2)}) collective-permute-start(f32[2,136,128]{2,1,0:T(8,128)S(1)} %fusion.47), channel_id=1, source_target_pairs={{0,96},{16,48},{32,0},{48,80},{64,32},{80,112},{96,64},{112,16},{1... | collective-permute-start | bytes 417800 | tf_op jit(solution)/shard_map/ppermute | solution.py:29
  23.8 3.4 %collective-permute-start.2 = (f32[2,136,128]{2,1,0:T(8,128)S(1)}, f32[2,136,128]{2,1,0:T(8,128)S(1)}, u32[]{:S(2)}, u32[]{:S(2)}) collective-permute-start(f32[2,136,128]{2,1,0:T(8,128)S(1)} %fusion.47), channel_id=1, source_target_pairs={{0,64},{16,80},{32,96},{48,112},{64,0},{80,16},{96,32},{112,48},{1... | collective-permute-start | bytes 417800 | tf_op jit(solution)/shard_map/ppermute | solution.py:29
  27.2 0.1 slice_reduce_fusion.5
  27.3 0.0 collective-permute-done.1
  27.3 0.1 fusion.44
  27.4 0.1 slice_reduce_fusion.4
  27.5 5.5 %collective-permute-done.2 = f32[2,136,128]{2,1,0:T(8,128)S(1)} collective-permute-done((f32[2,136,128]{2,1,0:T(8,128)S(1)}, f32[2,136,128]{2,1,0:T(8,128)S(1)}, u32[]{:S(2)}, u32[]{:S(2)}) %collective-permute-start.2) | collective-permute-done | bytes 139296 | tf_op jit(solution)/shard_map/ppermute | solution.py:29
  33.0 0.1 add_select_fusion.3
  33.1 0.1 slice_reduce_fusion.3
  33.2 0.1 slice_reduce_fusion.7
  33.3 0.1 slice_reduce_fusion.8
  33.4 0.0 collective-permute-done.3
  33.5 0.1 slice_reduce_fusion.6
  33.6 0.8 select_select_fusion
  34.4 2.3 %collective-permute-start.6 = (f32[2,136,128]{2,1,0:T(8,128)}, f32[2,136,128]{2,1,0:T(8,128)}, u32[]{:S(2)}, u32[]{:S(2)}) collective-permute-start(f32[2,136,128]{2,1,0:T(8,128)} %get-tuple-element.15), channel_id=1, source_target_pairs={{0,384},{32,416},{64,448},{96,480},{400,16},{432,48},{464,80},{496... | collective-permute-start | bytes 417800 | tf_op jit(solution)/shard_map/ppermute | solution.py:29
  36.7 1.9 %collective-permute-start.5 = (f32[2,136,128]{2,1,0:T(8,128)}, f32[2,136,128]{2,1,0:T(8,128)}, u32[]{:S(2)}, u32[]{:S(2)}) collective-permute-start(f32[2,136,128]{2,1,0:T(8,128)} %get-tuple-element.15), channel_id=1, source_target_pairs={{0,256},{32,288},{64,320},{96,352},{128,384},{160,416},{192,448},{... | collective-permute-start | bytes 417800 | tf_op jit(solution)/shard_map/ppermute | solution.py:29
  38.6 2.1 %collective-permute-start.4 = (f32[2,136,128]{2,1,0:T(8,128)}, f32[2,136,128]{2,1,0:T(8,128)S(1)}, u32[]{:S(2)}, u32[]{:S(2)}) collective-permute-start(f32[2,136,128]{2,1,0:T(8,128)} %get-tuple-element.15), channel_id=1, source_target_pairs={{0,128},{32,160},{64,192},{96,224},{128,256},{144,16},{160,288},{1... | collective-permute-start | bytes 417800 | tf_op jit(solution)/shard_map/ppermute | solution.py:29
  40.8 0.0 copy-done
  40.8 0.0 copy-done.3
  40.8 3.0 %fusion.9 = f32[768,2,128]{2,0,1:T(8,128)} fusion(s32[2,768]{1,0:T(2,128)S(1)} %bitcast.80, bf16[768,2,128]{0,2,1:T(8,128)(2,1)S(1)} %bitcast.77, bf16[768,256]{1,0:T(8,128)(2,1)S(1)} %copy-done, bf16[768,256]{1,0:T(8,128)(2,1)S(1)} %copy-done.3), kind=kOutput, calls=%fused_computation.8 | convolution fusion | flops 612237312 | bytes 1972224 | tf_op jit(solution)/shard_map/hts,shd->thd/dot_general | solution.py:98
  43.8 0.0 copy-start.2
  43.8 0.0 copy-start.1
  43.8 0.1 slice_reduce_fusion.2
  43.9 0.0 collective-permute-done.6
  43.9 0.0 collective-permute-done.5
  43.9 0.0 collective-permute-done.4
  43.9 0.1 fusion.45
  44.0 0.1 slice_reduce_fusion.1
  44.1 1.2 add_select_fusion.1
  45.3 0.1 slice_reduce_fusion
  45.4 1.0 multiply_add_fusion
  46.4 1.9 %collective-permute-start.7 = (bf16[2,128,128]{2,1,0:T(8,128)(2,1)S(1)}, bf16[2,128,128]{2,1,0:T(8,128)(2,1)S(1)}, u32[]{:S(2)}, u32[]{:S(2)}) collective-permute-start(bf16[2,128,128]{2,1,0:T(8,128)(2,1)S(1)} %get-tuple-element.13), channel_id=1, source_target_pairs={{0,16},{16,0},{32,48},{48,32},{64,80},{80,64},{96,112},{112,96},{1... | collective-permute-start | bytes 196616 | tf_op jit(solution)/shard_map/ppermute | solution.py:70
  48.4 1.2 collective-permute-done.7
  49.6 0.3 fusion.11
  49.9 1.7 %multiply_reduce_fusion = (f32[768,2]{0,1:T(2,128)S(1)}, f32[768,2,128]{2,0,1:T(8,128)S(1)}) fusion(f32[768,2]{0,1:T(2,128)S(1)} %get-tuple-element.18, bf16[2,128,128]{2,1,0:T(8,128)(2,1)S(1)} %get-tuple-element.14, bf16[2,128,128]{2,1,0:T(8,128)(2,1)S(1)} %collective-permute-done.7, pred[]{:T(512)S(6)} %eq.8, f32[768,2,128]{2,0,1:T(8,128)} %fusion.9, ...), kind=kOutput, calls=%fused_computation.21 | convolution fusion | flops 51345920 | bytes 2895873 | tf_op jit(solution)/shard_map/thd,hde->the/dot_general | solution.py:125
  51.6 0.0 copy-done.2
  51.6 1.0 fusion.21
  52.6 0.0 all-gather.3.cloned.1.call-update
  52.7 0.0 copy-done.1
  52.7 3.6 %reshape.56 = bf16[16,2,128,320]{2,1,0,3:T(2,128)(2,1)} reshape(bf16[4096,320]{0,1:T(8,128)(2,1)S(1)} %copy-done.1) | data formatting | bytes 5242880 | tf_op jit(solution)/shard_map/reshape | solution.py:137
  56.2 85.9 %all-gather.3.cloned.1.call-done = bf16[32,768,128]{2,1,0:T(8,128)(2,1)} async-done(((bf16[2,768,128]{2,1,0:T(8,128)(2,1)}), bf16[32,768,128]{2,1,0:T(8,128)(2,1)}) %all-gather.3.cloned.1.call-update) | async-done | bytes 6291472 | tf_op jit(solution)/shard_map/all_gather | solution.py:134
  142.1 6.8 %fusion.15 = bf16[768,320]{0,1:T(8,128)(2,1)} fusion(bf16[16,2,768,128]{3,2,1,0:T(8,128)(2,1)} %bitcast.82, bf16[16,2,128,320]{2,1,0,3:T(2,128)(2,1)} %reshape.56, bf16[768,320]{0,1:T(8,128)(2,1)} %param.13), kind=kOutput, calls=%fused_computation.14 | convolution fusion | flops 2014003200 | bytes 9895936 | tf_op jit(solution)/shard_map/dot_general | solution.py:135
  (7 shorter events, 0.1 us)
Async XLA Ops:
  6.5 34.2 %copy-start = (bf16[768,256]{1,0:T(8,128)(2,1)S(1)}, bf16[768,256]{1,0:T(8,128)(2,1)}, u32[]{:S(2)}) copy-start(bf16[768,256]{1,0:T(8,128)(2,1)} %param.7) | copy-start | bytes 1179652
  6.5 34.2 %copy-start.3 = (bf16[768,256]{1,0:T(8,128)(2,1)S(1)}, bf16[768,256]{1,0:T(8,128)(2,1)}, u32[]{:S(2)}) copy-start(bf16[768,256]{1,0:T(8,128)(2,1)} %param.9) | copy-start | bytes 1179652
  6.5 135.5 %all-gather.3.cloned.1.call-start = ((), (), s32[]{:S(2)}) async-start(), calls=%async_computation | async-start | bytes 6684672 | tf_op jit(solution)/shard_map/all_gather | solution.py:134
  10.6 3.3 %collective-permute-start = (f32[2,136,128]{2,1,0:T(8,128)S(1)}, f32[2,136,128]{2,1,0:T(8,128)S(1)}, u32[]{:S(2)}, u32[]{:S(2)}) collective-permute-start(f32[2,136,128]{2,1,0:T(8,128)S(1)} %pad_maximum_fusion.1), channel_id=1, source_target_pairs={{0,16},{16,0},{32,48},{48,32},{64,80},{80,64},{96,112},{112,96},{1... | collective-permute-start | bytes 417800 | tf_op jit(solution)/shard_map/ppermute | solution.py:48
  14.0 13.2 %collective-permute-start.1 = (f32[2,136,128]{2,1,0:T(8,128)S(1)}, f32[2,136,128]{2,1,0:T(8,128)S(1)}, u32[]{:S(2)}, u32[]{:S(2)}) collective-permute-start(f32[2,136,128]{2,1,0:T(8,128)S(1)} %fusion.47), channel_id=1, source_target_pairs={{0,32},{16,112},{32,64},{48,16},{64,96},{80,48},{96,0},{112,80},{1... | collective-permute-start | bytes 417800 | tf_op jit(solution)/shard_map/ppermute | solution.py:29
  21.9 11.6 %collective-permute-start.3 = (f32[2,136,128]{2,1,0:T(8,128)S(1)}, f32[2,136,128]{2,1,0:T(8,128)S(1)}, u32[]{:S(2)}, u32[]{:S(2)}) collective-permute-start(f32[2,136,128]{2,1,0:T(8,128)S(1)} %fusion.47), channel_id=1, source_target_pairs={{0,96},{16,48},{32,0},{48,80},{64,32},{80,112},{96,64},{112,16},{1... | collective-permute-start | bytes 417800 | tf_op jit(solution)/shard_map/ppermute | solution.py:29
  23.8 9.2 %collective-permute-start.2 = (f32[2,136,128]{2,1,0:T(8,128)S(1)}, f32[2,136,128]{2,1,0:T(8,128)S(1)}, u32[]{:S(2)}, u32[]{:S(2)}) collective-permute-start(f32[2,136,128]{2,1,0:T(8,128)S(1)} %fusion.47), channel_id=1, source_target_pairs={{0,64},{16,80},{32,96},{48,112},{64,0},{80,16},{96,32},{112,48},{1... | collective-permute-start | bytes 417800 | tf_op jit(solution)/shard_map/ppermute | solution.py:29
  34.4 9.5 %collective-permute-start.6 = (f32[2,136,128]{2,1,0:T(8,128)}, f32[2,136,128]{2,1,0:T(8,128)}, u32[]{:S(2)}, u32[]{:S(2)}) collective-permute-start(f32[2,136,128]{2,1,0:T(8,128)} %get-tuple-element.15), channel_id=1, source_target_pairs={{0,384},{32,416},{64,448},{96,480},{400,16},{432,48},{464,80},{496... | collective-permute-start | bytes 417800 | tf_op jit(solution)/shard_map/ppermute | solution.py:29
  36.7 7.2 %collective-permute-start.5 = (f32[2,136,128]{2,1,0:T(8,128)}, f32[2,136,128]{2,1,0:T(8,128)}, u32[]{:S(2)}, u32[]{:S(2)}) collective-permute-start(f32[2,136,128]{2,1,0:T(8,128)} %get-tuple-element.15), channel_id=1, source_target_pairs={{0,256},{32,288},{64,320},{96,352},{128,384},{160,416},{192,448},{... | collective-permute-start | bytes 417800 | tf_op jit(solution)/shard_map/ppermute | solution.py:29
  38.6 5.2 %collective-permute-start.4 = (f32[2,136,128]{2,1,0:T(8,128)}, f32[2,136,128]{2,1,0:T(8,128)S(1)}, u32[]{:S(2)}, u32[]{:S(2)}) collective-permute-start(f32[2,136,128]{2,1,0:T(8,128)} %get-tuple-element.15), channel_id=1, source_target_pairs={{0,128},{32,160},{64,192},{96,224},{128,256},{144,16},{160,288},{1... | collective-permute-start | bytes 417800 | tf_op jit(solution)/shard_map/ppermute | solution.py:29
  43.8 7.8 %copy-start.2 = (f32[256]{0:T(256)S(1)}, f32[256]{0:T(256)}, u32[]{:S(2)}) copy-start(f32[256]{0:T(256)} %param.11) | copy-start | bytes 3076
  43.8 8.9 %copy-start.1 = (bf16[4096,320]{0,1:T(8,128)(2,1)S(1)}, bf16[4096,320]{0,1:T(8,128)(2,1)}, u32[]{:S(2)}) copy-start(bf16[4096,320]{0,1:T(8,128)(2,1)} %param.12) | copy-start | bytes 7864324
  46.4 3.1 %collective-permute-start.7 = (bf16[2,128,128]{2,1,0:T(8,128)(2,1)S(1)}, bf16[2,128,128]{2,1,0:T(8,128)(2,1)S(1)}, u32[]{:S(2)}, u32[]{:S(2)}) collective-permute-start(bf16[2,128,128]{2,1,0:T(8,128)(2,1)S(1)} %get-tuple-element.13), channel_id=1, source_target_pairs={{0,16},{16,0},{32,48},{48,32},{64,80},{80,64},{96,112},{112,96},{1... | collective-permute-start | bytes 196616 | tf_op jit(solution)/shard_map/ppermute | solution.py:70
Sparse Core Ops, SparseCore 0:
  52.8 89.2 all-gather.2
